TPU v7x, 128 devices: a whole 4x4x4 slice. The times are simulated.
128 devices in a mesh: trace: 8 (over x, core), seq: 16 (over y, z).
Axes of the slice: x: 4, y: 4, z: 4, core: 2. Of those that a mesh axis runs over, the one named last changes fastest.
Arguments:
- tokens: bfloat16 [131072, 1024], P(('trace', 'seq')), parts along dimension 0, may hold values from -6 to 6
- norm_gain: float32 [1024], replicated, may hold values from 0.1 to 1.9
- w_qkv: bfloat16 [1024, 3072], replicated, may hold values from -0.02734375 to 0.02734375
- conv_weight: float32 [4, 3072], replicated, may hold values from -3 to 3
- head_gain: float32 [1024], replicated, may hold values from 0.1 to 1.9
- w_out: bfloat16 [1024, 1024], replicated, may hold values from -0.1875 to 0.1875
Outputs:
- layer_out: bfloat16 [131072, 1024], P(('trace', 'seq')), parts along dimension 0
There are 8 independent parts, one for each index of `trace`. A program takes and returns all parts, laid end to end along the dimension named above; an argument that names none is the same for every part. Nothing has to cross between parts.
All inputs are finite; a program needn't handle non-finite values.
Results may differ from a plain program's by a relative error of at most 0.012.
Values may be sent and summed in bfloat16 or wider, within the bound.
No kernel may reach another device: no remote copies, remote signals or barrier semaphores. Data moves between devices by JAX's collectives and lax.ppermute only.
A program may use at most 128 MiB of HBM per device.

v0:
```python
import jax
import jax.numpy as jnp
from jax import lax
from jax.sharding import PartitionSpec as P

H = 8
DH = 128
KW = 4


def from_behind(value, axis, steps):
    count = lax.axis_size(axis)
    first, last = (max(0, -steps), min(count, count - steps))
    return lax.ppermute(value, axis, [(source, source + steps) for source in range(first, last)])


def entering(x, axis, join, neutral):
    place = lax.axis_index(axis)
    gathered = lax.all_gather(x.astype(jnp.bfloat16), axis)
    state = jnp.zeros_like(x) + jnp.asarray(neutral, x.dtype)

    def one(hop, state):
        return join(state, lax.dynamic_index_in_dim(gathered, hop, 0, False).astype(x.dtype))

    return lax.fori_loop(0, place, one, state)


def input_norm(values, norm_gain):
    values_f = values.astype(jnp.float32)
    scale = lax.rsqrt(jnp.mean(values_f * values_f, -1, keepdims=True) + 1e-06)
    return (values_f * scale * norm_gain).astype(jnp.bfloat16)


def add_states(earlier, later):
    return earlier + later


def local(tokens, norm_gain, w_qkv, conv_weight, head_gain, w_out):
    row_count = tokens.shape[0]
    model_width = tokens.shape[1]
    normed = input_norm(tokens, norm_gain)
    projected = jnp.dot(normed, w_qkv, preferred_element_type=jnp.float32).astype(jnp.bfloat16)
    earlier_rows = from_behind(projected[row_count - (KW - 1) :], "seq", 1)
    padded = jnp.concatenate([earlier_rows, projected], 0)
    summed = jnp.zeros(projected.shape, jnp.float32)
    for offset in range(KW):
        begin = KW - 1 - offset
        summed = summed + conv_weight[offset] * padded[begin : begin + row_count].astype(
            jnp.float32
        )
    mixed = jax.nn.silu(summed).astype(jnp.bfloat16)
    block_rows = min(512, row_count)
    count = row_count // block_rows
    query_rows = mixed[:, :model_width].reshape(count, block_rows, H, DH)
    key_rows = mixed[:, model_width : 2 * model_width].reshape(count, block_rows, H, DH)
    value_rows = mixed[:, 2 * model_width :].reshape(count, block_rows, H, DH)
    block_states = jnp.einsum(
        "bthd,bthe->bhde", key_rows, value_rows, preferred_element_type=jnp.float32
    )
    local_state = jnp.sum(block_states, 0)
    empty_state = jnp.zeros((H, DH, DH), jnp.float32)
    prefix = entering(local_state, "seq", add_states, empty_state)
    causal = jnp.tril(jnp.ones((block_rows, block_rows), jnp.bool_))

    def advance(carried, blocks):
        query_block, key_block, value_block, block_state = blocks
        carried_part = jnp.einsum(
            "thd,hde->the",
            query_block.astype(jnp.float32),
            carried,
            precision=lax.Precision.HIGHEST,
        )
        scores = jnp.einsum(
            "thd,shd->hts", query_block, key_block, preferred_element_type=jnp.float32
        )
        scores = jnp.where(causal[None], scores, 0.0).astype(jnp.bfloat16)
        local_part = jnp.einsum(
            "hts,she->the", scores, value_block, preferred_element_type=jnp.float32
        )
        return (carried + block_state, carried_part + local_part)

    _, attended = lax.scan(advance, prefix, (query_rows, key_rows, value_rows, block_states))
    attended = attended.reshape(row_count, H, DH)
    scaled = attended * lax.rsqrt(jnp.mean(attended * attended, -1, keepdims=True) + 1e-05)
    headed = (scaled.reshape(row_count, model_width) * head_gain).astype(jnp.bfloat16)
    return jnp.dot(headed, w_out, preferred_element_type=jnp.float32).astype(jnp.bfloat16)


def solution(mesh):
    placed = (P(("trace", "seq"), None), P(), P(), P(), P(), P())
    return jax.shard_map(
        local, mesh=mesh, in_specs=placed, out_specs=P(("trace", "seq"), None), check_vma=False
    )
```

profile of v0, /device:TPU:120, one launch (start us, length us, event | category | flops | bytes accessed | tf_op | source)
XLA Modules:
  0.0 165.6 jit_solution(15872454961483827567)
XLA Ops:
  6.5 2.2 %fusion.12 = f32[1024]{0:T(1024)S(1)} fusion(bf16[1024,1024]{1,0:T(8,128)(2,1)} %param.10), kind=kLoop, calls=%fused_computation.28 | loop fusion | flops 3144704 | bytes 2101248 | tf_op jit(solution)/shard_map/reduce_sum | solution.py:30
  8.8 9.6 %convolution_convert_fusion = bf16[1024,3072]{1,0:T(8,128)(2,1)S(1)} fusion(bf16[1024,3072]{1,0:T(8,128)(2,1)} %param.12, bf16[1024,1024]{1,0:T(8,128)(2,1)} %param.10, f32[1024]{0:T(1024)} %param.11, f32[1024]{0:T(1024)S(1)} %add_rsqrt_fusion.1), kind=kOutput, calls=%fused_computation.25 | convolution fusion | flops 6449790976 | bytes 14688256 | tf_op jit(solution)/shard_map/dot_general | solution.py:42
  18.4 1.3 collective-permute-start
  19.7 4.4 %collective-permute-done = bf16[3,3072]{1,0:T(4,128)(2,1)S(1)} collective-permute-done((bf16[3,3072]{1,0:T(4,128)(2,1)S(1)}, bf16[3,3072]{1,0:T(4,128)(2,1)S(1)}, u32[]{:S(2)}, u32[]{:S(2)}) %collective-permute-start) | collective-permute-done | bytes 18464 | tf_op jit(solution)/shard_map/ppermute | solution.py:14
  24.1 8.6 %multiply_convert_fusion = bf16[1024,3072]{1,0:T(8,128)(2,1)S(1)} fusion(bf16[1024,3072]{1,0:T(8,128)(2,1)S(1)} %convolution_convert_fusion, bf16[3,3072]{1,0:T(4,128)(2,1)S(1)} %collective-permute-done, f32[3072]{0:T(1024)S(1)} %bitcast.94, f32[3072]{0:T(1024)S(1)} %bitcast.95, f32[3072]{0:T(1024)S(1)} %bitcast.93, f32[3072]{0:T(1024)S(1)} %bitcast.92), kind=kLoop, calls=%fused_computation.19 | loop fusion | flops 78643200 | bytes 12650496 | tf_op jit(solution)/shard_map/convert_element_type | solution.py:51
  32.7 3.5 %slice_bitcast_fusion = (bf16[128,8,8,128]{3,1,2,0:T(8,128)(2,1)}, bf16[128,8,8,128]{3,1,2,0:T(8,128)(2,1)S(1)}, bf16[128,8,8,128]{3,1,2,0:T(8,128)(2,1)S(1)}) fusion(bf16[1024,3072]{1,0:T(8,128)(2,1)S(1)} %multiply_convert_fusion), kind=kLoop, calls=%fused_computation.36 | loop fusion | bytes 12582912
  36.3 0.6 copy.37
  36.9 0.6 copy.38
  37.5 1.4 copy-done.3
  38.9 2.9 %fusion.30 = (bf16[8,128,128]{2,1,0:T(8,128)(2,1)}, f32[2,8,128,128]{3,2,1,0:T(8,128)}) fusion(bf16[2,512,8,128]{3,2,1,0:T(8,128)(2,1)S(1)} %bitcast.85, bf16[2,512,8,128]{3,2,1,0:T(8,128)(2,1)S(1)} %bitcast.83), kind=kOutput, calls=%fused_computation.49 | convolution fusion | flops 268566528 | bytes 5505024 | tf_op jit(solution)/shard_map/bthd,bthe->bhde/dot_general | solution.py:57
  41.8 3.6 %copy.39 = bf16[128,8,8,128]{3,2,1,0:T(8,128)(2,1)} copy(bf16[128,8,8,128]{3,1,2,0:T(8,128)(2,1)} %get-tuple-element.140) | data formatting | bytes 4194304
  45.4 47.2 %all-gather.3.cloned.1.call-done = bf16[128,128,128]{2,1,0:T(8,128)(2,1)} async-done(((bf16[8,128,128]{2,1,0:T(8,128)(2,1)}), bf16[128,128,128]{2,1,0:T(8,128)(2,1)}) %all-gather.3.cloned.1.call-update) | async-done | bytes 4194320 | tf_op jit(solution)/shard_map/all_gather | solution.py:19
  92.6 16.6 %while.23 = (s32[]{:T(128)}, f32[8,128,128]{2,1,0:T(8,128)S(1)}, s32[]{:T(128)}, bf16[16,8,128,128]{3,2,1,0:T(8,128)(2,1)}, s32[]{:T(128)}, /*index=5*/s32[]{:T(128)}, s32[]{:T(128)}) while((s32[]{:T(128)}, f32[8,128,128]{2,1,0:T(8,128)S(1)}, s32[]{:T(128)}, bf16[16,8,128,128]{3,2,1,0:T(8,128)(2,1)}, s32[]{:T(128)}, /*index=5*/s32[]{:T(128)}, ...), condition=%wide.region_3.4_spmd, body=%wide.region_2.3_spmd.sunk | while | flops 262149 | bytes 1310835 | solution.py:25
  92.6 1.1 convert_add_fusion.2
  93.7 1.1 convert_add_fusion.2
  94.8 1.1 convert_add_fusion.2
  95.9 1.1 convert_add_fusion.2
  97.0 1.1 convert_add_fusion.2
  98.1 1.1 convert_add_fusion.2
  99.2 1.1 convert_add_fusion.2
  100.3 1.1 convert_add_fusion.2
  101.4 1.1 convert_add_fusion.2
  102.5 1.1 convert_add_fusion.2
  103.6 1.1 convert_add_fusion.2
  104.6 1.1 convert_add_fusion.2
  105.7 1.1 convert_add_fusion.2
  106.8 1.1 convert_add_fusion.2
  107.9 1.1 convert_add_fusion.2
  109.2 35.1 %while.24 = (s32[]{:T(128)}, f32[8,128,128]{2,1,0:T(8,128)S(1)}, f32[2,512,8,128]{3,1,2,0:T(8,128)}, f32[2,8,128,128]{3,2,1,0:T(8,128)}, bf16[2,512,8,128]{3,2,1...) while((s32[]{:T(128)}, f32[8,128,128]{2,1,0:T(8,128)S(1)}, ...), condition=%wide.region_5.6_spmd.clone, body=%wide.region_4.5_spmd.clone.sunk | while | flops 1884160000 | bytes 25690748 | solution.py:82
  109.2 3.0 %constant_dynamic-slice_fusion.6 = (bf16[1,512,8,128]{3,2,1,0:T(8,128)(2,1)}, bf16[1,512,8,128]{3,2,1,0:T(8,128)(2,1)}) fusion(bf16[2,512,8,128]{3,2,1,0:T(8,128)(2,1)} %get-tuple-element.265, s32[]{:T(128)} %get-tuple-element.251, bf16[2,512,8,128]{3,2,1,0:T(8,128)(2,1)} %get-tuple-element.264), kind=kLoop, calls=%fused_computation.15.clone.1 | loop fusion | bytes 4194308 | tf_op jit(solution)/shard_map/while/body/jit(dynamic_index_in_dim)/dynamic_slice | solution.py:82
  112.2 2.5 %copy.72 = bf16[1,512,8,128]{1,3,2,0:T(8,128)(2,1)} copy(bf16[1,512,8,128]{3,2,1,0:T(8,128)(2,1)} %get-tuple-element.221) | data formatting | bytes 2097152 | tf_op jit(solution)/shard_map/while/body/jit(dynamic_index_in_dim)/dynamic_slice | solution.py:82
  114.7 1.3 constant_dynamic-slice_fusion.5
  116.0 1.0 copy-done.1
  117.0 2.3 %fusion.39 = f32[8,512,128]{2,1,0:T(8,128)} fusion(f32[8,128,128]{2,1,0:T(8,128)S(1)} %get-tuple-element.252, bf16[1,512,8,128]{3,2,1,0:T(8,128)(2,1)S(1)} %constant_dynamic-slice_fusion.5), kind=kOutput, calls=%fused_computation.13.clone.1 | convolution fusion | flops 805306368 | bytes 3670016 | tf_op jit(solution)/shard_map/while/body/eval_jaxpr/thd,hde->the/dot_general | solution.py:67
  119.4 6.3 %bitcast_dynamic-update-slice_fusion.2 = f32[2,512,8,128]{3,1,2,0:T(8,128)} fusion(f32[2,512,8,128]{3,1,2,0:T(8,128)} %get-tuple-element.253, s32[]{:T(128)} %get-tuple-element.251, f32[8,512,128]{2,1,0:T(8,128)} %fusion.39, pred[512,512]{1,0:T(8,128)(4,1)S(1)} %iota_compare_fusion.2, bf16[1,512,8,128]{3,2,1,0:T(8,128)(2,1)} %get-tuple-element.220, ...), kind=kOutput, calls=%fused_computation.7.clone.1 | convolution fusion | flops 1078460416 | bytes 7602688 | tf_op jit(solution)/shard_map/while/body/eval_jaxpr/hts,she->the/dot_general | solution.py:77
  125.6 1.2 bitcast_add_fusion.3
  126.8 3.0 %constant_dynamic-slice_fusion.6 = (bf16[1,512,8,128]{3,2,1,0:T(8,128)(2,1)}, bf16[1,512,8,128]{3,2,1,0:T(8,128)(2,1)}) fusion(bf16[2,512,8,128]{3,2,1,0:T(8,128)(2,1)} %get-tuple-element.265, s32[]{:T(128)} %get-tuple-element.251, bf16[2,512,8,128]{3,2,1,0:T(8,128)(2,1)} %get-tuple-element.264), kind=kLoop, calls=%fused_computation.15.clone.1 | loop fusion | bytes 4194308 | tf_op jit(solution)/shard_map/while/body/jit(dynamic_index_in_dim)/dynamic_slice | solution.py:82
  129.8 2.5 %copy.72 = bf16[1,512,8,128]{1,3,2,0:T(8,128)(2,1)} copy(bf16[1,512,8,128]{3,2,1,0:T(8,128)(2,1)} %get-tuple-element.221) | data formatting | bytes 2097152 | tf_op jit(solution)/shard_map/while/body/jit(dynamic_index_in_dim)/dynamic_slice | solution.py:82
  132.3 1.3 constant_dynamic-slice_fusion.5
  133.6 1.0 copy-done.1
  134.6 2.3 %fusion.39 = f32[8,512,128]{2,1,0:T(8,128)} fusion(f32[8,128,128]{2,1,0:T(8,128)S(1)} %get-tuple-element.252, bf16[1,512,8,128]{3,2,1,0:T(8,128)(2,1)S(1)} %constant_dynamic-slice_fusion.5), kind=kOutput, calls=%fused_computation.13.clone.1 | convolution fusion | flops 805306368 | bytes 3670016 | tf_op jit(solution)/shard_map/while/body/eval_jaxpr/thd,hde->the/dot_general | solution.py:67
  136.9 6.2 %bitcast_dynamic-update-slice_fusion.2 = f32[2,512,8,128]{3,1,2,0:T(8,128)} fusion(f32[2,512,8,128]{3,1,2,0:T(8,128)} %get-tuple-element.253, s32[]{:T(128)} %get-tuple-element.251, f32[8,512,128]{2,1,0:T(8,128)} %fusion.39, pred[512,512]{1,0:T(8,128)(4,1)S(1)} %iota_compare_fusion.2, bf16[1,512,8,128]{3,2,1,0:T(8,128)(2,1)} %get-tuple-element.220, ...), kind=kOutput, calls=%fused_computation.7.clone.1 | convolution fusion | flops 1078460416 | bytes 7602688 | tf_op jit(solution)/shard_map/while/body/eval_jaxpr/hts,she->the/dot_general | solution.py:77
  143.2 1.2 bitcast_add_fusion.3
  144.4 3.5 %multiply_reduce_fusion = f32[2,512,8]{1,2,0:T(8,128)S(1)} fusion(f32[2,512,8,128]{3,1,2,0:T(8,128)} %get-tuple-element.71), kind=kLoop, calls=%fused_computation.34 | loop fusion | flops 2088960 | bytes 4227072 | tf_op jit(solution)/shard_map/reduce_sum | solution.py:84
  147.9 4.4 %copy.31 = f32[2,512,8,128]{3,2,1,0:T(8,128)} copy(f32[2,512,8,128]{3,1,2,0:T(8,128)S(1)} %copy-done.4) | data formatting | bytes 8388608 | tf_op jit(solution)/shard_map/while | solution.py:82
  152.5 1.1 mul.105
  153.6 1.0 copy-done.5
  154.7 4.1 %fusion.26 = bf16[1024,1024]{1,0:T(8,128)(2,1)} fusion(bf16[1024,1024]{1,0:T(8,128)(2,1)S(1)} %copy-done, f32[128,8,8,128]{3,2,1,0:T(8,128)S(1)} %bitcast.88, f32[128,8,8,128]{3,2,1,0:T(8,128)S(1)} %bitcast.89, f32[1024]{0:T(1024)S(1)} %copy-done.7), kind=kOutput, calls=%fused_computation.45 | convolution fusion | flops 2151677952 | bytes 12587008 | tf_op jit(solution)/shard_map/dot_general | solution.py:86
  (25 shorter events, 0.5 us)
Async XLA Ops:
  6.5 147.1 %copy-start = (bf16[1024,1024]{1,0:T(8,128)(2,1)S(1)}, bf16[1024,1024]{1,0:T(8,128)(2,1)}, u32[]{:S(2)}) copy-start(bf16[1024,1024]{1,0:T(8,128)(2,1)} %param.15) | copy-start | bytes 6291460
  6.5 86.0 %all-gather.3.cloned.1.call-start = ((), (), s32[]{:S(2)}) async-start(), calls=%async_computation | async-start | bytes 4456448 | tf_op jit(solution)/shard_map/all_gather | solution.py:19
  8.8 10.9 %copy-start.6 = (f32[4,3072]{1,0:T(4,128)S(1)}, f32[4,3072]{1,0:T(4,128)}, u32[]{:S(2)}) copy-start(f32[4,3072]{1,0:T(4,128)} %param.13) | copy-start | bytes 147460
  18.4 5.7 %collective-permute-start = (bf16[3,3072]{1,0:T(4,128)(2,1)S(1)}, bf16[3,3072]{1,0:T(4,128)(2,1)S(1)}, u32[]{:S(2)}, u32[]{:S(2)}) collective-permute-start(bf16[3,3072]{1,0:T(4,128)(2,1)S(1)} %slice.44), channel_id=1, source_target_pairs={{0,1},{1,2},{2,3},{3,4},{4,5},{5,6},{6,7},{7,8},{8,9},{9,10},{10,1... | collective-permute-start | bytes 55304 | tf_op jit(solution)/shard_map/ppermute | solution.py:14
  36.9 4.9 %copy-start.2 = (bf16[128,8,8,128]{3,2,1,0:T(8,128)(2,1)}, bf16[128,8,8,128]{3,2,1,0:T(8,128)(2,1)S(1)}, u32[]{:S(2)}) copy-start(bf16[128,8,8,128]{3,2,1,0:T(8,128)(2,1)S(1)} %copy.37) | copy-start | bytes 6291460
  37.5 1.4 copy-start.3
  116.0 1.0 copy-start.1
  133.6 1.0 copy-start.1
  144.4 3.5 %copy-start.4 = (f32[2,512,8,128]{3,1,2,0:T(8,128)S(1)}, f32[2,512,8,128]{3,1,2,0:T(8,128)}, u32[]{:S(2)}) copy-start(f32[2,512,8,128]{3,1,2,0:T(8,128)} %get-tuple-element.71) | copy-start | bytes 12582916
  152.2 1.4 copy-start.7
  152.5 2.2 %copy-start.5 = (f32[2,512,8,128]{3,2,1,0:T(8,128)S(1)}, f32[2,512,8,128]{3,2,1,0:T(8,128)}, u32[]{:S(2)}) copy-start(f32[2,512,8,128]{3,2,1,0:T(8,128)} %copy.31) | copy-start | bytes 12582916
Sparse Core Ops, SparseCore 0:
  41.9 50.5 all-gather.2
where the time goes:
time: 166 us
  waiting for transfers between devices  51.5 us (31%)
  matrix products  33.6 us (20%)
  other arithmetic  32.9 us (20%)
  local copies, waits for them, and re-layouts  32 us (19%)
  between operations  13.6 us (8%)
    all_gather x1, waiting for transfers between devices, entering(): gathered = lax.all_gather(x.astype(jnp.bfloat16), axis)  47.2 us
    add x15, other arithmetic, add_states(): return earlier + later  16 us
    dynamic_slice x6, local copies, waits for them, and re-layouts, local(): lax.scan(advance, prefix, (query_rows, key_rows, value_rows, block_states))  13.5 us
    dot_general x2, matrix products, advance(): jnp.einsum('hts,she->the', scores, value_block, preferred_element_type=jn...  12.5 us
    unnamed x18, local copies, waits for them, and re-layouts  10.7 us
    dot_general x1, matrix products, local(): jnp.dot(normed, w_qkv, preferred_element_type=jnp.float32)  9.55 us
    convert_element_type x1, other arithmetic, local(): mixed = jax.nn.silu(summed).astype(jnp.bfloat16)  8.64 us
    dot_general x2, matrix products, advance(): jnp.einsum('thd,hde->the', query_block.astype(jnp.float32), carried, prec...  4.6 us
  transfers between devices with their start and end apart: 2, of which 2 were waited for; matrix products, arithmetic and copies ran while one was open for 2% of the time, Pallas kernels for 0%

commit v1 on v0

v1 whole, which is shorter than its diff:
```python
import jax
import jax.numpy as jnp
from jax import lax
from jax.sharding import Mesh
from jax.sharding import PartitionSpec as P

H = 8
DH = 128
KW = 4
BLOCK = 512


def split_bf16(x):
    hi = x.astype(jnp.bfloat16)
    lo = (x - hi.astype(jnp.float32)).astype(jnp.bfloat16)
    return hi, lo


def earlier_sum(gathered, axis):
    place = lax.axis_index(axis)
    count = gathered.shape[0]
    mask = (lax.iota(jnp.int32, count) < place).astype(jnp.float32)
    values = gathered.astype(jnp.float32)
    before = jnp.sum(values * mask[:, None, None, None], 0)
    return before, jnp.sum(values, 0)


def local(tokens, norm_gain, w_qkv, conv_weight, head_gain, w_out):
    rows, width = tokens.shape
    tokens_f = tokens.astype(jnp.float32)
    scale = lax.rsqrt(jnp.mean(tokens_f * tokens_f, -1, keepdims=True) + 1e-06)
    normed = (tokens_f * scale * norm_gain).astype(jnp.bfloat16)

    slabs = w_qkv.shape[1] // DH
    projected = jnp.einsum(
        "td,dje->jte", normed, w_qkv.reshape(width, slabs, DH), preferred_element_type=jnp.float32
    ).astype(jnp.bfloat16)

    seq_axes = ("sy", "sz")
    count = lax.axis_size("sy") * lax.axis_size("sz")
    earlier_rows = lax.ppermute(
        projected[:, rows - (KW - 1) :, :], seq_axes, [(i, i + 1) for i in range(count - 1)]
    )
    padded = jnp.concatenate([earlier_rows, projected], 1)
    taps = conv_weight.reshape(KW, slabs, 1, DH)
    summed = jnp.zeros(projected.shape, jnp.float32)
    for offset in range(KW):
        begin = KW - 1 - offset
        summed = summed + taps[offset] * padded[:, begin : begin + rows].astype(jnp.float32)
    mixed = jax.nn.silu(summed).astype(jnp.bfloat16)

    block = min(BLOCK, rows)
    nb = rows // block
    query = mixed[:H].reshape(H, nb, block, DH)
    key = mixed[H : 2 * H].reshape(H, nb, block, DH)
    value = mixed[2 * H :].reshape(H, nb, block, DH)

    block_states = jnp.einsum("hbsd,hbse->bhde", key, value, preferred_element_type=jnp.float32)
    inner = jnp.concatenate(
        [jnp.zeros_like(block_states[:1]), jnp.cumsum(block_states, 0)[:-1]], 0
    )
    state = jnp.sum(block_states, 0)

    zbefore, row_total = earlier_sum(lax.all_gather(state.astype(jnp.bfloat16), "sz"), "sz")
    ybefore, _ = earlier_sum(lax.all_gather(row_total.astype(jnp.bfloat16), "sy"), "sy")
    prefix = ybefore + zbefore

    causal = jnp.tril(jnp.ones((block, block), jnp.bool_))
    scores = jnp.einsum("hbtd,hbsd->hbts", query, key, preferred_element_type=jnp.float32)
    scores = jnp.where(causal, scores, 0.0).astype(jnp.bfloat16)
    local_part = jnp.einsum("hbts,hbse->hbte", scores, value, preferred_element_type=jnp.float32)

    carried = prefix[None] + inner
    carried_hi, carried_lo = split_bf16(carried)
    carried_part = jnp.einsum(
        "hbtd,bhde->hbte", query, carried_hi, preferred_element_type=jnp.float32
    ) + jnp.einsum("hbtd,bhde->hbte", query, carried_lo, preferred_element_type=jnp.float32)
    attended = (local_part + carried_part).reshape(H, rows, DH)

    scaled = attended * lax.rsqrt(jnp.mean(attended * attended, -1, keepdims=True) + 1e-05)
    headed = (scaled * head_gain.reshape(H, 1, DH)).astype(jnp.bfloat16)
    out = jnp.einsum(
        "hte,hen->tn", headed, w_out.reshape(H, DH, width), preferred_element_type=jnp.float32
    )
    return out.astype(jnp.bfloat16)


def solution(mesh):
    seq = mesh.shape["seq"]
    inner = 4 if seq % 4 == 0 else 1
    grid = Mesh(
        mesh.devices.reshape(mesh.shape["trace"], seq // inner, inner), ("trace", "sy", "sz")
    )
    rows = P(("trace", "sy", "sz"), None)
    placed = (rows, P(), P(), P(), P(), P())
    return jax.shard_map(local, mesh=grid, in_specs=placed, out_specs=rows, check_vma=False)
```

time: 166 us -> 127 us (0.77)
  the two profiles are of different devices: /device:TPU:120 before, /device:TPU:0 now
where the time goes in v1:
time: 127 us
  waiting for transfers between devices  49.6 us (39%)
  matrix products  32.7 us (26%)
  other arithmetic  22.6 us (18%)
  between operations  13.6 us (11%)
  local copies, waits for them, and re-layouts  4.26 us (3%)
  starting transfers between devices  4.12 us (3%)
    all_gather x1, waiting for transfers between devices, local(): lax.all_gather(state.astype(jnp.bfloat16), 'sz')  26.9 us
    all_gather x1, waiting for transfers between devices, local(): lax.all_gather(row_total.astype(jnp.bfloat16), 'sy')  21.2 us
    dot_general x1, matrix products, local(): jnp.einsum('hbts,hbse->hbte', scores, value, preferred_element_type=jnp.f...  11.8 us
    dot_general x1, matrix products, local(): jnp.einsum('td,dje->jte', normed, w_qkv.reshape(width, slabs, DH), prefer...  9.57 us
    convert_element_type x1, other arithmetic, local(): mixed = jax.nn.silu(summed).astype(jnp.bfloat16)  8.75 us
    ppermute x1, starting transfers between devices, local(): lax.ppermute(projected[:, rows - (KW - 1):, :], seq_axes, [(i, i + 1) for...  3.9 us
    dot_general x1, matrix products, local(): jnp.einsum('hte,hen->tn', headed, w_out.reshape(H, DH, width), preferred_...  3.52 us
    convert_element_type x1, other arithmetic, local(): headed = (scaled * head_gain.reshape(H, 1, DH)).astype(jnp.bfloat16)  2.86 us
  transfers between devices with their start and end apart: 3, of which 3 were waited for; matrix products, arithmetic and copies ran while one was open for 3% of the time, Pallas kernels for 0%

profile of v1, /device:TPU:0, one launch (start us, length us, event | category | flops | bytes accessed | tf_op | source)
XLA Modules:
  0.0 126.8 jit_solution(6549717448463214056)
XLA Ops:
  6.5 0.0 copy-start
  6.5 0.0 all-gather.5.cloned.1.call-start
  6.5 2.2 %fusion.5 = f32[1024]{0:T(1024)S(1)} fusion(bf16[1024,1024]{1,0:T(8,128)(2,1)} %param.6), kind=kLoop, calls=%fused_computation.13 | loop fusion | flops 3144704 | bytes 2101248 | tf_op jit(solution)/shard_map/reduce_sum | solution.py:31
  8.8 0.0 copy-start.5
  8.8 9.6 %convert_bitcast_fusion = bf16[24,1024,128]{2,1,0:T(8,128)(2,1)S(1)} fusion(bf16[1024,1024]{1,0:T(8,128)(2,1)} %param.6, f32[1024]{0:T(1024)} %param.7, f32[1024]{0:T(1024)S(1)} %add_rsqrt_fusion, bf16[1024,3072]{1,0:T(8,128)(2,1)} %param.8), kind=kOutput, calls=%fused_computation.10 | convolution fusion | flops 6449790976 | bytes 14688256 | tf_op jit(solution)/shard_map/td,dje->jte/dot_general | solution.py:35
  18.4 3.9 %collective-permute-start = (bf16[24,3,128]{2,1,0:T(4,128)(2,1)S(1)}, bf16[24,3,128]{2,1,0:T(4,128)(2,1)S(1)}, u32[]{:S(2)}, u32[]{:S(2)}) collective-permute-start(bf16[24,3,128]{2,1,0:T(4,128)(2,1)S(1)} %slice.52), channel_id=1, source_target_pairs={{0,1},{1,2},{2,3},{3,4},{4,5},{5,6},{6,7},{7,8},{8,9},{9,10},{10,1... | collective-permute-start | bytes 55304 | tf_op jit(solution)/shard_map/ppermute | solution.py:41
  22.3 0.0 copy-done.5
  22.3 1.4 %collective-permute-done = bf16[24,3,128]{2,1,0:T(4,128)(2,1)S(1)} collective-permute-done((bf16[24,3,128]{2,1,0:T(4,128)(2,1)S(1)}, bf16[24,3,128]{2,1,0:T(4,128)(2,1)S(1)}, u32[]{:S(2)}, u32[]{:S(2)}) %collective-permute-start) | collective-permute-done | bytes 18464 | tf_op jit(solution)/shard_map/ppermute | solution.py:41
  23.8 8.7 %multiply_convert_fusion = bf16[24,1024,128]{2,1,0:T(8,128)(2,1)S(1)} fusion(bf16[24,1024,128]{2,1,0:T(8,128)(2,1)S(1)} %convert_bitcast_fusion, bf16[24,3,128]{2,1,0:T(4,128)(2,1)S(1)} %collective-permute-done, f32[24,128]{1,0:T(8,128)S(1)} %bitcast.59, f32[24,128]{1,0:T(8,128)S(1)} %bitcast.60, f32[24,128]{1,0:T(8,128)S(1)} %bitcast.58, ...), kind=kLoop, calls=%fused_computation.1 | loop fusion | flops 78643200 | bytes 12650496 | tf_op jit(solution)/shard_map/convert_element_type | solution.py:50
  32.5 1.9 %fusion.27 = (bf16[8,1024,128]{2,1,0:T(8,128)(2,1)S(1)}, bf16[8,1024,128]{2,1,0:T(8,128)(2,1)S(1)}, bf16[8,1024,128]{2,1,0:T(8,128)(2,1)}) fusion(bf16[24,1024,128]{2,1,0:T(8,128)(2,1)S(1)} %multiply_convert_fusion), kind=kLoop, calls=%fused_computation.45 | loop fusion | bytes 12582912 | tf_op jit(solution)/shard_map/slice | solution.py:56
  34.5 0.0 copy-start.3
  34.5 0.0 copy-start.4
  34.5 1.4 %copy-done.3 = bf16[8,1024,128]{2,1,0:T(8,128)(2,1)} copy-done((bf16[8,1024,128]{2,1,0:T(8,128)(2,1)}, bf16[8,1024,128]{2,1,0:T(8,128)(2,1)S(1)}, u32[]{:S(2)}) %copy-start.3) | copy-done | bytes 2097176
  35.9 2.6 %fusion.29 = (bf16[8,128,128]{2,1,0:T(8,128)(2,1)}, f32[2,8,128,128]{3,2,1,0:T(8,128)}) fusion(bf16[8,2,512,128]{3,2,1,0:T(8,128)(2,1)S(1)} %bitcast.51, bf16[8,2,512,128]{3,2,1,0:T(8,128)(2,1)S(1)} %bitcast.53), kind=kOutput, calls=%fused_computation.47 | convolution fusion | flops 268566528 | bytes 5505024 | tf_op jit(solution)/shard_map/hbsd,hbse->bhde/dot_general | solution.py:58
  38.4 0.0 copy-done.4
  38.4 0.0 all-gather.5.cloned.1.call-update
  38.5 0.2 all-gather.7.cloned.1.call-start
  38.7 26.9 %all-gather.5.cloned.1.call-done = bf16[32,128,128]{2,1,0:T(8,128)(2,1)} async-done(((bf16[8,128,128]{2,1,0:T(8,128)(2,1)}), bf16[32,128,128]{2,1,0:T(8,128)(2,1)}) %all-gather.5.cloned.1.call-update) | async-done | bytes 1048592 | tf_op jit(solution)/shard_map/all_gather | solution.py:64
  65.6 0.0 copy-start.2
  65.6 2.3 %reduce_sum.59 = bf16[8,128,128]{2,1,0:T(8,128)(2,1)} reduce(bf16[4,8,128,128]{3,2,1,0:T(8,128)(2,1)} %bitcast.49, bf16[]{:T(256)} %constant.26.clone.1), dimensions={0}, to_apply=%region_2.3 | reduce | flops 393216 | bytes 1310722 | tf_op jit(solution)/shard_map/reduce_sum | solution.py:25
  67.9 0.0 all-gather.7.cloned.1.call-update
  67.9 0.1 iota_compare_fusion
  68.0 1.3 %fusion.30 = f32[2,8,128,128]{3,2,1,0:T(8,128)S(1)} fusion(f32[2,8,128,128]{3,2,1,0:T(8,128)} %get-tuple-element.15), kind=kOutput, calls=%fused_computation.48 | output fusion | flops 262144 | bytes 2097152 | tf_op jit(solution)/shard_map/jit(cumsum)/reduce_window_sum | solution.py:60
  69.3 0.8 slice.60
  70.1 0.0 copy-done.2
  70.1 1.1 multiply_reduce_fusion.1
  71.2 21.2 %all-gather.7.cloned.1.call-done = bf16[32,128,128]{2,1,0:T(8,128)(2,1)} async-done(((bf16[8,128,128]{2,1,0:T(8,128)(2,1)}), bf16[32,128,128]{2,1,0:T(8,128)(2,1)}) %all-gather.7.cloned.1.call-update) | async-done | bytes 1048592 | tf_op jit(solution)/shard_map/all_gather | solution.py:65
  92.4 0.0 copy-start.1
  92.4 1.7 %fusion.15 = f32[8,128,128]{2,1,0:T(8,128)S(1)} fusion(bf16[4,8,128,128]{3,2,1,0:T(8,128)(2,1)} %bitcast.55, f32[4]{0:T(128)S(1)} %compare_convert_fusion.1), kind=kLoop, calls=%fused_computation.25 | loop fusion | flops 1441792 | bytes 1572880 | tf_op jit(solution)/shard_map/reduce_sum | solution.py:24
  94.1 1.1 add.65
  95.2 1.2 subtract_convert_fusion
  96.4 0.0 copy-done.1
  96.4 2.6 %fusion.22 = f32[8,2,512,128]{3,2,1,0:T(8,128)} fusion(bf16[8,2,512,128]{3,2,1,0:T(8,128)(2,1)S(1)} %bitcast.47, bf16[2,8,128,128]{3,2,1,0:T(8,128)(2,1)S(1)} %get-tuple-element.8), kind=kOutput, calls=%fused_computation.36 | convolution fusion | flops 268435456 | bytes 6815744 | tf_op jit(solution)/shard_map/hbtd,bhde->hbte/dot_general | solution.py:77
  99.1 2.7 %fusion.24 = f32[8,2,512,128]{3,2,1,0:T(8,128)} fusion(bf16[8,2,512,128]{3,2,1,0:T(8,128)(2,1)S(1)} %bitcast.48, bf16[2,8,128,128]{3,2,1,0:T(8,128)(2,1)S(1)} %get-tuple-element.9), kind=kOutput, calls=%fused_computation.38 | convolution fusion | flops 268435456 | bytes 6815744 | tf_op jit(solution)/shard_map/hbtd,bhde->hbte/dot_general | solution.py:75
  101.7 0.0 copy-start.6
  101.7 11.8 %multiply_reduce_fusion = (f32[8,2,512]{2,1,0:T(2,128)S(1)}, f32[8,2,512,128]{3,2,1,0:T(8,128)}) fusion(f32[8,2,512,128]{3,2,1,0:T(8,128)} %fusion.24, f32[8,2,512,128]{3,2,1,0:T(8,128)} %fusion.22, bf16[8,2,512,128]{3,2,1,0:T(8,128)(2,1)} %bitcast.52, bf16[8,2,512,128]{3,2,1,0:T(8,128)(2,1)} %bitcast.46, bf16[8,2,512,128]{3,2,1,0:T(8,128)(2,1)} %bitcast.54, ...), kind=kOutput, calls=%fused_computation.20 | convolution fusion | flops 2160058368 | bytes 19169280 | tf_op jit(solution)/shard_map/hbts,hbse->hbte/dot_general | solution.py:71
  113.6 0.0 copy-done.6
  113.6 2.9 %fusion.9 = bf16[8,1024,128]{2,1,0:T(8,128)(2,1)S(1)} fusion(f32[8,2,512,128]{3,2,1,0:T(8,128)} %get-tuple-element.17, f32[8,128]{1,0:T(8,128)S(1)} %bitcast.61, f32[8,1024]{1,0:T(8,128)S(1)} %bitcast.56), kind=kLoop, calls=%fused_computation.19 | loop fusion | flops 3145728 | bytes 6328320 | tf_op jit(solution)/shard_map/convert_element_type | solution.py:81
  116.4 0.0 copy-done
  116.4 3.5 %bitcast_convert_fusion = bf16[1024,1024]{1,0:T(8,128)(2,1)} fusion(bf16[8,1024,128]{2,1,0:T(8,128)(2,1)S(1)} %fusion.9, bf16[8,128,1024]{2,1,0:T(8,128)(2,1)S(1)} %bitcast.45), kind=kOutput, calls=%fused_computation.16 | convolution fusion | flops 2148532224 | bytes 6291456 | tf_op jit(solution)/shard_map/hte,hen->tn/dot_general | solution.py:82
  (7 shorter events, 0.1 us)
Async XLA Ops:
  6.5 109.9 %copy-start = (bf16[1024,1024]{1,0:T(8,128)(2,1)S(1)}, bf16[1024,1024]{1,0:T(8,128)(2,1)}, u32[]{:S(2)}) copy-start(bf16[1024,1024]{1,0:T(8,128)(2,1)} %param.11) | copy-start | bytes 6291460
  6.5 59.1 %all-gather.5.cloned.1.call-start = ((), (), s32[]{:S(2)}) async-start(), calls=%async_computation | async-start | bytes 1310720 | tf_op jit(solution)/shard_map/all_gather | solution.py:64
  8.8 13.5 %copy-start.5 = (f32[4,3072]{1,0:T(4,128)S(1)}, f32[4,3072]{1,0:T(4,128)}, u32[]{:S(2)}) copy-start(f32[4,3072]{1,0:T(4,128)} %param.9) | copy-start | bytes 147460
  18.4 5.4 %collective-permute-start = (bf16[24,3,128]{2,1,0:T(4,128)(2,1)S(1)}, bf16[24,3,128]{2,1,0:T(4,128)(2,1)S(1)}, u32[]{:S(2)}, u32[]{:S(2)}) collective-permute-start(bf16[24,3,128]{2,1,0:T(4,128)(2,1)S(1)} %slice.52), channel_id=1, source_target_pairs={{0,1},{1,2},{2,3},{3,4},{4,5},{5,6},{6,7},{7,8},{8,9},{9,10},{10,1... | collective-permute-start | bytes 55304 | tf_op jit(solution)/shard_map/ppermute | solution.py:41
  34.5 1.4 %copy-start.3 = (bf16[8,1024,128]{2,1,0:T(8,128)(2,1)}, bf16[8,1024,128]{2,1,0:T(8,128)(2,1)S(1)}, u32[]{:S(2)}) copy-start(bf16[8,1024,128]{2,1,0:T(8,128)(2,1)S(1)} %get-tuple-element.5) | copy-start | bytes 6291460
  34.5 3.9 %copy-start.4 = (bf16[8,1024,128]{2,1,0:T(8,128)(2,1)}, bf16[8,1024,128]{2,1,0:T(8,128)(2,1)S(1)}, u32[]{:S(2)}) copy-start(bf16[8,1024,128]{2,1,0:T(8,128)(2,1)S(1)} %get-tuple-element.6) | copy-start | bytes 6291460
  38.5 54.0 %all-gather.7.cloned.1.call-start = ((), (), s32[]{:S(2)}) async-start(), calls=%async_computation.1 | async-start | bytes 1310720 | tf_op jit(solution)/shard_map/all_gather | solution.py:65
  65.6 4.6 %copy-start.2 = (bf16[32,128,128]{2,1,0:T(8,128)(2,1)S(1)}, bf16[32,128,128]{2,1,0:T(8,128)(2,1)}, u32[]{:S(2)}) copy-start(bf16[32,128,128]{2,1,0:T(8,128)(2,1)} %all-gather.5.cloned.1.call-done) | copy-start | bytes 3145732
  92.4 4.0 %copy-start.1 = (bf16[8,1024,128]{2,1,0:T(8,128)(2,1)S(1)}, bf16[8,1024,128]{2,1,0:T(8,128)(2,1)}, u32[]{:S(2)}) copy-start(bf16[8,1024,128]{2,1,0:T(8,128)(2,1)} %get-tuple-element.7) | copy-start | bytes 6291460
  101.7 11.8 %copy-start.6 = (f32[1024]{0:T(1024)S(1)}, f32[1024]{0:T(1024)}, u32[]{:S(2)}) copy-start(f32[1024]{0:T(1024)} %param.10) | copy-start | bytes 12292
Sparse Core Ops, SparseCore 0:
  38.6 26.9 all-gather.4
  68.0 24.3 all-gather.6

commit v2 on v1

--- a/solution.py
+++ b/solution.py
@@ -11,18 +11,30 @@
 
 
 def split_bf16(x):
-    hi = x.astype(jnp.bfloat16)
-    lo = (x - hi.astype(jnp.float32)).astype(jnp.bfloat16)
-    return hi, lo
+    hi = lax.reduce_precision(x, exponent_bits=8, mantissa_bits=7)
+    return hi.astype(jnp.bfloat16), (x - hi).astype(jnp.bfloat16)
 
 
-def earlier_sum(gathered, axis):
+def ring_earlier(x, axis):
+    count = lax.axis_size(axis)
     place = lax.axis_index(axis)
-    count = gathered.shape[0]
-    mask = (lax.iota(jnp.int32, count) < place).astype(jnp.float32)
-    values = gathered.astype(jnp.float32)
-    before = jnp.sum(values * mask[:, None, None, None], 0)
-    return before, jnp.sum(values, 0)
+    forward = [(i, (i + 1) % count) for i in range(count)]
+    backward = [(i, (i - 1) % count) for i in range(count)]
+    from_prev = lax.ppermute(x, axis, forward)
+    from_next = lax.ppermute(x, axis, backward)
+    half = x.shape[0] // 2
+    from_far = jnp.concatenate(
+        [lax.ppermute(from_prev[:half], axis, forward), lax.ppermute(from_next[half:], axis, backward)],
+        0,
+    )
+    before = jnp.zeros(x.shape, jnp.float32)
+    total = x.astype(jnp.float32)
+    for offset, part in ((-1, from_prev), (1, from_next), (2, from_far)):
+        part = part.astype(jnp.float32)
+        earlier = ((place + offset) % count < place).astype(jnp.float32)
+        before = before + earlier * part
+        total = total + part
+    return before, total
 
 
 def local(tokens, norm_gain, w_qkv, conv_weight, head_gain, w_out):
@@ -61,8 +73,8 @@
     )
     state = jnp.sum(block_states, 0)
 
-    zbefore, row_total = earlier_sum(lax.all_gather(state.astype(jnp.bfloat16), "sz"), "sz")
-    ybefore, _ = earlier_sum(lax.all_gather(row_total.astype(jnp.bfloat16), "sy"), "sy")
+    zbefore, row_total = ring_earlier(state.astype(jnp.bfloat16), "sz")
+    ybefore, _ = ring_earlier(row_total.astype(jnp.bfloat16), "sy")
     prefix = ybefore + zbefore
 
     causal = jnp.tril(jnp.ones((block, block), jnp.bool_))

time: 127 us -> 88.1 us (0.69)
  waiting for transfers between devices: 49.6 us -> 14.9 us
  starting transfers between devices: 4.12 us -> 20 us
  between operations: 13.6 us -> 0.2 us
  other arithmetic: 22.6 us -> 17.4 us
    all_gather x2 -> x0, waiting for transfers between devices: 48.1 us -> none  [the longest x1 26.9 us: local(): lax.all_gather(state.astype(jnp.bfloat16), 'sz')]
    ppermute x0 -> x8, starting transfers between devices: none -> 16.1 us  [the longest x2 5.46 us: ring_earlier(): lax.ppermute(from_next[half:], axis, backward)]
    ppermute x0 -> x8, waiting for transfers between devices: none -> 13.4 us  [the longest x2 8.87 us: ring_earlier(): from_prev = lax.ppermute(x, axis, forward)]
    reduce_sum x3 -> x0, other arithmetic: 5.02 us -> none  [the longest x2 2.76 us: earlier_sum(): before = jnp.sum(values * mask[:, None, None, None], 0)]
  transfers between devices with their start and end apart: 3 -> 9, of which waited for: 3 -> 6; matrix products, arithmetic and copies ran while one was open for 3% -> 3% of each run, Pallas kernels for 0% -> 0%
where the time goes in v2:
time: 88.1 us; the launch traced here: 87.8 us
  matrix products  31.9 us (36%)
  starting transfers between devices  20 us (23%)
  other arithmetic  17.4 us (20%)
  waiting for transfers between devices  14.9 us (17%)
  local copies, waits for them, and re-layouts  3.47 us (4%)
    dot_general x1, matrix products, local(): jnp.einsum('hbts,hbse->hbte', scores, value, preferred_element_type=jnp.f...  11.8 us
    dot_general x1, matrix products, local(): jnp.einsum('td,dje->jte', normed, w_qkv.reshape(width, slabs, DH), prefer...  9.57 us
    ppermute x2, waiting for transfers between devices, ring_earlier(): from_prev = lax.ppermute(x, axis, forward)  8.87 us
    convert_element_type x1, other arithmetic, local(): mixed = jax.nn.silu(summed).astype(jnp.bfloat16)  8.75 us
    ppermute x2, starting transfers between devices, ring_earlier(): lax.ppermute(from_next[half:], axis, backward)  5.46 us
    ppermute x2, starting transfers between devices, ring_earlier(): from_prev = lax.ppermute(x, axis, forward)  5.05 us
    ppermute x2, waiting for transfers between devices, ring_earlier(): lax.ppermute(from_prev[:half], axis, forward)  4.15 us
    ppermute x2, starting transfers between devices, ring_earlier(): from_next = lax.ppermute(x, axis, backward)  3.94 us
  transfers between devices with their start and end apart: 9, of which 6 were waited for; matrix products, arithmetic and copies ran while one was open for 3% of the time, Pallas kernels for 0%

profile of v2, /device:TPU:0, one launch (start us, length us, event | category | flops | bytes accessed | tf_op | source)
XLA Modules:
  0.0 87.8 jit_solution(5016390642479633111)
XLA Ops:
  0.0 0.0 copy-start
  0.0 2.2 %fusion.5 = f32[1024]{0:T(1024)S(1)} fusion(bf16[1024,1024]{1,0:T(8,128)(2,1)} %param.6), kind=kLoop, calls=%fused_computation.13 | loop fusion | flops 3144704 | bytes 2101248 | tf_op jit(solution)/shard_map/reduce_sum | solution.py:43
  2.2 0.0 copy-start.5
  2.2 9.6 %convert_bitcast_fusion = bf16[24,1024,128]{2,1,0:T(8,128)(2,1)S(1)} fusion(bf16[1024,1024]{1,0:T(8,128)(2,1)} %param.6, f32[1024]{0:T(1024)} %param.7, f32[1024]{0:T(1024)S(1)} %add_rsqrt_fusion, bf16[1024,3072]{1,0:T(8,128)(2,1)} %param.8), kind=kOutput, calls=%fused_computation.10 | convolution fusion | flops 6449790976 | bytes 14688256 | tf_op jit(solution)/shard_map/td,dje->jte/dot_general | solution.py:47
  11.9 3.9 %collective-permute-start = (bf16[24,3,128]{2,1,0:T(4,128)(2,1)S(1)}, bf16[24,3,128]{2,1,0:T(4,128)(2,1)S(1)}, u32[]{:S(2)}, u32[]{:S(2)}) collective-permute-start(bf16[24,3,128]{2,1,0:T(4,128)(2,1)S(1)} %slice.68), channel_id=1, source_target_pairs={{0,1},{1,2},{2,3},{3,4},{4,5},{5,6},{6,7},{7,8},{8,9},{9,10},{10,1... | collective-permute-start | bytes 55304 | tf_op jit(solution)/shard_map/ppermute | solution.py:53
  15.8 0.0 copy-done.5
  15.8 1.4 %collective-permute-done = bf16[24,3,128]{2,1,0:T(4,128)(2,1)S(1)} collective-permute-done((bf16[24,3,128]{2,1,0:T(4,128)(2,1)S(1)}, bf16[24,3,128]{2,1,0:T(4,128)(2,1)S(1)}, u32[]{:S(2)}, u32[]{:S(2)}) %collective-permute-start) | collective-permute-done | bytes 18464 | tf_op jit(solution)/shard_map/ppermute | solution.py:53
  17.3 8.7 %multiply_convert_fusion = bf16[24,1024,128]{2,1,0:T(8,128)(2,1)S(1)} fusion(bf16[24,1024,128]{2,1,0:T(8,128)(2,1)S(1)} %convert_bitcast_fusion, bf16[24,3,128]{2,1,0:T(4,128)(2,1)S(1)} %collective-permute-done, f32[24,128]{1,0:T(8,128)S(1)} %bitcast.53, f32[24,128]{1,0:T(8,128)S(1)} %bitcast.54, f32[24,128]{1,0:T(8,128)S(1)} %bitcast.52, ...), kind=kLoop, calls=%fused_computation.1 | loop fusion | flops 78643200 | bytes 12650496 | tf_op jit(solution)/shard_map/convert_element_type | solution.py:62
  26.0 1.9 %fusion.30 = (bf16[8,1024,128]{2,1,0:T(8,128)(2,1)S(1)}, bf16[8,1024,128]{2,1,0:T(8,128)(2,1)S(1)}, bf16[8,1024,128]{2,1,0:T(8,128)(2,1)}) fusion(bf16[24,1024,128]{2,1,0:T(8,128)(2,1)S(1)} %multiply_convert_fusion), kind=kLoop, calls=%fused_computation.52 | loop fusion | bytes 12582912 | tf_op jit(solution)/shard_map/slice | solution.py:68
  28.0 0.0 copy-start.2
  28.0 0.0 copy-start.3
  28.0 1.4 %copy-done.2 = bf16[8,1024,128]{2,1,0:T(8,128)(2,1)} copy-done((bf16[8,1024,128]{2,1,0:T(8,128)(2,1)}, bf16[8,1024,128]{2,1,0:T(8,128)(2,1)S(1)}, u32[]{:S(2)}) %copy-start.2) | copy-done | bytes 2097176
  29.3 1.8 %fusion.32 = (bf16[8,128,128]{2,1,0:T(8,128)(2,1)S(1)}, f32[2,8,128,128]{3,2,1,0:T(8,128)}) fusion(bf16[8,2,512,128]{3,2,1,0:T(8,128)(2,1)S(1)} %bitcast.46, bf16[8,2,512,128]{3,2,1,0:T(8,128)(2,1)S(1)} %bitcast.48), kind=kOutput, calls=%fused_computation.54 | convolution fusion | flops 268566528 | bytes 5505024 | tf_op jit(solution)/shard_map/hbsd,hbse->bhde/dot_general | solution.py:70
  31.1 0.0 copy-done.3
  31.1 2.4 %collective-permute-start.1 = (bf16[8,128,128]{2,1,0:T(8,128)(2,1)S(1)}, bf16[8,128,128]{2,1,0:T(8,128)(2,1)S(1)}, u32[]{:S(2)}, u32[]{:S(2)}) collective-permute-start(bf16[8,128,128]{2,1,0:T(8,128)(2,1)S(1)} %get-tuple-element.14), channel_id=1, source_target_pairs={{0,1},{1,2},{2,3},{3,0},{4,5},{5,6},{6,7},{7,4},{8,9},{9,10},{10,1... | collective-permute-start | bytes 786440 | tf_op jit(solution)/shard_map/ppermute | solution.py:23
  33.5 2.2 %collective-permute-start.2 = (bf16[8,128,128]{2,1,0:T(8,128)(2,1)S(1)}, bf16[8,128,128]{2,1,0:T(8,128)(2,1)S(1)}, u32[]{:S(2)}, u32[]{:S(2)}) collective-permute-start(bf16[8,128,128]{2,1,0:T(8,128)(2,1)S(1)} %get-tuple-element.14), channel_id=1, source_target_pairs={{0,3},{1,0},{2,1},{3,2},{4,7},{5,4},{6,5},{7,6},{8,11},{9,8},{10,9... | collective-permute-start | bytes 786440 | tf_op jit(solution)/shard_map/ppermute | solution.py:24
  35.7 5.1 %collective-permute-done.1 = bf16[8,128,128]{2,1,0:T(8,128)(2,1)S(1)} collective-permute-done((bf16[8,128,128]{2,1,0:T(8,128)(2,1)S(1)}, bf16[8,128,128]{2,1,0:T(8,128)(2,1)S(1)}, u32[]{:S(2)}, u32[]{:S(2)}) %collective-permute-start.1) | collective-permute-done | bytes 262176 | tf_op jit(solution)/shard_map/ppermute | solution.py:23
  40.8 0.1 collective-permute-start.3
  40.9 0.0 collective-permute-done.2
  40.9 3.3 %collective-permute-start.4 = (bf16[4,128,128]{2,1,0:T(8,128)(2,1)S(1)}, bf16[4,128,128]{2,1,0:T(8,128)(2,1)S(1)}, u32[]{:S(2)}, u32[]{:S(2)}) collective-permute-start(bf16[4,128,128]{2,1,0:T(8,128)(2,1)S(1)} %slice.77), channel_id=1, source_target_pairs={{0,3},{1,0},{2,1},{3,2},{4,7},{5,4},{6,5},{7,6},{8,11},{9,8},{10,9... | collective-permute-start | bytes 393224 | tf_op jit(solution)/shard_map/ppermute | solution.py:27
  44.2 2.9 %collective-permute-done.3 = bf16[4,128,128]{2,1,0:T(8,128)(2,1)S(1)} collective-permute-done((bf16[4,128,128]{2,1,0:T(8,128)(2,1)S(1)}, bf16[4,128,128]{2,1,0:T(8,128)(2,1)S(1)}, u32[]{:S(2)}, u32[]{:S(2)}) %collective-permute-start.3) | collective-permute-done | bytes 131104 | tf_op jit(solution)/shard_map/ppermute | solution.py:27
  47.0 0.0 collective-permute-done.4
  47.0 0.9 fusion.24
  47.9 2.7 %collective-permute-start.5 = (bf16[8,128,128]{2,1,0:T(8,128)(2,1)}, bf16[8,128,128]{2,1,0:T(8,128)(2,1)S(1)}, u32[]{:S(2)}, u32[]{:S(2)}) collective-permute-start(bf16[8,128,128]{2,1,0:T(8,128)(2,1)} %fusion.24), channel_id=1, source_target_pairs={{0,4},{4,8},{8,12},{12,0},{1,5},{5,9},{9,13},{13,1},{2,6},{6,10},{... | collective-permute-start | bytes 786440 | tf_op jit(solution)/shard_map/ppermute | solution.py:23
  50.6 1.7 %collective-permute-start.6 = (bf16[8,128,128]{2,1,0:T(8,128)(2,1)}, bf16[8,128,128]{2,1,0:T(8,128)(2,1)S(1)}, u32[]{:S(2)}, u32[]{:S(2)}) collective-permute-start(bf16[8,128,128]{2,1,0:T(8,128)(2,1)} %fusion.24), channel_id=1, source_target_pairs={{0,12},{4,0},{8,4},{12,8},{1,13},{5,1},{9,5},{13,9},{2,14},{6,2},{... | collective-permute-start | bytes 786440 | tf_op jit(solution)/shard_map/ppermute | solution.py:24
  52.3 0.0 copy-start.1
  52.3 0.8 iota_compare_fusion
  53.1 3.8 %collective-permute-done.5 = bf16[8,128,128]{2,1,0:T(8,128)(2,1)S(1)} collective-permute-done((bf16[8,128,128]{2,1,0:T(8,128)(2,1)}, bf16[8,128,128]{2,1,0:T(8,128)(2,1)S(1)}, u32[]{:S(2)}, u32[]{:S(2)}) %collective-permute-start.5) | collective-permute-done | bytes 262176 | tf_op jit(solution)/shard_map/ppermute | solution.py:23
  56.9 1.6 %collective-permute-start.7 = (bf16[4,128,128]{2,1,0:T(8,128)(2,1)S(1)}, bf16[4,128,128]{2,1,0:T(8,128)(2,1)S(1)}, u32[]{:S(2)}, u32[]{:S(2)}) collective-permute-start(bf16[4,128,128]{2,1,0:T(8,128)(2,1)S(1)} %slice.78), channel_id=1, source_target_pairs={{0,4},{4,8},{8,12},{12,0},{1,5},{5,9},{9,13},{13,1},{2,6},{6,10},{... | collective-permute-start | bytes 393224 | tf_op jit(solution)/shard_map/ppermute | solution.py:27
  58.4 0.0 collective-permute-done.6
  58.5 2.2 %collective-permute-start.8 = (bf16[4,128,128]{2,1,0:T(8,128)(2,1)S(1)}, bf16[4,128,128]{2,1,0:T(8,128)(2,1)S(1)}, u32[]{:S(2)}, u32[]{:S(2)}) collective-permute-start(bf16[4,128,128]{2,1,0:T(8,128)(2,1)S(1)} %slice.79), channel_id=1, source_target_pairs={{0,12},{4,0},{8,4},{12,8},{1,13},{5,1},{9,5},{13,9},{2,14},{6,2},{... | collective-permute-start | bytes 393224 | tf_op jit(solution)/shard_map/ppermute | solution.py:27
  60.6 1.3 %fusion.33 = f32[2,8,128,128]{3,2,1,0:T(8,128)S(1)} fusion(f32[2,8,128,128]{3,2,1,0:T(8,128)} %get-tuple-element.15), kind=kOutput, calls=%fused_computation.55 | output fusion | flops 262144 | bytes 2097152 | tf_op jit(solution)/shard_map/jit(cumsum)/reduce_window_sum | solution.py:72
  62.0 1.3 %collective-permute-done.7 = bf16[4,128,128]{2,1,0:T(8,128)(2,1)S(1)} collective-permute-done((bf16[4,128,128]{2,1,0:T(8,128)(2,1)S(1)}, bf16[4,128,128]{2,1,0:T(8,128)(2,1)S(1)}, u32[]{:S(2)}, u32[]{:S(2)}) %collective-permute-start.7) | collective-permute-done | bytes 131104 | tf_op jit(solution)/shard_map/ppermute | solution.py:27
  63.3 0.4 collective-permute-done.8
  63.7 0.3 fusion.23
  64.0 0.3 fusion.20
  64.2 0.0 copy-done.1
  64.3 2.6 %fusion.25 = f32[8,2,512,128]{3,2,1,0:T(8,128)} fusion(bf16[8,2,512,128]{3,2,1,0:T(8,128)(2,1)S(1)} %bitcast.44, bf16[2,8,128,128]{3,2,1,0:T(8,128)(2,1)S(1)} %get-tuple-element.8), kind=kOutput, calls=%fused_computation.44 | convolution fusion | flops 268435456 | bytes 6815744 | tf_op jit(solution)/shard_map/hbtd,bhde->hbte/dot_general | solution.py:89
  66.9 0.0 copy-start.4
  66.9 2.7 %fusion.27 = f32[8,2,512,128]{3,2,1,0:T(8,128)} fusion(bf16[8,2,512,128]{3,2,1,0:T(8,128)(2,1)S(1)} %bitcast.45, bf16[2,8,128,128]{3,2,1,0:T(8,128)(2,1)S(1)} %get-tuple-element.9), kind=kOutput, calls=%fused_computation.46 | convolution fusion | flops 268435456 | bytes 6815744 | tf_op jit(solution)/shard_map/hbtd,bhde->hbte/dot_general | solution.py:87
  69.6 0.0 copy-done.4
  69.6 0.0 copy-start.6
  69.6 11.8 %multiply_reduce_fusion = (f32[8,2,512]{2,1,0:T(2,128)S(1)}, f32[8,2,512,128]{3,2,1,0:T(8,128)}) fusion(f32[8,2,512,128]{3,2,1,0:T(8,128)} %fusion.27, f32[8,2,512,128]{3,2,1,0:T(8,128)} %fusion.25, bf16[8,2,512,128]{3,2,1,0:T(8,128)(2,1)} %bitcast.47, bf16[8,2,512,128]{3,2,1,0:T(8,128)(2,1)} %bitcast.43, bf16[8,2,512,128]{3,2,1,0:T(8,128)(2,1)} %bitcast.49, ...), kind=kOutput, calls=%fused_computation.20 | convolution fusion | flops 2160058368 | bytes 19169280 | tf_op jit(solution)/shard_map/hbts,hbse->hbte/dot_general | solution.py:83
  81.4 0.0 copy-done.6
  81.4 2.9 %fusion.9 = bf16[8,1024,128]{2,1,0:T(8,128)(2,1)S(1)} fusion(f32[8,2,512,128]{3,2,1,0:T(8,128)} %get-tuple-element.17, f32[8,128]{1,0:T(8,128)S(1)} %bitcast.55, f32[8,1024]{1,0:T(8,128)S(1)} %bitcast.50), kind=kLoop, calls=%fused_computation.19 | loop fusion | flops 3145728 | bytes 6328320 | tf_op jit(solution)/shard_map/convert_element_type | solution.py:93
  84.3 0.0 copy-done
  84.3 3.5 %bitcast_convert_fusion = bf16[1024,1024]{1,0:T(8,128)(2,1)} fusion(bf16[8,1024,128]{2,1,0:T(8,128)(2,1)S(1)} %fusion.9, bf16[8,128,1024]{2,1,0:T(8,128)(2,1)S(1)} %bitcast.42), kind=kOutput, calls=%fused_computation.16 | convolution fusion | flops 2148532224 | bytes 6291456 | tf_op jit(solution)/shard_map/hte,hen->tn/dot_general | solution.py:94
  (10 shorter events, 0.2 us)
Async XLA Ops:
  0.0 84.3 %copy-start = (bf16[1024,1024]{1,0:T(8,128)(2,1)S(1)}, bf16[1024,1024]{1,0:T(8,128)(2,1)}, u32[]{:S(2)}) copy-start(bf16[1024,1024]{1,0:T(8,128)(2,1)} %param.11) | copy-start | bytes 6291460
  2.2 13.5 %copy-start.5 = (f32[4,3072]{1,0:T(4,128)S(1)}, f32[4,3072]{1,0:T(4,128)}, u32[]{:S(2)}) copy-start(f32[4,3072]{1,0:T(4,128)} %param.9) | copy-start | bytes 147460
  11.9 5.4 %collective-permute-start = (bf16[24,3,128]{2,1,0:T(4,128)(2,1)S(1)}, bf16[24,3,128]{2,1,0:T(4,128)(2,1)S(1)}, u32[]{:S(2)}, u32[]{:S(2)}) collective-permute-start(bf16[24,3,128]{2,1,0:T(4,128)(2,1)S(1)} %slice.68), channel_id=1, source_target_pairs={{0,1},{1,2},{2,3},{3,4},{4,5},{5,6},{6,7},{7,8},{8,9},{9,10},{10,1... | collective-permute-start | bytes 55304 | tf_op jit(solution)/shard_map/ppermute | solution.py:53
  28.0 1.4 %copy-start.2 = (bf16[8,1024,128]{2,1,0:T(8,128)(2,1)}, bf16[8,1024,128]{2,1,0:T(8,128)(2,1)S(1)}, u32[]{:S(2)}) copy-start(bf16[8,1024,128]{2,1,0:T(8,128)(2,1)S(1)} %get-tuple-element.5) | copy-start | bytes 6291460
  28.0 3.1 %copy-start.3 = (bf16[8,1024,128]{2,1,0:T(8,128)(2,1)}, bf16[8,1024,128]{2,1,0:T(8,128)(2,1)S(1)}, u32[]{:S(2)}) copy-start(bf16[8,1024,128]{2,1,0:T(8,128)(2,1)S(1)} %get-tuple-element.6) | copy-start | bytes 6291460
  31.1 9.6 %collective-permute-start.1 = (bf16[8,128,128]{2,1,0:T(8,128)(2,1)S(1)}, bf16[8,128,128]{2,1,0:T(8,128)(2,1)S(1)}, u32[]{:S(2)}, u32[]{:S(2)}) collective-permute-start(bf16[8,128,128]{2,1,0:T(8,128)(2,1)S(1)} %get-tuple-element.14), channel_id=1, source_target_pairs={{0,1},{1,2},{2,3},{3,0},{4,5},{5,6},{6,7},{7,4},{8,9},{9,10},{10,1... | collective-permute-start | bytes 786440 | tf_op jit(solution)/shard_map/ppermute | solution.py:23
  33.5 7.4 %collective-permute-start.2 = (bf16[8,128,128]{2,1,0:T(8,128)(2,1)S(1)}, bf16[8,128,128]{2,1,0:T(8,128)(2,1)S(1)}, u32[]{:S(2)}, u32[]{:S(2)}) collective-permute-start(bf16[8,128,128]{2,1,0:T(8,128)(2,1)S(1)} %get-tuple-element.14), channel_id=1, source_target_pairs={{0,3},{1,0},{2,1},{3,2},{4,7},{5,4},{6,5},{7,6},{8,11},{9,8},{10,9... | collective-permute-start | bytes 786440 | tf_op jit(solution)/shard_map/ppermute | solution.py:24
  40.8 6.2 %collective-permute-start.3 = (bf16[4,128,128]{2,1,0:T(8,128)(2,1)S(1)}, bf16[4,128,128]{2,1,0:T(8,128)(2,1)S(1)}, u32[]{:S(2)}, u32[]{:S(2)}) collective-permute-start(bf16[4,128,128]{2,1,0:T(8,128)(2,1)S(1)} %slice.76), channel_id=1, source_target_pairs={{0,1},{1,2},{2,3},{3,0},{4,5},{5,6},{6,7},{7,4},{8,9},{9,10},{10,1... | collective-permute-start | bytes 393224 | tf_op jit(solution)/shard_map/ppermute | solution.py:27
  40.9 6.1 %collective-permute-start.4 = (bf16[4,128,128]{2,1,0:T(8,128)(2,1)S(1)}, bf16[4,128,128]{2,1,0:T(8,128)(2,1)S(1)}, u32[]{:S(2)}, u32[]{:S(2)}) collective-permute-start(bf16[4,128,128]{2,1,0:T(8,128)(2,1)S(1)} %slice.77), channel_id=1, source_target_pairs={{0,3},{1,0},{2,1},{3,2},{4,7},{5,4},{6,5},{7,6},{8,11},{9,8},{10,9... | collective-permute-start | bytes 393224 | tf_op jit(solution)/shard_map/ppermute | solution.py:27
  47.9 9.0 %collective-permute-start.5 = (bf16[8,128,128]{2,1,0:T(8,128)(2,1)}, bf16[8,128,128]{2,1,0:T(8,128)(2,1)S(1)}, u32[]{:S(2)}, u32[]{:S(2)}) collective-permute-start(bf16[8,128,128]{2,1,0:T(8,128)(2,1)} %fusion.24), channel_id=1, source_target_pairs={{0,4},{4,8},{8,12},{12,0},{1,5},{5,9},{9,13},{13,1},{2,6},{6,10},{... | collective-permute-start | bytes 786440 | tf_op jit(solution)/shard_map/ppermute | solution.py:23
  50.6 7.9 %collective-permute-start.6 = (bf16[8,128,128]{2,1,0:T(8,128)(2,1)}, bf16[8,128,128]{2,1,0:T(8,128)(2,1)S(1)}, u32[]{:S(2)}, u32[]{:S(2)}) collective-permute-start(bf16[8,128,128]{2,1,0:T(8,128)(2,1)} %fusion.24), channel_id=1, source_target_pairs={{0,12},{4,0},{8,4},{12,8},{1,13},{5,1},{9,5},{13,9},{2,14},{6,2},{... | collective-permute-start | bytes 786440 | tf_op jit(solution)/shard_map/ppermute | solution.py:24
  52.3 12.0 %copy-start.1 = (bf16[8,1024,128]{2,1,0:T(8,128)(2,1)S(1)}, bf16[8,1024,128]{2,1,0:T(8,128)(2,1)}, u32[]{:S(2)}) copy-start(bf16[8,1024,128]{2,1,0:T(8,128)(2,1)} %get-tuple-element.7) | copy-start | bytes 6291460
  56.9 6.4 %collective-permute-start.7 = (bf16[4,128,128]{2,1,0:T(8,128)(2,1)S(1)}, bf16[4,128,128]{2,1,0:T(8,128)(2,1)S(1)}, u32[]{:S(2)}, u32[]{:S(2)}) collective-permute-start(bf16[4,128,128]{2,1,0:T(8,128)(2,1)S(1)} %slice.78), channel_id=1, source_target_pairs={{0,4},{4,8},{8,12},{12,0},{1,5},{5,9},{9,13},{13,1},{2,6},{6,10},{... | collective-permute-start | bytes 393224 | tf_op jit(solution)/shard_map/ppermute | solution.py:27
  58.5 5.2 %collective-permute-start.8 = (bf16[4,128,128]{2,1,0:T(8,128)(2,1)S(1)}, bf16[4,128,128]{2,1,0:T(8,128)(2,1)S(1)}, u32[]{:S(2)}, u32[]{:S(2)}) collective-permute-start(bf16[4,128,128]{2,1,0:T(8,128)(2,1)S(1)} %slice.79), channel_id=1, source_target_pairs={{0,12},{4,0},{8,4},{12,8},{1,13},{5,1},{9,5},{13,9},{2,14},{6,2},{... | collective-permute-start | bytes 393224 | tf_op jit(solution)/shard_map/ppermute | solution.py:27
  66.9 2.7 %copy-start.4 = (pred[512,512]{1,0:T(8,128)(4,1)S(1)}, pred[512,512]{1,0:T(8,128)(4,1)}, u32[]{:S(2)}) copy-start(pred[512,512]{1,0:T(8,128)(4,1)} %iota_compare_fusion) | copy-start | bytes 786436
  69.6 11.8 %copy-start.6 = (f32[1024]{0:T(1024)S(1)}, f32[1024]{0:T(1024)}, u32[]{:S(2)}) copy-start(f32[1024]{0:T(1024)} %param.10) | copy-start | bytes 12292

commit v3 on v2

v3 whole, which is shorter than its diff:
```python
import jax
import jax.numpy as jnp
from jax import lax
from jax.experimental import pallas as pl
from jax.experimental.pallas import tpu as pltpu
from jax.sharding import Mesh
from jax.sharding import PartitionSpec as P

H = 8
DH = 128
KW = 4
BLOCK = 512
PAD = 8


def split_bf16(x):
    hi = lax.reduce_precision(x, exponent_bits=8, mantissa_bits=7)
    return hi.astype(jnp.bfloat16), (x - hi).astype(jnp.bfloat16)


def ring_earlier(x, axis):
    count = lax.axis_size(axis)
    place = lax.axis_index(axis)
    forward = [(i, (i + 1) % count) for i in range(count)]
    backward = [(i, (i - 1) % count) for i in range(count)]
    from_prev = lax.ppermute(x, axis, forward)
    from_next = lax.ppermute(x, axis, backward)
    half = x.shape[0] // 2
    from_far = jnp.concatenate(
        [lax.ppermute(from_prev[:half], axis, forward), lax.ppermute(from_next[half:], axis, backward)],
        0,
    )
    before = jnp.zeros(x.shape, jnp.float32)
    total = x.astype(jnp.float32)
    for offset, part in ((-1, from_prev), (1, from_next), (2, from_far)):
        part = part.astype(jnp.float32)
        earlier = ((place + offset) % count < place).astype(jnp.float32)
        before = before + earlier * part
        total = total + part
    return before, total


def conv_kernel(pq, pk, pv, eq, ek, ev, tq, tk, tv, oq, ok, ov, state_ref, buf):
    rows = pq.shape[0]
    for proj, early, taps, out in ((pq, eq, tq, oq), (pk, ek, tk, ok), (pv, ev, tv, ov)):
        buf[0:PAD, :] = early[...].astype(jnp.float32)
        buf[PAD:, :] = proj[...].astype(jnp.float32)
        summed = jnp.zeros((rows, DH), jnp.float32)
        for offset in range(KW):
            summed = summed + taps[offset : offset + 1, :] * buf[pl.ds(PAD - offset, rows), :]
        out[...] = (summed * jax.nn.sigmoid(summed)).astype(out.dtype)
    state_ref[...] = lax.dot_general(
        ok[...], ov[...], (((0,), (0,)), ((), ())), preferred_element_type=jnp.float32
    )


def local_kernel(q_ref, k_ref, v_ref, out_ref):
    rows = q_ref.shape[0]
    block = min(BLOCK, rows)
    causal = lax.broadcasted_iota(jnp.int32, (block, block), 0) >= lax.broadcasted_iota(
        jnp.int32, (block, block), 1
    )
    inner = jnp.zeros((DH, DH), jnp.float32)
    for b in range(rows // block):
        span = pl.ds(b * block, block)
        query, key, value = q_ref[span, :], k_ref[span, :], v_ref[span, :]
        scores = lax.dot_general(
            query, key, (((1,), (1,)), ((), ())), preferred_element_type=jnp.float32
        )
        scores = jnp.where(causal, scores, 0.0).astype(jnp.bfloat16)
        part = jnp.dot(scores, value, preferred_element_type=jnp.float32)
        if b > 0:
            hi, lo = split_bf16(inner)
            part = part + jnp.dot(query, hi, preferred_element_type=jnp.float32)
            part = part + jnp.dot(query, lo, preferred_element_type=jnp.float32)
        out_ref[span, :] = part
        inner = inner + lax.dot_general(
            key, value, (((0,), (0,)), ((), ())), preferred_element_type=jnp.float32
        )


def out_kernel(q_ref, local_ref, prefix_ref, gain_ref, w_ref, out_ref, acc):
    head = pl.program_id(0)
    hi, lo = split_bf16(prefix_ref[...])
    query = q_ref[...]
    attended = local_ref[...] + jnp.dot(query, hi, preferred_element_type=jnp.float32)
    attended = attended + jnp.dot(query, lo, preferred_element_type=jnp.float32)
    scaled = attended * lax.rsqrt(jnp.mean(attended * attended, -1, keepdims=True) + 1e-05)
    headed = (scaled * gain_ref[...]).astype(jnp.bfloat16)
    part = jnp.dot(headed, w_ref[...], preferred_element_type=jnp.float32)

    @pl.when(head == 0)
    def _():
        acc[...] = part

    @pl.when(head > 0)
    def _():
        acc[...] += part

    @pl.when(head == pl.num_programs(0) - 1)
    def _():
        out_ref[...] = acc[...].astype(out_ref.dtype)


def slab(shift, rows, cols):
    return pl.BlockSpec((None, rows, cols), lambda h: (h + shift, 0, 0))


def local(tokens, norm_gain, w_qkv, conv_weight, head_gain, w_out):
    rows, width = tokens.shape
    tokens_f = tokens.astype(jnp.float32)
    scale = lax.rsqrt(jnp.mean(tokens_f * tokens_f, -1, keepdims=True) + 1e-06)
    normed = (tokens_f * scale * norm_gain).astype(jnp.bfloat16)

    slabs = w_qkv.shape[1] // DH
    projected = jnp.einsum(
        "td,dje->jte", normed, w_qkv.reshape(width, slabs, DH), preferred_element_type=jnp.float32
    ).astype(jnp.bfloat16)

    seq_axes = ("sy", "sz")
    count = lax.axis_size("sy") * lax.axis_size("sz")
    earlier_rows = lax.ppermute(
        projected[:, rows - (KW - 1) :, :], seq_axes, [(i, i + 1) for i in range(count - 1)]
    )
    earlier_rows = jnp.pad(earlier_rows, ((0, 0), (PAD - (KW - 1), 0), (0, 0)))
    taps = jnp.pad(
        conv_weight.reshape(KW, slabs, DH).transpose(1, 0, 2), ((0, 0), (0, PAD - KW), (0, 0))
    )

    mixed_shape = jax.ShapeDtypeStruct((H, rows, DH), jnp.bfloat16)
    query, key, value, state = pl.pallas_call(
        conv_kernel,
        grid=(H,),
        in_specs=[slab(0, rows, DH), slab(H, rows, DH), slab(2 * H, rows, DH)]
        + [slab(0, PAD, DH), slab(H, PAD, DH), slab(2 * H, PAD, DH)]
        + [slab(0, PAD, DH), slab(H, PAD, DH), slab(2 * H, PAD, DH)],
        out_specs=[slab(0, rows, DH)] * 3 + [slab(0, DH, DH)],
        out_shape=[mixed_shape] * 3 + [jax.ShapeDtypeStruct((H, DH, DH), jnp.float32)],
        scratch_shapes=[pltpu.VMEM((rows + PAD, DH), jnp.float32)],
        cost_estimate=pl.CostEstimate(
            flops=H * (3 * rows * DH * 12 + 2 * rows * DH * DH),
            transcendentals=H * 3 * rows * DH,
            bytes_accessed=H * 3 * rows * DH * 4,
        ),
    )(projected, projected, projected, earlier_rows, earlier_rows, earlier_rows, taps, taps, taps)

    block = min(BLOCK, rows)
    local_part = pl.pallas_call(
        local_kernel,
        grid=(H,),
        in_specs=[slab(0, rows, DH)] * 3,
        out_specs=slab(0, rows, DH),
        out_shape=jax.ShapeDtypeStruct((H, rows, DH), jnp.float32),
        cost_estimate=pl.CostEstimate(
            flops=H * (4 * rows * block * DH + 6 * rows * DH * DH),
            transcendentals=0,
            bytes_accessed=H * rows * DH * 10,
        ),
    )(query, key, value)

    zbefore, row_total = ring_earlier(state.astype(jnp.bfloat16), "sz")
    ybefore, _ = ring_earlier(row_total.astype(jnp.bfloat16), "sy")
    prefix = ybefore + zbefore

    out = pl.pallas_call(
        out_kernel,
        grid=(H,),
        in_specs=[
            slab(0, rows, DH),
            slab(0, rows, DH),
            slab(0, DH, DH),
            slab(0, 1, DH),
            slab(0, DH, width),
        ],
        out_specs=pl.BlockSpec((rows, width), lambda h: (0, 0)),
        out_shape=jax.ShapeDtypeStruct((rows, width), jnp.bfloat16),
        scratch_shapes=[pltpu.VMEM((rows, width), jnp.float32)],
        cost_estimate=pl.CostEstimate(
            flops=H * (4 * rows * DH * DH + 2 * rows * DH * width),
            transcendentals=H * rows,
            bytes_accessed=H * rows * DH * 6 + width * width * 2 + rows * width * 2,
        ),
    )(query, local_part, prefix, head_gain.reshape(H, 1, DH), w_out.reshape(H, DH, width))
    return out


def solution(mesh):
    seq = mesh.shape["seq"]
    inner = 4 if seq % 4 == 0 else 1
    grid = Mesh(
        mesh.devices.reshape(mesh.shape["trace"], seq // inner, inner), ("trace", "sy", "sz")
    )
    rows = P(("trace", "sy", "sz"), None)
    placed = (rows, P(), P(), P(), P(), P())
    return jax.shard_map(local, mesh=grid, in_specs=placed, out_specs=rows, check_vma=False)
```

time: 88.1 us -> 89.7 us (1.018)
  Pallas kernels: 0 us -> 34.4 us
  matrix products: 31.9 us -> 9.57 us
  other arithmetic: 17.4 us -> 5.43 us
  waiting for transfers between devices: 14.9 us -> 16.3 us
  starting transfers between devices: 20 us -> 19.1 us
    pallas_call x0 -> x3, Pallas kernels: none -> 34.4 us  [the longest x1 13.6 us: local(): pl.pallas_call(out_kernel, grid=(H,), in_specs=[slab(0, rows, DH), slab(0...]
    dot_general x5 -> x0, matrix products: 22.4 us -> none  [the longest x1 11.8 us: local(): jnp.einsum('hbts,hbse->hbte', scores, value, preferred_element_type=jnp.f...]
    convert_element_type x3 -> x1, other arithmetic: 11.9 us -> 1.08 us  [local(): zbefore, row_total = ring_earlier(state.astype(jnp.bfloat16), 'sz')]
    ppermute x2, waiting for transfers between devices: 0.01 us -> 9.17 us  [ring_earlier(): from_next = lax.ppermute(x, axis, backward)]
    ppermute x2, waiting for transfers between devices: 8.87 us -> 0.12 us  [ring_earlier(): from_prev = lax.ppermute(x, axis, forward)]
    ppermute x2, starting transfers between devices: 5.05 us -> 0.01 us  [ring_earlier(): from_prev = lax.ppermute(x, axis, forward)]
    ppermute x2, starting transfers between devices: 3.94 us -> 7.57 us  [ring_earlier(): from_next = lax.ppermute(x, axis, backward)]
    ppermute x2, starting transfers between devices: 5.46 us -> 7.52 us  [ring_earlier(): lax.ppermute(from_next[half:], axis, backward)]
  transfers between devices with their start and end apart: 9 -> 9, of which waited for: 6 -> 6; matrix products, arithmetic and copies ran while one was open for 3% -> 1% of each run, Pallas kernels for 0% -> 11%
where the time goes in v3:
time: 89.7 us; the launch traced here: 88.9 us
  Pallas kernels  34.4 us (38%)
  starting transfers between devices  19.1 us (21%)
  waiting for transfers between devices  16.3 us (18%)
  matrix products  9.57 us (11%)
  other arithmetic  5.43 us (6%)
  local copies, waits for them, and re-layouts  4 us (4%)
    pallas_call x1, Pallas kernels, local(): pl.pallas_call(out_kernel, grid=(H,), in_specs=[slab(0, rows, DH), slab(0...  13.6 us
    pallas_call x1, Pallas kernels, local(): pl.pallas_call(conv_kernel, grid=(H,), in_specs=[slab(0, rows, DH), slab(...  10.6 us
    pallas_call x1, Pallas kernels, local(): pl.pallas_call(local_kernel, grid=(H,), in_specs=[slab(0, rows, DH)] * 3,...  10.2 us
    dot_general x1, matrix products, local(): jnp.einsum('td,dje->jte', normed, w_qkv.reshape(width, slabs, DH), prefer...  9.57 us
    ppermute x2, waiting for transfers between devices, ring_earlier(): from_next = lax.ppermute(x, axis, backward)  9.17 us
    ppermute x2, starting transfers between devices, ring_earlier(): from_next = lax.ppermute(x, axis, backward)  7.57 us
    ppermute x2, starting transfers between devices, ring_earlier(): lax.ppermute(from_next[half:], axis, backward)  7.52 us
    ppermute x1, starting transfers between devices, local(): lax.ppermute(projected[:, rows - (KW - 1):, :], seq_axes, [(i, i + 1) for...  3.9 us
  transfers between devices with their start and end apart: 9, of which 6 were waited for; matrix products, arithmetic and copies ran while one was open for 1% of the time, Pallas kernels for 11%

profile of v3, /device:TPU:0, one launch (start us, length us, event | category | flops | bytes accessed | tf_op | source)
XLA Modules:
  0.0 88.9 jit_solution(8743524131968800186)
XLA Ops:
  0.0 2.1 %fusion.3 = f32[1024]{0:T(1024)S(1)} fusion(bf16[1024,1024]{1,0:T(8,128)(2,1)} %param.6), kind=kLoop, calls=%fused_computation.6 | loop fusion | flops 3144704 | bytes 2101248 | tf_op jit(solution)/shard_map/reduce_sum | solution.py:112
  2.1 0.0 copy-start.1
  2.1 9.6 %convert_bitcast_fusion.pq.pk.pv = bf16[24,1024,128]{2,1,0:T(8,128)(2,1)S(1)} fusion(bf16[1024,1024]{1,0:T(8,128)(2,1)} %param.6, f32[1024]{0:T(1024)} %param.7, f32[1024]{0:T(1024)S(1)} %add_rsqrt_fusion, bf16[1024,3072]{1,0:T(8,128)(2,1)} %param.8), kind=kOutput, calls=%fused_computation.3 | convolution fusion | flops 6449790976 | bytes 14688256 | tf_op jit(solution)/shard_map/td,dje->jte/dot_general | solution.py:116
  11.7 0.0 copy-start
  11.7 2.7 %copy-done = bf16[24,1024,128]{2,1,0:T(8,128)(2,1)} copy-done((bf16[24,1024,128]{2,1,0:T(8,128)(2,1)}, bf16[24,1024,128]{2,1,0:T(8,128)(2,1)S(1)}, u32[]{:S(2)}) %copy-start) | copy-done | bytes 6291480
  14.4 3.9 %collective-permute-start = (bf16[24,3,128]{2,1,0:T(4,128)(2,1)S(1)}, bf16[24,3,128]{2,1,0:T(4,128)(2,1)S(1)}, u32[]{:S(2)}, u32[]{:S(2)}) collective-permute-start(bf16[24,3,128]{2,1,0:T(4,128)(2,1)S(1)} %slice.20), channel_id=1, source_target_pairs={{0,1},{1,2},{2,3},{3,4},{4,5},{5,6},{6,7},{7,8},{8,9},{9,10},{10,1... | collective-permute-start | bytes 55304 | tf_op jit(solution)/shard_map/ppermute | solution.py:122
  18.3 0.0 copy-done.1
  18.3 0.7 pad.9.tq.tk.tv
  18.9 0.8 collective-permute-done
  19.8 0.6 pad.8.eq.ek.ev
  20.4 10.6 %shard_map.64 = (bf16[8,1024,128]{2,1,0:T(8,128)(2,1)}, bf16[8,1024,128]{2,1,0:T(8,128)(2,1)}, bf16[8,1024,128]{2,1,0:T(8,128)(2,1)}, f32[8,128,128]{2,1,0:T(8,128)}) custom-call(bf16[24,1024,128]{2,1,0:T(8,128)(2,1)} %copy-done, bf16[24,1024,128]{2,1,0:T(8,128)(2,1)} %copy-done, bf16[24,1024,128]{2,1,0:T(8,128)(2,1)} %copy-done, ...), custom_call_target="tpu_custom_call" | custom-call | flops 306184192 | bytes 12582912 | tf_op jit(solution)/shard_map/pallas_call | solution.py:131
  31.0 1.1 %convert_element_type.65 = bf16[8,128,128]{2,1,0:T(8,128)(2,1)S(1)} convert(f32[8,128,128]{2,1,0:T(8,128)} %get-tuple-element.12) | non-fusion elementwise | flops 131072 | bytes 786432 | tf_op jit(solution)/shard_map/convert_element_type | solution.py:161
  32.1 4.5 %collective-permute-start.2 = (bf16[8,128,128]{2,1,0:T(8,128)(2,1)S(1)}, bf16[8,128,128]{2,1,0:T(8,128)(2,1)S(1)}, u32[]{:S(2)}, u32[]{:S(2)}) collective-permute-start(bf16[8,128,128]{2,1,0:T(8,128)(2,1)S(1)} %convert_element_type.65), channel_id=1, source_target_pairs={{0,3},{1,0},{2,1},{3,2},{4,7},{5,4},{6,5},{7,6},{8,11},{9,8},{10,9... | collective-permute-start | bytes 786440 | tf_op jit(solution)/shard_map/ppermute | solution.py:27
  36.6 0.0 collective-permute-start.1
  36.6 4.4 %collective-permute-done.2 = bf16[8,128,128]{2,1,0:T(8,128)(2,1)S(1)} collective-permute-done((bf16[8,128,128]{2,1,0:T(8,128)(2,1)S(1)}, bf16[8,128,128]{2,1,0:T(8,128)(2,1)S(1)}, u32[]{:S(2)}, u32[]{:S(2)}) %collective-permute-start.2) | collective-permute-done | bytes 262176 | tf_op jit(solution)/shard_map/ppermute | solution.py:27
  41.0 3.8 %collective-permute-start.4 = (bf16[4,128,128]{2,1,0:T(8,128)(2,1)S(1)}, bf16[4,128,128]{2,1,0:T(8,128)(2,1)S(1)}, u32[]{:S(2)}, u32[]{:S(2)}) collective-permute-start(bf16[4,128,128]{2,1,0:T(8,128)(2,1)S(1)} %slice.22), channel_id=1, source_target_pairs={{0,3},{1,0},{2,1},{3,2},{4,7},{5,4},{6,5},{7,6},{8,11},{9,8},{10,9... | collective-permute-start | bytes 393224 | tf_op jit(solution)/shard_map/ppermute | solution.py:30
  44.8 0.0 collective-permute-done.1
  44.8 0.1 collective-permute-start.3
  44.9 2.4 %collective-permute-done.4 = bf16[4,128,128]{2,1,0:T(8,128)(2,1)S(1)} collective-permute-done((bf16[4,128,128]{2,1,0:T(8,128)(2,1)S(1)}, bf16[4,128,128]{2,1,0:T(8,128)(2,1)S(1)}, u32[]{:S(2)}, u32[]{:S(2)}) %collective-permute-start.4) | collective-permute-done | bytes 131104 | tf_op jit(solution)/shard_map/ppermute | solution.py:30
  47.3 3.7 %collective-permute-done.3 = bf16[4,128,128]{2,1,0:T(8,128)(2,1)S(1)} collective-permute-done((bf16[4,128,128]{2,1,0:T(8,128)(2,1)S(1)}, bf16[4,128,128]{2,1,0:T(8,128)(2,1)S(1)}, u32[]{:S(2)}, u32[]{:S(2)}) %collective-permute-start.3) | collective-permute-done | bytes 131104 | tf_op jit(solution)/shard_map/ppermute | solution.py:30
  51.0 1.2 %fusion.15 = bf16[8,128,128]{2,1,0:T(8,128)(2,1)S(1)} fusion(bf16[8,128,128]{2,1,0:T(8,128)(2,1)S(1)} %collective-permute-done.2, bf16[8,128,128]{2,1,0:T(8,128)(2,1)S(1)} %collective-permute-done.1, bf16[4,128,128]{2,1,0:T(8,128)(2,1)S(1)} %collective-permute-done.4, bf16[4,128,128]{2,1,0:T(8,128)(2,1)S(1)} %collective-permute-done.3, ...), kind=kLoop, calls=%fused_computation.21 | loop fusion | flops 1310720 | bytes 1572864 | tf_op jit(solution)/shard_map/convert_element_type | solution.py:162
  52.2 3.1 %collective-permute-start.6 = (bf16[8,128,128]{2,1,0:T(8,128)(2,1)S(1)}, bf16[8,128,128]{2,1,0:T(8,128)(2,1)S(1)}, u32[]{:S(2)}, u32[]{:S(2)}) collective-permute-start(bf16[8,128,128]{2,1,0:T(8,128)(2,1)S(1)} %fusion.15), channel_id=1, source_target_pairs={{0,12},{4,0},{8,4},{12,8},{1,13},{5,1},{9,5},{13,9},{2,14},{6,2},{... | collective-permute-start | bytes 786440 | tf_op jit(solution)/shard_map/ppermute | solution.py:27
  55.3 0.0 collective-permute-start.5
  55.3 4.8 %collective-permute-done.6 = bf16[8,128,128]{2,1,0:T(8,128)(2,1)S(1)} collective-permute-done((bf16[8,128,128]{2,1,0:T(8,128)(2,1)S(1)}, bf16[8,128,128]{2,1,0:T(8,128)(2,1)S(1)}, u32[]{:S(2)}, u32[]{:S(2)}) %collective-permute-start.6) | collective-permute-done | bytes 262176 | tf_op jit(solution)/shard_map/ppermute | solution.py:27
  60.0 3.8 %collective-permute-start.8 = (bf16[4,128,128]{2,1,0:T(8,128)(2,1)S(1)}, bf16[4,128,128]{2,1,0:T(8,128)(2,1)S(1)}, u32[]{:S(2)}, u32[]{:S(2)}) collective-permute-start(bf16[4,128,128]{2,1,0:T(8,128)(2,1)S(1)} %slice.24), channel_id=1, source_target_pairs={{0,12},{4,0},{8,4},{12,8},{1,13},{5,1},{9,5},{13,9},{2,14},{6,2},{... | collective-permute-start | bytes 393224 | tf_op jit(solution)/shard_map/ppermute | solution.py:30
  63.8 0.1 collective-permute-done.5
  63.9 0.1 collective-permute-start.7
  64.0 10.2 %shard_map.65.local_ref = f32[8,1024,128]{2,1,0:T(8,128)} custom-call(bf16[8,1024,128]{2,1,0:T(8,128)(2,1)} %get-tuple-element.9.q_ref, bf16[8,1024,128]{2,1,0:T(8,128)(2,1)} %get-tuple-element.10.k_ref, bf16[8,1024,128]{2,1,0:T(8,128)(2,1)} %get-tuple-element.11.v_ref), custom_call_target="tpu_custom_call" | custom-call | flops 2952790016 | bytes 10485760 | tf_op jit(solution)/shard_map/pallas_call | solution.py:148
  74.2 0.0 collective-permute-done.8
  74.2 0.0 collective-permute-done.7
  74.2 1.1 %fusion.14.prefix_ref = f32[8,128,128]{2,1,0:T(8,128)} fusion(bf16[8,128,128]{2,1,0:T(8,128)(2,1)S(1)} %collective-permute-done.1, bf16[8,128,128]{2,1,0:T(8,128)(2,1)S(1)} %collective-permute-done.2, bf16[8,128,128]{2,1,0:T(8,128)(2,1)S(1)} %collective-permute-done.6, bf16[8,128,128]{2,1,0:T(8,128)(2,1)S(1)} %collective-permute-done.5, ...), kind=kLoop, calls=%fused_computation.20 | loop fusion | flops 2490368 | bytes 2097176 | tf_op jit(solution)/shard_map/add | solution.py:163
  75.3 13.6 %shard_map.66 = bf16[1024,1024]{1,0:T(8,128)(2,1)} custom-call(bf16[8,1024,128]{2,1,0:T(8,128)(2,1)} %get-tuple-element.9.q_ref, f32[8,1024,128]{2,1,0:T(8,128)} %shard_map.65.local_ref, f32[8,128,128]{2,1,0:T(8,128)} %fusion.14.prefix_ref, f32[8,1,128]{2,1,0:T(1,128)} %bitcast.21, bf16[8,128,1024]{2,1,0:T(8,128)(2,1)} %bitcast.19), custom_call_target="tpu_custom_call" | custom-call | flops 2684354560 | bytes 10485760 | tf_op jit(solution)/shard_map/pallas_call | solution.py:165
  (6 shorter events, 0.1 us)
Async XLA Ops:
  2.1 16.2 %copy-start.1 = (f32[4,3072]{1,0:T(4,128)S(1)}, f32[4,3072]{1,0:T(4,128)}, u32[]{:S(2)}) copy-start(f32[4,3072]{1,0:T(4,128)} %param.9) | copy-start | bytes 147460
  11.7 2.7 %copy-start = (bf16[24,1024,128]{2,1,0:T(8,128)(2,1)}, bf16[24,1024,128]{2,1,0:T(8,128)(2,1)S(1)}, u32[]{:S(2)}) copy-start(bf16[24,1024,128]{2,1,0:T(8,128)(2,1)S(1)} %convert_bitcast_fusion.pq.pk.pv) | copy-start | bytes 18874372
  14.4 5.4 %collective-permute-start = (bf16[24,3,128]{2,1,0:T(4,128)(2,1)S(1)}, bf16[24,3,128]{2,1,0:T(4,128)(2,1)S(1)}, u32[]{:S(2)}, u32[]{:S(2)}) collective-permute-start(bf16[24,3,128]{2,1,0:T(4,128)(2,1)S(1)} %slice.20), channel_id=1, source_target_pairs={{0,1},{1,2},{2,3},{3,4},{4,5},{5,6},{6,7},{7,8},{8,9},{9,10},{10,1... | collective-permute-start | bytes 55304 | tf_op jit(solution)/shard_map/ppermute | solution.py:122
  32.1 8.9 %collective-permute-start.2 = (bf16[8,128,128]{2,1,0:T(8,128)(2,1)S(1)}, bf16[8,128,128]{2,1,0:T(8,128)(2,1)S(1)}, u32[]{:S(2)}, u32[]{:S(2)}) collective-permute-start(bf16[8,128,128]{2,1,0:T(8,128)(2,1)S(1)} %convert_element_type.65), channel_id=1, source_target_pairs={{0,3},{1,0},{2,1},{3,2},{4,7},{5,4},{6,5},{7,6},{8,11},{9,8},{10,9... | collective-permute-start | bytes 786440 | tf_op jit(solution)/shard_map/ppermute | solution.py:27
  36.6 8.2 %collective-permute-start.1 = (bf16[8,128,128]{2,1,0:T(8,128)(2,1)S(1)}, bf16[8,128,128]{2,1,0:T(8,128)(2,1)S(1)}, u32[]{:S(2)}, u32[]{:S(2)}) collective-permute-start(bf16[8,128,128]{2,1,0:T(8,128)(2,1)S(1)} %convert_element_type.65), channel_id=1, source_target_pairs={{0,1},{1,2},{2,3},{3,0},{4,5},{5,6},{6,7},{7,4},{8,9},{9,10},{10,1... | collective-permute-start | bytes 786440 | tf_op jit(solution)/shard_map/ppermute | solution.py:26
  41.0 6.3 %collective-permute-start.4 = (bf16[4,128,128]{2,1,0:T(8,128)(2,1)S(1)}, bf16[4,128,128]{2,1,0:T(8,128)(2,1)S(1)}, u32[]{:S(2)}, u32[]{:S(2)}) collective-permute-start(bf16[4,128,128]{2,1,0:T(8,128)(2,1)S(1)} %slice.22), channel_id=1, source_target_pairs={{0,3},{1,0},{2,1},{3,2},{4,7},{5,4},{6,5},{7,6},{8,11},{9,8},{10,9... | collective-permute-start | bytes 393224 | tf_op jit(solution)/shard_map/ppermute | solution.py:30
  44.8 6.2 %collective-permute-start.3 = (bf16[4,128,128]{2,1,0:T(8,128)(2,1)S(1)}, bf16[4,128,128]{2,1,0:T(8,128)(2,1)S(1)}, u32[]{:S(2)}, u32[]{:S(2)}) collective-permute-start(bf16[4,128,128]{2,1,0:T(8,128)(2,1)S(1)} %slice.21), channel_id=1, source_target_pairs={{0,1},{1,2},{2,3},{3,0},{4,5},{5,6},{6,7},{7,4},{8,9},{9,10},{10,1... | collective-permute-start | bytes 393224 | tf_op jit(solution)/shard_map/ppermute | solution.py:30
  52.2 7.8 %collective-permute-start.6 = (bf16[8,128,128]{2,1,0:T(8,128)(2,1)S(1)}, bf16[8,128,128]{2,1,0:T(8,128)(2,1)S(1)}, u32[]{:S(2)}, u32[]{:S(2)}) collective-permute-start(bf16[8,128,128]{2,1,0:T(8,128)(2,1)S(1)} %fusion.15), channel_id=1, source_target_pairs={{0,12},{4,0},{8,4},{12,8},{1,13},{5,1},{9,5},{13,9},{2,14},{6,2},{... | collective-permute-start | bytes 786440 | tf_op jit(solution)/shard_map/ppermute | solution.py:27
  55.3 8.6 %collective-permute-start.5 = (bf16[8,128,128]{2,1,0:T(8,128)(2,1)S(1)}, bf16[8,128,128]{2,1,0:T(8,128)(2,1)S(1)}, u32[]{:S(2)}, u32[]{:S(2)}) collective-permute-start(bf16[8,128,128]{2,1,0:T(8,128)(2,1)S(1)} %fusion.15), channel_id=1, source_target_pairs={{0,4},{4,8},{8,12},{12,0},{1,5},{5,9},{9,13},{13,1},{2,6},{6,10},{... | collective-permute-start | bytes 786440 | tf_op jit(solution)/shard_map/ppermute | solution.py:26
  60.0 14.2 %collective-permute-start.8 = (bf16[4,128,128]{2,1,0:T(8,128)(2,1)S(1)}, bf16[4,128,128]{2,1,0:T(8,128)(2,1)S(1)}, u32[]{:S(2)}, u32[]{:S(2)}) collective-permute-start(bf16[4,128,128]{2,1,0:T(8,128)(2,1)S(1)} %slice.24), channel_id=1, source_target_pairs={{0,12},{4,0},{8,4},{12,8},{1,13},{5,1},{9,5},{13,9},{2,14},{6,2},{... | collective-permute-start | bytes 393224 | tf_op jit(solution)/shard_map/ppermute | solution.py:30
  63.9 10.3 %collective-permute-start.7 = (bf16[4,128,128]{2,1,0:T(8,128)(2,1)S(1)}, bf16[4,128,128]{2,1,0:T(8,128)(2,1)S(1)}, u32[]{:S(2)}, u32[]{:S(2)}) collective-permute-start(bf16[4,128,128]{2,1,0:T(8,128)(2,1)S(1)} %slice.23), channel_id=1, source_target_pairs={{0,4},{4,8},{8,12},{12,0},{1,5},{5,9},{9,13},{13,1},{2,6},{6,10},{... | collective-permute-start | bytes 393224 | tf_op jit(solution)/shard_map/ppermute | solution.py:30

commit v4 on v3

--- a/solution.py
+++ b/solution.py
@@ -79,27 +79,13 @@
         )
 
 
-def out_kernel(q_ref, local_ref, prefix_ref, gain_ref, w_ref, out_ref, acc):
-    head = pl.program_id(0)
+def head_kernel(q_ref, local_ref, prefix_ref, gain_ref, out_ref):
     hi, lo = split_bf16(prefix_ref[...])
     query = q_ref[...]
     attended = local_ref[...] + jnp.dot(query, hi, preferred_element_type=jnp.float32)
     attended = attended + jnp.dot(query, lo, preferred_element_type=jnp.float32)
     scaled = attended * lax.rsqrt(jnp.mean(attended * attended, -1, keepdims=True) + 1e-05)
-    headed = (scaled * gain_ref[...]).astype(jnp.bfloat16)
-    part = jnp.dot(headed, w_ref[...], preferred_element_type=jnp.float32)
-
-    @pl.when(head == 0)
-    def _():
-        acc[...] = part
-
-    @pl.when(head > 0)
-    def _():
-        acc[...] += part
-
-    @pl.when(head == pl.num_programs(0) - 1)
-    def _():
-        out_ref[...] = acc[...].astype(out_ref.dtype)
+    out_ref[...] = (scaled * gain_ref[...]).astype(out_ref.dtype)
 
 
 def slab(shift, rows, cols):
@@ -145,43 +131,42 @@
     )(projected, projected, projected, earlier_rows, earlier_rows, earlier_rows, taps, taps, taps)
 
     block = min(BLOCK, rows)
-    local_part = pl.pallas_call(
-        local_kernel,
-        grid=(H,),
-        in_specs=[slab(0, rows, DH)] * 3,
-        out_specs=slab(0, rows, DH),
-        out_shape=jax.ShapeDtypeStruct((H, rows, DH), jnp.float32),
-        cost_estimate=pl.CostEstimate(
-            flops=H * (4 * rows * block * DH + 6 * rows * DH * DH),
-            transcendentals=0,
-            bytes_accessed=H * rows * DH * 10,
-        ),
-    )(query, key, value)
+    group = 2
+
+    def local_call(first):
+        return pl.pallas_call(
+            local_kernel,
+            grid=(group,),
+            in_specs=[slab(first, rows, DH)] * 3,
+            out_specs=slab(0, rows, DH),
+            out_shape=jax.ShapeDtypeStruct((group, rows, DH), jnp.float32),
+            cost_estimate=pl.CostEstimate(
+                flops=group * (4 * rows * block * DH + 6 * rows * DH * DH),
+                transcendentals=0,
+                bytes_accessed=group * rows * DH * 10,
+            ),
+        )(query, key, value)
+
+    local_part = jnp.concatenate([local_call(g) for g in range(0, H, group)], 0)
 
     zbefore, row_total = ring_earlier(state.astype(jnp.bfloat16), "sz")
     ybefore, _ = ring_earlier(row_total.astype(jnp.bfloat16), "sy")
     prefix = ybefore + zbefore
 
-    out = pl.pallas_call(
-        out_kernel,
+    headed = pl.pallas_call(
+        head_kernel,
         grid=(H,),
-        in_specs=[
-            slab(0, rows, DH),
-            slab(0, rows, DH),
-            slab(0, DH, DH),
-            slab(0, 1, DH),
-            slab(0, DH, width),
-        ],
-        out_specs=pl.BlockSpec((rows, width), lambda h: (0, 0)),
-        out_shape=jax.ShapeDtypeStruct((rows, width), jnp.bfloat16),
-        scratch_shapes=[pltpu.VMEM((rows, width), jnp.float32)],
+        in_specs=[slab(0, rows, DH), slab(0, rows, DH), slab(0, DH, DH), slab(0, 1, DH)],
+        out_specs=slab(0, rows, DH),
+        out_shape=jax.ShapeDtypeStruct((H, rows, DH), jnp.bfloat16),
         cost_estimate=pl.CostEstimate(
-            flops=H * (4 * rows * DH * DH + 2 * rows * DH * width),
-            transcendentals=H * rows,
-            bytes_accessed=H * rows * DH * 6 + width * width * 2 + rows * width * 2,
+            flops=H * 4 * rows * DH * DH, transcendentals=H * rows, bytes_accessed=H * rows * DH * 8
         ),
-    )(query, local_part, prefix, head_gain.reshape(H, 1, DH), w_out.reshape(H, DH, width))
-    return out
+    )(query, local_part, prefix, head_gain.reshape(H, 1, DH))
+    out = jnp.einsum(
+        "hte,hen->tn", headed, w_out.reshape(H, DH, width), preferred_element_type=jnp.float32
+    )
+    return out.astype(jnp.bfloat16)
 
 
 def solution(mesh):

time: 89.7 us -> 97.9 us (1.091)
  other arithmetic: 5.43 us -> 11.5 us
  matrix products: 9.57 us -> 14.7 us
  waiting for transfers between devices: 16.3 us -> 13.3 us
  local copies, waits for them, and re-layouts: 4 us -> 5.88 us
  Pallas kernels: 34.4 us -> 32.9 us
    dot_general x0 -> x1, matrix products: none -> 5.1 us  [local(): jnp.einsum('hte,hen->tn', headed, w_out.reshape(H, DH, width), preferred_...]
    ppermute x2, waiting for transfers between devices: 9.17 us -> 4.42 us  [ring_earlier(): from_next = lax.ppermute(x, axis, backward)]
    concatenate x0 -> x1, other arithmetic: none -> 4.18 us  [local(): local_part = jnp.concatenate([local_call(g) for g in range(0, H, group)], 0)]
    ppermute x2, waiting for transfers between devices: 3.75 us -> 5.71 us  [ring_earlier(): lax.ppermute(from_prev[:half], axis, forward)]
    pallas_call x2 -> x5, Pallas kernels: 23.8 us -> 22.3 us  [the longest x4 14.5 us: local_call(): pl.pallas_call(local_kernel, grid=(group,), in_specs=[slab(first, rows, D...]
    add x1, other arithmetic: 1.11 us -> 2.14 us  [local(): prefix = ybefore + zbefore]
    unnamed x4 -> x16, local copies, waits for them, and re-layouts: 2.66 us -> 2.73 us
  transfers between devices with their start and end apart: 9 -> 9, of which waited for: 6 -> 5; matrix products, arithmetic and copies ran while one was open for 1% -> 7% of each run, Pallas kernels for 11% -> 15%
where the time goes in v4:
time: 97.9 us; the launch traced here: 97.1 us
  Pallas kernels  32.9 us (34%)
  starting transfers between devices  18.6 us (19%)
  matrix products  14.7 us (15%)
  waiting for transfers between devices  13.3 us (14%)
  other arithmetic  11.5 us (12%)
  local copies, waits for them, and re-layouts  5.88 us (6%)
    pallas_call x4, Pallas kernels, local_call(): pl.pallas_call(local_kernel, grid=(group,), in_specs=[slab(first, rows, D...  14.5 us
    pallas_call x1, Pallas kernels, local(): pl.pallas_call(conv_kernel, grid=(H,), in_specs=[slab(0, rows, DH), slab(...  10.6 us
    dot_general x1, matrix products, local(): jnp.einsum('td,dje->jte', normed, w_qkv.reshape(width, slabs, DH), prefer...  9.57 us
    pallas_call x1, Pallas kernels, local(): pl.pallas_call(head_kernel, grid=(H,), in_specs=[slab(0, rows, DH), slab(...  7.77 us
    ppermute x2, starting transfers between devices, ring_earlier(): from_next = lax.ppermute(x, axis, backward)  7.51 us
    ppermute x2, starting transfers between devices, ring_earlier(): lax.ppermute(from_next[half:], axis, backward)  7.06 us
    ppermute x2, waiting for transfers between devices, ring_earlier(): lax.ppermute(from_prev[:half], axis, forward)  5.71 us
    dot_general x1, matrix products, local(): jnp.einsum('hte,hen->tn', headed, w_out.reshape(H, DH, width), preferred_...  5.1 us
  transfers between devices with their start and end apart: 9, of which 5 were waited for; matrix products, arithmetic and copies ran while one was open for 7% of the time, Pallas kernels for 15%

profile of v4, /device:TPU:0, one launch (start us, length us, event | category | flops | bytes accessed | tf_op | source)
XLA Modules:
  0.0 97.1 jit_solution(14249795080910950895)
XLA Ops:
  0.0 0.0 copy-start
  0.0 2.2 %fusion.3 = f32[1024]{0:T(1024)S(1)} fusion(bf16[1024,1024]{1,0:T(8,128)(2,1)} %param.6), kind=kLoop, calls=%fused_computation.6 | loop fusion | flops 3144704 | bytes 2101248 | tf_op jit(solution)/shard_map/reduce_sum | solution.py:98
  2.2 0.0 copy-start.7
  2.2 9.6 %convert_bitcast_fusion.pq.pk.pv = bf16[24,1024,128]{2,1,0:T(8,128)(2,1)S(1)} fusion(bf16[1024,1024]{1,0:T(8,128)(2,1)} %param.6, f32[1024]{0:T(1024)} %param.7, f32[1024]{0:T(1024)S(1)} %add_rsqrt_fusion, bf16[1024,3072]{1,0:T(8,128)(2,1)} %param.8), kind=kOutput, calls=%fused_computation.3 | convolution fusion | flops 6449790976 | bytes 14688256 | tf_op jit(solution)/shard_map/td,dje->jte/dot_general | solution.py:102
  11.8 0.0 copy-start.1
  11.8 2.7 %copy-done.1 = bf16[24,1024,128]{2,1,0:T(8,128)(2,1)} copy-done((bf16[24,1024,128]{2,1,0:T(8,128)(2,1)}, bf16[24,1024,128]{2,1,0:T(8,128)(2,1)S(1)}, u32[]{:S(2)}) %copy-start.1) | copy-done | bytes 6291480
  14.6 3.9 %collective-permute-start = (bf16[24,3,128]{2,1,0:T(4,128)(2,1)S(1)}, bf16[24,3,128]{2,1,0:T(4,128)(2,1)S(1)}, u32[]{:S(2)}, u32[]{:S(2)}) collective-permute-start(bf16[24,3,128]{2,1,0:T(4,128)(2,1)S(1)} %slice.20), channel_id=1, source_target_pairs={{0,1},{1,2},{2,3},{3,4},{4,5},{5,6},{6,7},{7,8},{8,9},{9,10},{10,1... | collective-permute-start | bytes 55304 | tf_op jit(solution)/shard_map/ppermute | solution.py:108
  18.5 0.0 copy-done.7
  18.5 0.7 pad.9.tq.tk.tv
  19.1 0.8 collective-permute-done
  20.0 0.6 pad.8.eq.ek.ev
  20.6 10.6 %shard_map.64 = (bf16[8,1024,128]{2,1,0:T(8,128)(2,1)}, bf16[8,1024,128]{2,1,0:T(8,128)(2,1)}, bf16[8,1024,128]{2,1,0:T(8,128)(2,1)}, f32[8,128,128]{2,1,0:T(8,128)}) custom-call(bf16[24,1024,128]{2,1,0:T(8,128)(2,1)} %copy-done.1, bf16[24,1024,128]{2,1,0:T(8,128)(2,1)} %copy-done.1, bf16[24,1024,128]{2,1,0:T(8,128)(2,1)} %copy-done.1, ...), custom_call_target="tpu_custom_call" | custom-call | flops 306184192 | bytes 12582912 | tf_op jit(solution)/shard_map/pallas_call | solution.py:117
  31.2 1.1 %convert_element_type.68 = bf16[8,128,128]{2,1,0:T(8,128)(2,1)S(1)} convert(f32[8,128,128]{2,1,0:T(8,128)} %get-tuple-element.12) | non-fusion elementwise | flops 131072 | bytes 786432 | tf_op jit(solution)/shard_map/convert_element_type | solution.py:152
  32.3 4.5 %collective-permute-start.2 = (bf16[8,128,128]{2,1,0:T(8,128)(2,1)S(1)}, bf16[8,128,128]{2,1,0:T(8,128)(2,1)S(1)}, u32[]{:S(2)}, u32[]{:S(2)}) collective-permute-start(bf16[8,128,128]{2,1,0:T(8,128)(2,1)S(1)} %convert_element_type.68), channel_id=1, source_target_pairs={{0,3},{1,0},{2,1},{3,2},{4,7},{5,4},{6,5},{7,6},{8,11},{9,8},{10,9... | collective-permute-start | bytes 786440 | tf_op jit(solution)/shard_map/ppermute | solution.py:27
  36.7 0.0 collective-permute-start.1
  36.8 4.4 %collective-permute-done.2 = bf16[8,128,128]{2,1,0:T(8,128)(2,1)S(1)} collective-permute-done((bf16[8,128,128]{2,1,0:T(8,128)(2,1)S(1)}, bf16[8,128,128]{2,1,0:T(8,128)(2,1)S(1)}, u32[]{:S(2)}, u32[]{:S(2)}) %collective-permute-start.2) | collective-permute-done | bytes 262176 | tf_op jit(solution)/shard_map/ppermute | solution.py:27
  41.2 3.8 %collective-permute-start.4 = (bf16[4,128,128]{2,1,0:T(8,128)(2,1)S(1)}, bf16[4,128,128]{2,1,0:T(8,128)(2,1)S(1)}, u32[]{:S(2)}, u32[]{:S(2)}) collective-permute-start(bf16[4,128,128]{2,1,0:T(8,128)(2,1)S(1)} %slice.22), channel_id=1, source_target_pairs={{0,3},{1,0},{2,1},{3,2},{4,7},{5,4},{6,5},{7,6},{8,11},{9,8},{10,9... | collective-permute-start | bytes 393224 | tf_op jit(solution)/shard_map/ppermute | solution.py:30
  44.9 0.0 collective-permute-done.1
  45.0 0.1 collective-permute-start.3
  45.1 2.3 %collective-permute-done.4 = bf16[4,128,128]{2,1,0:T(8,128)(2,1)S(1)} collective-permute-done((bf16[4,128,128]{2,1,0:T(8,128)(2,1)S(1)}, bf16[4,128,128]{2,1,0:T(8,128)(2,1)S(1)}, u32[]{:S(2)}, u32[]{:S(2)}) %collective-permute-start.4) | collective-permute-done | bytes 131104 | tf_op jit(solution)/shard_map/ppermute | solution.py:30
  47.5 3.7 %collective-permute-done.3 = bf16[4,128,128]{2,1,0:T(8,128)(2,1)S(1)} collective-permute-done((bf16[4,128,128]{2,1,0:T(8,128)(2,1)S(1)}, bf16[4,128,128]{2,1,0:T(8,128)(2,1)S(1)}, u32[]{:S(2)}, u32[]{:S(2)}) %collective-permute-start.3) | collective-permute-done | bytes 131104 | tf_op jit(solution)/shard_map/ppermute | solution.py:30
  51.2 1.9 %fusion.15 = bf16[8,128,128]{2,1,0:T(8,128)(2,1)} fusion(bf16[8,128,128]{2,1,0:T(8,128)(2,1)S(1)} %collective-permute-done.2, bf16[8,128,128]{2,1,0:T(8,128)(2,1)S(1)} %collective-permute-done.1, bf16[4,128,128]{2,1,0:T(8,128)(2,1)S(1)} %collective-permute-done.4, bf16[4,128,128]{2,1,0:T(8,128)(2,1)S(1)} %collective-permute-done.3, ...), kind=kLoop, calls=%fused_computation.23 | loop fusion | flops 1310720 | bytes 1572864 | tf_op jit(solution)/shard_map/convert_element_type | solution.py:153
  53.1 3.0 %collective-permute-start.6 = (bf16[8,128,128]{2,1,0:T(8,128)(2,1)}, bf16[8,128,128]{2,1,0:T(8,128)(2,1)}, u32[]{:S(2)}, u32[]{:S(2)}) collective-permute-start(bf16[8,128,128]{2,1,0:T(8,128)(2,1)} %fusion.15), channel_id=1, source_target_pairs={{0,12},{4,0},{8,4},{12,8},{1,13},{5,1},{9,5},{13,9},{2,14},{6,2},{... | collective-permute-start | bytes 786440 | tf_op jit(solution)/shard_map/ppermute | solution.py:27
  56.1 0.0 collective-permute-start.5
  56.2 3.6 %shard_map.68 = f32[2,1024,128]{2,1,0:T(8,128)} custom-call(bf16[8,1024,128]{2,1,0:T(8,128)(2,1)} %get-tuple-element.9.q_ref, bf16[8,1024,128]{2,1,0:T(8,128)(2,1)} %get-tuple-element.10.k_ref, bf16[8,1024,128]{2,1,0:T(8,128)(2,1)} %get-tuple-element.11.v_ref), custom_call_target="tpu_custom_call" | custom-call | flops 738197504 | bytes 2621440 | tf_op jit(solution)/shard_map/pallas_call | solution.py:137
  59.7 0.0 copy-done.3
  59.8 0.0 copy-done.5
  59.8 3.6 %shard_map.67 = f32[2,1024,128]{2,1,0:T(8,128)} custom-call(bf16[8,1024,128]{2,1,0:T(8,128)(2,1)} %get-tuple-element.9.q_ref, bf16[8,1024,128]{2,1,0:T(8,128)(2,1)} %get-tuple-element.10.k_ref, bf16[8,1024,128]{2,1,0:T(8,128)(2,1)} %get-tuple-element.11.v_ref), custom_call_target="tpu_custom_call" | custom-call | flops 738197504 | bytes 2621440 | tf_op jit(solution)/shard_map/pallas_call | solution.py:137
  63.4 3.6 %shard_map.66 = f32[2,1024,128]{2,1,0:T(8,128)} custom-call(bf16[8,1024,128]{2,1,0:T(8,128)(2,1)} %get-tuple-element.9.q_ref, bf16[8,1024,128]{2,1,0:T(8,128)(2,1)} %get-tuple-element.10.k_ref, bf16[8,1024,128]{2,1,0:T(8,128)(2,1)} %get-tuple-element.11.v_ref), custom_call_target="tpu_custom_call" | custom-call | flops 738197504 | bytes 2621440 | tf_op jit(solution)/shard_map/pallas_call | solution.py:137
  67.0 3.7 %shard_map.65 = f32[2,1024,128]{2,1,0:T(8,128)} custom-call(bf16[8,1024,128]{2,1,0:T(8,128)(2,1)} %get-tuple-element.9.q_ref, bf16[8,1024,128]{2,1,0:T(8,128)(2,1)} %get-tuple-element.10.k_ref, bf16[8,1024,128]{2,1,0:T(8,128)(2,1)} %get-tuple-element.11.v_ref), custom_call_target="tpu_custom_call" | custom-call | flops 738197504 | bytes 2621440 | tf_op jit(solution)/shard_map/pallas_call | solution.py:137
  70.7 0.0 collective-permute-done.6
  70.7 0.9 slice.24
  71.6 3.3 %collective-permute-start.8 = (bf16[4,128,128]{2,1,0:T(8,128)(2,1)S(1)}, bf16[4,128,128]{2,1,0:T(8,128)(2,1)S(1)}, u32[]{:S(2)}, u32[]{:S(2)}) collective-permute-start(bf16[4,128,128]{2,1,0:T(8,128)(2,1)S(1)} %slice.24), channel_id=1, source_target_pairs={{0,12},{4,0},{8,4},{12,8},{1,13},{5,1},{9,5},{13,9},{2,14},{6,2},{... | collective-permute-start | bytes 393224 | tf_op jit(solution)/shard_map/ppermute | solution.py:30
  74.9 0.0 collective-permute-done.5
  74.9 0.9 slice.23
  75.8 0.0 copy-start.4
  75.9 0.0 copy-start.6
  75.9 0.1 collective-permute-start.7
  75.9 0.0 copy-done.2
  76.0 4.2 %pad_maximum_fusion.local_ref = f32[8,1024,128]{2,1,0:T(8,128)} fusion(f32[2,1024,128]{2,1,0:T(8,128)S(1)} %copy-done.2, f32[2,1024,128]{2,1,0:T(8,128)} %shard_map.67, f32[2,1024,128]{2,1,0:T(8,128)} %shard_map.66, f32[2,1024,128]{2,1,0:T(8,128)} %shard_map.65), kind=kLoop, calls=%fused_computation.9 | loop fusion | flops 3145728 | bytes 8388608 | tf_op jit(solution)/shard_map/concatenate | solution.py:150
  80.1 0.0 collective-permute-done.8
  80.1 2.0 %collective-permute-done.7 = bf16[4,128,128]{2,1,0:T(8,128)(2,1)S(1)} collective-permute-done((bf16[4,128,128]{2,1,0:T(8,128)(2,1)S(1)}, bf16[4,128,128]{2,1,0:T(8,128)(2,1)S(1)}, u32[]{:S(2)}, u32[]{:S(2)}) %collective-permute-start.7) | collective-permute-done | bytes 131104 | tf_op jit(solution)/shard_map/ppermute | solution.py:30
  82.1 0.0 copy-done.4
  82.1 0.0 copy-done.6
  82.1 2.1 %fusion.14.prefix_ref = f32[8,128,128]{2,1,0:T(8,128)} fusion(bf16[8,128,128]{2,1,0:T(8,128)(2,1)S(1)} %copy-done.4, bf16[8,128,128]{2,1,0:T(8,128)(2,1)S(1)} %collective-permute-done.2, bf16[8,128,128]{2,1,0:T(8,128)(2,1)} %collective-permute-done.6, bf16[8,128,128]{2,1,0:T(8,128)(2,1)} %collective-permute-done.5, ...), kind=kLoop, calls=%fused_computation.22 | loop fusion | flops 2490368 | bytes 2097176 | tf_op jit(solution)/shard_map/add | solution.py:154
  84.3 7.8 %shard_map.69 = bf16[8,1024,128]{2,1,0:T(8,128)(2,1)} custom-call(bf16[8,1024,128]{2,1,0:T(8,128)(2,1)} %get-tuple-element.9.q_ref, f32[8,1024,128]{2,1,0:T(8,128)} %pad_maximum_fusion.local_ref, f32[8,128,128]{2,1,0:T(8,128)} %fusion.14.prefix_ref, f32[8,1,128]{2,1,0:T(1,128)} %bitcast.25), custom_call_target="tpu_custom_call" | custom-call | flops 536870912 | bytes 8388608 | tf_op jit(solution)/shard_map/pallas_call | solution.py:156
  92.0 0.0 copy-done
  92.0 5.1 %bitcast_convert_fusion = bf16[1024,1024]{1,0:T(8,128)(2,1)} fusion(bf16[8,1024,128]{2,1,0:T(8,128)(2,1)} %shard_map.69, bf16[8,128,1024]{2,1,0:T(8,128)(2,1)S(1)} %bitcast.23), kind=kOutput, calls=%fused_computation.10 | convolution fusion | flops 2148532224 | bytes 6291456 | tf_op jit(solution)/shard_map/hte,hen->tn/dot_general | solution.py:166
  (7 shorter events, 0.0 us)
Async XLA Ops:
  0.0 92.0 %copy-start = (bf16[1024,1024]{1,0:T(8,128)(2,1)S(1)}, bf16[1024,1024]{1,0:T(8,128)(2,1)}, u32[]{:S(2)}) copy-start(bf16[1024,1024]{1,0:T(8,128)(2,1)} %param.11) | copy-start | bytes 6291460
  2.2 16.2 %copy-start.7 = (f32[4,3072]{1,0:T(4,128)S(1)}, f32[4,3072]{1,0:T(4,128)}, u32[]{:S(2)}) copy-start(f32[4,3072]{1,0:T(4,128)} %param.9) | copy-start | bytes 147460
  11.8 2.7 %copy-start.1 = (bf16[24,1024,128]{2,1,0:T(8,128)(2,1)}, bf16[24,1024,128]{2,1,0:T(8,128)(2,1)S(1)}, u32[]{:S(2)}) copy-start(bf16[24,1024,128]{2,1,0:T(8,128)(2,1)S(1)} %convert_bitcast_fusion.pq.pk.pv) | copy-start | bytes 18874372
  14.6 5.4 %collective-permute-start = (bf16[24,3,128]{2,1,0:T(4,128)(2,1)S(1)}, bf16[24,3,128]{2,1,0:T(4,128)(2,1)S(1)}, u32[]{:S(2)}, u32[]{:S(2)}) collective-permute-start(bf16[24,3,128]{2,1,0:T(4,128)(2,1)S(1)} %slice.20), channel_id=1, source_target_pairs={{0,1},{1,2},{2,3},{3,4},{4,5},{5,6},{6,7},{7,8},{8,9},{9,10},{10,1... | collective-permute-start | bytes 55304 | tf_op jit(solution)/shard_map/ppermute | solution.py:108
  32.3 8.9 %collective-permute-start.2 = (bf16[8,128,128]{2,1,0:T(8,128)(2,1)S(1)}, bf16[8,128,128]{2,1,0:T(8,128)(2,1)S(1)}, u32[]{:S(2)}, u32[]{:S(2)}) collective-permute-start(bf16[8,128,128]{2,1,0:T(8,128)(2,1)S(1)} %convert_element_type.68), channel_id=1, source_target_pairs={{0,3},{1,0},{2,1},{3,2},{4,7},{5,4},{6,5},{7,6},{8,11},{9,8},{10,9... | collective-permute-start | bytes 786440 | tf_op jit(solution)/shard_map/ppermute | solution.py:27
  36.7 8.2 %collective-permute-start.1 = (bf16[8,128,128]{2,1,0:T(8,128)(2,1)S(1)}, bf16[8,128,128]{2,1,0:T(8,128)(2,1)S(1)}, u32[]{:S(2)}, u32[]{:S(2)}) collective-permute-start(bf16[8,128,128]{2,1,0:T(8,128)(2,1)S(1)} %convert_element_type.68), channel_id=1, source_target_pairs={{0,1},{1,2},{2,3},{3,0},{4,5},{5,6},{6,7},{7,4},{8,9},{9,10},{10,1... | collective-permute-start | bytes 786440 | tf_op jit(solution)/shard_map/ppermute | solution.py:26
  41.2 6.3 %collective-permute-start.4 = (bf16[4,128,128]{2,1,0:T(8,128)(2,1)S(1)}, bf16[4,128,128]{2,1,0:T(8,128)(2,1)S(1)}, u32[]{:S(2)}, u32[]{:S(2)}) collective-permute-start(bf16[4,128,128]{2,1,0:T(8,128)(2,1)S(1)} %slice.22), channel_id=1, source_target_pairs={{0,3},{1,0},{2,1},{3,2},{4,7},{5,4},{6,5},{7,6},{8,11},{9,8},{10,9... | collective-permute-start | bytes 393224 | tf_op jit(solution)/shard_map/ppermute | solution.py:30
  44.9 14.8 %copy-start.3 = (bf16[8,128,128]{2,1,0:T(8,128)(2,1)}, bf16[8,128,128]{2,1,0:T(8,128)(2,1)S(1)}, u32[]{:S(2)}) copy-start(bf16[8,128,128]{2,1,0:T(8,128)(2,1)S(1)} %collective-permute-done.1) | copy-start | bytes 786436
  45.0 6.2 %collective-permute-start.3 = (bf16[4,128,128]{2,1,0:T(8,128)(2,1)S(1)}, bf16[4,128,128]{2,1,0:T(8,128)(2,1)S(1)}, u32[]{:S(2)}, u32[]{:S(2)}) collective-permute-start(bf16[4,128,128]{2,1,0:T(8,128)(2,1)S(1)} %slice.21), channel_id=1, source_target_pairs={{0,1},{1,2},{2,3},{3,0},{4,5},{5,6},{6,7},{7,4},{8,9},{9,10},{10,1... | collective-permute-start | bytes 393224 | tf_op jit(solution)/shard_map/ppermute | solution.py:30
  51.2 8.5 %copy-start.5 = (bf16[4,128,128]{2,1,0:T(8,128)(2,1)}, bf16[4,128,128]{2,1,0:T(8,128)(2,1)S(1)}, u32[]{:S(2)}) copy-start(bf16[4,128,128]{2,1,0:T(8,128)(2,1)S(1)} %collective-permute-done.3) | copy-start | bytes 393220
  53.1 17.6 %collective-permute-start.6 = (bf16[8,128,128]{2,1,0:T(8,128)(2,1)}, bf16[8,128,128]{2,1,0:T(8,128)(2,1)}, u32[]{:S(2)}, u32[]{:S(2)}) collective-permute-start(bf16[8,128,128]{2,1,0:T(8,128)(2,1)} %fusion.15), channel_id=1, source_target_pairs={{0,12},{4,0},{8,4},{12,8},{1,13},{5,1},{9,5},{13,9},{2,14},{6,2},{... | collective-permute-start | bytes 786440 | tf_op jit(solution)/shard_map/ppermute | solution.py:27
  56.1 18.8 %collective-permute-start.5 = (bf16[8,128,128]{2,1,0:T(8,128)(2,1)}, bf16[8,128,128]{2,1,0:T(8,128)(2,1)}, u32[]{:S(2)}, u32[]{:S(2)}) collective-permute-start(bf16[8,128,128]{2,1,0:T(8,128)(2,1)} %fusion.15), channel_id=1, source_target_pairs={{0,4},{4,8},{8,12},{12,0},{1,5},{5,9},{9,13},{13,1},{2,6},{6,10},{... | collective-permute-start | bytes 786440 | tf_op jit(solution)/shard_map/ppermute | solution.py:26
  67.0 9.0 %copy-start.2 = (f32[2,1024,128]{2,1,0:T(8,128)S(1)}, f32[2,1024,128]{2,1,0:T(8,128)}, u32[]{:S(2)}) copy-start(f32[2,1024,128]{2,1,0:T(8,128)} %shard_map.68) | copy-start | bytes 3145732
  71.6 8.5 %collective-permute-start.8 = (bf16[4,128,128]{2,1,0:T(8,128)(2,1)S(1)}, bf16[4,128,128]{2,1,0:T(8,128)(2,1)S(1)}, u32[]{:S(2)}, u32[]{:S(2)}) collective-permute-start(bf16[4,128,128]{2,1,0:T(8,128)(2,1)S(1)} %slice.24), channel_id=1, source_target_pairs={{0,12},{4,0},{8,4},{12,8},{1,13},{5,1},{9,5},{13,9},{2,14},{6,2},{... | collective-permute-start | bytes 393224 | tf_op jit(solution)/shard_map/ppermute | solution.py:30
  75.8 6.3 %copy-start.4 = (bf16[8,128,128]{2,1,0:T(8,128)(2,1)S(1)}, bf16[8,128,128]{2,1,0:T(8,128)(2,1)}, u32[]{:S(2)}) copy-start(bf16[8,128,128]{2,1,0:T(8,128)(2,1)} %copy-done.3) | copy-start | bytes 786436
  75.9 6.3 %copy-start.6 = (bf16[4,128,128]{2,1,0:T(8,128)(2,1)S(1)}, bf16[4,128,128]{2,1,0:T(8,128)(2,1)}, u32[]{:S(2)}) copy-start(bf16[4,128,128]{2,1,0:T(8,128)(2,1)} %copy-done.5) | copy-start | bytes 393220
  75.9 6.2 %collective-permute-start.7 = (bf16[4,128,128]{2,1,0:T(8,128)(2,1)S(1)}, bf16[4,128,128]{2,1,0:T(8,128)(2,1)S(1)}, u32[]{:S(2)}, u32[]{:S(2)}) collective-permute-start(bf16[4,128,128]{2,1,0:T(8,128)(2,1)S(1)} %slice.23), channel_id=1, source_target_pairs={{0,4},{4,8},{8,12},{12,0},{1,5},{5,9},{9,13},{13,1},{2,6},{6,10},{... | collective-permute-start | bytes 393224 | tf_op jit(solution)/shard_map/ppermute | solution.py:30

commit v5 on v3

--- a/solution.py
+++ b/solution.py
@@ -18,26 +18,13 @@
     return hi.astype(jnp.bfloat16), (x - hi).astype(jnp.bfloat16)
 
 
-def ring_earlier(x, axis):
+def gather_earlier(x, axis):
     count = lax.axis_size(axis)
     place = lax.axis_index(axis)
-    forward = [(i, (i + 1) % count) for i in range(count)]
-    backward = [(i, (i - 1) % count) for i in range(count)]
-    from_prev = lax.ppermute(x, axis, forward)
-    from_next = lax.ppermute(x, axis, backward)
-    half = x.shape[0] // 2
-    from_far = jnp.concatenate(
-        [lax.ppermute(from_prev[:half], axis, forward), lax.ppermute(from_next[half:], axis, backward)],
-        0,
-    )
-    before = jnp.zeros(x.shape, jnp.float32)
-    total = x.astype(jnp.float32)
-    for offset, part in ((-1, from_prev), (1, from_next), (2, from_far)):
-        part = part.astype(jnp.float32)
-        earlier = ((place + offset) % count < place).astype(jnp.float32)
-        before = before + earlier * part
-        total = total + part
-    return before, total
+    gathered = lax.all_to_all(jnp.broadcast_to(x, (count,) + x.shape), axis, 0, 0)
+    values = gathered.astype(jnp.float32)
+    earlier = (lax.iota(jnp.int32, count) < place).astype(jnp.float32)
+    return jnp.sum(values * earlier[:, None, None, None], 0), jnp.sum(values, 0)
 
 
 def conv_kernel(pq, pk, pv, eq, ek, ev, tq, tk, tv, oq, ok, ov, state_ref, buf):
@@ -158,8 +145,8 @@
         ),
     )(query, key, value)
 
-    zbefore, row_total = ring_earlier(state.astype(jnp.bfloat16), "sz")
-    ybefore, _ = ring_earlier(row_total.astype(jnp.bfloat16), "sy")
+    zbefore, row_total = gather_earlier(state.astype(jnp.bfloat16), "sz")
+    ybefore, _ = gather_earlier(row_total.astype(jnp.bfloat16), "sy")
     prefix = ybefore + zbefore
 
     out = pl.pallas_call(

time: 89.7 us -> 85.6 us (0.954)
  blocking collectives: 0 us -> 19.4 us
  waiting for transfers between devices: 16.3 us -> 2.79 us
  starting transfers between devices: 19.1 us -> 8.36 us
  local copies, waits for them, and re-layouts: 4 us -> 5.4 us
    all_to_all x0 -> x1, blocking collectives: none -> 19.4 us  [gather_earlier(): lax.all_to_all(jnp.broadcast_to(x, (count,) + x.shape), axis, 0, 0)]
    ppermute x8 -> x0, waiting for transfers between devices: 15.5 us -> none  [the longest x2 9.17 us: ring_earlier(): from_next = lax.ppermute(x, axis, backward)]
    ppermute x8 -> x0, starting transfers between devices: 15.2 us -> none  [the longest x2 7.57 us: ring_earlier(): from_next = lax.ppermute(x, axis, backward)]
    all_to_all x0 -> x1, starting transfers between devices: none -> 4.46 us  [gather_earlier(): lax.all_to_all(jnp.broadcast_to(x, (count,) + x.shape), axis, 0, 0)]
    all_to_all x0 -> x1, waiting for transfers between devices: none -> 1.94 us  [gather_earlier(): lax.all_to_all(jnp.broadcast_to(x, (count,) + x.shape), axis, 0, 0)]
    broadcast_in_dim x0 -> x2, local copies, waits for them, and re-layouts: none -> 1.45 us  [gather_earlier(): jnp.broadcast_to(x, (count,) + x.shape)]
    convert_element_type x2 -> x3, other arithmetic: 2.24 us -> 1.08 us  [the longest x1 1.08 us: local(): zbefore, row_total = gather_earlier(state.astype(jnp.bfloat16), 'sz')]
  transfers between devices with their start and end apart: 9 -> 2, of which waited for: 6 -> 2; matrix products, arithmetic and copies ran while one was open for 1% -> 1% of each run, Pallas kernels for 11% -> 12%
where the time goes in v5:
time: 85.6 us; the launch traced here: 84.8 us
  Pallas kernels  34.4 us (40%)
  blocking collectives  19.4 us (23%)
  matrix products  9.57 us (11%)
  starting transfers between devices  8.36 us (10%)
  local copies, waits for them, and re-layouts  5.4 us (6%)
  other arithmetic  4.77 us (6%)
  waiting for transfers between devices  2.79 us (3%)
    all_to_all x1, blocking collectives, gather_earlier(): lax.all_to_all(jnp.broadcast_to(x, (count,) + x.shape), axis, 0, 0)  19.4 us
    pallas_call x1, Pallas kernels, local(): pl.pallas_call(out_kernel, grid=(H,), in_specs=[slab(0, rows, DH), slab(0...  13.6 us
    pallas_call x1, Pallas kernels, local(): pl.pallas_call(conv_kernel, grid=(H,), in_specs=[slab(0, rows, DH), slab(...  10.6 us
    pallas_call x1, Pallas kernels, local(): pl.pallas_call(local_kernel, grid=(H,), in_specs=[slab(0, rows, DH)] * 3,...  10.2 us
    dot_general x1, matrix products, local(): jnp.einsum('td,dje->jte', normed, w_qkv.reshape(width, slabs, DH), prefer...  9.57 us
    all_to_all x1, starting transfers between devices, gather_earlier(): lax.all_to_all(jnp.broadcast_to(x, (count,) + x.shape), axis, 0, 0)  4.46 us
    ppermute x1, starting transfers between devices, local(): lax.ppermute(projected[:, rows - (KW - 1):, :], seq_axes, [(i, i + 1) for...  3.9 us
    unnamed x4, local copies, waits for them, and re-layouts  2.66 us
  transfers between devices with their start and end apart: 2, of which 2 were waited for; matrix products, arithmetic and copies ran while one was open for 1% of the time, Pallas kernels for 12%

profile of v5, /device:TPU:0, one launch (start us, length us, event | category | flops | bytes accessed | tf_op | source)
XLA Modules:
  0.0 84.8 jit_solution(15095498747007089634)
XLA Ops:
  0.0 2.1 %fusion.3 = f32[1024]{0:T(1024)S(1)} fusion(bf16[1024,1024]{1,0:T(8,128)(2,1)} %param.6), kind=kLoop, calls=%fused_computation.6 | loop fusion | flops 3144704 | bytes 2101248 | tf_op jit(solution)/shard_map/reduce_sum | solution.py:99
  2.1 0.0 copy-start.1
  2.1 9.6 %convert_bitcast_fusion.pq.pk.pv = bf16[24,1024,128]{2,1,0:T(8,128)(2,1)S(1)} fusion(bf16[1024,1024]{1,0:T(8,128)(2,1)} %param.6, f32[1024]{0:T(1024)} %param.7, f32[1024]{0:T(1024)S(1)} %add_rsqrt_fusion, bf16[1024,3072]{1,0:T(8,128)(2,1)} %param.8), kind=kOutput, calls=%fused_computation.3 | convolution fusion | flops 6449790976 | bytes 14688256 | tf_op jit(solution)/shard_map/td,dje->jte/dot_general | solution.py:103
  11.7 0.0 copy-start
  11.7 2.7 %copy-done = bf16[24,1024,128]{2,1,0:T(8,128)(2,1)} copy-done((bf16[24,1024,128]{2,1,0:T(8,128)(2,1)}, bf16[24,1024,128]{2,1,0:T(8,128)(2,1)S(1)}, u32[]{:S(2)}) %copy-start) | copy-done | bytes 6291480
  14.4 3.9 %collective-permute-start = (bf16[24,3,128]{2,1,0:T(4,128)(2,1)S(1)}, bf16[24,3,128]{2,1,0:T(4,128)(2,1)S(1)}, u32[]{:S(2)}, u32[]{:S(2)}) collective-permute-start(bf16[24,3,128]{2,1,0:T(4,128)(2,1)S(1)} %slice.4), channel_id=1, source_target_pairs={{0,1},{1,2},{2,3},{3,4},{4,5},{5,6},{6,7},{7,8},{8,9},{9,10},{10,1... | collective-permute-start | bytes 55304 | tf_op jit(solution)/shard_map/ppermute | solution.py:109
  18.3 0.0 copy-done.1
  18.3 0.6 pad.9.tq.tk.tv
  18.9 0.9 %collective-permute-done = bf16[24,3,128]{2,1,0:T(4,128)(2,1)S(1)} collective-permute-done((bf16[24,3,128]{2,1,0:T(4,128)(2,1)S(1)}, bf16[24,3,128]{2,1,0:T(4,128)(2,1)S(1)}, u32[]{:S(2)}, u32[]{:S(2)}) %collective-permute-start) | collective-permute-done | bytes 18464 | tf_op jit(solution)/shard_map/ppermute | solution.py:109
  19.8 0.6 pad.8.eq.ek.ev
  20.4 10.6 %shard_map.64 = (bf16[8,1024,128]{2,1,0:T(8,128)(2,1)}, bf16[8,1024,128]{2,1,0:T(8,128)(2,1)}, bf16[8,1024,128]{2,1,0:T(8,128)(2,1)}, f32[8,128,128]{2,1,0:T(8,128)}) custom-call(bf16[24,1024,128]{2,1,0:T(8,128)(2,1)} %copy-done, bf16[24,1024,128]{2,1,0:T(8,128)(2,1)} %copy-done, bf16[24,1024,128]{2,1,0:T(8,128)(2,1)} %copy-done, ...), custom_call_target="tpu_custom_call" | custom-call | flops 306184192 | bytes 12582912 | tf_op jit(solution)/shard_map/pallas_call | solution.py:118
  31.0 1.1 %convert_element_type.43 = bf16[8,128,128]{2,1,0:T(8,128)(2,1)S(1)} convert(f32[8,128,128]{2,1,0:T(8,128)} %get-tuple-element.12) | non-fusion elementwise | flops 131072 | bytes 786432 | tf_op jit(solution)/shard_map/convert_element_type | solution.py:148
  32.1 0.2 broadcast_in_dim.4
  32.3 19.4 %all_to_all.10 = bf16[4,8,128,128]{3,2,1,0:T(8,128)(2,1)S(1)} all-to-all(bf16[4,8,128,128]{3,2,1,0:T(8,128)(2,1)S(1)} %broadcast_in_dim.4), channel_id=1, replica_groups=mesh['trace'=8,'sy'=4,'sz'=4] {'sz'}, dimensions={0} | all-to-all | bytes 2097152 | tf_op jit(solution)/shard_map/all_to_all | solution.py:24
  51.8 0.2 reduce_sum.40
  52.0 1.2 %broadcast_in_dim.5 = bf16[4,8,128,128]{3,2,1,0:T(8,128)(2,1)} broadcast(bf16[8,128,128]{2,1,0:T(8,128)(2,1)S(1)} %reduce_sum.40), dimensions={1,2,3} | broadcast | bytes 1310720 | tf_op jit(solution)/shard_map/broadcast_in_dim | solution.py:24
  53.2 4.5 %all-to-all-start.1 = ((bf16[4,8,128,128]{3,2,1,0:T(8,128)(2,1)}), bf16[4,8,128,128]{3,2,1,0:T(8,128)(2,1)S(1)}, u32[]{:S(2)}, u32[]{:S(2)}) async-start(bf16[4,8,128,128]{3,2,1,0:T(8,128)(2,1)} %broadcast_in_dim.5), calls=%async_computation.1 | async-start | bytes 2097152 | tf_op jit(solution)/shard_map/all_to_all | solution.py:24
  57.6 10.2 %shard_map.65.local_ref = f32[8,1024,128]{2,1,0:T(8,128)} custom-call(bf16[8,1024,128]{2,1,0:T(8,128)(2,1)} %get-tuple-element.9.q_ref, bf16[8,1024,128]{2,1,0:T(8,128)(2,1)} %get-tuple-element.10.k_ref, bf16[8,1024,128]{2,1,0:T(8,128)(2,1)} %get-tuple-element.11.v_ref), custom_call_target="tpu_custom_call" | custom-call | flops 2952790016 | bytes 10485760 | tf_op jit(solution)/shard_map/pallas_call | solution.py:135
  67.9 0.3 multiply_reduce_fusion
  68.1 1.9 %all-to-all-done.1 = bf16[4,8,128,128]{3,2,1,0:T(8,128)(2,1)S(1)} async-done(((bf16[4,8,128,128]{3,2,1,0:T(8,128)(2,1)}), bf16[4,8,128,128]{3,2,1,0:T(8,128)(2,1)S(1)}, u32[]{:S(2)}, u32[]{:S(2)}) %all-to-all-start.1) | async-done | bytes 1048608 | tf_op jit(solution)/shard_map/all_to_all | solution.py:24
  70.1 0.3 multiply_reduce_fusion.1
  70.4 0.9 %add.20.prefix_ref = f32[8,128,128]{2,1,0:T(8,128)} add(f32[8,128,128]{2,1,0:T(8,128)S(1)} %multiply_reduce_fusion.1, f32[8,128,128]{2,1,0:T(8,128)S(1)} %multiply_reduce_fusion) | non-fusion elementwise | flops 131072 | bytes 1572864 | tf_op jit(solution)/shard_map/add | solution.py:150
  71.2 13.6 %shard_map.66 = bf16[1024,1024]{1,0:T(8,128)(2,1)} custom-call(bf16[8,1024,128]{2,1,0:T(8,128)(2,1)} %get-tuple-element.9.q_ref, f32[8,1024,128]{2,1,0:T(8,128)} %shard_map.65.local_ref, f32[8,128,128]{2,1,0:T(8,128)} %add.20.prefix_ref, f32[8,1,128]{2,1,0:T(1,128)} %bitcast.21, bf16[8,128,1024]{2,1,0:T(8,128)(2,1)} %bitcast.19), custom_call_target="tpu_custom_call" | custom-call | flops 2684354560 | bytes 10485760 | tf_op jit(solution)/shard_map/pallas_call | solution.py:152
  (4 shorter events, 0.0 us)
Async XLA Ops:
  2.1 16.2 %copy-start.1 = (f32[4,3072]{1,0:T(4,128)S(1)}, f32[4,3072]{1,0:T(4,128)}, u32[]{:S(2)}) copy-start(f32[4,3072]{1,0:T(4,128)} %param.9) | copy-start | bytes 147460
  11.7 2.7 %copy-start = (bf16[24,1024,128]{2,1,0:T(8,128)(2,1)}, bf16[24,1024,128]{2,1,0:T(8,128)(2,1)S(1)}, u32[]{:S(2)}) copy-start(bf16[24,1024,128]{2,1,0:T(8,128)(2,1)S(1)} %convert_bitcast_fusion.pq.pk.pv) | copy-start | bytes 18874372
  14.4 5.4 %collective-permute-start = (bf16[24,3,128]{2,1,0:T(4,128)(2,1)S(1)}, bf16[24,3,128]{2,1,0:T(4,128)(2,1)S(1)}, u32[]{:S(2)}, u32[]{:S(2)}) collective-permute-start(bf16[24,3,128]{2,1,0:T(4,128)(2,1)S(1)} %slice.4), channel_id=1, source_target_pairs={{0,1},{1,2},{2,3},{3,4},{4,5},{5,6},{6,7},{7,8},{8,9},{9,10},{10,1... | collective-permute-start | bytes 55304 | tf_op jit(solution)/shard_map/ppermute | solution.py:109
  53.2 16.9 %all-to-all-start.1 = ((bf16[4,8,128,128]{3,2,1,0:T(8,128)(2,1)}), bf16[4,8,128,128]{3,2,1,0:T(8,128)(2,1)S(1)}, u32[]{:S(2)}, u32[]{:S(2)}) async-start(bf16[4,8,128,128]{3,2,1,0:T(8,128)(2,1)} %broadcast_in_dim.5), calls=%async_computation.1 | async-start | bytes 2097152 | tf_op jit(solution)/shard_map/all_to_all | solution.py:24

commit v6 on v5

--- a/solution.py
+++ b/solution.py
@@ -18,13 +18,43 @@
     return hi.astype(jnp.bfloat16), (x - hi).astype(jnp.bfloat16)
 
 
-def gather_earlier(x, axis):
+def ring_sum(messages, axis, weight=None):
+    count = lax.axis_size(axis)
+    total = None
+    for offset, message in messages.items():
+        pairs = [(i, (i + offset) % count) for i in range(count)]
+        part = lax.ppermute(message.astype(jnp.bfloat16), axis, pairs).astype(jnp.float32)
+        if weight is not None:
+            part = weight(offset) * part
+        total = part if total is None else total + part
+    return total
+
+
+def before_mask(axis, offset):
     count = lax.axis_size(axis)
     place = lax.axis_index(axis)
-    gathered = lax.all_to_all(jnp.broadcast_to(x, (count,) + x.shape), axis, 0, 0)
-    values = gathered.astype(jnp.float32)
-    earlier = (lax.iota(jnp.int32, count) < place).astype(jnp.float32)
-    return jnp.sum(values * earlier[:, None, None, None], 0), jnp.sum(values, 0)
+    return (place < (place + offset) % count).astype(jnp.float32)
+
+
+def after_mask(axis, offset):
+    count = lax.axis_size(axis)
+    place = lax.axis_index(axis)
+    return ((place - offset) % count < place).astype(jnp.float32)
+
+
+def earlier_states(state):
+    offsets = (1, -1, 2)
+    half = state.shape[0] // 2
+    first, second = state[:half], state[half:]
+    both = lambda o: jnp.stack([after_mask("sz", o), jnp.float32(1.0)])[:, None, None, None]
+    row = ring_sum({o: first for o in offsets}, "sz", both)
+    row_before, row_total = row[0], row[1] + first
+    rows_before = ring_sum({o: row_total for o in offsets}, "sy", lambda o: after_mask("sy", o))
+    column_before = ring_sum({o: second for o in offsets}, "sy", lambda o: after_mask("sy", o))
+    mixed_before = column_before + ring_sum(
+        {o: column_before + second * before_mask("sz", o) for o in offsets}, "sz"
+    )
+    return jnp.concatenate([row_before + rows_before, mixed_before], 0)
 
 
 def conv_kernel(pq, pk, pv, eq, ek, ev, tq, tk, tv, oq, ok, ov, state_ref, buf):
@@ -145,9 +175,7 @@
         ),
     )(query, key, value)
 
-    zbefore, row_total = gather_earlier(state.astype(jnp.bfloat16), "sz")
-    ybefore, _ = gather_earlier(row_total.astype(jnp.bfloat16), "sy")
-    prefix = ybefore + zbefore
+    prefix = earlier_states(state)
 
     out = pl.pallas_call(
         out_kernel,

time: 85.6 us -> 88.2 us (1.030)
  blocking collectives: 19.4 us -> 0 us
  starting transfers between devices: 8.36 us -> 22.2 us
  waiting for transfers between devices: 2.79 us -> 11.4 us
    all_to_all x1 -> x0, blocking collectives: 19.4 us -> none  [gather_earlier(): lax.all_to_all(jnp.broadcast_to(x, (count,) + x.shape), axis, 0, 0)]
    ppermute x0 -> x12, starting transfers between devices: none -> 18.3 us  [ring_sum(): lax.ppermute(message.astype(jnp.bfloat16), axis, pairs).astype(jnp.float32)]
    ppermute x0 -> x12, waiting for transfers between devices: none -> 10.6 us  [ring_sum(): lax.ppermute(message.astype(jnp.bfloat16), axis, pairs).astype(jnp.float32)]
    all_to_all x1 -> x0, starting transfers between devices: 4.46 us -> none  [gather_earlier(): lax.all_to_all(jnp.broadcast_to(x, (count,) + x.shape), axis, 0, 0)]
    all_to_all x1 -> x0, waiting for transfers between devices: 1.94 us -> none  [gather_earlier(): lax.all_to_all(jnp.broadcast_to(x, (count,) + x.shape), axis, 0, 0)]
    broadcast_in_dim x2 -> x0, local copies, waits for them, and re-layouts: 1.45 us -> none  [gather_earlier(): jnp.broadcast_to(x, (count,) + x.shape)]
    slice x0 -> x1, local copies, waits for them, and re-layouts: none -> 1.07 us  [earlier_states(): first, second = (state[:half], state[half:])]
  transfers between devices with their start and end apart: 2 -> 13, of which waited for: 2 -> 6; matrix products, arithmetic and copies ran while one was open for 1% -> 1% of each run, Pallas kernels for 12% -> 12%
where the time goes in v6:
time: 88.2 us; the launch traced here: 87.6 us
  Pallas kernels  34.4 us (39%)
  starting transfers between devices  22.2 us (25%)
  waiting for transfers between devices  11.4 us (13%)
  matrix products  9.57 us (11%)
  local copies, waits for them, and re-layouts  5.02 us (6%)
  other arithmetic  4.7 us (5%)
    ppermute x12, starting transfers between devices, ring_sum(): lax.ppermute(message.astype(jnp.bfloat16), axis, pairs).astype(jnp.float32)  18.3 us
    pallas_call x1, Pallas kernels, local(): pl.pallas_call(out_kernel, grid=(H,), in_specs=[slab(0, rows, DH), slab(0...  13.6 us
    pallas_call x1, Pallas kernels, local(): pl.pallas_call(conv_kernel, grid=(H,), in_specs=[slab(0, rows, DH), slab(...  10.6 us
    ppermute x12, waiting for transfers between devices, ring_sum(): lax.ppermute(message.astype(jnp.bfloat16), axis, pairs).astype(jnp.float32)  10.6 us
    pallas_call x1, Pallas kernels, local(): pl.pallas_call(local_kernel, grid=(H,), in_specs=[slab(0, rows, DH)] * 3,...  10.2 us
    dot_general x1, matrix products, local(): jnp.einsum('td,dje->jte', normed, w_qkv.reshape(width, slabs, DH), prefer...  9.57 us
    ppermute x1, starting transfers between devices, local(): lax.ppermute(projected[:, rows - (KW - 1):, :], seq_axes, [(i, i + 1) for...  3.9 us
    unnamed x4, local copies, waits for them, and re-layouts  2.66 us
  transfers between devices with their start and end apart: 13, of which 6 were waited for; matrix products, arithmetic and copies ran while one was open for 1% of the time, Pallas kernels for 12%

profile of v6, /device:TPU:0, one launch (start us, length us, event | category | flops | bytes accessed | tf_op | source)
XLA Modules:
  0.0 87.6 jit_solution(10518112321195989929)
XLA Ops:
  0.0 2.1 %fusion.3 = f32[1024]{0:T(1024)S(1)} fusion(bf16[1024,1024]{1,0:T(8,128)(2,1)} %param.6), kind=kLoop, calls=%fused_computation.6 | loop fusion | flops 3144704 | bytes 2101248 | tf_op jit(solution)/shard_map/reduce_sum | solution.py:129
  2.1 0.0 copy-start.1
  2.1 9.6 %convert_bitcast_fusion.pq.pk.pv = bf16[24,1024,128]{2,1,0:T(8,128)(2,1)S(1)} fusion(bf16[1024,1024]{1,0:T(8,128)(2,1)} %param.6, f32[1024]{0:T(1024)} %param.7, f32[1024]{0:T(1024)S(1)} %add_rsqrt_fusion, bf16[1024,3072]{1,0:T(8,128)(2,1)} %param.8), kind=kOutput, calls=%fused_computation.3 | convolution fusion | flops 6449790976 | bytes 14688256 | tf_op jit(solution)/shard_map/td,dje->jte/dot_general | solution.py:133
  11.7 0.0 copy-start
  11.7 2.7 %copy-done = bf16[24,1024,128]{2,1,0:T(8,128)(2,1)} copy-done((bf16[24,1024,128]{2,1,0:T(8,128)(2,1)}, bf16[24,1024,128]{2,1,0:T(8,128)(2,1)S(1)}, u32[]{:S(2)}) %copy-start) | copy-done | bytes 6291480
  14.4 3.9 %collective-permute-start = (bf16[24,3,128]{2,1,0:T(4,128)(2,1)S(1)}, bf16[24,3,128]{2,1,0:T(4,128)(2,1)S(1)}, u32[]{:S(2)}, u32[]{:S(2)}) collective-permute-start(bf16[24,3,128]{2,1,0:T(4,128)(2,1)S(1)} %slice.20), channel_id=1, source_target_pairs={{0,1},{1,2},{2,3},{3,4},{4,5},{5,6},{6,7},{7,8},{8,9},{9,10},{10,1... | collective-permute-start | bytes 55304 | tf_op jit(solution)/shard_map/ppermute | solution.py:139
  18.3 0.0 copy-done.1
  18.3 0.6 pad.9.tq.tk.tv
  18.9 0.8 collective-permute-done
  19.8 0.6 pad.8.eq.ek.ev
  20.4 10.6 %shard_map.64 = (bf16[8,1024,128]{2,1,0:T(8,128)(2,1)}, bf16[8,1024,128]{2,1,0:T(8,128)(2,1)}, bf16[8,1024,128]{2,1,0:T(8,128)(2,1)}, f32[8,128,128]{2,1,0:T(8,128)}) custom-call(bf16[24,1024,128]{2,1,0:T(8,128)(2,1)} %copy-done, bf16[24,1024,128]{2,1,0:T(8,128)(2,1)} %copy-done, bf16[24,1024,128]{2,1,0:T(8,128)(2,1)} %copy-done, ...), custom_call_target="tpu_custom_call" | custom-call | flops 306184192 | bytes 12582912 | tf_op jit(solution)/shard_map/pallas_call | solution.py:148
  31.0 1.1 %fusion.18 = (bf16[4,128,128]{2,1,0:T(8,128)(2,1)S(1)}, bf16[4,128,128]{2,1,0:T(8,128)(2,1)S(1)}) fusion(f32[8,128,128]{2,1,0:T(8,128)} %get-tuple-element.12), kind=kLoop, calls=%fused_computation.33 | loop fusion | bytes 524288 | tf_op jit(solution)/shard_map/slice | solution.py:48
  32.1 4.3 %collective-permute-start.3 = (bf16[4,128,128]{2,1,0:T(8,128)(2,1)S(1)}, bf16[4,128,128]{2,1,0:T(8,128)(2,1)S(1)}, u32[]{:S(2)}, u32[]{:S(2)}) collective-permute-start(bf16[4,128,128]{2,1,0:T(8,128)(2,1)S(1)} %get-tuple-element.17), channel_id=1, source_target_pairs={{0,2},{1,3},{2,0},{3,1},{4,6},{5,7},{6,4},{7,5},{8,10},{9,11},{10,... | collective-permute-start | bytes 393224 | tf_op jit(solution)/shard_map/ppermute | solution.py:26
  36.4 0.7 collective-permute-start.2
  37.1 1.3 %collective-permute-start.1 = (bf16[4,128,128]{2,1,0:T(8,128)(2,1)S(1)}, bf16[4,128,128]{2,1,0:T(8,128)(2,1)S(1)}, u32[]{:S(2)}, u32[]{:S(2)}) collective-permute-start(bf16[4,128,128]{2,1,0:T(8,128)(2,1)S(1)} %get-tuple-element.17), channel_id=1, source_target_pairs={{0,1},{1,2},{2,3},{3,0},{4,5},{5,6},{6,7},{7,4},{8,9},{9,10},{10,1... | collective-permute-start | bytes 393224 | tf_op jit(solution)/shard_map/ppermute | solution.py:26
  38.5 0.1 fusion.17
  38.6 0.1 fusion.15
  38.7 3.2 %collective-permute-start.9 = (bf16[4,128,128]{2,1,0:T(8,128)(2,1)S(1)}, bf16[4,128,128]{2,1,0:T(8,128)(2,1)S(1)}, u32[]{:S(2)}, u32[]{:S(2)}) collective-permute-start(bf16[4,128,128]{2,1,0:T(8,128)(2,1)S(1)} %get-tuple-element.18), channel_id=1, source_target_pairs={{0,8},{4,12},{8,0},{12,4},{1,9},{5,13},{9,1},{13,5},{2,10},{6,14},... | collective-permute-start | bytes 393224 | tf_op jit(solution)/shard_map/ppermute | solution.py:26
  41.9 1.1 %collective-permute-start.8 = (bf16[4,128,128]{2,1,0:T(8,128)(2,1)S(1)}, bf16[4,128,128]{2,1,0:T(8,128)(2,1)S(1)}, u32[]{:S(2)}, u32[]{:S(2)}) collective-permute-start(bf16[4,128,128]{2,1,0:T(8,128)(2,1)S(1)} %get-tuple-element.18), channel_id=1, source_target_pairs={{0,12},{4,0},{8,4},{12,8},{1,13},{5,1},{9,5},{13,9},{2,14},{6,2},{... | collective-permute-start | bytes 393224 | tf_op jit(solution)/shard_map/ppermute | solution.py:26
  42.9 0.0 collective-permute-done.3
  42.9 1.0 %collective-permute-start.7 = (bf16[4,128,128]{2,1,0:T(8,128)(2,1)S(1)}, bf16[4,128,128]{2,1,0:T(8,128)(2,1)S(1)}, u32[]{:S(2)}, u32[]{:S(2)}) collective-permute-start(bf16[4,128,128]{2,1,0:T(8,128)(2,1)S(1)} %get-tuple-element.18), channel_id=1, source_target_pairs={{0,4},{4,8},{8,12},{12,0},{1,5},{5,9},{9,13},{13,1},{2,6},{6,10},{... | collective-permute-start | bytes 393224 | tf_op jit(solution)/shard_map/ppermute | solution.py:26
  43.9 0.0 collective-permute-done.2
  44.0 0.0 collective-permute-done.1
  44.0 0.2 multiply_add_fusion
  44.2 2.1 %collective-permute-done.9 = bf16[4,128,128]{2,1,0:T(8,128)(2,1)S(1)} collective-permute-done((bf16[4,128,128]{2,1,0:T(8,128)(2,1)S(1)}, bf16[4,128,128]{2,1,0:T(8,128)(2,1)S(1)}, u32[]{:S(2)}, u32[]{:S(2)}) %collective-permute-start.9) | collective-permute-done | bytes 131104 | tf_op jit(solution)/shard_map/ppermute | solution.py:26
  46.3 0.6 collective-permute-done.8
  46.9 2.2 %collective-permute-done.7 = bf16[4,128,128]{2,1,0:T(8,128)(2,1)S(1)} collective-permute-done((bf16[4,128,128]{2,1,0:T(8,128)(2,1)S(1)}, bf16[4,128,128]{2,1,0:T(8,128)(2,1)S(1)}, u32[]{:S(2)}, u32[]{:S(2)}) %collective-permute-start.7) | collective-permute-done | bytes 131104 | tf_op jit(solution)/shard_map/ppermute | solution.py:26
  49.1 1.2 %add_convert_fusion.2 = (bf16[4,128,128]{2,1,0:T(8,128)(2,1)S(1)}, bf16[4,128,128]{2,1,0:T(8,128)(2,1)S(1)}, bf16[4,128,128]{2,1,0:T(8,128)(2,1)S(1)}, bf16[4,128,128]{2,1,0:T(8,128)(2,1)S(1)}) fusion(f32[8,128,128]{2,1,0:T(8,128)} %get-tuple-element.12, f32[]{:T(128)S(6)} %convert_element_type.118, bf16[4,128,128]{2,1,0:T(8,128)(2,1)S(1)} %collective-permute-done.9, ...), kind=kLoop, calls=%fused_computation.22 | loop fusion | flops 1245184 | bytes 1703960 | tf_op jit(solution)/shard_map/convert_element_type | solution.py:26
  50.3 1.9 %collective-permute-start.12 = (bf16[4,128,128]{2,1,0:T(8,128)(2,1)S(1)}, bf16[4,128,128]{2,1,0:T(8,128)(2,1)S(1)}, u32[]{:S(2)}, u32[]{:S(2)}) collective-permute-start(bf16[4,128,128]{2,1,0:T(8,128)(2,1)S(1)} %get-tuple-element.15), channel_id=1, source_target_pairs={{0,2},{1,3},{2,0},{3,1},{4,6},{5,7},{6,4},{7,5},{8,10},{9,11},{10,... | collective-permute-start | bytes 393224 | tf_op jit(solution)/shard_map/ppermute | solution.py:26
  52.2 1.9 %collective-permute-start.11 = (bf16[4,128,128]{2,1,0:T(8,128)(2,1)S(1)}, bf16[4,128,128]{2,1,0:T(8,128)(2,1)S(1)}, u32[]{:S(2)}, u32[]{:S(2)}) collective-permute-start(bf16[4,128,128]{2,1,0:T(8,128)(2,1)S(1)} %get-tuple-element.14), channel_id=1, source_target_pairs={{0,3},{1,0},{2,1},{3,2},{4,7},{5,4},{6,5},{7,6},{8,11},{9,8},{10,9... | collective-permute-start | bytes 393224 | tf_op jit(solution)/shard_map/ppermute | solution.py:26
  54.1 0.1 collective-permute-start.10
  54.2 10.2 %shard_map.65.local_ref = f32[8,1024,128]{2,1,0:T(8,128)} custom-call(bf16[8,1024,128]{2,1,0:T(8,128)(2,1)} %get-tuple-element.9.q_ref, bf16[8,1024,128]{2,1,0:T(8,128)(2,1)} %get-tuple-element.10.k_ref, bf16[8,1024,128]{2,1,0:T(8,128)(2,1)} %get-tuple-element.11.v_ref), custom_call_target="tpu_custom_call" | custom-call | flops 2952790016 | bytes 10485760 | tf_op jit(solution)/shard_map/pallas_call | solution.py:165
  64.4 0.8 collective-permute-start.6
  65.2 1.6 %collective-permute-start.5 = (bf16[4,128,128]{2,1,0:T(8,128)(2,1)S(1)}, bf16[4,128,128]{2,1,0:T(8,128)(2,1)S(1)}, u32[]{:S(2)}, u32[]{:S(2)}) collective-permute-start(bf16[4,128,128]{2,1,0:T(8,128)(2,1)S(1)} %get-tuple-element.16), channel_id=1, source_target_pairs={{0,12},{4,0},{8,4},{12,8},{1,13},{5,1},{9,5},{13,9},{2,14},{6,2},{... | collective-permute-start | bytes 393224 | tf_op jit(solution)/shard_map/ppermute | solution.py:26
  66.8 0.0 collective-permute-done.12
  66.8 0.4 collective-permute-start.4
  67.2 0.0 collective-permute-done.11
  67.2 0.0 collective-permute-done.10
  67.2 0.1 add_add_fusion
  67.4 3.5 %collective-permute-done.6 = bf16[4,128,128]{2,1,0:T(8,128)(2,1)S(1)} collective-permute-done((bf16[4,128,128]{2,1,0:T(8,128)(2,1)S(1)}, bf16[4,128,128]{2,1,0:T(8,128)(2,1)S(1)}, u32[]{:S(2)}, u32[]{:S(2)}) %collective-permute-start.6) | collective-permute-done | bytes 131104 | tf_op jit(solution)/shard_map/ppermute | solution.py:26
  70.9 0.0 collective-permute-done.5
  70.9 2.1 %collective-permute-done.4 = bf16[4,128,128]{2,1,0:T(8,128)(2,1)S(1)} collective-permute-done((bf16[4,128,128]{2,1,0:T(8,128)(2,1)S(1)}, bf16[4,128,128]{2,1,0:T(8,128)(2,1)S(1)}, u32[]{:S(2)}, u32[]{:S(2)}) %collective-permute-start.4) | collective-permute-done | bytes 131104 | tf_op jit(solution)/shard_map/ppermute | solution.py:26
  73.0 0.1 fusion.14
  73.1 0.8 pad_maximum_fusion.prefix_ref
  73.9 13.6 %shard_map.66 = bf16[1024,1024]{1,0:T(8,128)(2,1)} custom-call(bf16[8,1024,128]{2,1,0:T(8,128)(2,1)} %get-tuple-element.9.q_ref, f32[8,1024,128]{2,1,0:T(8,128)} %shard_map.65.local_ref, f32[8,128,128]{2,1,0:T(8,128)} %pad_maximum_fusion.prefix_ref, f32[8,1,128]{2,1,0:T(1,128)} %bitcast.34, bf16[8,128,1024]{2,1,0:T(8,128)(2,1)} %bitcast.32), custom_call_target="tpu_custom_call" | custom-call | flops 2684354560 | bytes 10485760 | tf_op jit(solution)/shard_map/pallas_call | solution.py:180
  (5 shorter events, 0.1 us)
Async XLA Ops:
  2.1 16.2 %copy-start.1 = (f32[4,3072]{1,0:T(4,128)S(1)}, f32[4,3072]{1,0:T(4,128)}, u32[]{:S(2)}) copy-start(f32[4,3072]{1,0:T(4,128)} %param.9) | copy-start | bytes 147460
  11.7 2.7 %copy-start = (bf16[24,1024,128]{2,1,0:T(8,128)(2,1)}, bf16[24,1024,128]{2,1,0:T(8,128)(2,1)S(1)}, u32[]{:S(2)}) copy-start(bf16[24,1024,128]{2,1,0:T(8,128)(2,1)S(1)} %convert_bitcast_fusion.pq.pk.pv) | copy-start | bytes 18874372
  14.4 5.4 %collective-permute-start = (bf16[24,3,128]{2,1,0:T(4,128)(2,1)S(1)}, bf16[24,3,128]{2,1,0:T(4,128)(2,1)S(1)}, u32[]{:S(2)}, u32[]{:S(2)}) collective-permute-start(bf16[24,3,128]{2,1,0:T(4,128)(2,1)S(1)} %slice.20), channel_id=1, source_target_pairs={{0,1},{1,2},{2,3},{3,4},{4,5},{5,6},{6,7},{7,8},{8,9},{9,10},{10,1... | collective-permute-start | bytes 55304 | tf_op jit(solution)/shard_map/ppermute | solution.py:139
  32.1 10.8 %collective-permute-start.3 = (bf16[4,128,128]{2,1,0:T(8,128)(2,1)S(1)}, bf16[4,128,128]{2,1,0:T(8,128)(2,1)S(1)}, u32[]{:S(2)}, u32[]{:S(2)}) collective-permute-start(bf16[4,128,128]{2,1,0:T(8,128)(2,1)S(1)} %get-tuple-element.17), channel_id=1, source_target_pairs={{0,2},{1,3},{2,0},{3,1},{4,6},{5,7},{6,4},{7,5},{8,10},{9,11},{10,... | collective-permute-start | bytes 393224 | tf_op jit(solution)/shard_map/ppermute | solution.py:26
  36.4 7.5 %collective-permute-start.2 = (bf16[4,128,128]{2,1,0:T(8,128)(2,1)S(1)}, bf16[4,128,128]{2,1,0:T(8,128)(2,1)S(1)}, u32[]{:S(2)}, u32[]{:S(2)}) collective-permute-start(bf16[4,128,128]{2,1,0:T(8,128)(2,1)S(1)} %get-tuple-element.17), channel_id=1, source_target_pairs={{0,3},{1,0},{2,1},{3,2},{4,7},{5,4},{6,5},{7,6},{8,11},{9,8},{10,9... | collective-permute-start | bytes 393224 | tf_op jit(solution)/shard_map/ppermute | solution.py:26
  37.1 6.8 %collective-permute-start.1 = (bf16[4,128,128]{2,1,0:T(8,128)(2,1)S(1)}, bf16[4,128,128]{2,1,0:T(8,128)(2,1)S(1)}, u32[]{:S(2)}, u32[]{:S(2)}) collective-permute-start(bf16[4,128,128]{2,1,0:T(8,128)(2,1)S(1)} %get-tuple-element.17), channel_id=1, source_target_pairs={{0,1},{1,2},{2,3},{3,0},{4,5},{5,6},{6,7},{7,4},{8,9},{9,10},{10,1... | collective-permute-start | bytes 393224 | tf_op jit(solution)/shard_map/ppermute | solution.py:26
  38.7 7.6 %collective-permute-start.9 = (bf16[4,128,128]{2,1,0:T(8,128)(2,1)S(1)}, bf16[4,128,128]{2,1,0:T(8,128)(2,1)S(1)}, u32[]{:S(2)}, u32[]{:S(2)}) collective-permute-start(bf16[4,128,128]{2,1,0:T(8,128)(2,1)S(1)} %get-tuple-element.18), channel_id=1, source_target_pairs={{0,8},{4,12},{8,0},{12,4},{1,9},{5,13},{9,1},{13,5},{2,10},{6,14},... | collective-permute-start | bytes 393224 | tf_op jit(solution)/shard_map/ppermute | solution.py:26
  41.9 5.0 %collective-permute-start.8 = (bf16[4,128,128]{2,1,0:T(8,128)(2,1)S(1)}, bf16[4,128,128]{2,1,0:T(8,128)(2,1)S(1)}, u32[]{:S(2)}, u32[]{:S(2)}) collective-permute-start(bf16[4,128,128]{2,1,0:T(8,128)(2,1)S(1)} %get-tuple-element.18), channel_id=1, source_target_pairs={{0,12},{4,0},{8,4},{12,8},{1,13},{5,1},{9,5},{13,9},{2,14},{6,2},{... | collective-permute-start | bytes 393224 | tf_op jit(solution)/shard_map/ppermute | solution.py:26
  42.9 6.2 %collective-permute-start.7 = (bf16[4,128,128]{2,1,0:T(8,128)(2,1)S(1)}, bf16[4,128,128]{2,1,0:T(8,128)(2,1)S(1)}, u32[]{:S(2)}, u32[]{:S(2)}) collective-permute-start(bf16[4,128,128]{2,1,0:T(8,128)(2,1)S(1)} %get-tuple-element.18), channel_id=1, source_target_pairs={{0,4},{4,8},{8,12},{12,0},{1,5},{5,9},{9,13},{13,1},{2,6},{6,10},{... | collective-permute-start | bytes 393224 | tf_op jit(solution)/shard_map/ppermute | solution.py:26
  50.3 16.5 %collective-permute-start.12 = (bf16[4,128,128]{2,1,0:T(8,128)(2,1)S(1)}, bf16[4,128,128]{2,1,0:T(8,128)(2,1)S(1)}, u32[]{:S(2)}, u32[]{:S(2)}) collective-permute-start(bf16[4,128,128]{2,1,0:T(8,128)(2,1)S(1)} %get-tuple-element.15), channel_id=1, source_target_pairs={{0,2},{1,3},{2,0},{3,1},{4,6},{5,7},{6,4},{7,5},{8,10},{9,11},{10,... | collective-permute-start | bytes 393224 | tf_op jit(solution)/shard_map/ppermute | solution.py:26
  52.2 15.1 %collective-permute-start.11 = (bf16[4,128,128]{2,1,0:T(8,128)(2,1)S(1)}, bf16[4,128,128]{2,1,0:T(8,128)(2,1)S(1)}, u32[]{:S(2)}, u32[]{:S(2)}) collective-permute-start(bf16[4,128,128]{2,1,0:T(8,128)(2,1)S(1)} %get-tuple-element.14), channel_id=1, source_target_pairs={{0,3},{1,0},{2,1},{3,2},{4,7},{5,4},{6,5},{7,6},{8,11},{9,8},{10,9... | collective-permute-start | bytes 393224 | tf_op jit(solution)/shard_map/ppermute | solution.py:26
  54.1 13.2 %collective-permute-start.10 = (bf16[4,128,128]{2,1,0:T(8,128)(2,1)S(1)}, bf16[4,128,128]{2,1,0:T(8,128)(2,1)S(1)}, u32[]{:S(2)}, u32[]{:S(2)}) collective-permute-start(bf16[4,128,128]{2,1,0:T(8,128)(2,1)S(1)} %get-tuple-element.13), channel_id=1, source_target_pairs={{0,1},{1,2},{2,3},{3,0},{4,5},{5,6},{6,7},{7,4},{8,9},{9,10},{10,1... | collective-permute-start | bytes 393224 | tf_op jit(solution)/shard_map/ppermute | solution.py:26
  64.4 6.5 %collective-permute-start.6 = (bf16[4,128,128]{2,1,0:T(8,128)(2,1)S(1)}, bf16[4,128,128]{2,1,0:T(8,128)(2,1)S(1)}, u32[]{:S(2)}, u32[]{:S(2)}) collective-permute-start(bf16[4,128,128]{2,1,0:T(8,128)(2,1)S(1)} %get-tuple-element.16), channel_id=1, source_target_pairs={{0,8},{4,12},{8,0},{12,4},{1,9},{5,13},{9,1},{13,5},{2,10},{6,14},... | collective-permute-start | bytes 393224 | tf_op jit(solution)/shard_map/ppermute | solution.py:26
  65.2 5.7 %collective-permute-start.5 = (bf16[4,128,128]{2,1,0:T(8,128)(2,1)S(1)}, bf16[4,128,128]{2,1,0:T(8,128)(2,1)S(1)}, u32[]{:S(2)}, u32[]{:S(2)}) collective-permute-start(bf16[4,128,128]{2,1,0:T(8,128)(2,1)S(1)} %get-tuple-element.16), channel_id=1, source_target_pairs={{0,12},{4,0},{8,4},{12,8},{1,13},{5,1},{9,5},{13,9},{2,14},{6,2},{... | collective-permute-start | bytes 393224 | tf_op jit(solution)/shard_map/ppermute | solution.py:26
  66.8 6.2 %collective-permute-start.4 = (bf16[4,128,128]{2,1,0:T(8,128)(2,1)S(1)}, bf16[4,128,128]{2,1,0:T(8,128)(2,1)S(1)}, u32[]{:S(2)}, u32[]{:S(2)}) collective-permute-start(bf16[4,128,128]{2,1,0:T(8,128)(2,1)S(1)} %get-tuple-element.16), channel_id=1, source_target_pairs={{0,4},{4,8},{8,12},{12,0},{1,5},{5,9},{9,13},{13,1},{2,6},{6,10},{... | collective-permute-start | bytes 393224 | tf_op jit(solution)/shard_map/ppermute | solution.py:26

commit v7 on v6

--- a/solution.py
+++ b/solution.py
@@ -1,3 +1,5 @@
+import functools
+
 import jax
 import jax.numpy as jnp
 from jax import lax
@@ -57,18 +59,46 @@
     return jnp.concatenate([row_before + rows_before, mixed_before], 0)
 
 
-def conv_kernel(pq, pk, pv, eq, ek, ev, tq, tk, tv, oq, ok, ov, state_ref, buf):
-    rows = pq.shape[0]
-    for proj, early, taps, out in ((pq, eq, tq, oq), (pk, ek, tk, ok), (pv, ev, tv, ov)):
+def conv_kernel(count, with_state, *refs):
+    projs, earlies, tapss = refs[:count], refs[count : 2 * count], refs[2 * count : 3 * count]
+    outs, buf = refs[3 * count : 4 * count], refs[-1]
+    rows = projs[0].shape[0]
+    for proj, early, taps, out in zip(projs, earlies, tapss, outs):
         buf[0:PAD, :] = early[...].astype(jnp.float32)
         buf[PAD:, :] = proj[...].astype(jnp.float32)
         summed = jnp.zeros((rows, DH), jnp.float32)
         for offset in range(KW):
             summed = summed + taps[offset : offset + 1, :] * buf[pl.ds(PAD - offset, rows), :]
         out[...] = (summed * jax.nn.sigmoid(summed)).astype(out.dtype)
-    state_ref[...] = lax.dot_general(
-        ok[...], ov[...], (((0,), (0,)), ((), ())), preferred_element_type=jnp.float32
-    )
+    if with_state:
+        refs[4 * count][...] = lax.dot_general(
+            outs[0][...], outs[1][...], (((0,), (0,)), ((), ())), preferred_element_type=jnp.float32
+        )
+
+
+def conv_call(projected, earlier, taps, shifts, base, with_state):
+    count = len(shifts)
+    rows = projected.shape[1]
+    mixed = jax.ShapeDtypeStruct((H, rows, DH), jnp.bfloat16)
+    out_specs = [slab(0, rows, DH)] * count
+    out_shape = [mixed] * count
+    if with_state:
+        out_specs.append(slab(0, DH, DH))
+        out_shape.append(jax.ShapeDtypeStruct((H, DH, DH), jnp.float32))
+    return pl.pallas_call(
+        functools.partial(conv_kernel, count, with_state),
+        grid=(H,),
+        in_specs=[slab(shift, rows, DH) for shift in shifts]
+        + [slab(base + shift, PAD, DH) for shift in shifts] * 2,
+        out_specs=out_specs,
+        out_shape=out_shape,
+        scratch_shapes=[pltpu.VMEM((rows + PAD, DH), jnp.float32)],
+        cost_estimate=pl.CostEstimate(
+            flops=H * count * rows * DH * (12 + 2 * DH),
+            transcendentals=H * count * rows * DH,
+            bytes_accessed=H * count * rows * DH * 4,
+        ),
+    )(*([projected] * count + [earlier] * count + [taps] * count))
 
 
 def local_kernel(q_ref, k_ref, v_ref, out_ref):
@@ -125,41 +155,38 @@
 
 def local(tokens, norm_gain, w_qkv, conv_weight, head_gain, w_out):
     rows, width = tokens.shape
-    tokens_f = tokens.astype(jnp.float32)
-    scale = lax.rsqrt(jnp.mean(tokens_f * tokens_f, -1, keepdims=True) + 1e-06)
-    normed = (tokens_f * scale * norm_gain).astype(jnp.bfloat16)
-
-    slabs = w_qkv.shape[1] // DH
-    projected = jnp.einsum(
-        "td,dje->jte", normed, w_qkv.reshape(width, slabs, DH), preferred_element_type=jnp.float32
-    ).astype(jnp.bfloat16)
-
     seq_axes = ("sy", "sz")
     count = lax.axis_size("sy") * lax.axis_size("sz")
-    earlier_rows = lax.ppermute(
-        projected[:, rows - (KW - 1) :, :], seq_axes, [(i, i + 1) for i in range(count - 1)]
-    )
-    earlier_rows = jnp.pad(earlier_rows, ((0, 0), (PAD - (KW - 1), 0), (0, 0)))
+    earlier_tokens = lax.ppermute(
+        tokens[rows - (KW - 1) :], seq_axes, [(i, i + 1) for i in range(count - 1)]
+    )
+    earlier_tokens = jnp.pad(earlier_tokens, ((PAD - (KW - 1), 0), (0, 0)))
+
+    def input_norm(values):
+        values_f = values.astype(jnp.float32)
+        scale = lax.rsqrt(jnp.mean(values_f * values_f, -1, keepdims=True) + 1e-06)
+        return (values_f * scale * norm_gain).astype(jnp.bfloat16)
+
+    slabs = w_qkv.shape[1] // DH
+    weights = w_qkv.reshape(width, slabs, DH)
+
+    def project(values, first, last):
+        return jnp.einsum(
+            "td,dje->jte", values, weights[:, first:last], preferred_element_type=jnp.float32
+        ).astype(jnp.bfloat16)
+
+    normed = input_norm(tokens)
+    earlier_rows = project(input_norm(earlier_tokens), 0, slabs)
     taps = jnp.pad(
         conv_weight.reshape(KW, slabs, DH).transpose(1, 0, 2), ((0, 0), (0, PAD - KW), (0, 0))
     )
 
-    mixed_shape = jax.ShapeDtypeStruct((H, rows, DH), jnp.bfloat16)
-    query, key, value, state = pl.pallas_call(
-        conv_kernel,
-        grid=(H,),
-        in_specs=[slab(0, rows, DH), slab(H, rows, DH), slab(2 * H, rows, DH)]
-        + [slab(0, PAD, DH), slab(H, PAD, DH), slab(2 * H, PAD, DH)]
-        + [slab(0, PAD, DH), slab(H, PAD, DH), slab(2 * H, PAD, DH)],
-        out_specs=[slab(0, rows, DH)] * 3 + [slab(0, DH, DH)],
-        out_shape=[mixed_shape] * 3 + [jax.ShapeDtypeStruct((H, DH, DH), jnp.float32)],
-        scratch_shapes=[pltpu.VMEM((rows + PAD, DH), jnp.float32)],
-        cost_estimate=pl.CostEstimate(
-            flops=H * (3 * rows * DH * 12 + 2 * rows * DH * DH),
-            transcendentals=H * 3 * rows * DH,
-            bytes_accessed=H * 3 * rows * DH * 4,
-        ),
-    )(projected, projected, projected, earlier_rows, earlier_rows, earlier_rows, taps, taps, taps)
+    kv_projected = project(normed, H, slabs)
+    key, value, state = conv_call(kv_projected, earlier_rows, taps, (0, H), H, True)
+    prefix = earlier_states(state)
+
+    q_projected = project(normed, 0, H)
+    (query,) = conv_call(q_projected, earlier_rows, taps, (0,), 0, False)
 
     block = min(BLOCK, rows)
     local_part = pl.pallas_call(
@@ -174,8 +201,6 @@
             bytes_accessed=H * rows * DH * 10,
         ),
     )(query, key, value)
-
-    prefix = earlier_states(state)
 
     out = pl.pallas_call(
         out_kernel,

time: 88.2 us -> 104 us (1.18)
  matrix products: 9.57 us -> 16.9 us
  local copies, waits for them, and re-layouts: 5.02 us -> 11.3 us
  Pallas kernels: 34.4 us -> 39.3 us
  starting transfers between devices: 22.2 us -> 20.5 us
    dot_general x1 -> x3, matrix products: 9.57 us -> 16.9 us  [project(): jnp.einsum('td,dje->jte', values, weights[:, first:last], preferred_eleme...]
    unnamed x4 -> x11, local copies, waits for them, and re-layouts: 2.66 us -> 8.83 us
    pallas_call x1 -> x2, Pallas kernels: 10.6 us -> 15.4 us  [conv_call(): pl.pallas_call(functools.partial(conv_kernel, count, with_state), grid=(H...]
    ppermute x12, starting transfers between devices: 18.3 us -> 16.6 us  [ring_sum(): lax.ppermute(message.astype(jnp.bfloat16), axis, pairs).astype(jnp.float32)]
    reduce_sum x1 -> x2, other arithmetic: 2.07 us -> 2.19 us  [input_norm(): scale = lax.rsqrt(jnp.mean(values_f * values_f, -1, keepdims=True) + 1e-06)]
  transfers between devices with their start and end apart: 13 -> 13, of which waited for: 6 -> 3; matrix products, arithmetic and copies ran while one was open for 1% -> 23% of each run, Pallas kernels for 12% -> 17%
where the time goes in v7:
time: 104 us; the launch traced here: 103 us
  Pallas kernels  39.3 us (38%)
  starting transfers between devices  20.5 us (20%)
  matrix products  16.9 us (16%)
  local copies, waits for them, and re-layouts  11.3 us (11%)
  waiting for transfers between devices  10.9 us (10%)
  other arithmetic  3.8 us (4%)
    dot_general x3, matrix products, project(): jnp.einsum('td,dje->jte', values, weights[:, first:last], preferred_eleme...  16.9 us
    ppermute x12, starting transfers between devices, ring_sum(): lax.ppermute(message.astype(jnp.bfloat16), axis, pairs).astype(jnp.float32)  16.6 us
    pallas_call x2, Pallas kernels, conv_call(): pl.pallas_call(functools.partial(conv_kernel, count, with_state), grid=(H...  15.4 us
    pallas_call x1, Pallas kernels, local(): pl.pallas_call(out_kernel, grid=(H,), in_specs=[slab(0, rows, DH), slab(0...  13.6 us
    ppermute x12, waiting for transfers between devices, ring_sum(): lax.ppermute(message.astype(jnp.bfloat16), axis, pairs).astype(jnp.float32)  10.9 us
    pallas_call x1, Pallas kernels, local(): pl.pallas_call(local_kernel, grid=(H,), in_specs=[slab(0, rows, DH)] * 3,...  10.2 us
    unnamed x11, local copies, waits for them, and re-layouts  8.83 us
    ppermute x1, starting transfers between devices, local(): lax.ppermute(tokens[rows - (KW - 1):], seq_axes, [(i, i + 1) for i in ran...  3.89 us
  transfers between devices with their start and end apart: 13, of which 3 were waited for; matrix products, arithmetic and copies ran while one was open for 23% of the time, Pallas kernels for 17%

profile of v7, /device:TPU:0, one launch (start us, length us, event | category | flops | bytes accessed | tf_op | source)
XLA Modules:
  0.0 102.8 jit_solution(8814439678994990575)
XLA Ops:
  0.0 0.7 slice.22
  0.7 3.9 %collective-permute-start = (bf16[3,1024]{1,0:T(4,128)(2,1)S(1)}, bf16[3,1024]{1,0:T(4,128)(2,1)S(1)}, u32[]{:S(2)}, u32[]{:S(2)}) collective-permute-start(bf16[3,1024]{1,0:T(4,128)(2,1)S(1)} %slice.22), channel_id=1, source_target_pairs={{0,1},{1,2},{2,3},{3,4},{4,5},{5,6},{6,7},{7,8},{8,9},{9,10},{10,1... | collective-permute-start | bytes 18440 | tf_op jit(solution)/shard_map/ppermute | solution.py:160
  4.6 2.1 %fusion = f32[1024]{0:T(1024)S(1)} fusion(bf16[1024,1024]{1,0:T(8,128)(2,1)} %param.6), kind=kLoop, calls=%fused_computation.2 | loop fusion | flops 3144704 | bytes 2101248 | tf_op jit(solution)/shard_map/reduce_sum | solution.py:167
  6.7 0.0 copy-start.1
  6.7 0.0 copy-start.4
  6.7 8.8 %copy.7 = bf16[1024,3072]{0,1:T(8,128)(2,1)} copy(bf16[1024,3072]{1,0:T(8,128)(2,1)} %param.8) | data formatting | bytes 12582912 | tf_op args[2]
  15.6 5.5 %convert_bitcast_fusion.1.refs_0_ = bf16[8,1024,128]{2,1,0:T(8,128)(2,1)} fusion(bf16[1024,24,128]{0,2,1:T(8,128)(2,1)} %bitcast.33, bf16[1024,1024]{1,0:T(8,128)(2,1)S(1)} %copy-done.1, f32[1024]{0:T(1024)S(1)} %copy-done.4, f32[1024]{0:T(1024)S(1)} %add_rsqrt_fusion), kind=kOutput, calls=%fused_computation.11 | convolution fusion | flops 2152726528 | bytes 6299648 | tf_op jit(solution)/shard_map/td,dje->jte/dot_general | solution.py:174
  21.1 6.2 %convert_bitcast_fusion.refs_0_.refs_1_ = bf16[16,1024,128]{2,1,0:T(8,128)(2,1)} fusion(bf16[1024,24,128]{0,2,1:T(8,128)(2,1)S(1)} %bitcast.35, bf16[1024,1024]{1,0:T(8,128)(2,1)S(1)} %copy-done.1, f32[1024]{0:T(1024)S(1)} %copy-done.4, f32[1024]{0:T(1024)S(1)} %add_rsqrt_fusion), kind=kOutput, calls=%fused_computation.7 | convolution fusion | flops 4301258752 | bytes 10493952 | tf_op jit(solution)/shard_map/td,dje->jte/dot_general | solution.py:174
  27.3 0.1 fusion.25
  27.4 0.6 pad.9.refs_2_.refs_4_.refs_5_
  28.1 0.0 collective-permute-done
  28.1 0.1 fusion.18
  28.2 5.1 %fusion.12.refs_1_.refs_2_.refs_3_ = bf16[24,8,128]{2,1,0:T(8,128)(2,1)} fusion(bf16[1024,24,128]{0,2,1:T(8,128)(2,1)} %bitcast.34, bf16[3,1024]{1,0:T(4,128)(2,1)S(1)} %collective-permute-done, f32[1024]{0:T(1024)S(1)} %copy-done.4, f32[8]{0:T(128)S(1)} %add_rsqrt_fusion.1), kind=kOutput, calls=%fused_computation.13 | convolution fusion | flops 50388992 | bytes 6350880 | tf_op jit(solution)/shard_map/td,dje->jte/dot_general | solution.py:174
  33.3 8.5 %shard_map.65 = (bf16[8,1024,128]{2,1,0:T(8,128)(2,1)}, bf16[8,1024,128]{2,1,0:T(8,128)(2,1)}, f32[8,128,128]{2,1,0:T(8,128)}) custom-call(bf16[16,1024,128]{2,1,0:T(8,128)(2,1)} %convert_bitcast_fusion.refs_0_.refs_1_, bf16[16,1024,128]{2,1,0:T(8,128)(2,1)} %convert_bitcast_fusion.refs_0_.refs_1_, bf16[24,8,128]{2,1,0:T(8,128)(2,1)} %fusion.12.refs_1_.refs_2_.refs_3_, ...), custom_call_target="tpu_custom_call" | custom-call | flops 562036736 | bytes 8388608 | tf_op jit(solution)/shard_map/pallas_call | solution.py:88
  41.9 1.1 %fusion.29 = (bf16[4,128,128]{2,1,0:T(8,128)(2,1)S(1)}, bf16[4,128,128]{2,1,0:T(8,128)(2,1)S(1)}) fusion(f32[8,128,128]{2,1,0:T(8,128)} %get-tuple-element.10), kind=kLoop, calls=%fused_computation.45 | loop fusion | bytes 524288 | tf_op jit(solution)/shard_map/slice | solution.py:50
  43.0 3.7 %collective-permute-start.3 = (bf16[4,128,128]{2,1,0:T(8,128)(2,1)S(1)}, bf16[4,128,128]{2,1,0:T(8,128)(2,1)S(1)}, u32[]{:S(2)}, u32[]{:S(2)}) collective-permute-start(bf16[4,128,128]{2,1,0:T(8,128)(2,1)S(1)} %get-tuple-element.15), channel_id=1, source_target_pairs={{0,2},{1,3},{2,0},{3,1},{4,6},{5,7},{6,4},{7,5},{8,10},{9,11},{10,... | collective-permute-start | bytes 393224 | tf_op jit(solution)/shard_map/ppermute | solution.py:28
  46.7 1.0 collective-permute-start.2
  47.7 1.0 collective-permute-start.1
  48.7 0.1 fusion.27
  48.8 3.2 %collective-permute-start.9 = (bf16[4,128,128]{2,1,0:T(8,128)(2,1)S(1)}, bf16[4,128,128]{2,1,0:T(8,128)(2,1)S(1)}, u32[]{:S(2)}, u32[]{:S(2)}) collective-permute-start(bf16[4,128,128]{2,1,0:T(8,128)(2,1)S(1)} %get-tuple-element.16), channel_id=1, source_target_pairs={{0,8},{4,12},{8,0},{12,4},{1,9},{5,13},{9,1},{13,5},{2,10},{6,14},... | collective-permute-start | bytes 393224 | tf_op jit(solution)/shard_map/ppermute | solution.py:28
  52.0 1.1 %collective-permute-start.8 = (bf16[4,128,128]{2,1,0:T(8,128)(2,1)S(1)}, bf16[4,128,128]{2,1,0:T(8,128)(2,1)S(1)}, u32[]{:S(2)}, u32[]{:S(2)}) collective-permute-start(bf16[4,128,128]{2,1,0:T(8,128)(2,1)S(1)} %get-tuple-element.16), channel_id=1, source_target_pairs={{0,12},{4,0},{8,4},{12,8},{1,13},{5,1},{9,5},{13,9},{2,14},{6,2},{... | collective-permute-start | bytes 393224 | tf_op jit(solution)/shard_map/ppermute | solution.py:28
  53.0 6.9 %shard_map.64.q_ref = bf16[8,1024,128]{2,1,0:T(8,128)(2,1)} custom-call(bf16[8,1024,128]{2,1,0:T(8,128)(2,1)} %convert_bitcast_fusion.1.refs_0_, bf16[24,8,128]{2,1,0:T(8,128)(2,1)} %fusion.12.refs_1_.refs_2_.refs_3_, f32[24,8,128]{2,1,0:T(8,128)} %pad.9.refs_2_.refs_4_.refs_5_), custom_call_target="tpu_custom_call" | custom-call | flops 281018368 | bytes 4194304 | tf_op jit(solution)/shard_map/pallas_call | solution.py:88
  59.9 0.0 collective-permute-done.3
  60.0 1.0 collective-permute-start.7
  60.9 0.0 collective-permute-done.2
  61.0 0.0 collective-permute-done.1
  61.0 0.2 multiply_add_fusion
  61.2 0.0 collective-permute-done.9
  61.2 0.0 collective-permute-done.8
  61.2 4.9 %collective-permute-done.7 = bf16[4,128,128]{2,1,0:T(8,128)(2,1)S(1)} collective-permute-done((bf16[4,128,128]{2,1,0:T(8,128)(2,1)S(1)}, bf16[4,128,128]{2,1,0:T(8,128)(2,1)S(1)}, u32[]{:S(2)}, u32[]{:S(2)}) %collective-permute-start.7) | collective-permute-done | bytes 131104 | tf_op jit(solution)/shard_map/ppermute | solution.py:28
  66.1 0.2 add_convert_fusion.2
  66.3 0.5 collective-permute-start.12
  66.8 2.2 %collective-permute-start.11 = (bf16[4,128,128]{2,1,0:T(8,128)(2,1)S(1)}, bf16[4,128,128]{2,1,0:T(8,128)(2,1)S(1)}, u32[]{:S(2)}, u32[]{:S(2)}) collective-permute-start(bf16[4,128,128]{2,1,0:T(8,128)(2,1)S(1)} %get-tuple-element.12), channel_id=1, source_target_pairs={{0,3},{1,0},{2,1},{3,2},{4,7},{5,4},{6,5},{7,6},{8,11},{9,8},{10,9... | collective-permute-start | bytes 393224 | tf_op jit(solution)/shard_map/ppermute | solution.py:28
  69.1 0.4 collective-permute-start.10
  69.5 10.2 %shard_map.66.local_ref = f32[8,1024,128]{2,1,0:T(8,128)} custom-call(bf16[8,1024,128]{2,1,0:T(8,128)(2,1)} %shard_map.64.q_ref, bf16[8,1024,128]{2,1,0:T(8,128)(2,1)} %get-tuple-element.8.k_ref, bf16[8,1024,128]{2,1,0:T(8,128)(2,1)} %get-tuple-element.9.v_ref), custom_call_target="tpu_custom_call" | custom-call | flops 2952790016 | bytes 10485760 | tf_op jit(solution)/shard_map/pallas_call | solution.py:192
  79.7 0.5 collective-permute-start.6
  80.1 1.9 %collective-permute-start.5 = (bf16[4,128,128]{2,1,0:T(8,128)(2,1)S(1)}, bf16[4,128,128]{2,1,0:T(8,128)(2,1)S(1)}, u32[]{:S(2)}, u32[]{:S(2)}) collective-permute-start(bf16[4,128,128]{2,1,0:T(8,128)(2,1)S(1)} %get-tuple-element.14), channel_id=1, source_target_pairs={{0,12},{4,0},{8,4},{12,8},{1,13},{5,1},{9,5},{13,9},{2,14},{6,2},{... | collective-permute-start | bytes 393224 | tf_op jit(solution)/shard_map/ppermute | solution.py:28
  82.1 0.0 collective-permute-done.12
  82.1 0.1 collective-permute-start.4
  82.2 0.0 collective-permute-done.11
  82.2 0.0 collective-permute-done.10
  82.2 0.1 add_add_fusion
  82.3 3.8 %collective-permute-done.6 = bf16[4,128,128]{2,1,0:T(8,128)(2,1)S(1)} collective-permute-done((bf16[4,128,128]{2,1,0:T(8,128)(2,1)S(1)}, bf16[4,128,128]{2,1,0:T(8,128)(2,1)S(1)}, u32[]{:S(2)}, u32[]{:S(2)}) %collective-permute-start.6) | collective-permute-done | bytes 131104 | tf_op jit(solution)/shard_map/ppermute | solution.py:28
  86.1 0.0 collective-permute-done.5
  86.1 2.1 %collective-permute-done.4 = bf16[4,128,128]{2,1,0:T(8,128)(2,1)S(1)} collective-permute-done((bf16[4,128,128]{2,1,0:T(8,128)(2,1)S(1)}, bf16[4,128,128]{2,1,0:T(8,128)(2,1)S(1)}, u32[]{:S(2)}, u32[]{:S(2)}) %collective-permute-start.4) | collective-permute-done | bytes 131104 | tf_op jit(solution)/shard_map/ppermute | solution.py:28
  88.3 0.1 fusion.17
  88.4 0.8 pad_maximum_fusion.prefix_ref
  89.2 13.6 %shard_map.67 = bf16[1024,1024]{1,0:T(8,128)(2,1)} custom-call(bf16[8,1024,128]{2,1,0:T(8,128)(2,1)} %shard_map.64.q_ref, f32[8,1024,128]{2,1,0:T(8,128)} %shard_map.66.local_ref, f32[8,128,128]{2,1,0:T(8,128)} %pad_maximum_fusion.prefix_ref, f32[8,1,128]{2,1,0:T(1,128)} %bitcast.38, bf16[8,128,1024]{2,1,0:T(8,128)(2,1)} %bitcast.36), custom_call_target="tpu_custom_call" | custom-call | flops 2684354560 | bytes 10485760 | tf_op jit(solution)/shard_map/pallas_call | solution.py:205
  (13 shorter events, 0.1 us)
Async XLA Ops:
  0.7 27.3 %collective-permute-start = (bf16[3,1024]{1,0:T(4,128)(2,1)S(1)}, bf16[3,1024]{1,0:T(4,128)(2,1)S(1)}, u32[]{:S(2)}, u32[]{:S(2)}) collective-permute-start(bf16[3,1024]{1,0:T(4,128)(2,1)S(1)} %slice.22), channel_id=1, source_target_pairs={{0,1},{1,2},{2,3},{3,4},{4,5},{5,6},{6,7},{7,8},{8,9},{9,10},{10,1... | collective-permute-start | bytes 18440 | tf_op jit(solution)/shard_map/ppermute | solution.py:160
  6.7 8.8 %copy-start.1 = (bf16[1024,1024]{1,0:T(8,128)(2,1)S(1)}, bf16[1024,1024]{1,0:T(8,128)(2,1)}, u32[]{:S(2)}) copy-start(bf16[1024,1024]{1,0:T(8,128)(2,1)} %param.6) | copy-start | bytes 6291460
  6.7 8.8 %copy-start.4 = (f32[1024]{0:T(1024)S(1)}, f32[1024]{0:T(1024)}, u32[]{:S(2)}) copy-start(f32[1024]{0:T(1024)} %param.7) | copy-start | bytes 12292
  15.6 5.5 %copy-start = (bf16[1024,3072]{0,1:T(8,128)(2,1)S(1)}, bf16[1024,3072]{0,1:T(8,128)(2,1)}, u32[]{:S(2)}) copy-start(bf16[1024,3072]{0,1:T(8,128)(2,1)} %copy.7) | copy-start | bytes 18874372
  21.1 6.3 %copy-start.3 = (f32[4,3072]{1,0:T(4,128)S(1)}, f32[4,3072]{1,0:T(4,128)}, u32[]{:S(2)}) copy-start(f32[4,3072]{1,0:T(4,128)} %param.9) | copy-start | bytes 147460
  41.9 24.3 %copy-start.2 = (f32[8,128,128]{2,1,0:T(8,128)S(1)}, f32[8,128,128]{2,1,0:T(8,128)}, u32[]{:S(2)}) copy-start(f32[8,128,128]{2,1,0:T(8,128)} %get-tuple-element.10) | copy-start | bytes 1572868
  43.0 16.9 %collective-permute-start.3 = (bf16[4,128,128]{2,1,0:T(8,128)(2,1)S(1)}, bf16[4,128,128]{2,1,0:T(8,128)(2,1)S(1)}, u32[]{:S(2)}, u32[]{:S(2)}) collective-permute-start(bf16[4,128,128]{2,1,0:T(8,128)(2,1)S(1)} %get-tuple-element.15), channel_id=1, source_target_pairs={{0,2},{1,3},{2,0},{3,1},{4,6},{5,7},{6,4},{7,5},{8,10},{9,11},{10,... | collective-permute-start | bytes 393224 | tf_op jit(solution)/shard_map/ppermute | solution.py:28
  46.7 14.3 %collective-permute-start.2 = (bf16[4,128,128]{2,1,0:T(8,128)(2,1)S(1)}, bf16[4,128,128]{2,1,0:T(8,128)(2,1)S(1)}, u32[]{:S(2)}, u32[]{:S(2)}) collective-permute-start(bf16[4,128,128]{2,1,0:T(8,128)(2,1)S(1)} %get-tuple-element.15), channel_id=1, source_target_pairs={{0,3},{1,0},{2,1},{3,2},{4,7},{5,4},{6,5},{7,6},{8,11},{9,8},{10,9... | collective-permute-start | bytes 393224 | tf_op jit(solution)/shard_map/ppermute | solution.py:28
  47.7 13.3 %collective-permute-start.1 = (bf16[4,128,128]{2,1,0:T(8,128)(2,1)S(1)}, bf16[4,128,128]{2,1,0:T(8,128)(2,1)S(1)}, u32[]{:S(2)}, u32[]{:S(2)}) collective-permute-start(bf16[4,128,128]{2,1,0:T(8,128)(2,1)S(1)} %get-tuple-element.15), channel_id=1, source_target_pairs={{0,1},{1,2},{2,3},{3,0},{4,5},{5,6},{6,7},{7,4},{8,9},{9,10},{10,1... | collective-permute-start | bytes 393224 | tf_op jit(solution)/shard_map/ppermute | solution.py:28
  48.8 12.4 %collective-permute-start.9 = (bf16[4,128,128]{2,1,0:T(8,128)(2,1)S(1)}, bf16[4,128,128]{2,1,0:T(8,128)(2,1)S(1)}, u32[]{:S(2)}, u32[]{:S(2)}) collective-permute-start(bf16[4,128,128]{2,1,0:T(8,128)(2,1)S(1)} %get-tuple-element.16), channel_id=1, source_target_pairs={{0,8},{4,12},{8,0},{12,4},{1,9},{5,13},{9,1},{13,5},{2,10},{6,14},... | collective-permute-start | bytes 393224 | tf_op jit(solution)/shard_map/ppermute | solution.py:28
  52.0 9.2 %collective-permute-start.8 = (bf16[4,128,128]{2,1,0:T(8,128)(2,1)S(1)}, bf16[4,128,128]{2,1,0:T(8,128)(2,1)S(1)}, u32[]{:S(2)}, u32[]{:S(2)}) collective-permute-start(bf16[4,128,128]{2,1,0:T(8,128)(2,1)S(1)} %get-tuple-element.16), channel_id=1, source_target_pairs={{0,12},{4,0},{8,4},{12,8},{1,13},{5,1},{9,5},{13,9},{2,14},{6,2},{... | collective-permute-start | bytes 393224 | tf_op jit(solution)/shard_map/ppermute | solution.py:28
  60.0 6.2 %collective-permute-start.7 = (bf16[4,128,128]{2,1,0:T(8,128)(2,1)S(1)}, bf16[4,128,128]{2,1,0:T(8,128)(2,1)S(1)}, u32[]{:S(2)}, u32[]{:S(2)}) collective-permute-start(bf16[4,128,128]{2,1,0:T(8,128)(2,1)S(1)} %get-tuple-element.16), channel_id=1, source_target_pairs={{0,4},{4,8},{8,12},{12,0},{1,5},{5,9},{9,13},{13,1},{2,6},{6,10},{... | collective-permute-start | bytes 393224 | tf_op jit(solution)/shard_map/ppermute | solution.py:28
  66.3 15.8 %collective-permute-start.12 = (bf16[4,128,128]{2,1,0:T(8,128)(2,1)S(1)}, bf16[4,128,128]{2,1,0:T(8,128)(2,1)S(1)}, u32[]{:S(2)}, u32[]{:S(2)}) collective-permute-start(bf16[4,128,128]{2,1,0:T(8,128)(2,1)S(1)} %get-tuple-element.13), channel_id=1, source_target_pairs={{0,2},{1,3},{2,0},{3,1},{4,6},{5,7},{6,4},{7,5},{8,10},{9,11},{10,... | collective-permute-start | bytes 393224 | tf_op jit(solution)/shard_map/ppermute | solution.py:28
  66.8 15.3 %collective-permute-start.11 = (bf16[4,128,128]{2,1,0:T(8,128)(2,1)S(1)}, bf16[4,128,128]{2,1,0:T(8,128)(2,1)S(1)}, u32[]{:S(2)}, u32[]{:S(2)}) collective-permute-start(bf16[4,128,128]{2,1,0:T(8,128)(2,1)S(1)} %get-tuple-element.12), channel_id=1, source_target_pairs={{0,3},{1,0},{2,1},{3,2},{4,7},{5,4},{6,5},{7,6},{8,11},{9,8},{10,9... | collective-permute-start | bytes 393224 | tf_op jit(solution)/shard_map/ppermute | solution.py:28
  69.1 13.1 %collective-permute-start.10 = (bf16[4,128,128]{2,1,0:T(8,128)(2,1)S(1)}, bf16[4,128,128]{2,1,0:T(8,128)(2,1)S(1)}, u32[]{:S(2)}, u32[]{:S(2)}) collective-permute-start(bf16[4,128,128]{2,1,0:T(8,128)(2,1)S(1)} %get-tuple-element.11), channel_id=1, source_target_pairs={{0,1},{1,2},{2,3},{3,0},{4,5},{5,6},{6,7},{7,4},{8,9},{9,10},{10,1... | collective-permute-start | bytes 393224 | tf_op jit(solution)/shard_map/ppermute | solution.py:28
  79.7 6.5 %collective-permute-start.6 = (bf16[4,128,128]{2,1,0:T(8,128)(2,1)S(1)}, bf16[4,128,128]{2,1,0:T(8,128)(2,1)S(1)}, u32[]{:S(2)}, u32[]{:S(2)}) collective-permute-start(bf16[4,128,128]{2,1,0:T(8,128)(2,1)S(1)} %get-tuple-element.14), channel_id=1, source_target_pairs={{0,8},{4,12},{8,0},{12,4},{1,9},{5,13},{9,1},{13,5},{2,10},{6,14},... | collective-permute-start | bytes 393224 | tf_op jit(solution)/shard_map/ppermute | solution.py:28
  80.1 6.0 %collective-permute-start.5 = (bf16[4,128,128]{2,1,0:T(8,128)(2,1)S(1)}, bf16[4,128,128]{2,1,0:T(8,128)(2,1)S(1)}, u32[]{:S(2)}, u32[]{:S(2)}) collective-permute-start(bf16[4,128,128]{2,1,0:T(8,128)(2,1)S(1)} %get-tuple-element.14), channel_id=1, source_target_pairs={{0,12},{4,0},{8,4},{12,8},{1,13},{5,1},{9,5},{13,9},{2,14},{6,2},{... | collective-permute-start | bytes 393224 | tf_op jit(solution)/shard_map/ppermute | solution.py:28
  82.1 6.2 %collective-permute-start.4 = (bf16[4,128,128]{2,1,0:T(8,128)(2,1)S(1)}, bf16[4,128,128]{2,1,0:T(8,128)(2,1)S(1)}, u32[]{:S(2)}, u32[]{:S(2)}) collective-permute-start(bf16[4,128,128]{2,1,0:T(8,128)(2,1)S(1)} %get-tuple-element.14), channel_id=1, source_target_pairs={{0,4},{4,8},{8,12},{12,0},{1,5},{5,9},{9,13},{13,1},{2,6},{6,10},{... | collective-permute-start | bytes 393224 | tf_op jit(solution)/shard_map/ppermute | solution.py:28

commit v8 on v5

--- a/solution.py
+++ b/solution.py
@@ -1,3 +1,5 @@
+import functools
+
 import jax
 import jax.numpy as jnp
 from jax import lax
@@ -27,18 +29,46 @@
     return jnp.sum(values * earlier[:, None, None, None], 0), jnp.sum(values, 0)
 
 
-def conv_kernel(pq, pk, pv, eq, ek, ev, tq, tk, tv, oq, ok, ov, state_ref, buf):
-    rows = pq.shape[0]
-    for proj, early, taps, out in ((pq, eq, tq, oq), (pk, ek, tk, ok), (pv, ev, tv, ov)):
+def conv_kernel(count, with_state, *refs):
+    projs, earlies, tapss = refs[:count], refs[count : 2 * count], refs[2 * count : 3 * count]
+    outs, buf = refs[3 * count : 4 * count], refs[-1]
+    rows = projs[0].shape[0]
+    for proj, early, taps, out in zip(projs, earlies, tapss, outs):
         buf[0:PAD, :] = early[...].astype(jnp.float32)
         buf[PAD:, :] = proj[...].astype(jnp.float32)
         summed = jnp.zeros((rows, DH), jnp.float32)
         for offset in range(KW):
             summed = summed + taps[offset : offset + 1, :] * buf[pl.ds(PAD - offset, rows), :]
         out[...] = (summed * jax.nn.sigmoid(summed)).astype(out.dtype)
-    state_ref[...] = lax.dot_general(
-        ok[...], ov[...], (((0,), (0,)), ((), ())), preferred_element_type=jnp.float32
-    )
+    if with_state:
+        refs[4 * count][...] = lax.dot_general(
+            outs[0][...], outs[1][...], (((0,), (0,)), ((), ())), preferred_element_type=jnp.float32
+        )
+
+
+def conv_call(projected, earlier, taps, shifts, base, with_state):
+    count = len(shifts)
+    rows = projected.shape[1]
+    mixed = jax.ShapeDtypeStruct((H, rows, DH), jnp.bfloat16)
+    out_specs = [slab(0, rows, DH)] * count
+    out_shape = [mixed] * count
+    if with_state:
+        out_specs.append(slab(0, DH, DH))
+        out_shape.append(jax.ShapeDtypeStruct((H, DH, DH), jnp.float32))
+    return pl.pallas_call(
+        functools.partial(conv_kernel, count, with_state),
+        grid=(H,),
+        in_specs=[slab(shift, rows, DH) for shift in shifts]
+        + [slab(base + shift, PAD, DH) for shift in shifts] * 2,
+        out_specs=out_specs,
+        out_shape=out_shape,
+        scratch_shapes=[pltpu.VMEM((rows + PAD, DH), jnp.float32)],
+        cost_estimate=pl.CostEstimate(
+            flops=H * count * rows * DH * (12 + 2 * DH),
+            transcendentals=H * count * rows * DH,
+            bytes_accessed=H * count * rows * DH * 4,
+        ),
+    )(*([projected] * count + [earlier] * count + [taps] * count))
 
 
 def local_kernel(q_ref, k_ref, v_ref, out_ref):
@@ -114,22 +144,12 @@
         conv_weight.reshape(KW, slabs, DH).transpose(1, 0, 2), ((0, 0), (0, PAD - KW), (0, 0))
     )
 
-    mixed_shape = jax.ShapeDtypeStruct((H, rows, DH), jnp.bfloat16)
-    query, key, value, state = pl.pallas_call(
-        conv_kernel,
-        grid=(H,),
-        in_specs=[slab(0, rows, DH), slab(H, rows, DH), slab(2 * H, rows, DH)]
-        + [slab(0, PAD, DH), slab(H, PAD, DH), slab(2 * H, PAD, DH)]
-        + [slab(0, PAD, DH), slab(H, PAD, DH), slab(2 * H, PAD, DH)],
-        out_specs=[slab(0, rows, DH)] * 3 + [slab(0, DH, DH)],
-        out_shape=[mixed_shape] * 3 + [jax.ShapeDtypeStruct((H, DH, DH), jnp.float32)],
-        scratch_shapes=[pltpu.VMEM((rows + PAD, DH), jnp.float32)],
-        cost_estimate=pl.CostEstimate(
-            flops=H * (3 * rows * DH * 12 + 2 * rows * DH * DH),
-            transcendentals=H * 3 * rows * DH,
-            bytes_accessed=H * 3 * rows * DH * 4,
-        ),
-    )(projected, projected, projected, earlier_rows, earlier_rows, earlier_rows, taps, taps, taps)
+    key, value, state = conv_call(projected, earlier_rows, taps, (H, 2 * H), 0, True)
+    zbefore, row_total = gather_earlier(state.astype(jnp.bfloat16), "sz")
+    ybefore, _ = gather_earlier(row_total.astype(jnp.bfloat16), "sy")
+    prefix = ybefore + zbefore
+
+    (query,) = conv_call(projected, earlier_rows, taps, (0,), 0, False)
 
     block = min(BLOCK, rows)
     local_part = pl.pallas_call(
@@ -144,10 +164,6 @@
             bytes_accessed=H * rows * DH * 10,
         ),
     )(query, key, value)
-
-    zbefore, row_total = gather_earlier(state.astype(jnp.bfloat16), "sz")
-    ybefore, _ = gather_earlier(row_total.astype(jnp.bfloat16), "sy")
-    prefix = ybefore + zbefore
 
     out = pl.pallas_call(
         out_kernel,

time: 85.6 us -> 89 us (1.040)
  Pallas kernels: 34.4 us -> 39.3 us
  waiting for transfers between devices: 2.79 us -> 0.85 us
    pallas_call x1 -> x2, Pallas kernels: 10.6 us -> 15.4 us  [conv_call(): pl.pallas_call(functools.partial(conv_kernel, count, with_state), grid=(H...]
    all_to_all x1, waiting for transfers between devices: 1.94 us -> 0.01 us  [gather_earlier(): lax.all_to_all(jnp.broadcast_to(x, (count,) + x.shape), axis, 0, 0)]
  transfers between devices with their start and end apart: 2 -> 2, of which waited for: 2 -> 1; matrix products, arithmetic and copies ran while one was open for 1% -> 1% of each run, Pallas kernels for 12% -> 19%
where the time goes in v8:
time: 89 us; the launch traced here: 87.8 us
  Pallas kernels  39.3 us (44%)
  blocking collectives  19.4 us (22%)
  matrix products  9.57 us (11%)
  starting transfers between devices  8.36 us (9%)
  local copies, waits for them, and re-layouts  5.42 us (6%)
  other arithmetic  4.77 us (5%)
    all_to_all x1, blocking collectives, gather_earlier(): lax.all_to_all(jnp.broadcast_to(x, (count,) + x.shape), axis, 0, 0)  19.4 us
    pallas_call x2, Pallas kernels, conv_call(): pl.pallas_call(functools.partial(conv_kernel, count, with_state), grid=(H...  15.4 us
    pallas_call x1, Pallas kernels, local(): pl.pallas_call(out_kernel, grid=(H,), in_specs=[slab(0, rows, DH), slab(0...  13.6 us
    pallas_call x1, Pallas kernels, local(): pl.pallas_call(local_kernel, grid=(H,), in_specs=[slab(0, rows, DH)] * 3,...  10.2 us
    dot_general x1, matrix products, local(): jnp.einsum('td,dje->jte', normed, w_qkv.reshape(width, slabs, DH), prefer...  9.57 us
    all_to_all x1, starting transfers between devices, gather_earlier(): lax.all_to_all(jnp.broadcast_to(x, (count,) + x.shape), axis, 0, 0)  4.46 us
    ppermute x1, starting transfers between devices, local(): lax.ppermute(projected[:, rows - (KW - 1):, :], seq_axes, [(i, i + 1) for...  3.9 us
    unnamed x4, local copies, waits for them, and re-layouts  2.66 us
  transfers between devices with their start and end apart: 2, of which 1 were waited for; matrix products, arithmetic and copies ran while one was open for 1% of the time, Pallas kernels for 19%

profile of v8, /device:TPU:0, one launch (start us, length us, event | category | flops | bytes accessed | tf_op | source)
XLA Modules:
  0.0 87.8 jit_solution(8776509853995241409)
XLA Ops:
  0.0 2.1 %fusion.3 = f32[1024]{0:T(1024)S(1)} fusion(bf16[1024,1024]{1,0:T(8,128)(2,1)} %param.6), kind=kLoop, calls=%fused_computation.6 | loop fusion | flops 3144704 | bytes 2101248 | tf_op jit(solution)/shard_map/reduce_sum | solution.py:129
  2.1 0.0 copy-start.1
  2.1 9.6 %convert_bitcast_fusion.refs_0_.refs_1_ = bf16[24,1024,128]{2,1,0:T(8,128)(2,1)S(1)} fusion(bf16[1024,1024]{1,0:T(8,128)(2,1)} %param.6, f32[1024]{0:T(1024)} %param.7, f32[1024]{0:T(1024)S(1)} %add_rsqrt_fusion, bf16[1024,3072]{1,0:T(8,128)(2,1)} %param.8), kind=kOutput, calls=%fused_computation.3 | convolution fusion | flops 6449790976 | bytes 14688256 | tf_op jit(solution)/shard_map/td,dje->jte/dot_general | solution.py:133
  11.7 0.0 copy-start
  11.7 2.7 %copy-done = bf16[24,1024,128]{2,1,0:T(8,128)(2,1)} copy-done((bf16[24,1024,128]{2,1,0:T(8,128)(2,1)}, bf16[24,1024,128]{2,1,0:T(8,128)(2,1)S(1)}, u32[]{:S(2)}) %copy-start) | copy-done | bytes 6291480
  14.4 3.9 %collective-permute-start = (bf16[24,3,128]{2,1,0:T(4,128)(2,1)S(1)}, bf16[24,3,128]{2,1,0:T(4,128)(2,1)S(1)}, u32[]{:S(2)}, u32[]{:S(2)}) collective-permute-start(bf16[24,3,128]{2,1,0:T(4,128)(2,1)S(1)} %slice.4), channel_id=1, source_target_pairs={{0,1},{1,2},{2,3},{3,4},{4,5},{5,6},{6,7},{7,8},{8,9},{9,10},{10,1... | collective-permute-start | bytes 55304 | tf_op jit(solution)/shard_map/ppermute | solution.py:139
  18.3 0.0 copy-done.1
  18.3 0.6 pad.9.refs_2_.refs_4_.refs_5_
  18.9 0.8 collective-permute-done
  19.8 0.6 pad.8.refs_1_.refs_2_.refs_3_
  20.4 8.5 %shard_map.65 = (bf16[8,1024,128]{2,1,0:T(8,128)(2,1)}, bf16[8,1024,128]{2,1,0:T(8,128)(2,1)}, f32[8,128,128]{2,1,0:T(8,128)}) custom-call(bf16[24,1024,128]{2,1,0:T(8,128)(2,1)} %copy-done, bf16[24,1024,128]{2,1,0:T(8,128)(2,1)} %copy-done, bf16[24,8,128]{2,1,0:T(8,128)(2,1)} %pad.8.refs_1_.refs_2_.refs_3_, bf16[24,8,128]{2,1,0:T(8,128)(2,1)} %pad.8.refs_1_.refs_2_.refs_3_, ...), custom_call_target="tpu_custom_call" | custom-call | flops 562036736 | bytes 8388608 | tf_op jit(solution)/shard_map/pallas_call | solution.py:58
  29.0 1.1 %convert_element_type.43 = bf16[8,128,128]{2,1,0:T(8,128)(2,1)S(1)} convert(f32[8,128,128]{2,1,0:T(8,128)} %get-tuple-element.10) | non-fusion elementwise | flops 131072 | bytes 786432 | tf_op jit(solution)/shard_map/convert_element_type | solution.py:148
  30.0 0.2 broadcast_in_dim.4
  30.3 19.4 %all_to_all.10 = bf16[4,8,128,128]{3,2,1,0:T(8,128)(2,1)S(1)} all-to-all(bf16[4,8,128,128]{3,2,1,0:T(8,128)(2,1)S(1)} %broadcast_in_dim.4), channel_id=1, replica_groups=mesh['trace'=8,'sy'=4,'sz'=4] {'sz'}, dimensions={0} | all-to-all | bytes 2097152 | tf_op jit(solution)/shard_map/all_to_all | solution.py:26
  49.7 0.2 reduce_sum.40
  49.9 1.2 %broadcast_in_dim.5 = bf16[4,8,128,128]{3,2,1,0:T(8,128)(2,1)} broadcast(bf16[8,128,128]{2,1,0:T(8,128)(2,1)S(1)} %reduce_sum.40), dimensions={1,2,3} | broadcast | bytes 1310720 | tf_op jit(solution)/shard_map/broadcast_in_dim | solution.py:26
  51.1 4.5 %all-to-all-start.1 = ((bf16[4,8,128,128]{3,2,1,0:T(8,128)(2,1)}), bf16[4,8,128,128]{3,2,1,0:T(8,128)(2,1)S(1)}, u32[]{:S(2)}, u32[]{:S(2)}) async-start(bf16[4,8,128,128]{3,2,1,0:T(8,128)(2,1)} %broadcast_in_dim.5), calls=%async_computation.1 | async-start | bytes 2097152 | tf_op jit(solution)/shard_map/all_to_all | solution.py:26
  55.6 6.9 %shard_map.64.q_ref = bf16[8,1024,128]{2,1,0:T(8,128)(2,1)} custom-call(bf16[24,1024,128]{2,1,0:T(8,128)(2,1)} %copy-done, bf16[24,8,128]{2,1,0:T(8,128)(2,1)} %pad.8.refs_1_.refs_2_.refs_3_, f32[24,8,128]{2,1,0:T(8,128)} %pad.9.refs_2_.refs_4_.refs_5_), custom_call_target="tpu_custom_call" | custom-call | flops 281018368 | bytes 4194304 | tf_op jit(solution)/shard_map/pallas_call | solution.py:58
  62.5 10.2 %shard_map.66.local_ref = f32[8,1024,128]{2,1,0:T(8,128)} custom-call(bf16[8,1024,128]{2,1,0:T(8,128)(2,1)} %shard_map.64.q_ref, bf16[8,1024,128]{2,1,0:T(8,128)(2,1)} %get-tuple-element.8.k_ref, bf16[8,1024,128]{2,1,0:T(8,128)(2,1)} %get-tuple-element.9.v_ref), custom_call_target="tpu_custom_call" | custom-call | flops 2952790016 | bytes 10485760 | tf_op jit(solution)/shard_map/pallas_call | solution.py:155
  72.7 0.3 multiply_reduce_fusion
  73.0 0.0 all-to-all-done.1
  73.0 0.3 multiply_reduce_fusion.1
  73.3 0.9 add.20.prefix_ref
  74.1 13.6 %shard_map.67 = bf16[1024,1024]{1,0:T(8,128)(2,1)} custom-call(bf16[8,1024,128]{2,1,0:T(8,128)(2,1)} %shard_map.64.q_ref, f32[8,1024,128]{2,1,0:T(8,128)} %shard_map.66.local_ref, f32[8,128,128]{2,1,0:T(8,128)} %add.20.prefix_ref, f32[8,1,128]{2,1,0:T(1,128)} %bitcast.21, bf16[8,128,1024]{2,1,0:T(8,128)(2,1)} %bitcast.19), custom_call_target="tpu_custom_call" | custom-call | flops 2684354560 | bytes 10485760 | tf_op jit(solution)/shard_map/pallas_call | solution.py:168
  (4 shorter events, 0.0 us)
Async XLA Ops:
  2.1 16.2 %copy-start.1 = (f32[4,3072]{1,0:T(4,128)S(1)}, f32[4,3072]{1,0:T(4,128)}, u32[]{:S(2)}) copy-start(f32[4,3072]{1,0:T(4,128)} %param.9) | copy-start | bytes 147460
  11.7 2.7 %copy-start = (bf16[24,1024,128]{2,1,0:T(8,128)(2,1)}, bf16[24,1024,128]{2,1,0:T(8,128)(2,1)S(1)}, u32[]{:S(2)}) copy-start(bf16[24,1024,128]{2,1,0:T(8,128)(2,1)S(1)} %convert_bitcast_fusion.refs_0_.refs_1_) | copy-start | bytes 18874372
  14.4 5.4 %collective-permute-start = (bf16[24,3,128]{2,1,0:T(4,128)(2,1)S(1)}, bf16[24,3,128]{2,1,0:T(4,128)(2,1)S(1)}, u32[]{:S(2)}, u32[]{:S(2)}) collective-permute-start(bf16[24,3,128]{2,1,0:T(4,128)(2,1)S(1)} %slice.4), channel_id=1, source_target_pairs={{0,1},{1,2},{2,3},{3,4},{4,5},{5,6},{6,7},{7,8},{8,9},{9,10},{10,1... | collective-permute-start | bytes 55304 | tf_op jit(solution)/shard_map/ppermute | solution.py:139
  51.1 21.8 %all-to-all-start.1 = ((bf16[4,8,128,128]{3,2,1,0:T(8,128)(2,1)}), bf16[4,8,128,128]{3,2,1,0:T(8,128)(2,1)S(1)}, u32[]{:S(2)}, u32[]{:S(2)}) async-start(bf16[4,8,128,128]{3,2,1,0:T(8,128)(2,1)} %broadcast_in_dim.5), calls=%async_computation.1 | async-start | bytes 2097152 | tf_op jit(solution)/shard_map/all_to_all | solution.py:26

commit v9 on v5

--- a/solution.py
+++ b/solution.py
@@ -66,27 +66,17 @@
         )
 
 
-def out_kernel(q_ref, local_ref, prefix_ref, gain_ref, w_ref, out_ref, acc):
-    head = pl.program_id(0)
-    hi, lo = split_bf16(prefix_ref[...])
-    query = q_ref[...]
-    attended = local_ref[...] + jnp.dot(query, hi, preferred_element_type=jnp.float32)
-    attended = attended + jnp.dot(query, lo, preferred_element_type=jnp.float32)
-    scaled = attended * lax.rsqrt(jnp.mean(attended * attended, -1, keepdims=True) + 1e-05)
-    headed = (scaled * gain_ref[...]).astype(jnp.bfloat16)
-    part = jnp.dot(headed, w_ref[...], preferred_element_type=jnp.float32)
-
-    @pl.when(head == 0)
-    def _():
-        acc[...] = part
-
-    @pl.when(head > 0)
-    def _():
-        acc[...] += part
-
-    @pl.when(head == pl.num_programs(0) - 1)
-    def _():
-        out_ref[...] = acc[...].astype(out_ref.dtype)
+def out_kernel(q_ref, local_ref, prefix_ref, gain_ref, w_ref, out_ref, headed):
+    for head in range(q_ref.shape[0]):
+        hi, lo = split_bf16(prefix_ref[head])
+        query = q_ref[head]
+        attended = local_ref[head] + jnp.dot(query, hi, preferred_element_type=jnp.float32)
+        attended = attended + jnp.dot(query, lo, preferred_element_type=jnp.float32)
+        scaled = attended * lax.rsqrt(jnp.mean(attended * attended, -1, keepdims=True) + 1e-05)
+        headed[:, head * DH : (head + 1) * DH] = (scaled * gain_ref[head]).astype(headed.dtype)
+    out_ref[...] = jnp.dot(
+        headed[...], w_ref[...], preferred_element_type=jnp.float32
+    ).astype(out_ref.dtype)
 
 
 def slab(shift, rows, cols):
@@ -149,25 +139,26 @@
     ybefore, _ = gather_earlier(row_total.astype(jnp.bfloat16), "sy")
     prefix = ybefore + zbefore
 
+    tile = min(256, rows)
     out = pl.pallas_call(
         out_kernel,
-        grid=(H,),
+        grid=(rows // tile,),
         in_specs=[
-            slab(0, rows, DH),
-            slab(0, rows, DH),
-            slab(0, DH, DH),
-            slab(0, 1, DH),
-            slab(0, DH, width),
+            pl.BlockSpec((H, tile, DH), lambda i: (0, i, 0)),
+            pl.BlockSpec((H, tile, DH), lambda i: (0, i, 0)),
+            pl.BlockSpec((H, DH, DH), lambda i: (0, 0, 0)),
+            pl.BlockSpec((H, 1, DH), lambda i: (0, 0, 0)),
+            pl.BlockSpec((width, width), lambda i: (0, 0)),
         ],
-        out_specs=pl.BlockSpec((rows, width), lambda h: (0, 0)),
+        out_specs=pl.BlockSpec((tile, width), lambda i: (i, 0)),
         out_shape=jax.ShapeDtypeStruct((rows, width), jnp.bfloat16),
-        scratch_shapes=[pltpu.VMEM((rows, width), jnp.float32)],
+        scratch_shapes=[pltpu.VMEM((tile, H * DH), jnp.bfloat16)],
         cost_estimate=pl.CostEstimate(
-            flops=H * (4 * rows * DH * DH + 2 * rows * DH * width),
+            flops=H * 4 * rows * DH * DH + 2 * rows * width * width,
             transcendentals=H * rows,
             bytes_accessed=H * rows * DH * 6 + width * width * 2 + rows * width * 2,
         ),
-    )(query, local_part, prefix, head_gain.reshape(H, 1, DH), w_out.reshape(H, DH, width))
+    )(query, local_part, prefix, head_gain.reshape(H, 1, DH), w_out)
     return out
 
 

time: 85.6 us -> 79.9 us (0.933)
  Pallas kernels: 34.4 us -> 28.8 us
    pallas_call x1, Pallas kernels: 13.6 us -> 7.97 us  [local(): pl.pallas_call(out_kernel, grid=(rows // tile,), in_specs=[pl.BlockSpec((...]
  transfers between devices with their start and end apart: 2 -> 2, of which waited for: 2 -> 2; matrix products, arithmetic and copies ran while one was open for 1% -> 1% of each run, Pallas kernels for 12% -> 13%
where the time goes in v9:
time: 79.9 us; the launch traced here: 79.2 us
  Pallas kernels  28.8 us (36%)
  blocking collectives  19.4 us (24%)
  matrix products  9.57 us (12%)
  starting transfers between devices  8.36 us (10%)
  local copies, waits for them, and re-layouts  5.4 us (7%)
  other arithmetic  4.77 us (6%)
  waiting for transfers between devices  2.79 us (3%)
    all_to_all x1, blocking collectives, gather_earlier(): lax.all_to_all(jnp.broadcast_to(x, (count,) + x.shape), axis, 0, 0)  19.4 us
    pallas_call x1, Pallas kernels, local(): pl.pallas_call(conv_kernel, grid=(H,), in_specs=[slab(0, rows, DH), slab(...  10.6 us
    pallas_call x1, Pallas kernels, local(): pl.pallas_call(local_kernel, grid=(H,), in_specs=[slab(0, rows, DH)] * 3,...  10.2 us
    dot_general x1, matrix products, local(): jnp.einsum('td,dje->jte', normed, w_qkv.reshape(width, slabs, DH), prefer...  9.57 us
    pallas_call x1, Pallas kernels, local(): pl.pallas_call(out_kernel, grid=(rows // tile,), in_specs=[pl.BlockSpec((...  7.97 us
    all_to_all x1, starting transfers between devices, gather_earlier(): lax.all_to_all(jnp.broadcast_to(x, (count,) + x.shape), axis, 0, 0)  4.46 us
    ppermute x1, starting transfers between devices, local(): lax.ppermute(projected[:, rows - (KW - 1):, :], seq_axes, [(i, i + 1) for...  3.9 us
    unnamed x4, local copies, waits for them, and re-layouts  2.66 us
  transfers between devices with their start and end apart: 2, of which 2 were waited for; matrix products, arithmetic and copies ran while one was open for 1% of the time, Pallas kernels for 13%

profile of v9, /device:TPU:0, one launch (start us, length us, event | category | flops | bytes accessed | tf_op | source)
XLA Modules:
  0.0 79.2 jit_solution(8209052618832632829)
XLA Ops:
  0.0 2.1 %fusion.3 = f32[1024]{0:T(1024)S(1)} fusion(bf16[1024,1024]{1,0:T(8,128)(2,1)} %param.6), kind=kLoop, calls=%fused_computation.6 | loop fusion | flops 3144704 | bytes 2101248 | tf_op jit(solution)/shard_map/reduce_sum | solution.py:89
  2.1 0.0 copy-start.1
  2.1 9.6 %convert_bitcast_fusion.pq.pk.pv = bf16[24,1024,128]{2,1,0:T(8,128)(2,1)S(1)} fusion(bf16[1024,1024]{1,0:T(8,128)(2,1)} %param.6, f32[1024]{0:T(1024)} %param.7, f32[1024]{0:T(1024)S(1)} %add_rsqrt_fusion, bf16[1024,3072]{1,0:T(8,128)(2,1)} %param.8), kind=kOutput, calls=%fused_computation.3 | convolution fusion | flops 6449790976 | bytes 14688256 | tf_op jit(solution)/shard_map/td,dje->jte/dot_general | solution.py:93
  11.7 0.0 copy-start
  11.7 2.7 %copy-done = bf16[24,1024,128]{2,1,0:T(8,128)(2,1)} copy-done((bf16[24,1024,128]{2,1,0:T(8,128)(2,1)}, bf16[24,1024,128]{2,1,0:T(8,128)(2,1)S(1)}, u32[]{:S(2)}) %copy-start) | copy-done | bytes 6291480
  14.4 3.9 %collective-permute-start = (bf16[24,3,128]{2,1,0:T(4,128)(2,1)S(1)}, bf16[24,3,128]{2,1,0:T(4,128)(2,1)S(1)}, u32[]{:S(2)}, u32[]{:S(2)}) collective-permute-start(bf16[24,3,128]{2,1,0:T(4,128)(2,1)S(1)} %slice.4), channel_id=1, source_target_pairs={{0,1},{1,2},{2,3},{3,4},{4,5},{5,6},{6,7},{7,8},{8,9},{9,10},{10,1... | collective-permute-start | bytes 55304 | tf_op jit(solution)/shard_map/ppermute | solution.py:99
  18.3 0.0 copy-done.1
  18.3 0.6 pad.9.tq.tk.tv
  18.9 0.9 %collective-permute-done = bf16[24,3,128]{2,1,0:T(4,128)(2,1)S(1)} collective-permute-done((bf16[24,3,128]{2,1,0:T(4,128)(2,1)S(1)}, bf16[24,3,128]{2,1,0:T(4,128)(2,1)S(1)}, u32[]{:S(2)}, u32[]{:S(2)}) %collective-permute-start) | collective-permute-done | bytes 18464 | tf_op jit(solution)/shard_map/ppermute | solution.py:99
  19.8 0.6 pad.8.eq.ek.ev
  20.4 10.6 %shard_map.64 = (bf16[8,1024,128]{2,1,0:T(8,128)(2,1)}, bf16[8,1024,128]{2,1,0:T(8,128)(2,1)}, bf16[8,1024,128]{2,1,0:T(8,128)(2,1)}, f32[8,128,128]{2,1,0:T(8,128)}) custom-call(bf16[24,1024,128]{2,1,0:T(8,128)(2,1)} %copy-done, bf16[24,1024,128]{2,1,0:T(8,128)(2,1)} %copy-done, bf16[24,1024,128]{2,1,0:T(8,128)(2,1)} %copy-done, ...), custom_call_target="tpu_custom_call" | custom-call | flops 306184192 | bytes 12582912 | tf_op jit(solution)/shard_map/pallas_call | solution.py:108
  31.0 1.1 %convert_element_type.43 = bf16[8,128,128]{2,1,0:T(8,128)(2,1)S(1)} convert(f32[8,128,128]{2,1,0:T(8,128)} %get-tuple-element.12) | non-fusion elementwise | flops 131072 | bytes 786432 | tf_op jit(solution)/shard_map/convert_element_type | solution.py:138
  32.1 0.2 broadcast_in_dim.4
  32.3 19.4 %all_to_all.10 = bf16[4,8,128,128]{3,2,1,0:T(8,128)(2,1)S(1)} all-to-all(bf16[4,8,128,128]{3,2,1,0:T(8,128)(2,1)S(1)} %broadcast_in_dim.4), channel_id=1, replica_groups=mesh['trace'=8,'sy'=4,'sz'=4] {'sz'}, dimensions={0} | all-to-all | bytes 2097152 | tf_op jit(solution)/shard_map/all_to_all | solution.py:24
  51.8 0.2 reduce_sum.40
  52.0 1.2 %broadcast_in_dim.5 = bf16[4,8,128,128]{3,2,1,0:T(8,128)(2,1)} broadcast(bf16[8,128,128]{2,1,0:T(8,128)(2,1)S(1)} %reduce_sum.40), dimensions={1,2,3} | broadcast | bytes 1310720 | tf_op jit(solution)/shard_map/broadcast_in_dim | solution.py:24
  53.2 4.5 %all-to-all-start.1 = ((bf16[4,8,128,128]{3,2,1,0:T(8,128)(2,1)}), bf16[4,8,128,128]{3,2,1,0:T(8,128)(2,1)S(1)}, u32[]{:S(2)}, u32[]{:S(2)}) async-start(bf16[4,8,128,128]{3,2,1,0:T(8,128)(2,1)} %broadcast_in_dim.5), calls=%async_computation.1 | async-start | bytes 2097152 | tf_op jit(solution)/shard_map/all_to_all | solution.py:24
  57.6 10.2 %shard_map.65.local_ref = f32[8,1024,128]{2,1,0:T(8,128)} custom-call(bf16[8,1024,128]{2,1,0:T(8,128)(2,1)} %get-tuple-element.9.q_ref, bf16[8,1024,128]{2,1,0:T(8,128)(2,1)} %get-tuple-element.10.k_ref, bf16[8,1024,128]{2,1,0:T(8,128)(2,1)} %get-tuple-element.11.v_ref), custom_call_target="tpu_custom_call" | custom-call | flops 2952790016 | bytes 10485760 | tf_op jit(solution)/shard_map/pallas_call | solution.py:125
  67.9 0.3 multiply_reduce_fusion
  68.1 1.9 %all-to-all-done.1 = bf16[4,8,128,128]{3,2,1,0:T(8,128)(2,1)S(1)} async-done(((bf16[4,8,128,128]{3,2,1,0:T(8,128)(2,1)}), bf16[4,8,128,128]{3,2,1,0:T(8,128)(2,1)S(1)}, u32[]{:S(2)}, u32[]{:S(2)}) %all-to-all-start.1) | async-done | bytes 1048608 | tf_op jit(solution)/shard_map/all_to_all | solution.py:24
  70.1 0.3 multiply_reduce_fusion.1
  70.4 0.9 %add.20.prefix_ref = f32[8,128,128]{2,1,0:T(8,128)} add(f32[8,128,128]{2,1,0:T(8,128)S(1)} %multiply_reduce_fusion.1, f32[8,128,128]{2,1,0:T(8,128)S(1)} %multiply_reduce_fusion) | non-fusion elementwise | flops 131072 | bytes 1572864 | tf_op jit(solution)/shard_map/add | solution.py:140
  71.2 8.0 %shard_map.66 = bf16[1024,1024]{1,0:T(8,128)(2,1)} custom-call(bf16[8,1024,128]{2,1,0:T(8,128)(2,1)} %get-tuple-element.9.q_ref, f32[8,1024,128]{2,1,0:T(8,128)} %shard_map.65.local_ref, f32[8,128,128]{2,1,0:T(8,128)} %add.20.prefix_ref, f32[8,1,128]{2,1,0:T(1,128)} %bitcast.19, bf16[1024,1024]{1,0:T(8,128)(2,1)} %w_ref.1), custom_call_target="tpu_custom_call" | custom-call | flops 2684354560 | bytes 10485760 | tf_op jit(solution)/shard_map/pallas_call | solution.py:143
  (4 shorter events, 0.0 us)
Async XLA Ops:
  2.1 16.2 %copy-start.1 = (f32[4,3072]{1,0:T(4,128)S(1)}, f32[4,3072]{1,0:T(4,128)}, u32[]{:S(2)}) copy-start(f32[4,3072]{1,0:T(4,128)} %param.9) | copy-start | bytes 147460
  11.7 2.7 %copy-start = (bf16[24,1024,128]{2,1,0:T(8,128)(2,1)}, bf16[24,1024,128]{2,1,0:T(8,128)(2,1)S(1)}, u32[]{:S(2)}) copy-start(bf16[24,1024,128]{2,1,0:T(8,128)(2,1)S(1)} %convert_bitcast_fusion.pq.pk.pv) | copy-start | bytes 18874372
  14.4 5.4 %collective-permute-start = (bf16[24,3,128]{2,1,0:T(4,128)(2,1)S(1)}, bf16[24,3,128]{2,1,0:T(4,128)(2,1)S(1)}, u32[]{:S(2)}, u32[]{:S(2)}) collective-permute-start(bf16[24,3,128]{2,1,0:T(4,128)(2,1)S(1)} %slice.4), channel_id=1, source_target_pairs={{0,1},{1,2},{2,3},{3,4},{4,5},{5,6},{6,7},{7,8},{8,9},{9,10},{10,1... | collective-permute-start | bytes 55304 | tf_op jit(solution)/shard_map/ppermute | solution.py:99
  53.2 16.9 %all-to-all-start.1 = ((bf16[4,8,128,128]{3,2,1,0:T(8,128)(2,1)}), bf16[4,8,128,128]{3,2,1,0:T(8,128)(2,1)S(1)}, u32[]{:S(2)}, u32[]{:S(2)}) async-start(bf16[4,8,128,128]{3,2,1,0:T(8,128)(2,1)} %broadcast_in_dim.5), calls=%async_computation.1 | async-start | bytes 2097152 | tf_op jit(solution)/shard_map/all_to_all | solution.py:24

commit v10 on v9

--- a/solution.py
+++ b/solution.py
@@ -18,13 +18,23 @@
     return hi.astype(jnp.bfloat16), (x - hi).astype(jnp.bfloat16)
 
 
-def gather_earlier(x, axis):
-    count = lax.axis_size(axis)
-    place = lax.axis_index(axis)
-    gathered = lax.all_to_all(jnp.broadcast_to(x, (count,) + x.shape), axis, 0, 0)
-    values = gathered.astype(jnp.float32)
-    earlier = (lax.iota(jnp.int32, count) < place).astype(jnp.float32)
-    return jnp.sum(values * earlier[:, None, None, None], 0), jnp.sum(values, 0)
+def earlier_states(state):
+    count = lax.axis_size("sz")
+    rows_count = lax.axis_size("sy")
+    quarters = state.astype(jnp.bfloat16).reshape((count, -1) + state.shape[1:])
+    mine = lax.all_to_all(quarters, "sz", 0, 0).astype(jnp.float32)
+    before = [jnp.zeros_like(mine[0])]
+    for z in range(1, count):
+        before.append(before[-1] + mine[z - 1])
+    row_total = before[-1] + mine[count - 1]
+    totals = lax.all_to_all(
+        jnp.broadcast_to(row_total.astype(jnp.bfloat16), (rows_count,) + row_total.shape), "sy", 0, 0
+    ).astype(jnp.float32)
+    earlier = (lax.iota(jnp.int32, rows_count) < lax.axis_index("sy")).astype(jnp.float32)
+    rows_before = jnp.sum(totals * earlier[:, None, None, None], 0)
+    finished = jnp.stack(before) + rows_before
+    prefix = lax.all_to_all(finished.astype(jnp.bfloat16), "sz", 0, 0)
+    return prefix.reshape(state.shape).astype(jnp.float32)
 
 
 def conv_kernel(pq, pk, pv, eq, ek, ev, tq, tk, tv, oq, ok, ov, state_ref, buf):
@@ -135,9 +145,7 @@
         ),
     )(query, key, value)
 
-    zbefore, row_total = gather_earlier(state.astype(jnp.bfloat16), "sz")
-    ybefore, _ = gather_earlier(row_total.astype(jnp.bfloat16), "sy")
-    prefix = ybefore + zbefore
+    prefix = earlier_states(state)
 
     tile = min(256, rows)
     out = pl.pallas_call(

time: 79.9 us -> 80.4 us (level)
  blocking collectives: 19.4 us -> 12.2 us
  waiting for transfers between devices: 2.79 us -> 7.48 us
  starting transfers between devices: 8.36 us -> 11.8 us
    all_to_all x1, blocking collectives: 19.4 us -> 12.2 us  [earlier_states(): mine = lax.all_to_all(quarters, 'sz', 0, 0).astype(jnp.float32)]
    all_to_all x1 -> x2, waiting for transfers between devices: 1.94 us -> 6.65 us  [the longest x1 6.65 us: earlier_states(): lax.all_to_all(jnp.broadcast_to(row_total.astype(jnp.bfloat16), (rows_cou...]
    all_to_all x1 -> x2, starting transfers between devices: 4.46 us -> 7.87 us  [the longest x1 4.47 us: earlier_states(): lax.all_to_all(jnp.broadcast_to(row_total.astype(jnp.bfloat16), (rows_cou...]
    convert_element_type x3 -> x6, other arithmetic: 1.08 us -> 2.84 us  [the longest x1 1.08 us: earlier_states(): quarters = state.astype(jnp.bfloat16).reshape((count, -1) + state.shape[1:])]
    add x1 -> x0, other arithmetic: 0.85 us -> none  [local(): prefix = ybefore + zbefore]
  transfers between devices with their start and end apart: 2 -> 3, of which waited for: 2 -> 2; matrix products, arithmetic and copies ran while one was open for 1% -> 1% of each run, Pallas kernels for 13% -> 13%
where the time goes in v10:
time: 80.4 us; the launch traced here: 79.5 us
  Pallas kernels  28.7 us (36%)
  blocking collectives  12.2 us (15%)
  starting transfers between devices  11.8 us (15%)
  matrix products  9.57 us (12%)
  waiting for transfers between devices  7.48 us (9%)
  other arithmetic  5.03 us (6%)
  local copies, waits for them, and re-layouts  4.7 us (6%)
    all_to_all x1, blocking collectives, earlier_states(): mine = lax.all_to_all(quarters, 'sz', 0, 0).astype(jnp.float32)  12.2 us
    pallas_call x1, Pallas kernels, local(): pl.pallas_call(conv_kernel, grid=(H,), in_specs=[slab(0, rows, DH), slab(...  10.6 us
    pallas_call x1, Pallas kernels, local(): pl.pallas_call(local_kernel, grid=(H,), in_specs=[slab(0, rows, DH)] * 3,...  10.2 us
    dot_general x1, matrix products, local(): jnp.einsum('td,dje->jte', normed, w_qkv.reshape(width, slabs, DH), prefer...  9.57 us
    pallas_call x1, Pallas kernels, local(): pl.pallas_call(out_kernel, grid=(rows // tile,), in_specs=[pl.BlockSpec((...  7.96 us
    all_to_all x1, waiting for transfers between devices, earlier_states(): lax.all_to_all(jnp.broadcast_to(row_total.astype(jnp.bfloat16), (rows_cou...  6.65 us
    all_to_all x1, starting transfers between devices, earlier_states(): lax.all_to_all(jnp.broadcast_to(row_total.astype(jnp.bfloat16), (rows_cou...  4.47 us
    ppermute x1, starting transfers between devices, local(): lax.ppermute(projected[:, rows - (KW - 1):, :], seq_axes, [(i, i + 1) for...  3.9 us
  transfers between devices with their start and end apart: 3, of which 2 were waited for; matrix products, arithmetic and copies ran while one was open for 1% of the time, Pallas kernels for 13%

profile of v10, /device:TPU:0, one launch (start us, length us, event | category | flops | bytes accessed | tf_op | source)
XLA Modules:
  0.0 79.5 jit_solution(2190102218343419282)
XLA Ops:
  0.0 2.1 %fusion.3 = f32[1024]{0:T(1024)S(1)} fusion(bf16[1024,1024]{1,0:T(8,128)(2,1)} %param.6), kind=kLoop, calls=%fused_computation.6 | loop fusion | flops 3144704 | bytes 2101248 | tf_op jit(solution)/shard_map/reduce_sum | solution.py:99
  2.1 0.0 copy-start.1
  2.1 9.6 %convert_bitcast_fusion.pq.pk.pv = bf16[24,1024,128]{2,1,0:T(8,128)(2,1)S(1)} fusion(bf16[1024,1024]{1,0:T(8,128)(2,1)} %param.6, f32[1024]{0:T(1024)} %param.7, f32[1024]{0:T(1024)S(1)} %add_rsqrt_fusion, bf16[1024,3072]{1,0:T(8,128)(2,1)} %param.8), kind=kOutput, calls=%fused_computation.3 | convolution fusion | flops 6449790976 | bytes 14688256 | tf_op jit(solution)/shard_map/td,dje->jte/dot_general | solution.py:103
  11.7 0.0 copy-start
  11.7 2.6 %copy-done = bf16[24,1024,128]{2,1,0:T(8,128)(2,1)} copy-done((bf16[24,1024,128]{2,1,0:T(8,128)(2,1)}, bf16[24,1024,128]{2,1,0:T(8,128)(2,1)S(1)}, u32[]{:S(2)}) %copy-start) | copy-done | bytes 6291480
  14.3 3.9 %collective-permute-start = (bf16[24,3,128]{2,1,0:T(4,128)(2,1)S(1)}, bf16[24,3,128]{2,1,0:T(4,128)(2,1)S(1)}, u32[]{:S(2)}, u32[]{:S(2)}) collective-permute-start(bf16[24,3,128]{2,1,0:T(4,128)(2,1)S(1)} %slice.20), channel_id=1, source_target_pairs={{0,1},{1,2},{2,3},{3,4},{4,5},{5,6},{6,7},{7,8},{8,9},{9,10},{10,1... | collective-permute-start | bytes 55304 | tf_op jit(solution)/shard_map/ppermute | solution.py:109
  18.2 0.0 copy-done.1
  18.3 0.7 pad.9.tq.tk.tv
  18.9 0.8 %collective-permute-done = bf16[24,3,128]{2,1,0:T(4,128)(2,1)S(1)} collective-permute-done((bf16[24,3,128]{2,1,0:T(4,128)(2,1)S(1)}, bf16[24,3,128]{2,1,0:T(4,128)(2,1)S(1)}, u32[]{:S(2)}, u32[]{:S(2)}) %collective-permute-start) | collective-permute-done | bytes 18464 | tf_op jit(solution)/shard_map/ppermute | solution.py:109
  19.7 0.6 pad.8.eq.ek.ev
  20.4 10.6 %shard_map.64 = (bf16[8,1024,128]{2,1,0:T(8,128)(2,1)}, bf16[8,1024,128]{2,1,0:T(8,128)(2,1)}, bf16[8,1024,128]{2,1,0:T(8,128)(2,1)}, f32[8,128,128]{2,1,0:T(8,128)}) custom-call(bf16[24,1024,128]{2,1,0:T(8,128)(2,1)} %copy-done, bf16[24,1024,128]{2,1,0:T(8,128)(2,1)} %copy-done, bf16[24,1024,128]{2,1,0:T(8,128)(2,1)} %copy-done, ...), custom_call_target="tpu_custom_call" | custom-call | flops 306184192 | bytes 12582912 | tf_op jit(solution)/shard_map/pallas_call | solution.py:118
  31.0 1.1 %convert_element_type.49 = bf16[8,128,128]{2,1,0:T(8,128)(2,1)S(1)} convert(f32[8,128,128]{2,1,0:T(8,128)} %get-tuple-element.12) | non-fusion elementwise | flops 131072 | bytes 786432 | tf_op jit(solution)/shard_map/convert_element_type | solution.py:24
  32.0 12.2 %all_to_all.15 = bf16[4,2,128,128]{3,2,1,0:T(8,128)(2,1)S(1)} all-to-all(bf16[4,2,128,128]{3,2,1,0:T(8,128)(2,1)S(1)} %bitcast.25), channel_id=1, replica_groups=mesh['trace'=8,'sy'=4,'sz'=4] {'sz'}, dimensions={0} | all-to-all | bytes 524288 | tf_op jit(solution)/shard_map/all_to_all | solution.py:25
  44.3 0.7 broadcast_in_dim.2
  45.0 4.5 %all-to-all-start.1 = ((bf16[4,2,128,128]{3,2,1,0:T(8,128)(2,1)}), bf16[4,2,128,128]{3,2,1,0:T(8,128)(2,1)S(1)}, u32[]{:S(2)}, u32[]{:S(2)}) async-start(bf16[4,2,128,128]{3,2,1,0:T(8,128)(2,1)} %broadcast_in_dim.2), calls=%async_computation.1 | async-start | bytes 524288 | tf_op jit(solution)/shard_map/all_to_all | solution.py:30
  49.5 6.6 %all-to-all-done.1 = bf16[4,2,128,128]{3,2,1,0:T(8,128)(2,1)S(1)} async-done(((bf16[4,2,128,128]{3,2,1,0:T(8,128)(2,1)}), bf16[4,2,128,128]{3,2,1,0:T(8,128)(2,1)S(1)}, u32[]{:S(2)}, u32[]{:S(2)}) %all-to-all-start.1) | async-done | bytes 262176 | tf_op jit(solution)/shard_map/all_to_all | solution.py:30
  56.2 0.1 multiply_reduce_fusion
  56.3 0.8 %fusion.12 = bf16[4,2,128,128]{3,2,1,0:T(8,128)(2,1)} fusion(f32[1,2,128,128]{3,2,1,0:T(8,128)S(1)} %get-tuple-element.14, f32[1,2,128,128]{3,2,1,0:T(8,128)S(1)} %get-tuple-element.15, f32[1,2,128,128]{3,2,1,0:T(8,128)S(1)} %slice.21, f32[4]{0:T(128)S(1)} %pad.10.clone, f32[2,128,128]{2,1,0:T(8,128)S(1)} %multiply_reduce_fusion), kind=kLoop, calls=%fused_computation.13 | loop fusion | flops 655360 | bytes 786448 | tf_op jit(solution)/shard_map/convert_element_type | solution.py:36
  57.1 3.4 %all-to-all-start.2 = ((bf16[4,2,128,128]{3,2,1,0:T(8,128)(2,1)}), bf16[4,2,128,128]{3,2,1,0:T(8,128)(2,1)S(1)}, u32[]{:S(2)}, u32[]{:S(2)}) async-start(bf16[4,2,128,128]{3,2,1,0:T(8,128)(2,1)} %fusion.12), calls=%async_computation.2 | async-start | bytes 524288 | tf_op jit(solution)/shard_map/all_to_all | solution.py:36
  60.5 10.2 %shard_map.65.local_ref = f32[8,1024,128]{2,1,0:T(8,128)} custom-call(bf16[8,1024,128]{2,1,0:T(8,128)(2,1)} %get-tuple-element.9.q_ref, bf16[8,1024,128]{2,1,0:T(8,128)(2,1)} %get-tuple-element.10.k_ref, bf16[8,1024,128]{2,1,0:T(8,128)(2,1)} %get-tuple-element.11.v_ref), custom_call_target="tpu_custom_call" | custom-call | flops 2952790016 | bytes 10485760 | tf_op jit(solution)/shard_map/pallas_call | solution.py:135
  70.7 0.0 all-to-all-done.2
  70.7 0.9 %bitcast_convert_fusion.prefix_ref = f32[8,128,128]{2,1,0:T(8,128)} fusion(bf16[4,2,128,128]{3,2,1,0:T(8,128)(2,1)S(1)} %all-to-all-done.2), kind=kLoop, calls=%fused_computation.15 | loop fusion | flops 131072 | bytes 786432 | tf_op jit(solution)/shard_map/convert_element_type | solution.py:37
  71.6 8.0 %shard_map.66 = bf16[1024,1024]{1,0:T(8,128)(2,1)} custom-call(bf16[8,1024,128]{2,1,0:T(8,128)(2,1)} %get-tuple-element.9.q_ref, f32[8,1024,128]{2,1,0:T(8,128)} %shard_map.65.local_ref, f32[8,128,128]{2,1,0:T(8,128)} %bitcast_convert_fusion.prefix_ref, f32[8,1,128]{2,1,0:T(1,128)} %bitcast.27, bf16[1024,1024]{1,0:T(8,128)(2,1)} %w_ref.1), custom_call_target="tpu_custom_call" | custom-call | flops 2684354560 | bytes 10485760 | tf_op jit(solution)/shard_map/pallas_call | solution.py:151
  (7 shorter events, 0.1 us)
Async XLA Ops:
  2.1 16.2 %copy-start.1 = (f32[4,3072]{1,0:T(4,128)S(1)}, f32[4,3072]{1,0:T(4,128)}, u32[]{:S(2)}) copy-start(f32[4,3072]{1,0:T(4,128)} %param.9) | copy-start | bytes 147460
  11.7 2.6 %copy-start = (bf16[24,1024,128]{2,1,0:T(8,128)(2,1)}, bf16[24,1024,128]{2,1,0:T(8,128)(2,1)S(1)}, u32[]{:S(2)}) copy-start(bf16[24,1024,128]{2,1,0:T(8,128)(2,1)S(1)} %convert_bitcast_fusion.pq.pk.pv) | copy-start | bytes 18874372
  14.3 5.4 %collective-permute-start = (bf16[24,3,128]{2,1,0:T(4,128)(2,1)S(1)}, bf16[24,3,128]{2,1,0:T(4,128)(2,1)S(1)}, u32[]{:S(2)}, u32[]{:S(2)}) collective-permute-start(bf16[24,3,128]{2,1,0:T(4,128)(2,1)S(1)} %slice.20), channel_id=1, source_target_pairs={{0,1},{1,2},{2,3},{3,4},{4,5},{5,6},{6,7},{7,8},{8,9},{9,10},{10,1... | collective-permute-start | bytes 55304 | tf_op jit(solution)/shard_map/ppermute | solution.py:109
  45.0 11.1 %all-to-all-start.1 = ((bf16[4,2,128,128]{3,2,1,0:T(8,128)(2,1)}), bf16[4,2,128,128]{3,2,1,0:T(8,128)(2,1)S(1)}, u32[]{:S(2)}, u32[]{:S(2)}) async-start(bf16[4,2,128,128]{3,2,1,0:T(8,128)(2,1)} %broadcast_in_dim.2), calls=%async_computation.1 | async-start | bytes 524288 | tf_op jit(solution)/shard_map/all_to_all | solution.py:30
  57.1 13.6 %all-to-all-start.2 = ((bf16[4,2,128,128]{3,2,1,0:T(8,128)(2,1)}), bf16[4,2,128,128]{3,2,1,0:T(8,128)(2,1)S(1)}, u32[]{:S(2)}, u32[]{:S(2)}) async-start(bf16[4,2,128,128]{3,2,1,0:T(8,128)(2,1)} %fusion.12), calls=%async_computation.2 | async-start | bytes 524288 | tf_op jit(solution)/shard_map/all_to_all | solution.py:36

commit v11 on v9

--- a/solution.py
+++ b/solution.py
@@ -11,6 +11,7 @@
 KW = 4
 BLOCK = 512
 PAD = 8
+LEAD = 16
 
 
 def split_bf16(x):
@@ -27,14 +28,13 @@
     return jnp.sum(values * earlier[:, None, None, None], 0), jnp.sum(values, 0)
 
 
-def conv_kernel(pq, pk, pv, eq, ek, ev, tq, tk, tv, oq, ok, ov, state_ref, buf):
-    rows = pq.shape[0]
-    for proj, early, taps, out in ((pq, eq, tq, oq), (pk, ek, tk, ok), (pv, ev, tv, ov)):
-        buf[0:PAD, :] = early[...].astype(jnp.float32)
-        buf[PAD:, :] = proj[...].astype(jnp.float32)
+def conv_kernel(pq, pk, pv, tq, tk, tv, oq, ok, ov, state_ref, buf):
+    rows = oq.shape[0]
+    for proj, taps, out in ((pq, tq, oq), (pk, tk, ok), (pv, tv, ov)):
+        buf[...] = proj[...].astype(jnp.float32)
         summed = jnp.zeros((rows, DH), jnp.float32)
         for offset in range(KW):
-            summed = summed + taps[offset : offset + 1, :] * buf[pl.ds(PAD - offset, rows), :]
+            summed = summed + taps[offset : offset + 1, :] * buf[pl.ds(LEAD - offset, rows), :]
         out[...] = (summed * jax.nn.sigmoid(summed)).astype(out.dtype)
     state_ref[...] = lax.dot_general(
         ok[...], ov[...], (((0,), (0,)), ((), ())), preferred_element_type=jnp.float32
@@ -85,7 +85,15 @@
 
 def local(tokens, norm_gain, w_qkv, conv_weight, head_gain, w_out):
     rows, width = tokens.shape
-    tokens_f = tokens.astype(jnp.float32)
+    seq_axes = ("sy", "sz")
+    count = lax.axis_size("sy") * lax.axis_size("sz")
+    earlier_tokens = lax.ppermute(
+        tokens[rows - (KW - 1) :], seq_axes, [(i, i + 1) for i in range(count - 1)]
+    )
+    extended = jnp.concatenate(
+        [jnp.zeros((LEAD - (KW - 1), width), tokens.dtype), earlier_tokens, tokens], 0
+    )
+    tokens_f = extended.astype(jnp.float32)
     scale = lax.rsqrt(jnp.mean(tokens_f * tokens_f, -1, keepdims=True) + 1e-06)
     normed = (tokens_f * scale * norm_gain).astype(jnp.bfloat16)
 
@@ -93,33 +101,26 @@
     projected = jnp.einsum(
         "td,dje->jte", normed, w_qkv.reshape(width, slabs, DH), preferred_element_type=jnp.float32
     ).astype(jnp.bfloat16)
-
-    seq_axes = ("sy", "sz")
-    count = lax.axis_size("sy") * lax.axis_size("sz")
-    earlier_rows = lax.ppermute(
-        projected[:, rows - (KW - 1) :, :], seq_axes, [(i, i + 1) for i in range(count - 1)]
-    )
-    earlier_rows = jnp.pad(earlier_rows, ((0, 0), (PAD - (KW - 1), 0), (0, 0)))
     taps = jnp.pad(
         conv_weight.reshape(KW, slabs, DH).transpose(1, 0, 2), ((0, 0), (0, PAD - KW), (0, 0))
     )
 
     mixed_shape = jax.ShapeDtypeStruct((H, rows, DH), jnp.bfloat16)
+    longer = rows + LEAD
     query, key, value, state = pl.pallas_call(
         conv_kernel,
         grid=(H,),
-        in_specs=[slab(0, rows, DH), slab(H, rows, DH), slab(2 * H, rows, DH)]
-        + [slab(0, PAD, DH), slab(H, PAD, DH), slab(2 * H, PAD, DH)]
+        in_specs=[slab(0, longer, DH), slab(H, longer, DH), slab(2 * H, longer, DH)]
         + [slab(0, PAD, DH), slab(H, PAD, DH), slab(2 * H, PAD, DH)],
         out_specs=[slab(0, rows, DH)] * 3 + [slab(0, DH, DH)],
         out_shape=[mixed_shape] * 3 + [jax.ShapeDtypeStruct((H, DH, DH), jnp.float32)],
-        scratch_shapes=[pltpu.VMEM((rows + PAD, DH), jnp.float32)],
+        scratch_shapes=[pltpu.VMEM((longer, DH), jnp.float32)],
         cost_estimate=pl.CostEstimate(
             flops=H * (3 * rows * DH * 12 + 2 * rows * DH * DH),
             transcendentals=H * 3 * rows * DH,
             bytes_accessed=H * 3 * rows * DH * 4,
         ),
-    )(projected, projected, projected, earlier_rows, earlier_rows, earlier_rows, taps, taps, taps)
+    )(projected, projected, projected, taps, taps, taps)
 
     block = min(BLOCK, rows)
     local_part = pl.pallas_call(

time: 79.9 us -> 85.6 us (1.071)
  local copies, waits for them, and re-layouts: 5.4 us -> 11.2 us
  matrix products: 9.57 us -> 11.8 us
  other arithmetic: 4.77 us -> 3.21 us
    concatenate x0 -> x1, local copies, waits for them, and re-layouts: none -> 7.54 us  [local(): jnp.concatenate([jnp.zeros((LEAD - (KW - 1), width), tokens.dtype), earli...]
    unnamed x4 -> x2, local copies, waits for them, and re-layouts: 2.66 us -> 0.01 us
    dot_general x1, matrix products: 9.57 us -> 11.8 us  [local(): jnp.einsum('td,dje->jte', normed, w_qkv.reshape(width, slabs, DH), prefer...]
    reduce_sum x1, other arithmetic: 2.07 us -> 0.5 us  [local(): scale = lax.rsqrt(jnp.mean(tokens_f * tokens_f, -1, keepdims=True) + 1e-06)]
  transfers between devices with their start and end apart: 2 -> 2, of which waited for: 2 -> 1; matrix products, arithmetic and copies ran while one was open for 1% -> 2% of each run, Pallas kernels for 13% -> 12%
where the time goes in v11:
time: 85.6 us; the launch traced here: 84.6 us
  Pallas kernels  28.4 us (33%)
  blocking collectives  19.5 us (23%)
  matrix products  11.8 us (14%)
  local copies, waits for them, and re-layouts  11.2 us (13%)
  starting transfers between devices  8.36 us (10%)
  other arithmetic  3.21 us (4%)
  waiting for transfers between devices  2.12 us (2%)
    all_to_all x1, blocking collectives, gather_earlier(): lax.all_to_all(jnp.broadcast_to(x, (count,) + x.shape), axis, 0, 0)  19.5 us
    dot_general x1, matrix products, local(): jnp.einsum('td,dje->jte', normed, w_qkv.reshape(width, slabs, DH), prefer...  11.8 us
    pallas_call x1, Pallas kernels, local(): pl.pallas_call(local_kernel, grid=(H,), in_specs=[slab(0, rows, DH)] * 3,...  10.2 us
    pallas_call x1, Pallas kernels, local(): pl.pallas_call(conv_kernel, grid=(H,), in_specs=[slab(0, longer, DH), sla...  10.2 us
    pallas_call x1, Pallas kernels, local(): pl.pallas_call(out_kernel, grid=(rows // tile,), in_specs=[pl.BlockSpec((...  7.97 us
    concatenate x1, local copies, waits for them, and re-layouts, local(): jnp.concatenate([jnp.zeros((LEAD - (KW - 1), width), tokens.dtype), earli...  7.54 us
    all_to_all x1, starting transfers between devices, gather_earlier(): lax.all_to_all(jnp.broadcast_to(x, (count,) + x.shape), axis, 0, 0)  4.46 us
    ppermute x1, starting transfers between devices, local(): lax.ppermute(tokens[rows - (KW - 1):], seq_axes, [(i, i + 1) for i in ran...  3.89 us
  transfers between devices with their start and end apart: 2, of which 1 were waited for; matrix products, arithmetic and copies ran while one was open for 2% of the time, Pallas kernels for 12%

profile of v11, /device:TPU:0, one launch (start us, length us, event | category | flops | bytes accessed | tf_op | source)
XLA Modules:
  0.0 84.6 jit_solution(4019417015191869707)
XLA Ops:
  0.0 0.0 copy-start
  0.0 0.7 slice.3
  0.7 3.9 %collective-permute-start = (bf16[3,1024]{1,0:T(4,128)(2,1)S(1)}, bf16[3,1024]{1,0:T(4,128)(2,1)S(1)}, u32[]{:S(2)}, u32[]{:S(2)}) collective-permute-start(bf16[3,1024]{1,0:T(4,128)(2,1)S(1)} %slice.3), channel_id=1, source_target_pairs={{0,1},{1,2},{2,3},{3,4},{4,5},{5,6},{6,7},{7,8},{8,9},{9,10},{10,1... | collective-permute-start | bytes 18440 | tf_op jit(solution)/shard_map/ppermute | solution.py:90
  4.6 1.5 %pad.4.tq.tk.tv = f32[24,8,128]{2,1,0:T(8,128)} pad(f32[24,4,128]{2,1,0:T(4,128)} %bitcast.18, f32[]{:T(128)} %constant.14.clone.1), padding=0_0x0_4x0_0 | pad | bytes 147460 | tf_op jit(solution)/shard_map/jit(_pad)/pad | solution.py:104
  6.1 0.0 collective-permute-done
  6.1 7.5 %concatenate.3 = bf16[1040,1024]{1,0:T(8,128)(2,1)S(1)} concatenate(bf16[13,1024]{1,0:T(8,128)(2,1)S(1)} %broadcast_in_dim.6, bf16[3,1024]{1,0:T(4,128)(2,1)S(1)} %collective-permute-done, bf16[1024,1024]{1,0:T(8,128)(2,1)} %param.6), dimensions={0} | concatenate | bytes 4259840 | tf_op jit(solution)/shard_map/concatenate | solution.py:93
  13.7 0.5 fusion.5
  14.2 0.0 copy-done
  14.2 11.8 %fusion.2.pq.pk.pv = bf16[24,1040,128]{2,1,0:T(8,128)(2,1)} fusion(bf16[1040,1024]{1,0:T(8,128)(2,1)S(1)} %concatenate.3, f32[1024]{0:T(1024)S(1)} %copy-done, f32[1040]{0:T(1024)S(1)} %add_rsqrt_fusion, bf16[1024,3072]{1,0:T(8,128)(2,1)} %param.8), kind=kOutput, calls=%fused_computation.3 | convolution fusion | flops 6550568960 | bytes 14819392 | tf_op jit(solution)/shard_map/td,dje->jte/dot_general | solution.py:101
  26.0 10.2 %shard_map.64 = (bf16[8,1024,128]{2,1,0:T(8,128)(2,1)}, bf16[8,1024,128]{2,1,0:T(8,128)(2,1)}, bf16[8,1024,128]{2,1,0:T(8,128)(2,1)}, f32[8,128,128]{2,1,0:T(8,128)}) custom-call(bf16[24,1040,128]{2,1,0:T(8,128)(2,1)} %fusion.2.pq.pk.pv, bf16[24,1040,128]{2,1,0:T(8,128)(2,1)} %fusion.2.pq.pk.pv, bf16[24,1040,128]{2,1,0:T(8,128)(2,1)} %fusion.2.pq.pk.pv, ...), custom_call_target="tpu_custom_call" | custom-call | flops 306184192 | bytes 12582912 | tf_op jit(solution)/shard_map/pallas_call | solution.py:110
  36.2 1.1 %convert_element_type.41 = bf16[8,128,128]{2,1,0:T(8,128)(2,1)S(1)} convert(f32[8,128,128]{2,1,0:T(8,128)} %get-tuple-element.12) | non-fusion elementwise | flops 131072 | bytes 786432 | tf_op jit(solution)/shard_map/convert_element_type | solution.py:139
  37.3 0.2 broadcast_in_dim.14
  37.5 19.5 %all_to_all.10 = bf16[4,8,128,128]{3,2,1,0:T(8,128)(2,1)S(1)} all-to-all(bf16[4,8,128,128]{3,2,1,0:T(8,128)(2,1)S(1)} %broadcast_in_dim.14), channel_id=1, replica_groups=mesh['trace'=8,'sy'=4,'sz'=4] {'sz'}, dimensions={0} | all-to-all | bytes 2097152 | tf_op jit(solution)/shard_map/all_to_all | solution.py:25
  57.0 0.2 reduce_sum.40
  57.2 1.2 %broadcast_in_dim.15 = bf16[4,8,128,128]{3,2,1,0:T(8,128)(2,1)} broadcast(bf16[8,128,128]{2,1,0:T(8,128)(2,1)S(1)} %reduce_sum.40), dimensions={1,2,3} | broadcast | bytes 1310720 | tf_op jit(solution)/shard_map/broadcast_in_dim | solution.py:25
  58.4 4.5 %all-to-all-start.1 = ((bf16[4,8,128,128]{3,2,1,0:T(8,128)(2,1)}), bf16[4,8,128,128]{3,2,1,0:T(8,128)(2,1)S(1)}, u32[]{:S(2)}, u32[]{:S(2)}) async-start(bf16[4,8,128,128]{3,2,1,0:T(8,128)(2,1)} %broadcast_in_dim.15), calls=%async_computation.1 | async-start | bytes 2097152 | tf_op jit(solution)/shard_map/all_to_all | solution.py:25
  62.9 10.2 %shard_map.65.local_ref = f32[8,1024,128]{2,1,0:T(8,128)} custom-call(bf16[8,1024,128]{2,1,0:T(8,128)(2,1)} %get-tuple-element.9.q_ref, bf16[8,1024,128]{2,1,0:T(8,128)(2,1)} %get-tuple-element.10.k_ref, bf16[8,1024,128]{2,1,0:T(8,128)(2,1)} %get-tuple-element.11.v_ref), custom_call_target="tpu_custom_call" | custom-call | flops 2952790016 | bytes 10485760 | tf_op jit(solution)/shard_map/pallas_call | solution.py:126
  73.1 0.3 multiply_reduce_fusion
  73.4 2.1 %all-to-all-done.1 = bf16[4,8,128,128]{3,2,1,0:T(8,128)(2,1)S(1)} async-done(((bf16[4,8,128,128]{3,2,1,0:T(8,128)(2,1)}), bf16[4,8,128,128]{3,2,1,0:T(8,128)(2,1)S(1)}, u32[]{:S(2)}, u32[]{:S(2)}) %all-to-all-start.1) | async-done | bytes 1048608 | tf_op jit(solution)/shard_map/all_to_all | solution.py:25
  75.5 0.3 multiply_reduce_fusion.1
  75.8 0.9 %add.18.prefix_ref = f32[8,128,128]{2,1,0:T(8,128)} add(f32[8,128,128]{2,1,0:T(8,128)S(1)} %multiply_reduce_fusion.1, f32[8,128,128]{2,1,0:T(8,128)S(1)} %multiply_reduce_fusion) | non-fusion elementwise | flops 131072 | bytes 1572864 | tf_op jit(solution)/shard_map/add | solution.py:141
  76.6 8.0 %shard_map.66 = bf16[1024,1024]{1,0:T(8,128)(2,1)} custom-call(bf16[8,1024,128]{2,1,0:T(8,128)(2,1)} %get-tuple-element.9.q_ref, f32[8,1024,128]{2,1,0:T(8,128)} %shard_map.65.local_ref, f32[8,128,128]{2,1,0:T(8,128)} %add.18.prefix_ref, f32[8,1,128]{2,1,0:T(1,128)} %bitcast.19, bf16[1024,1024]{1,0:T(8,128)(2,1)} %w_ref.1), custom_call_target="tpu_custom_call" | custom-call | flops 2684354560 | bytes 10485760 | tf_op jit(solution)/shard_map/pallas_call | solution.py:144
  (4 shorter events, 0.0 us)
Async XLA Ops:
  0.0 14.2 %copy-start = (f32[1024]{0:T(1024)S(1)}, f32[1024]{0:T(1024)}, u32[]{:S(2)}) copy-start(f32[1024]{0:T(1024)} %param.7) | copy-start | bytes 12292
  0.7 5.4 %collective-permute-start = (bf16[3,1024]{1,0:T(4,128)(2,1)S(1)}, bf16[3,1024]{1,0:T(4,128)(2,1)S(1)}, u32[]{:S(2)}, u32[]{:S(2)}) collective-permute-start(bf16[3,1024]{1,0:T(4,128)(2,1)S(1)} %slice.3), channel_id=1, source_target_pairs={{0,1},{1,2},{2,3},{3,4},{4,5},{5,6},{6,7},{7,8},{8,9},{9,10},{10,1... | collective-permute-start | bytes 18440 | tf_op jit(solution)/shard_map/ppermute | solution.py:90
  58.4 17.1 %all-to-all-start.1 = ((bf16[4,8,128,128]{3,2,1,0:T(8,128)(2,1)}), bf16[4,8,128,128]{3,2,1,0:T(8,128)(2,1)S(1)}, u32[]{:S(2)}, u32[]{:S(2)}) async-start(bf16[4,8,128,128]{3,2,1,0:T(8,128)(2,1)} %broadcast_in_dim.15), calls=%async_computation.1 | async-start | bytes 2097152 | tf_op jit(solution)/shard_map/all_to_all | solution.py:25

commit v12 on v9

--- a/solution.py
+++ b/solution.py
@@ -30,15 +30,15 @@
 def conv_kernel(pq, pk, pv, eq, ek, ev, tq, tk, tv, oq, ok, ov, state_ref, buf):
     rows = pq.shape[0]
     for proj, early, taps, out in ((pq, eq, tq, oq), (pk, ek, tk, ok), (pv, ev, tv, ov)):
-        buf[0:PAD, :] = early[...].astype(jnp.float32)
+        buf[PAD - (KW - 1) : PAD, :] = early[...].astype(jnp.float32)
         buf[PAD:, :] = proj[...].astype(jnp.float32)
         summed = jnp.zeros((rows, DH), jnp.float32)
         for offset in range(KW):
             summed = summed + taps[offset : offset + 1, :] * buf[pl.ds(PAD - offset, rows), :]
-        out[...] = (summed * jax.nn.sigmoid(summed)).astype(out.dtype)
+        out[...] = (summed * (0.5 + 0.5 * jnp.tanh(0.5 * summed))).astype(out.dtype)
     state_ref[...] = lax.dot_general(
         ok[...], ov[...], (((0,), (0,)), ((), ())), preferred_element_type=jnp.float32
-    )
+    ).astype(state_ref.dtype)
 
 
 def local_kernel(q_ref, k_ref, v_ref, out_ref):
@@ -99,20 +99,17 @@
     earlier_rows = lax.ppermute(
         projected[:, rows - (KW - 1) :, :], seq_axes, [(i, i + 1) for i in range(count - 1)]
     )
-    earlier_rows = jnp.pad(earlier_rows, ((0, 0), (PAD - (KW - 1), 0), (0, 0)))
-    taps = jnp.pad(
-        conv_weight.reshape(KW, slabs, DH).transpose(1, 0, 2), ((0, 0), (0, PAD - KW), (0, 0))
-    )
+    taps = conv_weight.reshape(KW, slabs, DH).transpose(1, 0, 2)
 
     mixed_shape = jax.ShapeDtypeStruct((H, rows, DH), jnp.bfloat16)
     query, key, value, state = pl.pallas_call(
         conv_kernel,
         grid=(H,),
         in_specs=[slab(0, rows, DH), slab(H, rows, DH), slab(2 * H, rows, DH)]
-        + [slab(0, PAD, DH), slab(H, PAD, DH), slab(2 * H, PAD, DH)]
-        + [slab(0, PAD, DH), slab(H, PAD, DH), slab(2 * H, PAD, DH)],
+        + [slab(0, KW - 1, DH), slab(H, KW - 1, DH), slab(2 * H, KW - 1, DH)]
+        + [slab(0, KW, DH), slab(H, KW, DH), slab(2 * H, KW, DH)],
         out_specs=[slab(0, rows, DH)] * 3 + [slab(0, DH, DH)],
-        out_shape=[mixed_shape] * 3 + [jax.ShapeDtypeStruct((H, DH, DH), jnp.float32)],
+        out_shape=[mixed_shape] * 3 + [jax.ShapeDtypeStruct((H, DH, DH), jnp.bfloat16)],
         scratch_shapes=[pltpu.VMEM((rows + PAD, DH), jnp.float32)],
         cost_estimate=pl.CostEstimate(
             flops=H * (3 * rows * DH * 12 + 2 * rows * DH * DH),
@@ -135,7 +132,7 @@
         ),
     )(query, key, value)
 
-    zbefore, row_total = gather_earlier(state.astype(jnp.bfloat16), "sz")
+    zbefore, row_total = gather_earlier(state, "sz")
     ybefore, _ = gather_earlier(row_total.astype(jnp.bfloat16), "sy")
     prefix = ybefore + zbefore
 

time: 79.9 us -> 80.4 us (level)
  other arithmetic: 4.77 us -> 3.69 us
    pad x2 -> x0, local copies, waits for them, and re-layouts: 1.28 us -> none  [the longest x1 0.64 us: local(): jnp.pad(conv_weight.reshape(KW, slabs, DH).transpose(1, 0, 2), ((0, 0), (...]
    convert_element_type x1 -> x0, other arithmetic: 1.08 us -> none  [local(): zbefore, row_total = gather_earlier(state.astype(jnp.bfloat16), 'sz')]
    broadcast_in_dim x2, local copies, waits for them, and re-layouts: 1.45 us -> 2.4 us  [gather_earlier(): jnp.broadcast_to(x, (count,) + x.shape)]
  transfers between devices with their start and end apart: 2 -> 2, of which waited for: 2 -> 2; matrix products, arithmetic and copies ran while one was open for 1% -> 0% of each run, Pallas kernels for 13% -> 13%
where the time goes in v12:
time: 80.4 us; the launch traced here: 79.6 us
  Pallas kernels  29.4 us (37%)
  blocking collectives  19.4 us (24%)
  matrix products  9.56 us (12%)
  starting transfers between devices  8.38 us (10%)
  local copies, waits for them, and re-layouts  5.67 us (7%)
  other arithmetic  3.69 us (5%)
  waiting for transfers between devices  3.45 us (4%)
    all_to_all x1, blocking collectives, gather_earlier(): lax.all_to_all(jnp.broadcast_to(x, (count,) + x.shape), axis, 0, 0)  19.4 us
    pallas_call x1, Pallas kernels, local(): pl.pallas_call(conv_kernel, grid=(H,), in_specs=[slab(0, rows, DH), slab(...  11.2 us
    pallas_call x1, Pallas kernels, local(): pl.pallas_call(local_kernel, grid=(H,), in_specs=[slab(0, rows, DH)] * 3,...  10.2 us
    dot_general x1, matrix products, local(): jnp.einsum('td,dje->jte', normed, w_qkv.reshape(width, slabs, DH), prefer...  9.56 us
    pallas_call x1, Pallas kernels, local(): pl.pallas_call(out_kernel, grid=(rows // tile,), in_specs=[pl.BlockSpec((...  7.95 us
    all_to_all x1, starting transfers between devices, gather_earlier(): lax.all_to_all(jnp.broadcast_to(x, (count,) + x.shape), axis, 0, 0)  4.47 us
    ppermute x1, starting transfers between devices, local(): lax.ppermute(projected[:, rows - (KW - 1):, :], seq_axes, [(i, i + 1) for...  3.91 us
    unnamed x4, local copies, waits for them, and re-layouts  3.25 us
  transfers between devices with their start and end apart: 2, of which 2 were waited for; matrix products, arithmetic and copies ran while one was open for 0% of the time, Pallas kernels for 13%

profile of v12, /device:TPU:0, one launch (start us, length us, event | category | flops | bytes accessed | tf_op | source)
XLA Modules:
  0.0 79.6 jit_solution(2351637286228612684)
XLA Ops:
  0.0 2.1 %fusion.3 = f32[1024]{0:T(1024)S(1)} fusion(bf16[1024,1024]{1,0:T(8,128)(2,1)} %param.6), kind=kLoop, calls=%fused_computation.6 | loop fusion | flops 3144704 | bytes 2101248 | tf_op jit(solution)/shard_map/reduce_sum | solution.py:89
  2.1 9.6 %convert_bitcast_fusion.pq.pk.pv = bf16[24,1024,128]{2,1,0:T(8,128)(2,1)S(1)} fusion(bf16[1024,1024]{1,0:T(8,128)(2,1)} %param.6, f32[1024]{0:T(1024)} %param.7, f32[1024]{0:T(1024)S(1)} %add_rsqrt_fusion, bf16[1024,3072]{1,0:T(8,128)(2,1)} %param.8), kind=kOutput, calls=%fused_computation.3 | convolution fusion | flops 6449790976 | bytes 14688256 | tf_op jit(solution)/shard_map/td,dje->jte/dot_general | solution.py:93
  11.7 0.0 copy-start
  11.7 2.7 %copy-done = bf16[24,1024,128]{2,1,0:T(8,128)(2,1)} copy-done((bf16[24,1024,128]{2,1,0:T(8,128)(2,1)}, bf16[24,1024,128]{2,1,0:T(8,128)(2,1)S(1)}, u32[]{:S(2)}) %copy-start) | copy-done | bytes 6291480
  14.3 3.9 %collective-permute-start = (bf16[24,3,128]{2,1,0:T(4,128)(2,1)S(1)}, bf16[24,3,128]{2,1,0:T(4,128)(2,1)S(1)}, u32[]{:S(2)}, u32[]{:S(2)}) collective-permute-start(bf16[24,3,128]{2,1,0:T(4,128)(2,1)S(1)} %slice.4), channel_id=1, source_target_pairs={{0,1},{1,2},{2,3},{3,4},{4,5},{5,6},{6,7},{7,8},{8,9},{9,10},{10,1... | collective-permute-start | bytes 55304 | tf_op jit(solution)/shard_map/ppermute | solution.py:99
  18.3 1.5 %collective-permute-done.eq.ek.ev = bf16[24,3,128]{2,1,0:T(4,128)(2,1)S(1)} collective-permute-done((bf16[24,3,128]{2,1,0:T(4,128)(2,1)S(1)}, bf16[24,3,128]{2,1,0:T(4,128)(2,1)S(1)}, u32[]{:S(2)}, u32[]{:S(2)}) %collective-permute-start) | collective-permute-done | bytes 18464 | tf_op jit(solution)/shard_map/ppermute | solution.py:99
  19.8 0.0 copy-start.1
  19.8 0.6 copy-done.1
  20.4 11.2 %shard_map.64 = (bf16[8,1024,128]{2,1,0:T(8,128)(2,1)}, bf16[8,1024,128]{2,1,0:T(8,128)(2,1)}, bf16[8,1024,128]{2,1,0:T(8,128)(2,1)}, bf16[8,128,128]{2,1,0:T(8,128)(2,1)}) custom-call(bf16[24,1024,128]{2,1,0:T(8,128)(2,1)} %copy-done, bf16[24,1024,128]{2,1,0:T(8,128)(2,1)} %copy-done, bf16[24,1024,128]{2,1,0:T(8,128)(2,1)} %copy-done, ...), custom_call_target="tpu_custom_call" | custom-call | flops 306184192 | bytes 12582912 | tf_op jit(solution)/shard_map/pallas_call | solution.py:105
  31.6 1.2 %broadcast_in_dim.4 = bf16[4,8,128,128]{3,2,1,0:T(8,128)(2,1)S(1)} broadcast(bf16[8,128,128]{2,1,0:T(8,128)(2,1)} %get-tuple-element.12), dimensions={1,2,3} | broadcast | bytes 1310720 | tf_op jit(solution)/shard_map/broadcast_in_dim | solution.py:24
  32.7 19.4 %all_to_all.10 = bf16[4,8,128,128]{3,2,1,0:T(8,128)(2,1)S(1)} all-to-all(bf16[4,8,128,128]{3,2,1,0:T(8,128)(2,1)S(1)} %broadcast_in_dim.4), channel_id=1, replica_groups=mesh['trace'=8,'sy'=4,'sz'=4] {'sz'}, dimensions={0} | all-to-all | bytes 2097152 | tf_op jit(solution)/shard_map/all_to_all | solution.py:24
  52.2 0.2 reduce_sum.40
  52.4 1.2 %broadcast_in_dim.5 = bf16[4,8,128,128]{3,2,1,0:T(8,128)(2,1)} broadcast(bf16[8,128,128]{2,1,0:T(8,128)(2,1)S(1)} %reduce_sum.40), dimensions={1,2,3} | broadcast | bytes 1310720 | tf_op jit(solution)/shard_map/broadcast_in_dim | solution.py:24
  53.6 4.5 %all-to-all-start.1 = ((bf16[4,8,128,128]{3,2,1,0:T(8,128)(2,1)}), bf16[4,8,128,128]{3,2,1,0:T(8,128)(2,1)S(1)}, u32[]{:S(2)}, u32[]{:S(2)}) async-start(bf16[4,8,128,128]{3,2,1,0:T(8,128)(2,1)} %broadcast_in_dim.5), calls=%async_computation.1 | async-start | bytes 2097152 | tf_op jit(solution)/shard_map/all_to_all | solution.py:24
  58.1 10.2 %shard_map.65.local_ref = f32[8,1024,128]{2,1,0:T(8,128)} custom-call(bf16[8,1024,128]{2,1,0:T(8,128)(2,1)} %get-tuple-element.9.q_ref, bf16[8,1024,128]{2,1,0:T(8,128)(2,1)} %get-tuple-element.10.k_ref, bf16[8,1024,128]{2,1,0:T(8,128)(2,1)} %get-tuple-element.11.v_ref), custom_call_target="tpu_custom_call" | custom-call | flops 2952790016 | bytes 10485760 | tf_op jit(solution)/shard_map/pallas_call | solution.py:122
  68.3 0.3 multiply_reduce_fusion
  68.6 1.9 %all-to-all-done.1 = bf16[4,8,128,128]{3,2,1,0:T(8,128)(2,1)S(1)} async-done(((bf16[4,8,128,128]{3,2,1,0:T(8,128)(2,1)}), bf16[4,8,128,128]{3,2,1,0:T(8,128)(2,1)S(1)}, u32[]{:S(2)}, u32[]{:S(2)}) %all-to-all-start.1) | async-done | bytes 1048608 | tf_op jit(solution)/shard_map/all_to_all | solution.py:24
  70.5 0.3 multiply_reduce_fusion.1
  70.8 0.9 %add.16.prefix_ref = f32[8,128,128]{2,1,0:T(8,128)} add(f32[8,128,128]{2,1,0:T(8,128)S(1)} %multiply_reduce_fusion.1, f32[8,128,128]{2,1,0:T(8,128)S(1)} %multiply_reduce_fusion) | non-fusion elementwise | flops 131072 | bytes 1572864 | tf_op jit(solution)/shard_map/add | solution.py:137
  71.7 8.0 %shard_map.66 = bf16[1024,1024]{1,0:T(8,128)(2,1)} custom-call(bf16[8,1024,128]{2,1,0:T(8,128)(2,1)} %get-tuple-element.9.q_ref, f32[8,1024,128]{2,1,0:T(8,128)} %shard_map.65.local_ref, f32[8,128,128]{2,1,0:T(8,128)} %add.16.prefix_ref, f32[8,1,128]{2,1,0:T(1,128)} %bitcast.21, bf16[1024,1024]{1,0:T(8,128)(2,1)} %w_ref.1), custom_call_target="tpu_custom_call" | custom-call | flops 2684354560 | bytes 10485760 | tf_op jit(solution)/shard_map/pallas_call | solution.py:140
  (4 shorter events, 0.0 us)
Async XLA Ops:
  11.7 2.7 %copy-start = (bf16[24,1024,128]{2,1,0:T(8,128)(2,1)}, bf16[24,1024,128]{2,1,0:T(8,128)(2,1)S(1)}, u32[]{:S(2)}) copy-start(bf16[24,1024,128]{2,1,0:T(8,128)(2,1)S(1)} %convert_bitcast_fusion.pq.pk.pv) | copy-start | bytes 18874372
  14.3 5.4 %collective-permute-start = (bf16[24,3,128]{2,1,0:T(4,128)(2,1)S(1)}, bf16[24,3,128]{2,1,0:T(4,128)(2,1)S(1)}, u32[]{:S(2)}, u32[]{:S(2)}) collective-permute-start(bf16[24,3,128]{2,1,0:T(4,128)(2,1)S(1)} %slice.4), channel_id=1, source_target_pairs={{0,1},{1,2},{2,3},{3,4},{4,5},{5,6},{6,7},{7,8},{8,9},{9,10},{10,1... | collective-permute-start | bytes 55304 | tf_op jit(solution)/shard_map/ppermute | solution.py:99
  19.8 0.6 copy-start.1
  53.6 16.9 %all-to-all-start.1 = ((bf16[4,8,128,128]{3,2,1,0:T(8,128)(2,1)}), bf16[4,8,128,128]{3,2,1,0:T(8,128)(2,1)S(1)}, u32[]{:S(2)}, u32[]{:S(2)}) async-start(bf16[4,8,128,128]{3,2,1,0:T(8,128)(2,1)} %broadcast_in_dim.5), calls=%async_computation.1 | async-start | bytes 2097152 | tf_op jit(solution)/shard_map/all_to_all | solution.py:24

commit v13 on v10

--- a/solution.py
+++ b/solution.py
@@ -27,14 +27,21 @@
     for z in range(1, count):
         before.append(before[-1] + mine[z - 1])
     row_total = before[-1] + mine[count - 1]
-    totals = lax.all_to_all(
-        jnp.broadcast_to(row_total.astype(jnp.bfloat16), (rows_count,) + row_total.shape), "sy", 0, 0
-    ).astype(jnp.float32)
-    earlier = (lax.iota(jnp.int32, rows_count) < lax.axis_index("sy")).astype(jnp.float32)
-    rows_before = jnp.sum(totals * earlier[:, None, None, None], 0)
-    finished = jnp.stack(before) + rows_before
-    prefix = lax.all_to_all(finished.astype(jnp.bfloat16), "sz", 0, 0)
-    return prefix.reshape(state.shape).astype(jnp.float32)
+    row = lax.axis_index("sy")
+    later_row = (row < lax.iota(jnp.int32, rows_count)).astype(jnp.float32)
+    same_row = (row == lax.iota(jnp.int32, rows_count)).astype(jnp.float32)
+    messages = (
+        later_row[:, None, None, None, None] * row_total[None, None]
+        + same_row[:, None, None, None, None] * jnp.stack(before)[None]
+    )
+    received = lax.all_to_all(
+        messages.astype(jnp.bfloat16).reshape((rows_count * count,) + row_total.shape),
+        ("sy", "sz"),
+        0,
+        0,
+    )
+    received = received.reshape((rows_count, count) + row_total.shape).astype(jnp.float32)
+    return jnp.sum(received, 0).reshape(state.shape)
 
 
 def conv_kernel(pq, pk, pv, eq, ek, ev, tq, tk, tv, oq, ok, ov, state_ref, buf):

time: 80.4 us -> 77 us (0.958)
  blocking collectives: 12.2 us -> 0 us
  waiting for transfers between devices: 7.48 us -> 12.3 us
  starting transfers between devices: 11.8 us -> 15 us
  other arithmetic: 5.03 us -> 6.4 us
    all_to_all x1 -> x0, blocking collectives: 12.2 us -> none  [earlier_states(): mine = lax.all_to_all(quarters, 'sz', 0, 0).astype(jnp.float32)]
    all_to_all x2, waiting for transfers between devices: 6.65 us -> 11.5 us  [the longest x1 6.51 us: earlier_states(): mine = lax.all_to_all(quarters, 'sz', 0, 0).astype(jnp.float32)]
    all_to_all x2, starting transfers between devices: 7.87 us -> 11.1 us  [the longest x1 5.69 us: earlier_states(): mine = lax.all_to_all(quarters, 'sz', 0, 0).astype(jnp.float32)]
    reduce_sum x1, other arithmetic: 0.12 us -> 0.98 us  [earlier_states(): return jnp.sum(received, 0).reshape(state.shape)]
    convert_element_type x4 -> x3, other arithmetic: 1.73 us -> 1.34 us  [the longest x1 1.34 us: earlier_states(): messages.astype(jnp.bfloat16)]
  transfers between devices with their start and end apart: 3 -> 3, of which waited for: 2 -> 3; matrix products, arithmetic and copies ran while one was open for 1% -> 1% of each run, Pallas kernels for 13% -> 13%
where the time goes in v13:
time: 77 us; the launch traced here: 76.2 us
  Pallas kernels  28.7 us (37%)
  starting transfers between devices  15 us (19%)
  waiting for transfers between devices  12.3 us (16%)
  matrix products  9.57 us (12%)
  other arithmetic  6.4 us (8%)
  local copies, waits for them, and re-layouts  4.13 us (5%)
    pallas_call x1, Pallas kernels, local(): pl.pallas_call(conv_kernel, grid=(H,), in_specs=[slab(0, rows, DH), slab(...  10.6 us
    pallas_call x1, Pallas kernels, local(): pl.pallas_call(local_kernel, grid=(H,), in_specs=[slab(0, rows, DH)] * 3,...  10.2 us
    dot_general x1, matrix products, local(): jnp.einsum('td,dje->jte', normed, w_qkv.reshape(width, slabs, DH), prefer...  9.57 us
    pallas_call x1, Pallas kernels, local(): pl.pallas_call(out_kernel, grid=(rows // tile,), in_specs=[pl.BlockSpec((...  7.97 us
    all_to_all x1, waiting for transfers between devices, earlier_states(): mine = lax.all_to_all(quarters, 'sz', 0, 0).astype(jnp.float32)  6.51 us
    all_to_all x1, starting transfers between devices, earlier_states(): mine = lax.all_to_all(quarters, 'sz', 0, 0).astype(jnp.float32)  5.69 us
    all_to_all x1, starting transfers between devices, earlier_states(): lax.all_to_all(messages.astype(jnp.bfloat16).reshape((rows_count * count,...  5.36 us
    all_to_all x1, waiting for transfers between devices, earlier_states(): lax.all_to_all(messages.astype(jnp.bfloat16).reshape((rows_count * count,...  4.97 us
  transfers between devices with their start and end apart: 3, of which 3 were waited for; matrix products, arithmetic and copies ran while one was open for 1% of the time, Pallas kernels for 13%

profile of v13, /device:TPU:0, one launch (start us, length us, event | category | flops | bytes accessed | tf_op | source)
XLA Modules:
  0.0 76.2 jit_solution(16247058708412007266)
XLA Ops:
  0.0 2.1 %fusion.3 = f32[1024]{0:T(1024)S(1)} fusion(bf16[1024,1024]{1,0:T(8,128)(2,1)} %param.6), kind=kLoop, calls=%fused_computation.6 | loop fusion | flops 3144704 | bytes 2101248 | tf_op jit(solution)/shard_map/reduce_sum | solution.py:106
  2.1 0.0 copy-start.1
  2.1 9.6 %convert_bitcast_fusion.pq.pk.pv = bf16[24,1024,128]{2,1,0:T(8,128)(2,1)S(1)} fusion(bf16[1024,1024]{1,0:T(8,128)(2,1)} %param.6, f32[1024]{0:T(1024)} %param.7, f32[1024]{0:T(1024)S(1)} %add_rsqrt_fusion, bf16[1024,3072]{1,0:T(8,128)(2,1)} %param.8), kind=kOutput, calls=%fused_computation.3 | convolution fusion | flops 6449790976 | bytes 14688256 | tf_op jit(solution)/shard_map/td,dje->jte/dot_general | solution.py:110
  11.7 0.0 copy-start
  11.7 2.6 %copy-done = bf16[24,1024,128]{2,1,0:T(8,128)(2,1)} copy-done((bf16[24,1024,128]{2,1,0:T(8,128)(2,1)}, bf16[24,1024,128]{2,1,0:T(8,128)(2,1)S(1)}, u32[]{:S(2)}) %copy-start) | copy-done | bytes 6291480
  14.3 3.9 %collective-permute-start = (bf16[24,3,128]{2,1,0:T(4,128)(2,1)S(1)}, bf16[24,3,128]{2,1,0:T(4,128)(2,1)S(1)}, u32[]{:S(2)}, u32[]{:S(2)}) collective-permute-start(bf16[24,3,128]{2,1,0:T(4,128)(2,1)S(1)} %slice.20), channel_id=1, source_target_pairs={{0,1},{1,2},{2,3},{3,4},{4,5},{5,6},{6,7},{7,8},{8,9},{9,10},{10,1... | collective-permute-start | bytes 55304 | tf_op jit(solution)/shard_map/ppermute | solution.py:116
  18.3 0.0 copy-done.1
  18.3 0.7 pad.9.tq.tk.tv
  18.9 0.8 %collective-permute-done = bf16[24,3,128]{2,1,0:T(4,128)(2,1)S(1)} collective-permute-done((bf16[24,3,128]{2,1,0:T(4,128)(2,1)S(1)}, bf16[24,3,128]{2,1,0:T(4,128)(2,1)S(1)}, u32[]{:S(2)}, u32[]{:S(2)}) %collective-permute-start) | collective-permute-done | bytes 18464 | tf_op jit(solution)/shard_map/ppermute | solution.py:116
  19.8 0.6 pad.8.eq.ek.ev
  20.4 10.6 %shard_map.64 = (bf16[8,1024,128]{2,1,0:T(8,128)(2,1)}, bf16[8,1024,128]{2,1,0:T(8,128)(2,1)}, bf16[8,1024,128]{2,1,0:T(8,128)(2,1)}, f32[8,128,128]{2,1,0:T(8,128)}) custom-call(bf16[24,1024,128]{2,1,0:T(8,128)(2,1)} %copy-done, bf16[24,1024,128]{2,1,0:T(8,128)(2,1)} %copy-done, bf16[24,1024,128]{2,1,0:T(8,128)(2,1)} %copy-done, ...), custom_call_target="tpu_custom_call" | custom-call | flops 306184192 | bytes 12582912 | tf_op jit(solution)/shard_map/pallas_call | solution.py:125
  31.0 1.8 %convert_element_type.50 = bf16[8,128,128]{2,1,0:T(8,128)(2,1)} convert(f32[8,128,128]{2,1,0:T(8,128)} %get-tuple-element.12) | non-fusion elementwise | flops 131072 | bytes 786432 | tf_op jit(solution)/shard_map/convert_element_type | solution.py:24
  32.8 5.7 %all-to-all-start = ((bf16[4,2,128,128]{3,2,1,0:T(8,128)(2,1)}), bf16[4,2,128,128]{3,2,1,0:T(8,128)(2,1)S(1)}, u32[]{:S(2)}, u32[]{:S(2)}) async-start(bf16[4,2,128,128]{3,2,1,0:T(8,128)(2,1)} %bitcast.4), calls=%async_computation | async-start | bytes 524288 | tf_op jit(solution)/shard_map/all_to_all | solution.py:25
  38.4 0.1 mul.65
  38.5 0.1 mul.66
  38.6 6.5 %all-to-all-done = bf16[4,2,128,128]{3,2,1,0:T(8,128)(2,1)S(1)} async-done(((bf16[4,2,128,128]{3,2,1,0:T(8,128)(2,1)}), bf16[4,2,128,128]{3,2,1,0:T(8,128)(2,1)S(1)}, u32[]{:S(2)}, u32[]{:S(2)}) %all-to-all-start) | async-done | bytes 262176 | tf_op jit(solution)/shard_map/all_to_all | solution.py:25
  45.2 0.2 pad_maximum_fusion
  45.4 1.3 %fusion.11 = bf16[16,2,128,128]{3,2,1,0:T(8,128)(2,1)} fusion(f32[4,2,128,128]{3,2,1,0:T(8,128)S(1)} %get-tuple-element.16, f32[16]{0:T(128)S(1)} %mul.66, f32[4,2,128,128]{3,2,1,0:T(8,128)S(1)} %get-tuple-element.17), kind=kLoop, calls=%fused_computation.13 | loop fusion | flops 1572864 | bytes 2097216 | tf_op jit(solution)/shard_map/convert_element_type | solution.py:38
  46.7 5.4 %all-to-all-start.1 = ((bf16[16,2,128,128]{3,2,1,0:T(8,128)(2,1)}), bf16[16,2,128,128]{3,2,1,0:T(8,128)(2,1)S(1)}, u32[]{:S(2)}, u32[]{:S(2)}) async-start(bf16[16,2,128,128]{3,2,1,0:T(8,128)(2,1)} %fusion.11), calls=%async_computation.1 | async-start | bytes 2097152 | tf_op jit(solution)/shard_map/all_to_all | solution.py:37
  52.1 10.2 %shard_map.65.local_ref = f32[8,1024,128]{2,1,0:T(8,128)} custom-call(bf16[8,1024,128]{2,1,0:T(8,128)(2,1)} %get-tuple-element.9.q_ref, bf16[8,1024,128]{2,1,0:T(8,128)(2,1)} %get-tuple-element.10.k_ref, bf16[8,1024,128]{2,1,0:T(8,128)(2,1)} %get-tuple-element.11.v_ref), custom_call_target="tpu_custom_call" | custom-call | flops 2952790016 | bytes 10485760 | tf_op jit(solution)/shard_map/pallas_call | solution.py:142
  62.3 5.0 %all-to-all-done.1 = bf16[16,2,128,128]{3,2,1,0:T(8,128)(2,1)S(1)} async-done(((bf16[16,2,128,128]{3,2,1,0:T(8,128)(2,1)}), bf16[16,2,128,128]{3,2,1,0:T(8,128)(2,1)S(1)}, u32[]{:S(2)}, u32[]{:S(2)}) %all-to-all-start.1) | async-done | bytes 1048608 | tf_op jit(solution)/shard_map/all_to_all | solution.py:37
  67.3 1.0 %convert_reduce_fusion = f32[4,2,128,128]{3,2,1,0:T(8,128)} fusion(bf16[4,4,2,128,128]{4,3,2,1,0:T(8,128)(2,1)S(1)} %bitcast.33), kind=kLoop, calls=%fused_computation.10 | loop fusion | flops 917504 | bytes 1572864 | tf_op jit(solution)/shard_map/reduce_sum | solution.py:44
  68.2 8.0 %shard_map.66 = bf16[1024,1024]{1,0:T(8,128)(2,1)} custom-call(bf16[8,1024,128]{2,1,0:T(8,128)(2,1)} %get-tuple-element.9.q_ref, f32[8,1024,128]{2,1,0:T(8,128)} %shard_map.65.local_ref, f32[8,128,128]{2,1,0:T(8,128)} %bitcast.34, f32[8,1,128]{2,1,0:T(1,128)} %bitcast.36, bf16[1024,1024]{1,0:T(8,128)(2,1)} %w_ref.1), custom_call_target="tpu_custom_call" | custom-call | flops 2684354560 | bytes 10485760 | tf_op jit(solution)/shard_map/pallas_call | solution.py:158
  (8 shorter events, 0.1 us)
Async XLA Ops:
  2.1 16.2 %copy-start.1 = (f32[4,3072]{1,0:T(4,128)S(1)}, f32[4,3072]{1,0:T(4,128)}, u32[]{:S(2)}) copy-start(f32[4,3072]{1,0:T(4,128)} %param.9) | copy-start | bytes 147460
  11.7 2.7 %copy-start = (bf16[24,1024,128]{2,1,0:T(8,128)(2,1)}, bf16[24,1024,128]{2,1,0:T(8,128)(2,1)S(1)}, u32[]{:S(2)}) copy-start(bf16[24,1024,128]{2,1,0:T(8,128)(2,1)S(1)} %convert_bitcast_fusion.pq.pk.pv) | copy-start | bytes 18874372
  14.3 5.4 %collective-permute-start = (bf16[24,3,128]{2,1,0:T(4,128)(2,1)S(1)}, bf16[24,3,128]{2,1,0:T(4,128)(2,1)S(1)}, u32[]{:S(2)}, u32[]{:S(2)}) collective-permute-start(bf16[24,3,128]{2,1,0:T(4,128)(2,1)S(1)} %slice.20), channel_id=1, source_target_pairs={{0,1},{1,2},{2,3},{3,4},{4,5},{5,6},{6,7},{7,8},{8,9},{9,10},{10,1... | collective-permute-start | bytes 55304 | tf_op jit(solution)/shard_map/ppermute | solution.py:116
  32.8 12.4 %all-to-all-start = ((bf16[4,2,128,128]{3,2,1,0:T(8,128)(2,1)}), bf16[4,2,128,128]{3,2,1,0:T(8,128)(2,1)S(1)}, u32[]{:S(2)}, u32[]{:S(2)}) async-start(bf16[4,2,128,128]{3,2,1,0:T(8,128)(2,1)} %bitcast.4), calls=%async_computation | async-start | bytes 524288 | tf_op jit(solution)/shard_map/all_to_all | solution.py:25
  46.7 20.5 %all-to-all-start.1 = ((bf16[16,2,128,128]{3,2,1,0:T(8,128)(2,1)}), bf16[16,2,128,128]{3,2,1,0:T(8,128)(2,1)S(1)}, u32[]{:S(2)}, u32[]{:S(2)}) async-start(bf16[16,2,128,128]{3,2,1,0:T(8,128)(2,1)} %fusion.11), calls=%async_computation.1 | async-start | bytes 2097152 | tf_op jit(solution)/shard_map/all_to_all | solution.py:37

commit v14 on v13

--- a/solution.py
+++ b/solution.py
@@ -1,3 +1,5 @@
+import functools
+
 import jax
 import jax.numpy as jnp
 from jax import lax
@@ -18,7 +20,7 @@
     return hi.astype(jnp.bfloat16), (x - hi).astype(jnp.bfloat16)
 
 
-def earlier_states(state):
+def earlier_states(state, before_second=None):
     count = lax.axis_size("sz")
     rows_count = lax.axis_size("sy")
     quarters = state.astype(jnp.bfloat16).reshape((count, -1) + state.shape[1:])
@@ -34,28 +36,59 @@
         later_row[:, None, None, None, None] * row_total[None, None]
         + same_row[:, None, None, None, None] * jnp.stack(before)[None]
     )
+    messages = messages.astype(jnp.bfloat16)
+    if before_second is not None:
+        messages, before_second = lax.optimization_barrier((messages, before_second()))
     received = lax.all_to_all(
-        messages.astype(jnp.bfloat16).reshape((rows_count * count,) + row_total.shape),
+        messages.reshape((rows_count * count,) + row_total.shape),
         ("sy", "sz"),
         0,
         0,
     )
     received = received.reshape((rows_count, count) + row_total.shape).astype(jnp.float32)
-    return jnp.sum(received, 0).reshape(state.shape)
-
-
-def conv_kernel(pq, pk, pv, eq, ek, ev, tq, tk, tv, oq, ok, ov, state_ref, buf):
-    rows = pq.shape[0]
-    for proj, early, taps, out in ((pq, eq, tq, oq), (pk, ek, tk, ok), (pv, ev, tv, ov)):
+    return jnp.sum(received, 0).reshape(state.shape), before_second
+
+
+def conv_kernel(count, with_state, *refs):
+    projs, earlies, tapss = refs[:count], refs[count : 2 * count], refs[2 * count : 3 * count]
+    outs, buf = refs[3 * count : 4 * count], refs[-1]
+    rows = projs[0].shape[0]
+    for proj, early, taps, out in zip(projs, earlies, tapss, outs):
         buf[0:PAD, :] = early[...].astype(jnp.float32)
         buf[PAD:, :] = proj[...].astype(jnp.float32)
         summed = jnp.zeros((rows, DH), jnp.float32)
         for offset in range(KW):
             summed = summed + taps[offset : offset + 1, :] * buf[pl.ds(PAD - offset, rows), :]
         out[...] = (summed * jax.nn.sigmoid(summed)).astype(out.dtype)
-    state_ref[...] = lax.dot_general(
-        ok[...], ov[...], (((0,), (0,)), ((), ())), preferred_element_type=jnp.float32
-    )
+    if with_state:
+        refs[4 * count][...] = lax.dot_general(
+            outs[0][...], outs[1][...], (((0,), (0,)), ((), ())), preferred_element_type=jnp.float32
+        )
+
+
+def conv_call(projected, earlier, taps, shifts, base, with_state):
+    count = len(shifts)
+    rows = projected.shape[1]
+    mixed = jax.ShapeDtypeStruct((H, rows, DH), jnp.bfloat16)
+    out_specs = [slab(0, rows, DH)] * count
+    out_shape = [mixed] * count
+    if with_state:
+        out_specs.append(slab(0, DH, DH))
+        out_shape.append(jax.ShapeDtypeStruct((H, DH, DH), jnp.float32))
+    return pl.pallas_call(
+        functools.partial(conv_kernel, count, with_state),
+        grid=(H,),
+        in_specs=[slab(shift, rows, DH) for shift in shifts]
+        + [slab(base + shift, PAD, DH) for shift in shifts] * 2,
+        out_specs=out_specs,
+        out_shape=out_shape,
+        scratch_shapes=[pltpu.VMEM((rows + PAD, DH), jnp.float32)],
+        cost_estimate=pl.CostEstimate(
+            flops=H * count * rows * DH * (12 + 2 * DH),
+            transcendentals=H * count * rows * DH,
+            bytes_accessed=H * count * rows * DH * 4,
+        ),
+    )(*([projected] * count + [earlier] * count + [taps] * count))
 
 
 def local_kernel(q_ref, k_ref, v_ref, out_ref):
@@ -121,22 +154,10 @@
         conv_weight.reshape(KW, slabs, DH).transpose(1, 0, 2), ((0, 0), (0, PAD - KW), (0, 0))
     )
 
-    mixed_shape = jax.ShapeDtypeStruct((H, rows, DH), jnp.bfloat16)
-    query, key, value, state = pl.pallas_call(
-        conv_kernel,
-        grid=(H,),
-        in_specs=[slab(0, rows, DH), slab(H, rows, DH), slab(2 * H, rows, DH)]
-        + [slab(0, PAD, DH), slab(H, PAD, DH), slab(2 * H, PAD, DH)]
-        + [slab(0, PAD, DH), slab(H, PAD, DH), slab(2 * H, PAD, DH)],
-        out_specs=[slab(0, rows, DH)] * 3 + [slab(0, DH, DH)],
-        out_shape=[mixed_shape] * 3 + [jax.ShapeDtypeStruct((H, DH, DH), jnp.float32)],
-        scratch_shapes=[pltpu.VMEM((rows + PAD, DH), jnp.float32)],
-        cost_estimate=pl.CostEstimate(
-            flops=H * (3 * rows * DH * 12 + 2 * rows * DH * DH),
-            transcendentals=H * 3 * rows * DH,
-            bytes_accessed=H * 3 * rows * DH * 4,
-        ),
-    )(projected, projected, projected, earlier_rows, earlier_rows, earlier_rows, taps, taps, taps)
+    key, value, state = conv_call(projected, earlier_rows, taps, (H, 2 * H), 0, True)
+    prefix, (query,) = earlier_states(
+        state, lambda: conv_call(projected, earlier_rows, taps, (0,), 0, False)
+    )
 
     block = min(BLOCK, rows)
     local_part = pl.pallas_call(
@@ -151,8 +172,6 @@
             bytes_accessed=H * rows * DH * 10,
         ),
     )(query, key, value)
-
-    prefix = earlier_states(state)
 
     tile = min(256, rows)
     out = pl.pallas_call(

time: 77 us -> 78.4 us (1.018)
  waiting for transfers between devices: 12.3 us -> 6.51 us
  Pallas kernels: 28.7 us -> 33.6 us
  starting transfers between devices: 15 us -> 17.3 us
    all_to_all x1, waiting for transfers between devices: 6.51 us -> 0.01 us  [earlier_states(): mine = lax.all_to_all(quarters, 'sz', 0, 0).astype(jnp.float32)]
    pallas_call x1 -> x2, Pallas kernels: 10.6 us -> 15.5 us  [conv_call(): pl.pallas_call(functools.partial(conv_kernel, count, with_state), grid=(H...]
    all_to_all x1, starting transfers between devices: 5.36 us -> 7.72 us  [earlier_states(): lax.all_to_all(messages.reshape((rows_count * count,) + row_total.shape),...]
  transfers between devices with their start and end apart: 3 -> 3, of which waited for: 3 -> 2; matrix products, arithmetic and copies ran while one was open for 1% -> 1% of each run, Pallas kernels for 13% -> 22%
where the time goes in v14:
time: 78.4 us; the launch traced here: 77.5 us
  Pallas kernels  33.6 us (43%)
  starting transfers between devices  17.3 us (22%)
  matrix products  9.57 us (12%)
  waiting for transfers between devices  6.51 us (8%)
  other arithmetic  6.41 us (8%)
  local copies, waits for them, and re-layouts  3.97 us (5%)
    pallas_call x2, Pallas kernels, conv_call(): pl.pallas_call(functools.partial(conv_kernel, count, with_state), grid=(H...  15.5 us
    pallas_call x1, Pallas kernels, local(): pl.pallas_call(local_kernel, grid=(H,), in_specs=[slab(0, rows, DH)] * 3,...  10.2 us
    dot_general x1, matrix products, local(): jnp.einsum('td,dje->jte', normed, w_qkv.reshape(width, slabs, DH), prefer...  9.57 us
    pallas_call x1, Pallas kernels, local(): pl.pallas_call(out_kernel, grid=(rows // tile,), in_specs=[pl.BlockSpec((...  7.95 us
    all_to_all x1, starting transfers between devices, earlier_states(): lax.all_to_all(messages.reshape((rows_count * count,) + row_total.shape),...  7.72 us
    all_to_all x1, starting transfers between devices, earlier_states(): mine = lax.all_to_all(quarters, 'sz', 0, 0).astype(jnp.float32)  5.69 us
    all_to_all x1, waiting for transfers between devices, earlier_states(): lax.all_to_all(messages.reshape((rows_count * count,) + row_total.shape),...  5.67 us
    ppermute x1, starting transfers between devices, local(): lax.ppermute(projected[:, rows - (KW - 1):, :], seq_axes, [(i, i + 1) for...  3.9 us
  transfers between devices with their start and end apart: 3, of which 2 were waited for; matrix products, arithmetic and copies ran while one was open for 1% of the time, Pallas kernels for 22%

profile of v14, /device:TPU:0, one launch (start us, length us, event | category | flops | bytes accessed | tf_op | source)
XLA Modules:
  0.0 77.5 jit_solution(7403289262843456888)
XLA Ops:
  0.0 2.1 %fusion.3 = f32[1024]{0:T(1024)S(1)} fusion(bf16[1024,1024]{1,0:T(8,128)(2,1)} %param.6), kind=kLoop, calls=%fused_computation.6 | loop fusion | flops 3144704 | bytes 2101248 | tf_op jit(solution)/shard_map/reduce_sum | solution.py:139
  2.1 0.0 copy-start.1
  2.1 9.6 %convert_bitcast_fusion.refs_0_.refs_1_ = bf16[24,1024,128]{2,1,0:T(8,128)(2,1)S(1)} fusion(bf16[1024,1024]{1,0:T(8,128)(2,1)} %param.6, f32[1024]{0:T(1024)} %param.7, f32[1024]{0:T(1024)S(1)} %add_rsqrt_fusion, bf16[1024,3072]{1,0:T(8,128)(2,1)} %param.8), kind=kOutput, calls=%fused_computation.3 | convolution fusion | flops 6449790976 | bytes 14688256 | tf_op jit(solution)/shard_map/td,dje->jte/dot_general | solution.py:143
  11.7 0.0 copy-start
  11.7 2.6 %copy-done = bf16[24,1024,128]{2,1,0:T(8,128)(2,1)} copy-done((bf16[24,1024,128]{2,1,0:T(8,128)(2,1)}, bf16[24,1024,128]{2,1,0:T(8,128)(2,1)S(1)}, u32[]{:S(2)}) %copy-start) | copy-done | bytes 6291480
  14.3 3.9 %collective-permute-start = (bf16[24,3,128]{2,1,0:T(4,128)(2,1)S(1)}, bf16[24,3,128]{2,1,0:T(4,128)(2,1)S(1)}, u32[]{:S(2)}, u32[]{:S(2)}) collective-permute-start(bf16[24,3,128]{2,1,0:T(4,128)(2,1)S(1)} %slice.20), channel_id=1, source_target_pairs={{0,1},{1,2},{2,3},{3,4},{4,5},{5,6},{6,7},{7,8},{8,9},{9,10},{10,1... | collective-permute-start | bytes 55304 | tf_op jit(solution)/shard_map/ppermute | solution.py:149
  18.3 0.0 copy-done.1
  18.3 0.6 pad.9.refs_4_.refs_5_.refs_2_
  18.9 0.8 %collective-permute-done = bf16[24,3,128]{2,1,0:T(4,128)(2,1)S(1)} collective-permute-done((bf16[24,3,128]{2,1,0:T(4,128)(2,1)S(1)}, bf16[24,3,128]{2,1,0:T(4,128)(2,1)S(1)}, u32[]{:S(2)}, u32[]{:S(2)}) %collective-permute-start) | collective-permute-done | bytes 18464 | tf_op jit(solution)/shard_map/ppermute | solution.py:149
  19.8 0.6 pad.8.refs_2_.refs_3_.refs_1_
  20.4 8.5 %shard_map.64 = (bf16[8,1024,128]{2,1,0:T(8,128)(2,1)}, bf16[8,1024,128]{2,1,0:T(8,128)(2,1)}, f32[8,128,128]{2,1,0:T(8,128)}) custom-call(bf16[24,1024,128]{2,1,0:T(8,128)(2,1)} %copy-done, bf16[24,1024,128]{2,1,0:T(8,128)(2,1)} %copy-done, bf16[24,8,128]{2,1,0:T(8,128)(2,1)} %pad.8.refs_2_.refs_3_.refs_1_, bf16[24,8,128]{2,1,0:T(8,128)(2,1)} %pad.8.refs_2_.refs_3_.refs_1_, ...), custom_call_target="tpu_custom_call" | custom-call | flops 562036736 | bytes 8388608 | tf_op jit(solution)/shard_map/pallas_call | solution.py:78
  29.0 1.8 %convert_element_type.49 = bf16[8,128,128]{2,1,0:T(8,128)(2,1)} convert(f32[8,128,128]{2,1,0:T(8,128)} %get-tuple-element.10) | non-fusion elementwise | flops 131072 | bytes 786432 | tf_op jit(solution)/shard_map/convert_element_type | solution.py:26
  30.7 5.7 %all-to-all-start = ((bf16[4,2,128,128]{3,2,1,0:T(8,128)(2,1)}), bf16[4,2,128,128]{3,2,1,0:T(8,128)(2,1)S(1)}, u32[]{:S(2)}, u32[]{:S(2)}) async-start(bf16[4,2,128,128]{3,2,1,0:T(8,128)(2,1)} %bitcast.4), calls=%async_computation | async-start | bytes 524288 | tf_op jit(solution)/shard_map/all_to_all | solution.py:27
  36.4 6.9 %shard_map.65.q_ref = bf16[8,1024,128]{2,1,0:T(8,128)(2,1)} custom-call(bf16[24,1024,128]{2,1,0:T(8,128)(2,1)} %copy-done, bf16[24,8,128]{2,1,0:T(8,128)(2,1)} %pad.8.refs_2_.refs_3_.refs_1_, f32[24,8,128]{2,1,0:T(8,128)} %pad.9.refs_4_.refs_5_.refs_2_), custom_call_target="tpu_custom_call" | custom-call | flops 281018368 | bytes 4194304 | tf_op jit(solution)/shard_map/pallas_call | solution.py:78
  43.4 0.0 all-to-all-done
  43.5 0.2 pad_maximum_fusion
  43.6 1.3 %add_convert_fusion = bf16[4,4,2,128,128]{4,3,2,1,0:T(8,128)(2,1)} fusion(f32[4,2,128,128]{3,2,1,0:T(8,128)S(1)} %get-tuple-element.18, f32[4]{0:T(128)S(1)} %compare_convert_fusion, f32[4,2,128,128]{3,2,1,0:T(8,128)S(1)} %get-tuple-element.19), kind=kLoop, calls=%fused_computation.11 | loop fusion | flops 1572864 | bytes 2097168 | tf_op jit(solution)/shard_map/convert_element_type | solution.py:39
  45.0 7.7 %all-to-all-start.1 = ((bf16[16,2,128,128]{3,2,1,0:T(8,128)(2,1)}), bf16[16,2,128,128]{3,2,1,0:T(8,128)(2,1)S(1)}, u32[]{:S(2)}, u32[]{:S(2)}) async-start(bf16[16,2,128,128]{3,2,1,0:T(8,128)(2,1)} %bitcast.6), calls=%async_computation.1 | async-start | bytes 2097152 | tf_op jit(solution)/shard_map/all_to_all | solution.py:42
  52.7 10.2 %shard_map.66.local_ref = f32[8,1024,128]{2,1,0:T(8,128)} custom-call(bf16[8,1024,128]{2,1,0:T(8,128)(2,1)} %shard_map.65.q_ref, bf16[8,1024,128]{2,1,0:T(8,128)(2,1)} %get-tuple-element.12.k_ref, bf16[8,1024,128]{2,1,0:T(8,128)(2,1)} %get-tuple-element.13.v_ref), custom_call_target="tpu_custom_call" | custom-call | flops 2952790016 | bytes 10485760 | tf_op jit(solution)/shard_map/pallas_call | solution.py:163
  62.9 5.7 %all-to-all-done.1 = bf16[16,2,128,128]{3,2,1,0:T(8,128)(2,1)S(1)} async-done(((bf16[16,2,128,128]{3,2,1,0:T(8,128)(2,1)}), bf16[16,2,128,128]{3,2,1,0:T(8,128)(2,1)S(1)}, u32[]{:S(2)}, u32[]{:S(2)}) %all-to-all-start.1) | async-done | bytes 1048608 | tf_op jit(solution)/shard_map/all_to_all | solution.py:42
  68.6 1.0 %convert_reduce_fusion = f32[4,2,128,128]{3,2,1,0:T(8,128)} fusion(bf16[4,4,2,128,128]{4,3,2,1,0:T(8,128)(2,1)S(1)} %bitcast.26), kind=kLoop, calls=%fused_computation.10 | loop fusion | flops 917504 | bytes 1572864 | tf_op jit(solution)/shard_map/reduce_sum | solution.py:49
  69.5 8.0 %shard_map.67 = bf16[1024,1024]{1,0:T(8,128)(2,1)} custom-call(bf16[8,1024,128]{2,1,0:T(8,128)(2,1)} %shard_map.65.q_ref, f32[8,1024,128]{2,1,0:T(8,128)} %shard_map.66.local_ref, f32[8,128,128]{2,1,0:T(8,128)} %bitcast.27, f32[8,1,128]{2,1,0:T(1,128)} %bitcast.29, bf16[1024,1024]{1,0:T(8,128)(2,1)} %w_ref.1), custom_call_target="tpu_custom_call" | custom-call | flops 2684354560 | bytes 10485760 | tf_op jit(solution)/shard_map/pallas_call | solution.py:177
  (8 shorter events, 0.1 us)
Async XLA Ops:
  2.1 16.2 %copy-start.1 = (f32[4,3072]{1,0:T(4,128)S(1)}, f32[4,3072]{1,0:T(4,128)}, u32[]{:S(2)}) copy-start(f32[4,3072]{1,0:T(4,128)} %param.9) | copy-start | bytes 147460
  11.7 2.7 %copy-start = (bf16[24,1024,128]{2,1,0:T(8,128)(2,1)}, bf16[24,1024,128]{2,1,0:T(8,128)(2,1)S(1)}, u32[]{:S(2)}) copy-start(bf16[24,1024,128]{2,1,0:T(8,128)(2,1)S(1)} %convert_bitcast_fusion.refs_0_.refs_1_) | copy-start | bytes 18874372
  14.3 5.4 %collective-permute-start = (bf16[24,3,128]{2,1,0:T(4,128)(2,1)S(1)}, bf16[24,3,128]{2,1,0:T(4,128)(2,1)S(1)}, u32[]{:S(2)}, u32[]{:S(2)}) collective-permute-start(bf16[24,3,128]{2,1,0:T(4,128)(2,1)S(1)} %slice.20), channel_id=1, source_target_pairs={{0,1},{1,2},{2,3},{3,4},{4,5},{5,6},{6,7},{7,8},{8,9},{9,10},{10,1... | collective-permute-start | bytes 55304 | tf_op jit(solution)/shard_map/ppermute | solution.py:149
  30.7 12.6 %all-to-all-start = ((bf16[4,2,128,128]{3,2,1,0:T(8,128)(2,1)}), bf16[4,2,128,128]{3,2,1,0:T(8,128)(2,1)S(1)}, u32[]{:S(2)}, u32[]{:S(2)}) async-start(bf16[4,2,128,128]{3,2,1,0:T(8,128)(2,1)} %bitcast.4), calls=%async_computation | async-start | bytes 524288 | tf_op jit(solution)/shard_map/all_to_all | solution.py:27
  45.0 23.6 %all-to-all-start.1 = ((bf16[16,2,128,128]{3,2,1,0:T(8,128)(2,1)}), bf16[16,2,128,128]{3,2,1,0:T(8,128)(2,1)S(1)}, u32[]{:S(2)}, u32[]{:S(2)}) async-start(bf16[16,2,128,128]{3,2,1,0:T(8,128)(2,1)} %bitcast.6), calls=%async_computation.1 | async-start | bytes 2097152 | tf_op jit(solution)/shard_map/all_to_all | solution.py:42

commit v15 on v13

--- a/solution.py
+++ b/solution.py
@@ -47,7 +47,7 @@
 def conv_kernel(pq, pk, pv, eq, ek, ev, tq, tk, tv, oq, ok, ov, state_ref, buf):
     rows = pq.shape[0]
     for proj, early, taps, out in ((pq, eq, tq, oq), (pk, ek, tk, ok), (pv, ev, tv, ov)):
-        buf[0:PAD, :] = early[...].astype(jnp.float32)
+        buf[PAD - (KW - 1) : PAD, :] = early[...].astype(jnp.float32)
         buf[PAD:, :] = proj[...].astype(jnp.float32)
         summed = jnp.zeros((rows, DH), jnp.float32)
         for offset in range(KW):
@@ -55,7 +55,7 @@
         out[...] = (summed * jax.nn.sigmoid(summed)).astype(out.dtype)
     state_ref[...] = lax.dot_general(
         ok[...], ov[...], (((0,), (0,)), ((), ())), preferred_element_type=jnp.float32
-    )
+    ).astype(state_ref.dtype)
 
 
 def local_kernel(q_ref, k_ref, v_ref, out_ref):
@@ -116,20 +116,17 @@
     earlier_rows = lax.ppermute(
         projected[:, rows - (KW - 1) :, :], seq_axes, [(i, i + 1) for i in range(count - 1)]
     )
-    earlier_rows = jnp.pad(earlier_rows, ((0, 0), (PAD - (KW - 1), 0), (0, 0)))
-    taps = jnp.pad(
-        conv_weight.reshape(KW, slabs, DH).transpose(1, 0, 2), ((0, 0), (0, PAD - KW), (0, 0))
-    )
+    taps = conv_weight.reshape(KW, slabs, DH).transpose(1, 0, 2)
 
     mixed_shape = jax.ShapeDtypeStruct((H, rows, DH), jnp.bfloat16)
     query, key, value, state = pl.pallas_call(
         conv_kernel,
         grid=(H,),
         in_specs=[slab(0, rows, DH), slab(H, rows, DH), slab(2 * H, rows, DH)]
-        + [slab(0, PAD, DH), slab(H, PAD, DH), slab(2 * H, PAD, DH)]
-        + [slab(0, PAD, DH), slab(H, PAD, DH), slab(2 * H, PAD, DH)],
+        + [slab(0, KW - 1, DH), slab(H, KW - 1, DH), slab(2 * H, KW - 1, DH)]
+        + [slab(0, KW, DH), slab(H, KW, DH), slab(2 * H, KW, DH)],
         out_specs=[slab(0, rows, DH)] * 3 + [slab(0, DH, DH)],
-        out_shape=[mixed_shape] * 3 + [jax.ShapeDtypeStruct((H, DH, DH), jnp.float32)],
+        out_shape=[mixed_shape] * 3 + [jax.ShapeDtypeStruct((H, DH, DH), jnp.bfloat16)],
         scratch_shapes=[pltpu.VMEM((rows + PAD, DH), jnp.float32)],
         cost_estimate=pl.CostEstimate(
             flops=H * (3 * rows * DH * 12 + 2 * rows * DH * DH),
@@ -154,7 +151,7 @@
 
     prefix = earlier_states(state)
 
-    tile = min(256, rows)
+    tile = min(512, rows)
     out = pl.pallas_call(
         out_kernel,
         grid=(rows // tile,),

time: 77 us -> 74.7 us (0.970)
  other arithmetic: 6.4 us -> 4.62 us
    convert_element_type x1 -> x0, other arithmetic: 1.77 us -> none  [earlier_states(): quarters = state.astype(jnp.bfloat16).reshape((count, -1) + state.shape[1:])]
    pad x2 -> x0, local copies, waits for them, and re-layouts: 1.29 us -> none  [the longest x1 0.65 us: local(): jnp.pad(conv_weight.reshape(KW, slabs, DH).transpose(1, 0, 2), ((0, 0), (...]
  transfers between devices with their start and end apart: 3 -> 3, of which waited for: 3 -> 3; matrix products, arithmetic and copies ran while one was open for 1% -> 0% of each run, Pallas kernels for 13% -> 14%
where the time goes in v15:
time: 74.7 us; the launch traced here: 74 us
  Pallas kernels  28.4 us (38%)
  starting transfers between devices  15 us (20%)
  waiting for transfers between devices  13 us (17%)
  matrix products  9.56 us (13%)
  other arithmetic  4.62 us (6%)
  local copies, waits for them, and re-layouts  3.44 us (5%)
    pallas_call x1, Pallas kernels, local(): pl.pallas_call(conv_kernel, grid=(H,), in_specs=[slab(0, rows, DH), slab(...  10.6 us
    pallas_call x1, Pallas kernels, local(): pl.pallas_call(local_kernel, grid=(H,), in_specs=[slab(0, rows, DH)] * 3,...  10.2 us
    dot_general x1, matrix products, local(): jnp.einsum('td,dje->jte', normed, w_qkv.reshape(width, slabs, DH), prefer...  9.56 us
    pallas_call x1, Pallas kernels, local(): pl.pallas_call(out_kernel, grid=(rows // tile,), in_specs=[pl.BlockSpec((...  7.59 us
    all_to_all x1, waiting for transfers between devices, earlier_states(): mine = lax.all_to_all(quarters, 'sz', 0, 0).astype(jnp.float32)  6.51 us
    all_to_all x1, starting transfers between devices, earlier_states(): mine = lax.all_to_all(quarters, 'sz', 0, 0).astype(jnp.float32)  5.7 us
    all_to_all x1, starting transfers between devices, earlier_states(): lax.all_to_all(messages.astype(jnp.bfloat16).reshape((rows_count * count,...  5.36 us
    all_to_all x1, waiting for transfers between devices, earlier_states(): lax.all_to_all(messages.astype(jnp.bfloat16).reshape((rows_count * count,...  4.96 us
  transfers between devices with their start and end apart: 3, of which 3 were waited for; matrix products, arithmetic and copies ran while one was open for 0% of the time, Pallas kernels for 14%

profile of v15, /device:TPU:0, one launch (start us, length us, event | category | flops | bytes accessed | tf_op | source)
XLA Modules:
  0.0 74.0 jit_solution(3078197238190443972)
XLA Ops:
  0.0 2.1 %fusion.3 = f32[1024]{0:T(1024)S(1)} fusion(bf16[1024,1024]{1,0:T(8,128)(2,1)} %param.6), kind=kLoop, calls=%fused_computation.6 | loop fusion | flops 3144704 | bytes 2101248 | tf_op jit(solution)/shard_map/reduce_sum | solution.py:106
  2.1 9.6 %convert_bitcast_fusion.pq.pk.pv = bf16[24,1024,128]{2,1,0:T(8,128)(2,1)S(1)} fusion(bf16[1024,1024]{1,0:T(8,128)(2,1)} %param.6, f32[1024]{0:T(1024)} %param.7, f32[1024]{0:T(1024)S(1)} %add_rsqrt_fusion, bf16[1024,3072]{1,0:T(8,128)(2,1)} %param.8), kind=kOutput, calls=%fused_computation.3 | convolution fusion | flops 6449790976 | bytes 14688256 | tf_op jit(solution)/shard_map/td,dje->jte/dot_general | solution.py:110
  11.7 0.0 copy-start
  11.7 2.6 %copy-done = bf16[24,1024,128]{2,1,0:T(8,128)(2,1)} copy-done((bf16[24,1024,128]{2,1,0:T(8,128)(2,1)}, bf16[24,1024,128]{2,1,0:T(8,128)(2,1)S(1)}, u32[]{:S(2)}) %copy-start) | copy-done | bytes 6291480
  14.3 3.9 %collective-permute-start = (bf16[24,3,128]{2,1,0:T(4,128)(2,1)S(1)}, bf16[24,3,128]{2,1,0:T(4,128)(2,1)S(1)}, u32[]{:S(2)}, u32[]{:S(2)}) collective-permute-start(bf16[24,3,128]{2,1,0:T(4,128)(2,1)S(1)} %slice.20), channel_id=1, source_target_pairs={{0,1},{1,2},{2,3},{3,4},{4,5},{5,6},{6,7},{7,8},{8,9},{9,10},{10,1... | collective-permute-start | bytes 55304 | tf_op jit(solution)/shard_map/ppermute | solution.py:116
  18.3 1.5 %collective-permute-done.eq.ek.ev = bf16[24,3,128]{2,1,0:T(4,128)(2,1)S(1)} collective-permute-done((bf16[24,3,128]{2,1,0:T(4,128)(2,1)S(1)}, bf16[24,3,128]{2,1,0:T(4,128)(2,1)S(1)}, u32[]{:S(2)}, u32[]{:S(2)}) %collective-permute-start) | collective-permute-done | bytes 18464 | tf_op jit(solution)/shard_map/ppermute | solution.py:116
  19.7 0.0 copy-start.1
  19.8 0.6 copy-done.1
  20.4 10.6 %shard_map.64 = (bf16[8,1024,128]{2,1,0:T(8,128)(2,1)}, bf16[8,1024,128]{2,1,0:T(8,128)(2,1)}, bf16[8,1024,128]{2,1,0:T(8,128)(2,1)}, bf16[8,128,128]{2,1,0:T(8,128)(2,1)}) custom-call(bf16[24,1024,128]{2,1,0:T(8,128)(2,1)} %copy-done, bf16[24,1024,128]{2,1,0:T(8,128)(2,1)} %copy-done, bf16[24,1024,128]{2,1,0:T(8,128)(2,1)} %copy-done, ...), custom_call_target="tpu_custom_call" | custom-call | flops 306184192 | bytes 12582912 | tf_op jit(solution)/shard_map/pallas_call | solution.py:122
  30.9 5.7 %all-to-all-start = ((bf16[4,2,128,128]{3,2,1,0:T(8,128)(2,1)}), bf16[4,2,128,128]{3,2,1,0:T(8,128)(2,1)S(1)}, u32[]{:S(2)}, u32[]{:S(2)}) async-start(bf16[4,2,128,128]{3,2,1,0:T(8,128)(2,1)} %bitcast.38), calls=%async_computation | async-start | bytes 524288 | tf_op jit(solution)/shard_map/all_to_all | solution.py:25
  36.6 0.1 mul.65
  36.7 0.1 mul.66
  36.8 6.5 %all-to-all-done = bf16[4,2,128,128]{3,2,1,0:T(8,128)(2,1)S(1)} async-done(((bf16[4,2,128,128]{3,2,1,0:T(8,128)(2,1)}), bf16[4,2,128,128]{3,2,1,0:T(8,128)(2,1)S(1)}, u32[]{:S(2)}, u32[]{:S(2)}) %all-to-all-start) | async-done | bytes 262176 | tf_op jit(solution)/shard_map/all_to_all | solution.py:25
  43.4 0.2 pad_maximum_fusion
  43.6 1.3 %fusion.11 = bf16[16,2,128,128]{3,2,1,0:T(8,128)(2,1)} fusion(f32[4,2,128,128]{3,2,1,0:T(8,128)S(1)} %get-tuple-element.16, f32[16]{0:T(128)S(1)} %mul.66, f32[4,2,128,128]{3,2,1,0:T(8,128)S(1)} %get-tuple-element.17), kind=kLoop, calls=%fused_computation.13 | loop fusion | flops 1572864 | bytes 2097216 | tf_op jit(solution)/shard_map/convert_element_type | solution.py:38
  44.9 5.4 %all-to-all-start.1 = ((bf16[16,2,128,128]{3,2,1,0:T(8,128)(2,1)}), bf16[16,2,128,128]{3,2,1,0:T(8,128)(2,1)S(1)}, u32[]{:S(2)}, u32[]{:S(2)}) async-start(bf16[16,2,128,128]{3,2,1,0:T(8,128)(2,1)} %fusion.11), calls=%async_computation.1 | async-start | bytes 2097152 | tf_op jit(solution)/shard_map/all_to_all | solution.py:37
  50.3 10.2 %shard_map.65.local_ref = f32[8,1024,128]{2,1,0:T(8,128)} custom-call(bf16[8,1024,128]{2,1,0:T(8,128)(2,1)} %get-tuple-element.9.q_ref, bf16[8,1024,128]{2,1,0:T(8,128)(2,1)} %get-tuple-element.10.k_ref, bf16[8,1024,128]{2,1,0:T(8,128)(2,1)} %get-tuple-element.11.v_ref), custom_call_target="tpu_custom_call" | custom-call | flops 2952790016 | bytes 10485760 | tf_op jit(solution)/shard_map/pallas_call | solution.py:139
  60.5 5.0 %all-to-all-done.1 = bf16[16,2,128,128]{3,2,1,0:T(8,128)(2,1)S(1)} async-done(((bf16[16,2,128,128]{3,2,1,0:T(8,128)(2,1)}), bf16[16,2,128,128]{3,2,1,0:T(8,128)(2,1)S(1)}, u32[]{:S(2)}, u32[]{:S(2)}) %all-to-all-start.1) | async-done | bytes 1048608 | tf_op jit(solution)/shard_map/all_to_all | solution.py:37
  65.4 1.0 %convert_reduce_fusion = f32[4,2,128,128]{3,2,1,0:T(8,128)} fusion(bf16[4,4,2,128,128]{4,3,2,1,0:T(8,128)(2,1)S(1)} %bitcast.33), kind=kLoop, calls=%fused_computation.10 | loop fusion | flops 917504 | bytes 1572864 | tf_op jit(solution)/shard_map/reduce_sum | solution.py:44
  66.4 7.6 %shard_map.66 = bf16[1024,1024]{1,0:T(8,128)(2,1)} custom-call(bf16[8,1024,128]{2,1,0:T(8,128)(2,1)} %get-tuple-element.9.q_ref, f32[8,1024,128]{2,1,0:T(8,128)} %shard_map.65.local_ref, f32[8,128,128]{2,1,0:T(8,128)} %bitcast.34, f32[8,1,128]{2,1,0:T(1,128)} %bitcast.39, bf16[1024,1024]{1,0:T(8,128)(2,1)} %w_ref.1), custom_call_target="tpu_custom_call" | custom-call | flops 2684354560 | bytes 10485760 | tf_op jit(solution)/shard_map/pallas_call | solution.py:155
  (8 shorter events, 0.1 us)
Async XLA Ops:
  11.7 2.7 %copy-start = (bf16[24,1024,128]{2,1,0:T(8,128)(2,1)}, bf16[24,1024,128]{2,1,0:T(8,128)(2,1)S(1)}, u32[]{:S(2)}) copy-start(bf16[24,1024,128]{2,1,0:T(8,128)(2,1)S(1)} %convert_bitcast_fusion.pq.pk.pv) | copy-start | bytes 18874372
  14.3 5.4 %collective-permute-start = (bf16[24,3,128]{2,1,0:T(4,128)(2,1)S(1)}, bf16[24,3,128]{2,1,0:T(4,128)(2,1)S(1)}, u32[]{:S(2)}, u32[]{:S(2)}) collective-permute-start(bf16[24,3,128]{2,1,0:T(4,128)(2,1)S(1)} %slice.20), channel_id=1, source_target_pairs={{0,1},{1,2},{2,3},{3,4},{4,5},{5,6},{6,7},{7,8},{8,9},{9,10},{10,1... | collective-permute-start | bytes 55304 | tf_op jit(solution)/shard_map/ppermute | solution.py:116
  19.7 0.6 copy-start.1
  30.9 12.4 %all-to-all-start = ((bf16[4,2,128,128]{3,2,1,0:T(8,128)(2,1)}), bf16[4,2,128,128]{3,2,1,0:T(8,128)(2,1)S(1)}, u32[]{:S(2)}, u32[]{:S(2)}) async-start(bf16[4,2,128,128]{3,2,1,0:T(8,128)(2,1)} %bitcast.38), calls=%async_computation | async-start | bytes 524288 | tf_op jit(solution)/shard_map/all_to_all | solution.py:25
  44.9 20.5 %all-to-all-start.1 = ((bf16[16,2,128,128]{3,2,1,0:T(8,128)(2,1)}), bf16[16,2,128,128]{3,2,1,0:T(8,128)(2,1)S(1)}, u32[]{:S(2)}, u32[]{:S(2)}) async-start(bf16[16,2,128,128]{3,2,1,0:T(8,128)(2,1)} %fusion.11), calls=%async_computation.1 | async-start | bytes 2097152 | tf_op jit(solution)/shard_map/all_to_all | solution.py:37

commit v16 on v15

--- a/solution.py
+++ b/solution.py
@@ -40,8 +40,7 @@
         0,
         0,
     )
-    received = received.reshape((rows_count, count) + row_total.shape).astype(jnp.float32)
-    return jnp.sum(received, 0).reshape(state.shape)
+    return received.reshape((rows_count,) + state.shape)
 
 
 def conv_kernel(pq, pk, pv, eq, ek, ev, tq, tk, tv, oq, ok, ov, state_ref, buf):
@@ -85,7 +84,7 @@
 
 def out_kernel(q_ref, local_ref, prefix_ref, gain_ref, w_ref, out_ref, headed):
     for head in range(q_ref.shape[0]):
-        hi, lo = split_bf16(prefix_ref[head])
+        hi, lo = split_bf16(jnp.sum(prefix_ref[:, head].astype(jnp.float32), 0))
         query = q_ref[head]
         attended = local_ref[head] + jnp.dot(query, hi, preferred_element_type=jnp.float32)
         attended = attended + jnp.dot(query, lo, preferred_element_type=jnp.float32)
@@ -158,7 +157,7 @@
         in_specs=[
             pl.BlockSpec((H, tile, DH), lambda i: (0, i, 0)),
             pl.BlockSpec((H, tile, DH), lambda i: (0, i, 0)),
-            pl.BlockSpec((H, DH, DH), lambda i: (0, 0, 0)),
+            pl.BlockSpec(prefix.shape, lambda i: (0, 0, 0, 0)),
             pl.BlockSpec((H, 1, DH), lambda i: (0, 0, 0)),
             pl.BlockSpec((width, width), lambda i: (0, 0)),
         ],

time: 74.7 us -> 75 us (level)
  other arithmetic: 4.62 us -> 3.62 us
  local copies, waits for them, and re-layouts: 3.44 us -> 4.42 us
    reduce_sum x1 -> x0, other arithmetic: 0.98 us -> none  [earlier_states(): return jnp.sum(received, 0).reshape(state.shape)]
    unnamed x4 -> x6, local copies, waits for them, and re-layouts: 3.25 us -> 4.23 us
where the time goes in v16:
time: 75 us; the launch traced here: 74.3 us
  Pallas kernels  28.7 us (38%)
  starting transfers between devices  15 us (20%)
  waiting for transfers between devices  13 us (17%)
  matrix products  9.56 us (13%)
  local copies, waits for them, and re-layouts  4.42 us (6%)
  other arithmetic  3.62 us (5%)
    pallas_call x1, Pallas kernels, local(): pl.pallas_call(conv_kernel, grid=(H,), in_specs=[slab(0, rows, DH), slab(...  10.6 us
    pallas_call x1, Pallas kernels, local(): pl.pallas_call(local_kernel, grid=(H,), in_specs=[slab(0, rows, DH)] * 3,...  10.2 us
    dot_general x1, matrix products, local(): jnp.einsum('td,dje->jte', normed, w_qkv.reshape(width, slabs, DH), prefer...  9.56 us
    pallas_call x1, Pallas kernels, local(): pl.pallas_call(out_kernel, grid=(rows // tile,), in_specs=[pl.BlockSpec((...  7.87 us
    all_to_all x1, waiting for transfers between devices, earlier_states(): mine = lax.all_to_all(quarters, 'sz', 0, 0).astype(jnp.float32)  6.51 us
    all_to_all x1, starting transfers between devices, earlier_states(): mine = lax.all_to_all(quarters, 'sz', 0, 0).astype(jnp.float32)  5.7 us
    all_to_all x1, starting transfers between devices, earlier_states(): lax.all_to_all(messages.astype(jnp.bfloat16).reshape((rows_count * count,...  5.36 us
    all_to_all x1, waiting for transfers between devices, earlier_states(): lax.all_to_all(messages.astype(jnp.bfloat16).reshape((rows_count * count,...  4.97 us
  transfers between devices with their start and end apart: 3, of which 3 were waited for; matrix products, arithmetic and copies ran while one was open for 0% of the time, Pallas kernels for 14%

profile of v16, /device:TPU:0, one launch (start us, length us, event | category | flops | bytes accessed | tf_op | source)
XLA Modules:
  0.0 74.3 jit_solution(12333155426264859535)
XLA Ops:
  0.0 2.1 %fusion.3 = f32[1024]{0:T(1024)S(1)} fusion(bf16[1024,1024]{1,0:T(8,128)(2,1)} %param.6), kind=kLoop, calls=%fused_computation.6 | loop fusion | flops 3144704 | bytes 2101248 | tf_op jit(solution)/shard_map/reduce_sum | solution.py:105
  2.1 9.6 %convert_bitcast_fusion.pq.pk.pv = bf16[24,1024,128]{2,1,0:T(8,128)(2,1)S(1)} fusion(bf16[1024,1024]{1,0:T(8,128)(2,1)} %param.6, f32[1024]{0:T(1024)} %param.7, f32[1024]{0:T(1024)S(1)} %add_rsqrt_fusion, bf16[1024,3072]{1,0:T(8,128)(2,1)} %param.8), kind=kOutput, calls=%fused_computation.3 | convolution fusion | flops 6449790976 | bytes 14688256 | tf_op jit(solution)/shard_map/td,dje->jte/dot_general | solution.py:109
  11.7 0.0 copy-start
  11.7 2.7 %copy-done = bf16[24,1024,128]{2,1,0:T(8,128)(2,1)} copy-done((bf16[24,1024,128]{2,1,0:T(8,128)(2,1)}, bf16[24,1024,128]{2,1,0:T(8,128)(2,1)S(1)}, u32[]{:S(2)}) %copy-start) | copy-done | bytes 6291480
  14.3 3.9 %collective-permute-start = (bf16[24,3,128]{2,1,0:T(4,128)(2,1)S(1)}, bf16[24,3,128]{2,1,0:T(4,128)(2,1)S(1)}, u32[]{:S(2)}, u32[]{:S(2)}) collective-permute-start(bf16[24,3,128]{2,1,0:T(4,128)(2,1)S(1)} %slice.20), channel_id=1, source_target_pairs={{0,1},{1,2},{2,3},{3,4},{4,5},{5,6},{6,7},{7,8},{8,9},{9,10},{10,1... | collective-permute-start | bytes 55304 | tf_op jit(solution)/shard_map/ppermute | solution.py:115
  18.3 1.5 %collective-permute-done.eq.ek.ev = bf16[24,3,128]{2,1,0:T(4,128)(2,1)S(1)} collective-permute-done((bf16[24,3,128]{2,1,0:T(4,128)(2,1)S(1)}, bf16[24,3,128]{2,1,0:T(4,128)(2,1)S(1)}, u32[]{:S(2)}, u32[]{:S(2)}) %collective-permute-start) | collective-permute-done | bytes 18464 | tf_op jit(solution)/shard_map/ppermute | solution.py:115
  19.8 0.0 copy-start.2
  19.8 0.6 copy-done.2
  20.4 10.6 %shard_map.64 = (bf16[8,1024,128]{2,1,0:T(8,128)(2,1)}, bf16[8,1024,128]{2,1,0:T(8,128)(2,1)}, bf16[8,1024,128]{2,1,0:T(8,128)(2,1)}, bf16[8,128,128]{2,1,0:T(8,128)(2,1)}) custom-call(bf16[24,1024,128]{2,1,0:T(8,128)(2,1)} %copy-done, bf16[24,1024,128]{2,1,0:T(8,128)(2,1)} %copy-done, bf16[24,1024,128]{2,1,0:T(8,128)(2,1)} %copy-done, ...), custom_call_target="tpu_custom_call" | custom-call | flops 306184192 | bytes 12582912 | tf_op jit(solution)/shard_map/pallas_call | solution.py:121
  31.0 5.7 %all-to-all-start = ((bf16[4,2,128,128]{3,2,1,0:T(8,128)(2,1)}), bf16[4,2,128,128]{3,2,1,0:T(8,128)(2,1)S(1)}, u32[]{:S(2)}, u32[]{:S(2)}) async-start(bf16[4,2,128,128]{3,2,1,0:T(8,128)(2,1)} %bitcast.35), calls=%async_computation | async-start | bytes 524288 | tf_op jit(solution)/shard_map/all_to_all | solution.py:25
  36.7 0.1 mul.65
  36.7 0.1 mul.66
  36.8 6.5 %all-to-all-done = bf16[4,2,128,128]{3,2,1,0:T(8,128)(2,1)S(1)} async-done(((bf16[4,2,128,128]{3,2,1,0:T(8,128)(2,1)}), bf16[4,2,128,128]{3,2,1,0:T(8,128)(2,1)S(1)}, u32[]{:S(2)}, u32[]{:S(2)}) %all-to-all-start) | async-done | bytes 262176 | tf_op jit(solution)/shard_map/all_to_all | solution.py:25
  43.5 0.2 pad_maximum_fusion
  43.6 1.3 %fusion.11 = bf16[16,2,128,128]{3,2,1,0:T(8,128)(2,1)} fusion(f32[4,2,128,128]{3,2,1,0:T(8,128)S(1)} %get-tuple-element.16, f32[16]{0:T(128)S(1)} %mul.66, f32[4,2,128,128]{3,2,1,0:T(8,128)S(1)} %get-tuple-element.17), kind=kLoop, calls=%fused_computation.12 | loop fusion | flops 1572864 | bytes 2097216 | tf_op jit(solution)/shard_map/convert_element_type | solution.py:38
  44.9 5.4 %all-to-all-start.1 = ((bf16[16,2,128,128]{3,2,1,0:T(8,128)(2,1)}), bf16[16,2,128,128]{3,2,1,0:T(8,128)(2,1)S(1)}, u32[]{:S(2)}, u32[]{:S(2)}) async-start(bf16[16,2,128,128]{3,2,1,0:T(8,128)(2,1)} %fusion.11), calls=%async_computation.1 | async-start | bytes 2097152 | tf_op jit(solution)/shard_map/all_to_all | solution.py:37
  50.3 10.2 %shard_map.65.local_ref = f32[8,1024,128]{2,1,0:T(8,128)} custom-call(bf16[8,1024,128]{2,1,0:T(8,128)(2,1)} %get-tuple-element.9.q_ref, bf16[8,1024,128]{2,1,0:T(8,128)(2,1)} %get-tuple-element.10.k_ref, bf16[8,1024,128]{2,1,0:T(8,128)(2,1)} %get-tuple-element.11.v_ref), custom_call_target="tpu_custom_call" | custom-call | flops 2952790016 | bytes 10485760 | tf_op jit(solution)/shard_map/pallas_call | solution.py:138
  60.5 5.0 %all-to-all-done.1 = bf16[16,2,128,128]{3,2,1,0:T(8,128)(2,1)S(1)} async-done(((bf16[16,2,128,128]{3,2,1,0:T(8,128)(2,1)}), bf16[16,2,128,128]{3,2,1,0:T(8,128)(2,1)S(1)}, u32[]{:S(2)}, u32[]{:S(2)}) %all-to-all-start.1) | async-done | bytes 1048608 | tf_op jit(solution)/shard_map/all_to_all | solution.py:37
  65.5 0.0 copy-start.1
  65.5 1.0 %copy-done.1 = bf16[16,2,128,128]{3,2,1,0:T(8,128)(2,1)} copy-done((bf16[16,2,128,128]{3,2,1,0:T(8,128)(2,1)}, bf16[16,2,128,128]{3,2,1,0:T(8,128)(2,1)S(1)}, u32[]{:S(2)}) %copy-start.1) | copy-done | bytes 1048600
  66.4 7.9 %shard_map.66 = bf16[1024,1024]{1,0:T(8,128)(2,1)} custom-call(bf16[8,1024,128]{2,1,0:T(8,128)(2,1)} %get-tuple-element.9.q_ref, f32[8,1024,128]{2,1,0:T(8,128)} %shard_map.65.local_ref, bf16[4,8,128,128]{3,2,1,0:T(8,128)(2,1)} %bitcast.31, f32[8,1,128]{2,1,0:T(1,128)} %bitcast.36, bf16[1024,1024]{1,0:T(8,128)(2,1)} %w_ref.1), custom_call_target="tpu_custom_call" | custom-call | flops 2684354560 | bytes 10485760 | tf_op jit(solution)/shard_map/pallas_call | solution.py:154
  (8 shorter events, 0.1 us)
Async XLA Ops:
  11.7 2.7 %copy-start = (bf16[24,1024,128]{2,1,0:T(8,128)(2,1)}, bf16[24,1024,128]{2,1,0:T(8,128)(2,1)S(1)}, u32[]{:S(2)}) copy-start(bf16[24,1024,128]{2,1,0:T(8,128)(2,1)S(1)} %convert_bitcast_fusion.pq.pk.pv) | copy-start | bytes 18874372
  14.3 5.4 %collective-permute-start = (bf16[24,3,128]{2,1,0:T(4,128)(2,1)S(1)}, bf16[24,3,128]{2,1,0:T(4,128)(2,1)S(1)}, u32[]{:S(2)}, u32[]{:S(2)}) collective-permute-start(bf16[24,3,128]{2,1,0:T(4,128)(2,1)S(1)} %slice.20), channel_id=1, source_target_pairs={{0,1},{1,2},{2,3},{3,4},{4,5},{5,6},{6,7},{7,8},{8,9},{9,10},{10,1... | collective-permute-start | bytes 55304 | tf_op jit(solution)/shard_map/ppermute | solution.py:115
  19.8 0.6 copy-start.2
  31.0 12.4 %all-to-all-start = ((bf16[4,2,128,128]{3,2,1,0:T(8,128)(2,1)}), bf16[4,2,128,128]{3,2,1,0:T(8,128)(2,1)S(1)}, u32[]{:S(2)}, u32[]{:S(2)}) async-start(bf16[4,2,128,128]{3,2,1,0:T(8,128)(2,1)} %bitcast.35), calls=%async_computation | async-start | bytes 524288 | tf_op jit(solution)/shard_map/all_to_all | solution.py:25
  44.9 20.5 %all-to-all-start.1 = ((bf16[16,2,128,128]{3,2,1,0:T(8,128)(2,1)}), bf16[16,2,128,128]{3,2,1,0:T(8,128)(2,1)S(1)}, u32[]{:S(2)}, u32[]{:S(2)}) async-start(bf16[16,2,128,128]{3,2,1,0:T(8,128)(2,1)} %fusion.11), calls=%async_computation.1 | async-start | bytes 2097152 | tf_op jit(solution)/shard_map/all_to_all | solution.py:37
  65.5 1.0 %copy-start.1 = (bf16[16,2,128,128]{3,2,1,0:T(8,128)(2,1)}, bf16[16,2,128,128]{3,2,1,0:T(8,128)(2,1)S(1)}, u32[]{:S(2)}) copy-start(bf16[16,2,128,128]{3,2,1,0:T(8,128)(2,1)S(1)} %all-to-all-done.1) | copy-start | bytes 3145732

commit v17 on v15

--- a/solution.py
+++ b/solution.py
@@ -48,9 +48,10 @@
     rows = pq.shape[0]
     for proj, early, taps, out in ((pq, eq, tq, oq), (pk, ek, tk, ok), (pv, ev, tv, ov)):
         buf[PAD - (KW - 1) : PAD, :] = early[...].astype(jnp.float32)
-        buf[PAD:, :] = proj[...].astype(jnp.float32)
-        summed = jnp.zeros((rows, DH), jnp.float32)
-        for offset in range(KW):
+        current = proj[...].astype(jnp.float32)
+        buf[PAD:, :] = current
+        summed = taps[0:1, :] * current
+        for offset in range(1, KW):
             summed = summed + taps[offset : offset + 1, :] * buf[pl.ds(PAD - offset, rows), :]
         out[...] = (summed * jax.nn.sigmoid(summed)).astype(out.dtype)
     state_ref[...] = lax.dot_general(
@@ -86,9 +87,11 @@
 def out_kernel(q_ref, local_ref, prefix_ref, gain_ref, w_ref, out_ref, headed):
     for head in range(q_ref.shape[0]):
         hi, lo = split_bf16(prefix_ref[head])
-        query = q_ref[head]
-        attended = local_ref[head] + jnp.dot(query, hi, preferred_element_type=jnp.float32)
-        attended = attended + jnp.dot(query, lo, preferred_element_type=jnp.float32)
+        both = jnp.dot(
+            q_ref[head], jnp.concatenate([hi, lo], 1), preferred_element_type=jnp.float32
+        )
+        attended = local_ref[head] + both[:, :DH]
+        attended = attended + both[:, DH:]
         scaled = attended * lax.rsqrt(jnp.mean(attended * attended, -1, keepdims=True) + 1e-05)
         headed[:, head * DH : (head + 1) * DH] = (scaled * gain_ref[head]).astype(headed.dtype)
     out_ref[...] = jnp.dot(

time: 74.7 us -> 75 us (level)
  no operation moved by 1% of the time
where the time goes in v17:
time: 75 us; the launch traced here: 74.3 us
  Pallas kernels  28.6 us (38%)
  starting transfers between devices  15 us (20%)
  waiting for transfers between devices  13 us (17%)
  matrix products  9.56 us (13%)
  other arithmetic  4.62 us (6%)
  local copies, waits for them, and re-layouts  3.44 us (5%)
    pallas_call x1, Pallas kernels, local(): pl.pallas_call(conv_kernel, grid=(H,), in_specs=[slab(0, rows, DH), slab(...  10.7 us
    pallas_call x1, Pallas kernels, local(): pl.pallas_call(local_kernel, grid=(H,), in_specs=[slab(0, rows, DH)] * 3,...  10.2 us
    dot_general x1, matrix products, local(): jnp.einsum('td,dje->jte', normed, w_qkv.reshape(width, slabs, DH), prefer...  9.56 us
    pallas_call x1, Pallas kernels, local(): pl.pallas_call(out_kernel, grid=(rows // tile,), in_specs=[pl.BlockSpec((...  7.79 us
    all_to_all x1, waiting for transfers between devices, earlier_states(): mine = lax.all_to_all(quarters, 'sz', 0, 0).astype(jnp.float32)  6.51 us
    all_to_all x1, starting transfers between devices, earlier_states(): mine = lax.all_to_all(quarters, 'sz', 0, 0).astype(jnp.float32)  5.7 us
    all_to_all x1, starting transfers between devices, earlier_states(): lax.all_to_all(messages.astype(jnp.bfloat16).reshape((rows_count * count,...  5.36 us
    all_to_all x1, waiting for transfers between devices, earlier_states(): lax.all_to_all(messages.astype(jnp.bfloat16).reshape((rows_count * count,...  4.96 us
  transfers between devices with their start and end apart: 3, of which 3 were waited for; matrix products, arithmetic and copies ran while one was open for 0% of the time, Pallas kernels for 14%

profile of v17, /device:TPU:0, one launch (start us, length us, event | category | flops | bytes accessed | tf_op | source)
XLA Modules:
  0.0 74.3 jit_solution(8848508998074082274)
XLA Ops:
  0.0 2.1 %fusion.3 = f32[1024]{0:T(1024)S(1)} fusion(bf16[1024,1024]{1,0:T(8,128)(2,1)} %param.6), kind=kLoop, calls=%fused_computation.6 | loop fusion | flops 3144704 | bytes 2101248 | tf_op jit(solution)/shard_map/reduce_sum | solution.py:109
  2.1 9.6 %convert_bitcast_fusion.pq.pk.pv = bf16[24,1024,128]{2,1,0:T(8,128)(2,1)S(1)} fusion(bf16[1024,1024]{1,0:T(8,128)(2,1)} %param.6, f32[1024]{0:T(1024)} %param.7, f32[1024]{0:T(1024)S(1)} %add_rsqrt_fusion, bf16[1024,3072]{1,0:T(8,128)(2,1)} %param.8), kind=kOutput, calls=%fused_computation.3 | convolution fusion | flops 6449790976 | bytes 14688256 | tf_op jit(solution)/shard_map/td,dje->jte/dot_general | solution.py:113
  11.7 0.0 copy-start
  11.7 2.6 %copy-done = bf16[24,1024,128]{2,1,0:T(8,128)(2,1)} copy-done((bf16[24,1024,128]{2,1,0:T(8,128)(2,1)}, bf16[24,1024,128]{2,1,0:T(8,128)(2,1)S(1)}, u32[]{:S(2)}) %copy-start) | copy-done | bytes 6291480
  14.3 3.9 %collective-permute-start = (bf16[24,3,128]{2,1,0:T(4,128)(2,1)S(1)}, bf16[24,3,128]{2,1,0:T(4,128)(2,1)S(1)}, u32[]{:S(2)}, u32[]{:S(2)}) collective-permute-start(bf16[24,3,128]{2,1,0:T(4,128)(2,1)S(1)} %slice.20), channel_id=1, source_target_pairs={{0,1},{1,2},{2,3},{3,4},{4,5},{5,6},{6,7},{7,8},{8,9},{9,10},{10,1... | collective-permute-start | bytes 55304 | tf_op jit(solution)/shard_map/ppermute | solution.py:119
  18.3 1.5 %collective-permute-done.eq.ek.ev = bf16[24,3,128]{2,1,0:T(4,128)(2,1)S(1)} collective-permute-done((bf16[24,3,128]{2,1,0:T(4,128)(2,1)S(1)}, bf16[24,3,128]{2,1,0:T(4,128)(2,1)S(1)}, u32[]{:S(2)}, u32[]{:S(2)}) %collective-permute-start) | collective-permute-done | bytes 18464 | tf_op jit(solution)/shard_map/ppermute | solution.py:119
  19.7 0.0 copy-start.1
  19.8 0.6 copy-done.1
  20.4 10.7 %shard_map.64 = (bf16[8,1024,128]{2,1,0:T(8,128)(2,1)}, bf16[8,1024,128]{2,1,0:T(8,128)(2,1)}, bf16[8,1024,128]{2,1,0:T(8,128)(2,1)}, bf16[8,128,128]{2,1,0:T(8,128)(2,1)}) custom-call(bf16[24,1024,128]{2,1,0:T(8,128)(2,1)} %copy-done, bf16[24,1024,128]{2,1,0:T(8,128)(2,1)} %copy-done, bf16[24,1024,128]{2,1,0:T(8,128)(2,1)} %copy-done, ...), custom_call_target="tpu_custom_call" | custom-call | flops 306184192 | bytes 12582912 | tf_op jit(solution)/shard_map/pallas_call | solution.py:125
  31.0 5.7 %all-to-all-start = ((bf16[4,2,128,128]{3,2,1,0:T(8,128)(2,1)}), bf16[4,2,128,128]{3,2,1,0:T(8,128)(2,1)S(1)}, u32[]{:S(2)}, u32[]{:S(2)}) async-start(bf16[4,2,128,128]{3,2,1,0:T(8,128)(2,1)} %bitcast.38), calls=%async_computation | async-start | bytes 524288 | tf_op jit(solution)/shard_map/all_to_all | solution.py:25
  36.7 0.1 mul.65
  36.8 0.1 mul.66
  36.9 6.5 %all-to-all-done = bf16[4,2,128,128]{3,2,1,0:T(8,128)(2,1)S(1)} async-done(((bf16[4,2,128,128]{3,2,1,0:T(8,128)(2,1)}), bf16[4,2,128,128]{3,2,1,0:T(8,128)(2,1)S(1)}, u32[]{:S(2)}, u32[]{:S(2)}) %all-to-all-start) | async-done | bytes 262176 | tf_op jit(solution)/shard_map/all_to_all | solution.py:25
  43.5 0.2 pad_maximum_fusion
  43.7 1.3 %fusion.11 = bf16[16,2,128,128]{3,2,1,0:T(8,128)(2,1)} fusion(f32[4,2,128,128]{3,2,1,0:T(8,128)S(1)} %get-tuple-element.16, f32[16]{0:T(128)S(1)} %mul.66, f32[4,2,128,128]{3,2,1,0:T(8,128)S(1)} %get-tuple-element.17), kind=kLoop, calls=%fused_computation.13 | loop fusion | flops 1572864 | bytes 2097216 | tf_op jit(solution)/shard_map/convert_element_type | solution.py:38
  45.0 5.4 %all-to-all-start.1 = ((bf16[16,2,128,128]{3,2,1,0:T(8,128)(2,1)}), bf16[16,2,128,128]{3,2,1,0:T(8,128)(2,1)S(1)}, u32[]{:S(2)}, u32[]{:S(2)}) async-start(bf16[16,2,128,128]{3,2,1,0:T(8,128)(2,1)} %fusion.11), calls=%async_computation.1 | async-start | bytes 2097152 | tf_op jit(solution)/shard_map/all_to_all | solution.py:37
  50.4 10.2 %shard_map.65.local_ref = f32[8,1024,128]{2,1,0:T(8,128)} custom-call(bf16[8,1024,128]{2,1,0:T(8,128)(2,1)} %get-tuple-element.9.q_ref, bf16[8,1024,128]{2,1,0:T(8,128)(2,1)} %get-tuple-element.10.k_ref, bf16[8,1024,128]{2,1,0:T(8,128)(2,1)} %get-tuple-element.11.v_ref), custom_call_target="tpu_custom_call" | custom-call | flops 2952790016 | bytes 10485760 | tf_op jit(solution)/shard_map/pallas_call | solution.py:142
  60.5 5.0 %all-to-all-done.1 = bf16[16,2,128,128]{3,2,1,0:T(8,128)(2,1)S(1)} async-done(((bf16[16,2,128,128]{3,2,1,0:T(8,128)(2,1)}), bf16[16,2,128,128]{3,2,1,0:T(8,128)(2,1)S(1)}, u32[]{:S(2)}, u32[]{:S(2)}) %all-to-all-start.1) | async-done | bytes 1048608 | tf_op jit(solution)/shard_map/all_to_all | solution.py:37
  65.5 1.0 %convert_reduce_fusion = f32[4,2,128,128]{3,2,1,0:T(8,128)} fusion(bf16[4,4,2,128,128]{4,3,2,1,0:T(8,128)(2,1)S(1)} %bitcast.33), kind=kLoop, calls=%fused_computation.10 | loop fusion | flops 917504 | bytes 1572864 | tf_op jit(solution)/shard_map/reduce_sum | solution.py:44
  66.5 7.8 %shard_map.66 = bf16[1024,1024]{1,0:T(8,128)(2,1)} custom-call(bf16[8,1024,128]{2,1,0:T(8,128)(2,1)} %get-tuple-element.9.q_ref, f32[8,1024,128]{2,1,0:T(8,128)} %shard_map.65.local_ref, f32[8,128,128]{2,1,0:T(8,128)} %bitcast.34, f32[8,1,128]{2,1,0:T(1,128)} %bitcast.39, bf16[1024,1024]{1,0:T(8,128)(2,1)} %w_ref.1), custom_call_target="tpu_custom_call" | custom-call | flops 2684354560 | bytes 10485760 | tf_op jit(solution)/shard_map/pallas_call | solution.py:158
  (8 shorter events, 0.1 us)
Async XLA Ops:
  11.7 2.7 %copy-start = (bf16[24,1024,128]{2,1,0:T(8,128)(2,1)}, bf16[24,1024,128]{2,1,0:T(8,128)(2,1)S(1)}, u32[]{:S(2)}) copy-start(bf16[24,1024,128]{2,1,0:T(8,128)(2,1)S(1)} %convert_bitcast_fusion.pq.pk.pv) | copy-start | bytes 18874372
  14.3 5.4 %collective-permute-start = (bf16[24,3,128]{2,1,0:T(4,128)(2,1)S(1)}, bf16[24,3,128]{2,1,0:T(4,128)(2,1)S(1)}, u32[]{:S(2)}, u32[]{:S(2)}) collective-permute-start(bf16[24,3,128]{2,1,0:T(4,128)(2,1)S(1)} %slice.20), channel_id=1, source_target_pairs={{0,1},{1,2},{2,3},{3,4},{4,5},{5,6},{6,7},{7,8},{8,9},{9,10},{10,1... | collective-permute-start | bytes 55304 | tf_op jit(solution)/shard_map/ppermute | solution.py:119
  19.7 0.6 copy-start.1
  31.0 12.4 %all-to-all-start = ((bf16[4,2,128,128]{3,2,1,0:T(8,128)(2,1)}), bf16[4,2,128,128]{3,2,1,0:T(8,128)(2,1)S(1)}, u32[]{:S(2)}, u32[]{:S(2)}) async-start(bf16[4,2,128,128]{3,2,1,0:T(8,128)(2,1)} %bitcast.38), calls=%async_computation | async-start | bytes 524288 | tf_op jit(solution)/shard_map/all_to_all | solution.py:25
  45.0 20.5 %all-to-all-start.1 = ((bf16[16,2,128,128]{3,2,1,0:T(8,128)(2,1)}), bf16[16,2,128,128]{3,2,1,0:T(8,128)(2,1)S(1)}, u32[]{:S(2)}, u32[]{:S(2)}) async-start(bf16[16,2,128,128]{3,2,1,0:T(8,128)(2,1)} %fusion.11), calls=%async_computation.1 | async-start | bytes 2097152 | tf_op jit(solution)/shard_map/all_to_all | solution.py:37

commit v18 on v15

--- a/solution.py
+++ b/solution.py
@@ -11,6 +11,7 @@
 KW = 4
 BLOCK = 512
 PAD = 8
+LEAD = 16
 
 
 def split_bf16(x):
@@ -47,7 +48,7 @@
 def conv_kernel(pq, pk, pv, eq, ek, ev, tq, tk, tv, oq, ok, ov, state_ref, buf):
     rows = pq.shape[0]
     for proj, early, taps, out in ((pq, eq, tq, oq), (pk, ek, tk, ok), (pv, ev, tv, ov)):
-        buf[PAD - (KW - 1) : PAD, :] = early[...].astype(jnp.float32)
+        buf[PAD - (KW - 1) : PAD, :] = early[LEAD - (KW - 1) :, :].astype(jnp.float32)
         buf[PAD:, :] = proj[...].astype(jnp.float32)
         summed = jnp.zeros((rows, DH), jnp.float32)
         for offset in range(KW):
@@ -114,7 +115,7 @@
     seq_axes = ("sy", "sz")
     count = lax.axis_size("sy") * lax.axis_size("sz")
     earlier_rows = lax.ppermute(
-        projected[:, rows - (KW - 1) :, :], seq_axes, [(i, i + 1) for i in range(count - 1)]
+        projected[:, rows - LEAD :, :], seq_axes, [(i, i + 1) for i in range(count - 1)]
     )
     taps = conv_weight.reshape(KW, slabs, DH).transpose(1, 0, 2)
 
@@ -123,7 +124,7 @@
         conv_kernel,
         grid=(H,),
         in_specs=[slab(0, rows, DH), slab(H, rows, DH), slab(2 * H, rows, DH)]
-        + [slab(0, KW - 1, DH), slab(H, KW - 1, DH), slab(2 * H, KW - 1, DH)]
+        + [slab(0, LEAD, DH), slab(H, LEAD, DH), slab(2 * H, LEAD, DH)]
         + [slab(0, KW, DH), slab(H, KW, DH), slab(2 * H, KW, DH)],
         out_specs=[slab(0, rows, DH)] * 3 + [slab(0, DH, DH)],
         out_shape=[mixed_shape] * 3 + [jax.ShapeDtypeStruct((H, DH, DH), jnp.bfloat16)],

time: 74.7 us -> 76 us (1.017)
  waiting for transfers between devices: 13 us -> 14 us
where the time goes in v18:
time: 76 us; the launch traced here: 75.3 us
  Pallas kernels  28.4 us (37%)
  starting transfers between devices  15.2 us (20%)
  waiting for transfers between devices  14 us (18%)
  matrix products  9.56 us (13%)
  other arithmetic  4.62 us (6%)
  local copies, waits for them, and re-layouts  3.46 us (5%)
    pallas_call x1, Pallas kernels, local(): pl.pallas_call(conv_kernel, grid=(H,), in_specs=[slab(0, rows, DH), slab(...  10.6 us
    pallas_call x1, Pallas kernels, local(): pl.pallas_call(local_kernel, grid=(H,), in_specs=[slab(0, rows, DH)] * 3,...  10.2 us
    dot_general x1, matrix products, local(): jnp.einsum('td,dje->jte', normed, w_qkv.reshape(width, slabs, DH), prefer...  9.56 us
    pallas_call x1, Pallas kernels, local(): pl.pallas_call(out_kernel, grid=(rows // tile,), in_specs=[pl.BlockSpec((...  7.59 us
    all_to_all x1, waiting for transfers between devices, earlier_states(): mine = lax.all_to_all(quarters, 'sz', 0, 0).astype(jnp.float32)  6.51 us
    all_to_all x1, starting transfers between devices, earlier_states(): mine = lax.all_to_all(quarters, 'sz', 0, 0).astype(jnp.float32)  5.8 us
    all_to_all x1, starting transfers between devices, earlier_states(): lax.all_to_all(messages.astype(jnp.bfloat16).reshape((rows_count * count,...  5.47 us
    all_to_all x1, waiting for transfers between devices, earlier_states(): lax.all_to_all(messages.astype(jnp.bfloat16).reshape((rows_count * count,...  5.32 us
  transfers between devices with their start and end apart: 3, of which 3 were waited for; matrix products, arithmetic and copies ran while one was open for 0% of the time, Pallas kernels for 14%

profile of v18, /device:TPU:0, one launch (start us, length us, event | category | flops | bytes accessed | tf_op | source)
XLA Modules:
  0.0 75.3 jit_solution(8722497761389200573)
XLA Ops:
  0.0 2.1 %fusion.3 = f32[1024]{0:T(1024)S(1)} fusion(bf16[1024,1024]{1,0:T(8,128)(2,1)} %param.6), kind=kLoop, calls=%fused_computation.6 | loop fusion | flops 3144704 | bytes 2101248 | tf_op jit(solution)/shard_map/reduce_sum | solution.py:107
  2.1 9.6 %convert_bitcast_fusion.pq.pk.pv = bf16[24,1024,128]{2,1,0:T(8,128)(2,1)S(1)} fusion(bf16[1024,1024]{1,0:T(8,128)(2,1)} %param.6, f32[1024]{0:T(1024)} %param.7, f32[1024]{0:T(1024)S(1)} %add_rsqrt_fusion, bf16[1024,3072]{1,0:T(8,128)(2,1)} %param.8), kind=kOutput, calls=%fused_computation.3 | convolution fusion | flops 6449790976 | bytes 14688256 | tf_op jit(solution)/shard_map/td,dje->jte/dot_general | solution.py:111
  11.7 0.0 copy-start
  11.7 2.6 %copy-done = bf16[24,1024,128]{2,1,0:T(8,128)(2,1)} copy-done((bf16[24,1024,128]{2,1,0:T(8,128)(2,1)}, bf16[24,1024,128]{2,1,0:T(8,128)(2,1)S(1)}, u32[]{:S(2)}) %copy-start) | copy-done | bytes 6291480
  14.3 3.9 %collective-permute-start = (bf16[24,16,128]{2,1,0:T(8,128)(2,1)S(1)}, bf16[24,16,128]{2,1,0:T(8,128)(2,1)S(1)}, u32[]{:S(2)}, u32[]{:S(2)}) collective-permute-start(bf16[24,16,128]{2,1,0:T(8,128)(2,1)S(1)} %slice.20), channel_id=1, source_target_pairs={{0,1},{1,2},{2,3},{3,4},{4,5},{5,6},{6,7},{7,8},{8,9},{9,10},{10,1... | collective-permute-start | bytes 294920 | tf_op jit(solution)/shard_map/ppermute | solution.py:117
  18.3 2.2 %collective-permute-done.eq.ek.ev = bf16[24,16,128]{2,1,0:T(8,128)(2,1)S(1)} collective-permute-done((bf16[24,16,128]{2,1,0:T(8,128)(2,1)S(1)}, bf16[24,16,128]{2,1,0:T(8,128)(2,1)S(1)}, u32[]{:S(2)}, u32[]{:S(2)}) %collective-permute-start) | collective-permute-done | bytes 98336 | tf_op jit(solution)/shard_map/ppermute | solution.py:117
  20.4 0.0 copy-start.1
  20.4 0.6 copy-done.1
  21.1 10.6 %shard_map.64 = (bf16[8,1024,128]{2,1,0:T(8,128)(2,1)}, bf16[8,1024,128]{2,1,0:T(8,128)(2,1)}, bf16[8,1024,128]{2,1,0:T(8,128)(2,1)}, bf16[8,128,128]{2,1,0:T(8,128)(2,1)}) custom-call(bf16[24,1024,128]{2,1,0:T(8,128)(2,1)} %copy-done, bf16[24,1024,128]{2,1,0:T(8,128)(2,1)} %copy-done, bf16[24,1024,128]{2,1,0:T(8,128)(2,1)} %copy-done, ...), custom_call_target="tpu_custom_call" | custom-call | flops 306184192 | bytes 12582912 | tf_op jit(solution)/shard_map/pallas_call | solution.py:123
  31.7 5.8 %all-to-all-start = ((bf16[4,2,128,128]{3,2,1,0:T(8,128)(2,1)}), bf16[4,2,128,128]{3,2,1,0:T(8,128)(2,1)S(1)}, u32[]{:S(2)}, u32[]{:S(2)}) async-start(bf16[4,2,128,128]{3,2,1,0:T(8,128)(2,1)} %bitcast.38), calls=%async_computation | async-start | bytes 524288 | tf_op jit(solution)/shard_map/all_to_all | solution.py:26
  37.5 0.1 mul.65
  37.5 0.1 mul.66
  37.6 6.5 %all-to-all-done = bf16[4,2,128,128]{3,2,1,0:T(8,128)(2,1)S(1)} async-done(((bf16[4,2,128,128]{3,2,1,0:T(8,128)(2,1)}), bf16[4,2,128,128]{3,2,1,0:T(8,128)(2,1)S(1)}, u32[]{:S(2)}, u32[]{:S(2)}) %all-to-all-start) | async-done | bytes 262176 | tf_op jit(solution)/shard_map/all_to_all | solution.py:26
  44.2 0.2 pad_maximum_fusion
  44.4 1.3 %fusion.11 = bf16[16,2,128,128]{3,2,1,0:T(8,128)(2,1)} fusion(f32[4,2,128,128]{3,2,1,0:T(8,128)S(1)} %get-tuple-element.16, f32[16]{0:T(128)S(1)} %mul.66, f32[4,2,128,128]{3,2,1,0:T(8,128)S(1)} %get-tuple-element.17), kind=kLoop, calls=%fused_computation.13 | loop fusion | flops 1572864 | bytes 2097216 | tf_op jit(solution)/shard_map/convert_element_type | solution.py:39
  45.7 5.5 %all-to-all-start.1 = ((bf16[16,2,128,128]{3,2,1,0:T(8,128)(2,1)}), bf16[16,2,128,128]{3,2,1,0:T(8,128)(2,1)S(1)}, u32[]{:S(2)}, u32[]{:S(2)}) async-start(bf16[16,2,128,128]{3,2,1,0:T(8,128)(2,1)} %fusion.11), calls=%async_computation.1 | async-start | bytes 2097152 | tf_op jit(solution)/shard_map/all_to_all | solution.py:38
  51.2 10.2 %shard_map.65.local_ref = f32[8,1024,128]{2,1,0:T(8,128)} custom-call(bf16[8,1024,128]{2,1,0:T(8,128)(2,1)} %get-tuple-element.9.q_ref, bf16[8,1024,128]{2,1,0:T(8,128)(2,1)} %get-tuple-element.10.k_ref, bf16[8,1024,128]{2,1,0:T(8,128)(2,1)} %get-tuple-element.11.v_ref), custom_call_target="tpu_custom_call" | custom-call | flops 2952790016 | bytes 10485760 | tf_op jit(solution)/shard_map/pallas_call | solution.py:140
  61.4 5.3 %all-to-all-done.1 = bf16[16,2,128,128]{3,2,1,0:T(8,128)(2,1)S(1)} async-done(((bf16[16,2,128,128]{3,2,1,0:T(8,128)(2,1)}), bf16[16,2,128,128]{3,2,1,0:T(8,128)(2,1)S(1)}, u32[]{:S(2)}, u32[]{:S(2)}) %all-to-all-start.1) | async-done | bytes 1048608 | tf_op jit(solution)/shard_map/all_to_all | solution.py:38
  66.7 1.0 %convert_reduce_fusion = f32[4,2,128,128]{3,2,1,0:T(8,128)} fusion(bf16[4,4,2,128,128]{4,3,2,1,0:T(8,128)(2,1)S(1)} %bitcast.33), kind=kLoop, calls=%fused_computation.10 | loop fusion | flops 917504 | bytes 1572864 | tf_op jit(solution)/shard_map/reduce_sum | solution.py:45
  67.7 7.6 %shard_map.66 = bf16[1024,1024]{1,0:T(8,128)(2,1)} custom-call(bf16[8,1024,128]{2,1,0:T(8,128)(2,1)} %get-tuple-element.9.q_ref, f32[8,1024,128]{2,1,0:T(8,128)} %shard_map.65.local_ref, f32[8,128,128]{2,1,0:T(8,128)} %bitcast.34, f32[8,1,128]{2,1,0:T(1,128)} %bitcast.39, bf16[1024,1024]{1,0:T(8,128)(2,1)} %w_ref.1), custom_call_target="tpu_custom_call" | custom-call | flops 2684354560 | bytes 10485760 | tf_op jit(solution)/shard_map/pallas_call | solution.py:156
  (8 shorter events, 0.1 us)
Async XLA Ops:
  11.7 2.7 %copy-start = (bf16[24,1024,128]{2,1,0:T(8,128)(2,1)}, bf16[24,1024,128]{2,1,0:T(8,128)(2,1)S(1)}, u32[]{:S(2)}) copy-start(bf16[24,1024,128]{2,1,0:T(8,128)(2,1)S(1)} %convert_bitcast_fusion.pq.pk.pv) | copy-start | bytes 18874372
  14.3 6.1 %collective-permute-start = (bf16[24,16,128]{2,1,0:T(8,128)(2,1)S(1)}, bf16[24,16,128]{2,1,0:T(8,128)(2,1)S(1)}, u32[]{:S(2)}, u32[]{:S(2)}) collective-permute-start(bf16[24,16,128]{2,1,0:T(8,128)(2,1)S(1)} %slice.20), channel_id=1, source_target_pairs={{0,1},{1,2},{2,3},{3,4},{4,5},{5,6},{6,7},{7,8},{8,9},{9,10},{10,1... | collective-permute-start | bytes 294920 | tf_op jit(solution)/shard_map/ppermute | solution.py:117
  20.4 0.6 copy-start.1
  31.7 12.5 %all-to-all-start = ((bf16[4,2,128,128]{3,2,1,0:T(8,128)(2,1)}), bf16[4,2,128,128]{3,2,1,0:T(8,128)(2,1)S(1)}, u32[]{:S(2)}, u32[]{:S(2)}) async-start(bf16[4,2,128,128]{3,2,1,0:T(8,128)(2,1)} %bitcast.38), calls=%async_computation | async-start | bytes 524288 | tf_op jit(solution)/shard_map/all_to_all | solution.py:26
  45.7 21.0 %all-to-all-start.1 = ((bf16[16,2,128,128]{3,2,1,0:T(8,128)(2,1)}), bf16[16,2,128,128]{3,2,1,0:T(8,128)(2,1)S(1)}, u32[]{:S(2)}, u32[]{:S(2)}) async-start(bf16[16,2,128,128]{3,2,1,0:T(8,128)(2,1)} %fusion.11), calls=%async_computation.1 | async-start | bytes 2097152 | tf_op jit(solution)/shard_map/all_to_all | solution.py:38

commit v19 on v15

--- a/solution.py
+++ b/solution.py
@@ -128,6 +128,7 @@
         out_specs=[slab(0, rows, DH)] * 3 + [slab(0, DH, DH)],
         out_shape=[mixed_shape] * 3 + [jax.ShapeDtypeStruct((H, DH, DH), jnp.bfloat16)],
         scratch_shapes=[pltpu.VMEM((rows + PAD, DH), jnp.float32)],
+        compiler_params=pltpu.CompilerParams(vmem_limit_bytes=16 * 1024 * 1024),
         cost_estimate=pl.CostEstimate(
             flops=H * (3 * rows * DH * 12 + 2 * rows * DH * DH),
             transcendentals=H * 3 * rows * DH,

time: 74.7 us -> 78.8 us (1.055)
  local copies, waits for them, and re-layouts: 3.44 us -> 9.64 us
  Pallas kernels: 28.4 us -> 26.3 us
    unnamed x4 -> x12, local copies, waits for them, and re-layouts: 3.25 us -> 9.45 us
    pallas_call x1, Pallas kernels: 10.6 us -> 8.56 us  [local(): pl.pallas_call(conv_kernel, grid=(H,), in_specs=[slab(0, rows, DH), slab(...]
  transfers between devices with their start and end apart: 3 -> 3, of which waited for: 3 -> 3; matrix products, arithmetic and copies ran while one was open for 0% -> 0% of each run, Pallas kernels for 14% -> 13%
where the time goes in v19:
time: 78.8 us; the launch traced here: 78.3 us
  Pallas kernels  26.3 us (33%)
  starting transfers between devices  14.9 us (19%)
  waiting for transfers between devices  13 us (16%)
  local copies, waits for them, and re-layouts  9.64 us (12%)
  matrix products  9.57 us (12%)
  other arithmetic  4.69 us (6%)
    pallas_call x1, Pallas kernels, local(): pl.pallas_call(local_kernel, grid=(H,), in_specs=[slab(0, rows, DH)] * 3,...  10.2 us
    dot_general x1, matrix products, local(): jnp.einsum('td,dje->jte', normed, w_qkv.reshape(width, slabs, DH), prefer...  9.57 us
    unnamed x12, local copies, waits for them, and re-layouts  9.45 us
    pallas_call x1, Pallas kernels, local(): pl.pallas_call(conv_kernel, grid=(H,), in_specs=[slab(0, rows, DH), slab(...  8.56 us
    pallas_call x1, Pallas kernels, local(): pl.pallas_call(out_kernel, grid=(rows // tile,), in_specs=[pl.BlockSpec((...  7.59 us
    all_to_all x1, waiting for transfers between devices, earlier_states(): mine = lax.all_to_all(quarters, 'sz', 0, 0).astype(jnp.float32)  6.51 us
    all_to_all x1, starting transfers between devices, earlier_states(): mine = lax.all_to_all(quarters, 'sz', 0, 0).astype(jnp.float32)  5.69 us
    all_to_all x1, starting transfers between devices, earlier_states(): lax.all_to_all(messages.astype(jnp.bfloat16).reshape((rows_count * count,...  5.36 us
  transfers between devices with their start and end apart: 3, of which 3 were waited for; matrix products, arithmetic and copies ran while one was open for 0% of the time, Pallas kernels for 13%

profile of v19, /device:TPU:0, one launch (start us, length us, event | category | flops | bytes accessed | tf_op | source)
XLA Modules:
  0.0 78.3 jit_solution(8624417198660750860)
XLA Ops:
  0.0 2.1 %fusion.3 = f32[1024]{0:T(1024)S(1)} fusion(bf16[1024,1024]{1,0:T(8,128)(2,1)} %param.6), kind=kLoop, calls=%fused_computation.6 | loop fusion | flops 3144704 | bytes 2101248 | tf_op jit(solution)/shard_map/reduce_sum | solution.py:106
  2.1 0.0 copy-start.3
  2.1 9.6 %convert_bitcast_fusion.pq.pk.pv = bf16[24,1024,128]{2,1,0:T(8,128)(2,1)S(1)} fusion(bf16[1024,1024]{1,0:T(8,128)(2,1)} %param.6, f32[1024]{0:T(1024)} %param.7, f32[1024]{0:T(1024)S(1)} %add_rsqrt_fusion, bf16[1024,3072]{1,0:T(8,128)(2,1)} %param.8), kind=kOutput, calls=%fused_computation.3 | convolution fusion | flops 6449790976 | bytes 14688256 | tf_op jit(solution)/shard_map/td,dje->jte/dot_general | solution.py:110
  11.7 0.0 copy-start
  11.7 2.7 %copy-done = bf16[24,1024,128]{2,1,0:T(8,128)(2,1)} copy-done((bf16[24,1024,128]{2,1,0:T(8,128)(2,1)}, bf16[24,1024,128]{2,1,0:T(8,128)(2,1)S(1)}, u32[]{:S(2)}) %copy-start) | copy-done | bytes 6291480
  14.4 3.9 %collective-permute-start = (bf16[24,3,128]{2,1,0:T(4,128)(2,1)S(1)}, bf16[24,3,128]{2,1,0:T(4,128)(2,1)S(1)}, u32[]{:S(2)}, u32[]{:S(2)}) collective-permute-start(bf16[24,3,128]{2,1,0:T(4,128)(2,1)S(1)} %slice.20), channel_id=1, source_target_pairs={{0,1},{1,2},{2,3},{3,4},{4,5},{5,6},{6,7},{7,8},{8,9},{9,10},{10,1... | collective-permute-start | bytes 55304 | tf_op jit(solution)/shard_map/ppermute | solution.py:116
  18.3 1.5 %collective-permute-done.eq.ek.ev = bf16[24,3,128]{2,1,0:T(4,128)(2,1)S(1)} collective-permute-done((bf16[24,3,128]{2,1,0:T(4,128)(2,1)S(1)}, bf16[24,3,128]{2,1,0:T(4,128)(2,1)S(1)}, u32[]{:S(2)}, u32[]{:S(2)}) %collective-permute-start) | collective-permute-done | bytes 18464 | tf_op jit(solution)/shard_map/ppermute | solution.py:116
  19.8 0.0 copy-done.3
  19.8 0.0 copy-start.1
  19.8 2.8 %copy-done.1 = bf16[24,1024,128]{2,1,0:T(8,128)(2,1)S(1)} copy-done((bf16[24,1024,128]{2,1,0:T(8,128)(2,1)S(1)}, bf16[24,1024,128]{2,1,0:T(8,128)(2,1)}, u32[]{:S(2)}) %copy-start.1) | copy-done | bytes 6291480
  22.6 8.6 %shard_map.64 = (bf16[8,1024,128]{2,1,0:T(8,128)(2,1)S(1)}, bf16[8,1024,128]{2,1,0:T(8,128)(2,1)S(1)}, bf16[8,1024,128]{2,1,0:T(8,128)(2,1)S(1)}, bf16[8,128,128]{2,1,0:T(8,128)(2,1)}) custom-call(bf16[24,1024,128]{2,1,0:T(8,128)(2,1)S(1)} %copy-done.1, bf16[24,1024,128]{2,1,0:T(8,128)(2,1)S(1)} %copy-done.1, bf16[24,1024,128]{2,1,0:T(8,128)(2,1)S(1)} %copy-done.1, ...), custom_call_target="tpu_custom_call" | custom-call | flops 306184192 | bytes 12582912 | tf_op jit(solution)/shard_map/pallas_call | solution.py:122
  31.1 0.0 copy-start.2
  31.1 1.3 %copy-done.2 = bf16[8,1024,128]{2,1,0:T(8,128)(2,1)} copy-done((bf16[8,1024,128]{2,1,0:T(8,128)(2,1)}, bf16[8,1024,128]{2,1,0:T(8,128)(2,1)S(1)}, u32[]{:S(2)}) %copy-start.2) | copy-done | bytes 2097176
  32.4 0.0 copy-start.4
  32.4 1.3 %copy-done.4 = bf16[8,1024,128]{2,1,0:T(8,128)(2,1)} copy-done((bf16[8,1024,128]{2,1,0:T(8,128)(2,1)}, bf16[8,1024,128]{2,1,0:T(8,128)(2,1)S(1)}, u32[]{:S(2)}) %copy-start.4) | copy-done | bytes 2097176
  33.8 0.0 copy-start.5
  33.8 1.4 %copy-done.5 = bf16[8,1024,128]{2,1,0:T(8,128)(2,1)} copy-done((bf16[8,1024,128]{2,1,0:T(8,128)(2,1)}, bf16[8,1024,128]{2,1,0:T(8,128)(2,1)S(1)}, u32[]{:S(2)}) %copy-start.5) | copy-done | bytes 2097176
  35.1 5.7 %all-to-all-start = ((bf16[4,2,128,128]{3,2,1,0:T(8,128)(2,1)}), bf16[4,2,128,128]{3,2,1,0:T(8,128)(2,1)S(1)}, u32[]{:S(2)}, u32[]{:S(2)}) async-start(bf16[4,2,128,128]{3,2,1,0:T(8,128)(2,1)} %bitcast.4), calls=%async_computation | async-start | bytes 524288 | tf_op jit(solution)/shard_map/all_to_all | solution.py:25
  40.8 0.1 mul.65
  40.9 0.1 mul.66
  41.0 6.5 %all-to-all-done = bf16[4,2,128,128]{3,2,1,0:T(8,128)(2,1)S(1)} async-done(((bf16[4,2,128,128]{3,2,1,0:T(8,128)(2,1)}), bf16[4,2,128,128]{3,2,1,0:T(8,128)(2,1)S(1)}, u32[]{:S(2)}, u32[]{:S(2)}) %all-to-all-start) | async-done | bytes 262176 | tf_op jit(solution)/shard_map/all_to_all | solution.py:25
  47.6 0.2 pad_maximum_fusion
  47.7 1.4 %fusion.11 = bf16[16,2,128,128]{3,2,1,0:T(8,128)(2,1)} fusion(f32[4,2,128,128]{3,2,1,0:T(8,128)S(1)} %get-tuple-element.16, f32[16]{0:T(128)S(1)} %mul.66, f32[4,2,128,128]{3,2,1,0:T(8,128)S(1)} %get-tuple-element.17), kind=kLoop, calls=%fused_computation.13 | loop fusion | flops 1572864 | bytes 2097216 | tf_op jit(solution)/shard_map/convert_element_type | solution.py:38
  49.2 5.4 %all-to-all-start.1 = ((bf16[16,2,128,128]{3,2,1,0:T(8,128)(2,1)}), bf16[16,2,128,128]{3,2,1,0:T(8,128)(2,1)S(1)}, u32[]{:S(2)}, u32[]{:S(2)}) async-start(bf16[16,2,128,128]{3,2,1,0:T(8,128)(2,1)} %fusion.11), calls=%async_computation.1 | async-start | bytes 2097152 | tf_op jit(solution)/shard_map/all_to_all | solution.py:37
  54.5 10.2 %shard_map.65.local_ref = f32[8,1024,128]{2,1,0:T(8,128)} custom-call(bf16[8,1024,128]{2,1,0:T(8,128)(2,1)} %copy-done.2, bf16[8,1024,128]{2,1,0:T(8,128)(2,1)} %copy-done.4, bf16[8,1024,128]{2,1,0:T(8,128)(2,1)} %copy-done.5), custom_call_target="tpu_custom_call" | custom-call | flops 2952790016 | bytes 10485760 | tf_op jit(solution)/shard_map/pallas_call | solution.py:140
  64.7 5.0 %all-to-all-done.1 = bf16[16,2,128,128]{3,2,1,0:T(8,128)(2,1)S(1)} async-done(((bf16[16,2,128,128]{3,2,1,0:T(8,128)(2,1)}), bf16[16,2,128,128]{3,2,1,0:T(8,128)(2,1)S(1)}, u32[]{:S(2)}, u32[]{:S(2)}) %all-to-all-start.1) | async-done | bytes 1048608 | tf_op jit(solution)/shard_map/all_to_all | solution.py:37
  69.7 1.0 %convert_reduce_fusion = f32[4,2,128,128]{3,2,1,0:T(8,128)} fusion(bf16[4,4,2,128,128]{4,3,2,1,0:T(8,128)(2,1)S(1)} %bitcast.36), kind=kLoop, calls=%fused_computation.10 | loop fusion | flops 917504 | bytes 1572864 | tf_op jit(solution)/shard_map/reduce_sum | solution.py:44
  70.7 7.6 %shard_map.66 = bf16[1024,1024]{1,0:T(8,128)(2,1)} custom-call(bf16[8,1024,128]{2,1,0:T(8,128)(2,1)} %copy-done.2, f32[8,1024,128]{2,1,0:T(8,128)} %shard_map.65.local_ref, f32[8,128,128]{2,1,0:T(8,128)} %bitcast.37, f32[8,1,128]{2,1,0:T(1,128)} %bitcast.38, bf16[1024,1024]{1,0:T(8,128)(2,1)} %w_ref.1), custom_call_target="tpu_custom_call" | custom-call | flops 2684354560 | bytes 10485760 | tf_op jit(solution)/shard_map/pallas_call | solution.py:156
  (8 shorter events, 0.1 us)
Async XLA Ops:
  2.1 17.7 %copy-start.3 = (f32[4,3072]{1,0:T(4,128)S(1)}, f32[4,3072]{1,0:T(4,128)}, u32[]{:S(2)}) copy-start(f32[4,3072]{1,0:T(4,128)} %param.9) | copy-start | bytes 147460
  11.7 2.7 %copy-start = (bf16[24,1024,128]{2,1,0:T(8,128)(2,1)}, bf16[24,1024,128]{2,1,0:T(8,128)(2,1)S(1)}, u32[]{:S(2)}) copy-start(bf16[24,1024,128]{2,1,0:T(8,128)(2,1)S(1)} %convert_bitcast_fusion.pq.pk.pv) | copy-start | bytes 18874372
  14.4 5.4 %collective-permute-start = (bf16[24,3,128]{2,1,0:T(4,128)(2,1)S(1)}, bf16[24,3,128]{2,1,0:T(4,128)(2,1)S(1)}, u32[]{:S(2)}, u32[]{:S(2)}) collective-permute-start(bf16[24,3,128]{2,1,0:T(4,128)(2,1)S(1)} %slice.20), channel_id=1, source_target_pairs={{0,1},{1,2},{2,3},{3,4},{4,5},{5,6},{6,7},{7,8},{8,9},{9,10},{10,1... | collective-permute-start | bytes 55304 | tf_op jit(solution)/shard_map/ppermute | solution.py:116
  19.8 2.8 %copy-start.1 = (bf16[24,1024,128]{2,1,0:T(8,128)(2,1)S(1)}, bf16[24,1024,128]{2,1,0:T(8,128)(2,1)}, u32[]{:S(2)}) copy-start(bf16[24,1024,128]{2,1,0:T(8,128)(2,1)} %copy-done) | copy-start | bytes 18874372
  31.1 1.3 %copy-start.2 = (bf16[8,1024,128]{2,1,0:T(8,128)(2,1)}, bf16[8,1024,128]{2,1,0:T(8,128)(2,1)S(1)}, u32[]{:S(2)}) copy-start(bf16[8,1024,128]{2,1,0:T(8,128)(2,1)S(1)} %get-tuple-element.9.q_ref) | copy-start | bytes 6291460
  32.4 1.3 %copy-start.4 = (bf16[8,1024,128]{2,1,0:T(8,128)(2,1)}, bf16[8,1024,128]{2,1,0:T(8,128)(2,1)S(1)}, u32[]{:S(2)}) copy-start(bf16[8,1024,128]{2,1,0:T(8,128)(2,1)S(1)} %get-tuple-element.10.k_ref) | copy-start | bytes 6291460
  33.8 1.4 %copy-start.5 = (bf16[8,1024,128]{2,1,0:T(8,128)(2,1)}, bf16[8,1024,128]{2,1,0:T(8,128)(2,1)S(1)}, u32[]{:S(2)}) copy-start(bf16[8,1024,128]{2,1,0:T(8,128)(2,1)S(1)} %get-tuple-element.11.v_ref) | copy-start | bytes 6291460
  35.1 12.4 %all-to-all-start = ((bf16[4,2,128,128]{3,2,1,0:T(8,128)(2,1)}), bf16[4,2,128,128]{3,2,1,0:T(8,128)(2,1)S(1)}, u32[]{:S(2)}, u32[]{:S(2)}) async-start(bf16[4,2,128,128]{3,2,1,0:T(8,128)(2,1)} %bitcast.4), calls=%async_computation | async-start | bytes 524288 | tf_op jit(solution)/shard_map/all_to_all | solution.py:25
  49.2 20.5 %all-to-all-start.1 = ((bf16[16,2,128,128]{3,2,1,0:T(8,128)(2,1)}), bf16[16,2,128,128]{3,2,1,0:T(8,128)(2,1)S(1)}, u32[]{:S(2)}, u32[]{:S(2)}) async-start(bf16[16,2,128,128]{3,2,1,0:T(8,128)(2,1)} %fusion.11), calls=%async_computation.1 | async-start | bytes 2097152 | tf_op jit(solution)/shard_map/all_to_all | solution.py:37

commit v20 on v15

--- a/solution.py
+++ b/solution.py
@@ -165,6 +165,7 @@
         out_specs=pl.BlockSpec((tile, width), lambda i: (i, 0)),
         out_shape=jax.ShapeDtypeStruct((rows, width), jnp.bfloat16),
         scratch_shapes=[pltpu.VMEM((tile, H * DH), jnp.bfloat16)],
+        compiler_params=pltpu.CompilerParams(vmem_limit_bytes=24 * 1024 * 1024),
         cost_estimate=pl.CostEstimate(
             flops=H * 4 * rows * DH * DH + 2 * rows * width * width,
             transcendentals=H * rows,

time: 74.7 us -> 75.4 us (level)
  local copies, waits for them, and re-layouts: 3.44 us -> 7.25 us
  Pallas kernels: 28.4 us -> 26.2 us
  other arithmetic: 4.62 us -> 3.78 us
    unnamed x4 -> x12, local copies, waits for them, and re-layouts: 3.25 us -> 7.06 us
    pallas_call x1, Pallas kernels: 7.59 us -> 5.27 us  [local(): pl.pallas_call(out_kernel, grid=(rows // tile,), in_specs=[pl.BlockSpec((...]
    reduce_sum x1, other arithmetic: 0.98 us -> 0.16 us  [earlier_states(): return jnp.sum(received, 0).reshape(state.shape)]
where the time goes in v20:
time: 75.4 us; the launch traced here: 74.7 us
  Pallas kernels  26.2 us (35%)
  starting transfers between devices  15 us (20%)
  waiting for transfers between devices  12.8 us (17%)
  matrix products  9.56 us (13%)
  local copies, waits for them, and re-layouts  7.25 us (10%)
  other arithmetic  3.78 us (5%)
    pallas_call x1, Pallas kernels, local(): pl.pallas_call(conv_kernel, grid=(H,), in_specs=[slab(0, rows, DH), slab(...  10.6 us
    pallas_call x1, Pallas kernels, local(): pl.pallas_call(local_kernel, grid=(H,), in_specs=[slab(0, rows, DH)] * 3,...  10.3 us
    dot_general x1, matrix products, local(): jnp.einsum('td,dje->jte', normed, w_qkv.reshape(width, slabs, DH), prefer...  9.56 us
    unnamed x12, local copies, waits for them, and re-layouts  7.06 us
    all_to_all x1, waiting for transfers between devices, earlier_states(): mine = lax.all_to_all(quarters, 'sz', 0, 0).astype(jnp.float32)  6.51 us
    all_to_all x1, starting transfers between devices, earlier_states(): mine = lax.all_to_all(quarters, 'sz', 0, 0).astype(jnp.float32)  5.7 us
    all_to_all x1, starting transfers between devices, earlier_states(): lax.all_to_all(messages.astype(jnp.bfloat16).reshape((rows_count * count,...  5.36 us
    pallas_call x1, Pallas kernels, local(): pl.pallas_call(out_kernel, grid=(rows // tile,), in_specs=[pl.BlockSpec((...  5.27 us
  transfers between devices with their start and end apart: 3, of which 3 were waited for; matrix products, arithmetic and copies ran while one was open for 0% of the time, Pallas kernels for 14%

profile of v20, /device:TPU:0, one launch (start us, length us, event | category | flops | bytes accessed | tf_op | source)
XLA Modules:
  0.0 74.7 jit_solution(3133957328070568016)
XLA Ops:
  0.0 2.1 %fusion.3 = f32[1024]{0:T(1024)S(1)} fusion(bf16[1024,1024]{1,0:T(8,128)(2,1)} %param.6), kind=kLoop, calls=%fused_computation.6 | loop fusion | flops 3144704 | bytes 2101248 | tf_op jit(solution)/shard_map/reduce_sum | solution.py:106
  2.1 9.6 %convert_bitcast_fusion.pq.pk.pv = bf16[24,1024,128]{2,1,0:T(8,128)(2,1)S(1)} fusion(bf16[1024,1024]{1,0:T(8,128)(2,1)} %param.6, f32[1024]{0:T(1024)} %param.7, f32[1024]{0:T(1024)S(1)} %add_rsqrt_fusion, bf16[1024,3072]{1,0:T(8,128)(2,1)} %param.8), kind=kOutput, calls=%fused_computation.3 | convolution fusion | flops 6449790976 | bytes 14688256 | tf_op jit(solution)/shard_map/td,dje->jte/dot_general | solution.py:110
  11.7 0.0 copy-start.4
  11.7 2.7 %copy-done.4 = bf16[24,1024,128]{2,1,0:T(8,128)(2,1)} copy-done((bf16[24,1024,128]{2,1,0:T(8,128)(2,1)}, bf16[24,1024,128]{2,1,0:T(8,128)(2,1)S(1)}, u32[]{:S(2)}) %copy-start.4) | copy-done | bytes 6291480
  14.3 3.9 %collective-permute-start = (bf16[24,3,128]{2,1,0:T(4,128)(2,1)S(1)}, bf16[24,3,128]{2,1,0:T(4,128)(2,1)S(1)}, u32[]{:S(2)}, u32[]{:S(2)}) collective-permute-start(bf16[24,3,128]{2,1,0:T(4,128)(2,1)S(1)} %slice.20), channel_id=1, source_target_pairs={{0,1},{1,2},{2,3},{3,4},{4,5},{5,6},{6,7},{7,8},{8,9},{9,10},{10,1... | collective-permute-start | bytes 55304 | tf_op jit(solution)/shard_map/ppermute | solution.py:116
  18.3 1.5 %collective-permute-done.eq.ek.ev = bf16[24,3,128]{2,1,0:T(4,128)(2,1)S(1)} collective-permute-done((bf16[24,3,128]{2,1,0:T(4,128)(2,1)S(1)}, bf16[24,3,128]{2,1,0:T(4,128)(2,1)S(1)}, u32[]{:S(2)}, u32[]{:S(2)}) %collective-permute-start) | collective-permute-done | bytes 18464 | tf_op jit(solution)/shard_map/ppermute | solution.py:116
  19.8 0.0 copy-start.5
  19.8 0.6 copy-done.5
  20.4 10.6 %shard_map.64 = (bf16[8,1024,128]{2,1,0:T(8,128)(2,1)}, bf16[8,1024,128]{2,1,0:T(8,128)(2,1)}, bf16[8,1024,128]{2,1,0:T(8,128)(2,1)}, bf16[8,128,128]{2,1,0:T(8,128)(2,1)}) custom-call(bf16[24,1024,128]{2,1,0:T(8,128)(2,1)} %copy-done.4, bf16[24,1024,128]{2,1,0:T(8,128)(2,1)} %copy-done.4, bf16[24,1024,128]{2,1,0:T(8,128)(2,1)} %copy-done.4, ...), custom_call_target="tpu_custom_call" | custom-call | flops 306184192 | bytes 12582912 | tf_op jit(solution)/shard_map/pallas_call | solution.py:122
  31.0 5.7 %all-to-all-start = ((bf16[4,2,128,128]{3,2,1,0:T(8,128)(2,1)}), bf16[4,2,128,128]{3,2,1,0:T(8,128)(2,1)S(1)}, u32[]{:S(2)}, u32[]{:S(2)}) async-start(bf16[4,2,128,128]{3,2,1,0:T(8,128)(2,1)} %bitcast.39), calls=%async_computation | async-start | bytes 524288 | tf_op jit(solution)/shard_map/all_to_all | solution.py:25
  36.7 0.1 mul.65
  36.7 0.1 mul.66
  36.8 6.5 %all-to-all-done = bf16[4,2,128,128]{3,2,1,0:T(8,128)(2,1)S(1)} async-done(((bf16[4,2,128,128]{3,2,1,0:T(8,128)(2,1)}), bf16[4,2,128,128]{3,2,1,0:T(8,128)(2,1)S(1)}, u32[]{:S(2)}, u32[]{:S(2)}) %all-to-all-start) | async-done | bytes 262176 | tf_op jit(solution)/shard_map/all_to_all | solution.py:25
  43.5 0.2 pad_maximum_fusion
  43.6 1.3 %fusion.11 = bf16[16,2,128,128]{3,2,1,0:T(8,128)(2,1)} fusion(f32[4,2,128,128]{3,2,1,0:T(8,128)S(1)} %get-tuple-element.16, f32[16]{0:T(128)S(1)} %mul.66, f32[4,2,128,128]{3,2,1,0:T(8,128)S(1)} %get-tuple-element.17), kind=kLoop, calls=%fused_computation.13 | loop fusion | flops 1572864 | bytes 2097216 | tf_op jit(solution)/shard_map/convert_element_type | solution.py:38
  44.9 5.4 %all-to-all-start.1 = ((bf16[16,2,128,128]{3,2,1,0:T(8,128)(2,1)}), bf16[16,2,128,128]{3,2,1,0:T(8,128)(2,1)S(1)}, u32[]{:S(2)}, u32[]{:S(2)}) async-start(bf16[16,2,128,128]{3,2,1,0:T(8,128)(2,1)} %fusion.11), calls=%async_computation.1 | async-start | bytes 2097152 | tf_op jit(solution)/shard_map/all_to_all | solution.py:37
  50.3 0.0 copy-start.1
  50.3 0.0 copy-start.3
  50.3 10.3 %shard_map.65.local_ref = f32[8,1024,128]{2,1,0:T(8,128)} custom-call(bf16[8,1024,128]{2,1,0:T(8,128)(2,1)} %get-tuple-element.9.q_ref, bf16[8,1024,128]{2,1,0:T(8,128)(2,1)} %get-tuple-element.10.k_ref, bf16[8,1024,128]{2,1,0:T(8,128)(2,1)} %get-tuple-element.11.v_ref), custom_call_target="tpu_custom_call" | custom-call | flops 2952790016 | bytes 10485760 | tf_op jit(solution)/shard_map/pallas_call | solution.py:139
  60.6 4.8 %all-to-all-done.1 = bf16[16,2,128,128]{3,2,1,0:T(8,128)(2,1)S(1)} async-done(((bf16[16,2,128,128]{3,2,1,0:T(8,128)(2,1)}), bf16[16,2,128,128]{3,2,1,0:T(8,128)(2,1)S(1)}, u32[]{:S(2)}, u32[]{:S(2)}) %all-to-all-start.1) | async-done | bytes 1048608 | tf_op jit(solution)/shard_map/all_to_all | solution.py:37
  65.5 0.2 convert_reduce_fusion
  65.6 0.0 copy-done.1
  65.6 0.0 copy-done.3
  65.6 0.0 copy-start
  65.6 2.2 %copy-done = f32[8,1024,128]{2,1,0:T(8,128)S(1)} copy-done((f32[8,1024,128]{2,1,0:T(8,128)S(1)}, f32[8,1024,128]{2,1,0:T(8,128)}, u32[]{:S(2)}) %copy-start) | copy-done | bytes 4194328
  67.8 0.0 copy-start.2
  67.8 1.6 %copy-done.2 = bf16[8,1024,128]{2,1,0:T(8,128)(2,1)S(1)} copy-done((bf16[8,1024,128]{2,1,0:T(8,128)(2,1)S(1)}, bf16[8,1024,128]{2,1,0:T(8,128)(2,1)}, u32[]{:S(2)}) %copy-start.2) | copy-done | bytes 2097176
  69.4 5.3 %shard_map.66 = bf16[1024,1024]{1,0:T(8,128)(2,1)} custom-call(bf16[8,1024,128]{2,1,0:T(8,128)(2,1)S(1)} %copy-done.2, f32[8,1024,128]{2,1,0:T(8,128)S(1)} %copy-done, f32[8,128,128]{2,1,0:T(8,128)S(1)} %bitcast.33, f32[8,1,128]{2,1,0:T(1,128)S(1)} %bitcast.34, bf16[1024,1024]{1,0:T(8,128)(2,1)S(1)} %copy-done.1), custom_call_target="tpu_custom_call" | custom-call | flops 2684354560 | bytes 10485760 | tf_op jit(solution)/shard_map/pallas_call | solution.py:155
  (8 shorter events, 0.1 us)
Async XLA Ops:
  11.7 2.7 %copy-start.4 = (bf16[24,1024,128]{2,1,0:T(8,128)(2,1)}, bf16[24,1024,128]{2,1,0:T(8,128)(2,1)S(1)}, u32[]{:S(2)}) copy-start(bf16[24,1024,128]{2,1,0:T(8,128)(2,1)S(1)} %convert_bitcast_fusion.pq.pk.pv) | copy-start | bytes 18874372
  14.3 5.4 %collective-permute-start = (bf16[24,3,128]{2,1,0:T(4,128)(2,1)S(1)}, bf16[24,3,128]{2,1,0:T(4,128)(2,1)S(1)}, u32[]{:S(2)}, u32[]{:S(2)}) collective-permute-start(bf16[24,3,128]{2,1,0:T(4,128)(2,1)S(1)} %slice.20), channel_id=1, source_target_pairs={{0,1},{1,2},{2,3},{3,4},{4,5},{5,6},{6,7},{7,8},{8,9},{9,10},{10,1... | collective-permute-start | bytes 55304 | tf_op jit(solution)/shard_map/ppermute | solution.py:116
  19.8 0.6 copy-start.5
  31.0 12.4 %all-to-all-start = ((bf16[4,2,128,128]{3,2,1,0:T(8,128)(2,1)}), bf16[4,2,128,128]{3,2,1,0:T(8,128)(2,1)S(1)}, u32[]{:S(2)}, u32[]{:S(2)}) async-start(bf16[4,2,128,128]{3,2,1,0:T(8,128)(2,1)} %bitcast.39), calls=%async_computation | async-start | bytes 524288 | tf_op jit(solution)/shard_map/all_to_all | solution.py:25
  44.9 20.5 %all-to-all-start.1 = ((bf16[16,2,128,128]{3,2,1,0:T(8,128)(2,1)}), bf16[16,2,128,128]{3,2,1,0:T(8,128)(2,1)S(1)}, u32[]{:S(2)}, u32[]{:S(2)}) async-start(bf16[16,2,128,128]{3,2,1,0:T(8,128)(2,1)} %fusion.11), calls=%async_computation.1 | async-start | bytes 2097152 | tf_op jit(solution)/shard_map/all_to_all | solution.py:37
  50.3 15.3 %copy-start.1 = (bf16[1024,1024]{1,0:T(8,128)(2,1)S(1)}, bf16[1024,1024]{1,0:T(8,128)(2,1)}, u32[]{:S(2)}) copy-start(bf16[1024,1024]{1,0:T(8,128)(2,1)} %w_ref.1) | copy-start | bytes 6291460
  50.3 15.3 %copy-start.3 = (f32[1024]{0:T(1024)S(1)}, f32[1024]{0:T(1024)}, u32[]{:S(2)}) copy-start(f32[1024]{0:T(1024)} %param.10) | copy-start | bytes 12292
  65.6 2.2 %copy-start = (f32[8,1024,128]{2,1,0:T(8,128)S(1)}, f32[8,1024,128]{2,1,0:T(8,128)}, u32[]{:S(2)}) copy-start(f32[8,1024,128]{2,1,0:T(8,128)} %shard_map.65.local_ref) | copy-start | bytes 12582916
  67.8 1.6 %copy-start.2 = (bf16[8,1024,128]{2,1,0:T(8,128)(2,1)S(1)}, bf16[8,1024,128]{2,1,0:T(8,128)(2,1)}, u32[]{:S(2)}) copy-start(bf16[8,1024,128]{2,1,0:T(8,128)(2,1)} %get-tuple-element.9.q_ref) | copy-start | bytes 6291460

commit v21 on v14

--- a/solution.py
+++ b/solution.py
@@ -20,7 +20,7 @@
     return hi.astype(jnp.bfloat16), (x - hi).astype(jnp.bfloat16)
 
 
-def earlier_states(state, before_second=None):
+def earlier_states(state, before_second):
     count = lax.axis_size("sz")
     rows_count = lax.axis_size("sy")
     quarters = state.astype(jnp.bfloat16).reshape((count, -1) + state.shape[1:])
@@ -36,9 +36,7 @@
         later_row[:, None, None, None, None] * row_total[None, None]
         + same_row[:, None, None, None, None] * jnp.stack(before)[None]
     )
-    messages = messages.astype(jnp.bfloat16)
-    if before_second is not None:
-        messages, before_second = lax.optimization_barrier((messages, before_second()))
+    messages, early_work = lax.optimization_barrier((messages.astype(jnp.bfloat16), before_second()))
     received = lax.all_to_all(
         messages.reshape((rows_count * count,) + row_total.shape),
         ("sy", "sz"),
@@ -46,7 +44,7 @@
         0,
     )
     received = received.reshape((rows_count, count) + row_total.shape).astype(jnp.float32)
-    return jnp.sum(received, 0).reshape(state.shape), before_second
+    return jnp.sum(received, 0).reshape(state.shape), early_work
 
 
 def conv_kernel(count, with_state, *refs):
@@ -54,7 +52,7 @@
     outs, buf = refs[3 * count : 4 * count], refs[-1]
     rows = projs[0].shape[0]
     for proj, early, taps, out in zip(projs, earlies, tapss, outs):
-        buf[0:PAD, :] = early[...].astype(jnp.float32)
+        buf[PAD - (KW - 1) : PAD, :] = early[...].astype(jnp.float32)
         buf[PAD:, :] = proj[...].astype(jnp.float32)
         summed = jnp.zeros((rows, DH), jnp.float32)
         for offset in range(KW):
@@ -63,23 +61,23 @@
     if with_state:
         refs[4 * count][...] = lax.dot_general(
             outs[0][...], outs[1][...], (((0,), (0,)), ((), ())), preferred_element_type=jnp.float32
-        )
-
-
-def conv_call(projected, earlier, taps, shifts, base, with_state):
+        ).astype(jnp.bfloat16)
+
+
+def conv_call(projected, earlier, taps, shifts, with_state):
     count = len(shifts)
     rows = projected.shape[1]
-    mixed = jax.ShapeDtypeStruct((H, rows, DH), jnp.bfloat16)
     out_specs = [slab(0, rows, DH)] * count
-    out_shape = [mixed] * count
+    out_shape = [jax.ShapeDtypeStruct((H, rows, DH), jnp.bfloat16)] * count
     if with_state:
         out_specs.append(slab(0, DH, DH))
-        out_shape.append(jax.ShapeDtypeStruct((H, DH, DH), jnp.float32))
+        out_shape.append(jax.ShapeDtypeStruct((H, DH, DH), jnp.bfloat16))
     return pl.pallas_call(
         functools.partial(conv_kernel, count, with_state),
         grid=(H,),
         in_specs=[slab(shift, rows, DH) for shift in shifts]
-        + [slab(base + shift, PAD, DH) for shift in shifts] * 2,
+        + [slab(shift, KW - 1, DH) for shift in shifts]
+        + [slab(shift, KW, DH) for shift in shifts],
         out_specs=out_specs,
         out_shape=out_shape,
         scratch_shapes=[pltpu.VMEM((rows + PAD, DH), jnp.float32)],
@@ -149,14 +147,11 @@
     earlier_rows = lax.ppermute(
         projected[:, rows - (KW - 1) :, :], seq_axes, [(i, i + 1) for i in range(count - 1)]
     )
-    earlier_rows = jnp.pad(earlier_rows, ((0, 0), (PAD - (KW - 1), 0), (0, 0)))
-    taps = jnp.pad(
-        conv_weight.reshape(KW, slabs, DH).transpose(1, 0, 2), ((0, 0), (0, PAD - KW), (0, 0))
-    )
-
-    key, value, state = conv_call(projected, earlier_rows, taps, (H, 2 * H), 0, True)
+    taps = conv_weight.reshape(KW, slabs, DH).transpose(1, 0, 2)
+
+    key, value, state = conv_call(projected, earlier_rows, taps, (H, 2 * H), True)
     prefix, (query,) = earlier_states(
-        state, lambda: conv_call(projected, earlier_rows, taps, (0,), 0, False)
+        state, lambda: conv_call(projected, earlier_rows, taps, (0,), False)
     )
 
     block = min(BLOCK, rows)
@@ -173,7 +168,7 @@
         ),
     )(query, key, value)
 
-    tile = min(256, rows)
+    tile = min(512, rows)
     out = pl.pallas_call(
         out_kernel,
         grid=(rows // tile,),

time: 78.4 us -> 76 us (0.969)
  other arithmetic: 6.41 us -> 4.63 us
    convert_element_type x2 -> x1, other arithmetic: 3.13 us -> 1.35 us  [earlier_states(): messages.astype(jnp.bfloat16)]
    pad x2 -> x0, local copies, waits for them, and re-layouts: 1.29 us -> none  [the longest x1 0.65 us: local(): jnp.pad(conv_weight.reshape(KW, slabs, DH).transpose(1, 0, 2), ((0, 0), (...]
  transfers between devices with their start and end apart: 3 -> 3, of which waited for: 2 -> 2; matrix products, arithmetic and copies ran while one was open for 1% -> 0% of each run, Pallas kernels for 22% -> 23%
where the time goes in v21:
time: 76 us; the launch traced here: 75.2 us
  Pallas kernels  33.2 us (44%)
  starting transfers between devices  17.3 us (23%)
  matrix products  9.56 us (13%)
  waiting for transfers between devices  7.18 us (9%)
  other arithmetic  4.63 us (6%)
  local copies, waits for them, and re-layouts  3.29 us (4%)
    pallas_call x2, Pallas kernels, conv_call(): pl.pallas_call(functools.partial(conv_kernel, count, with_state), grid=(H...  15.4 us
    pallas_call x1, Pallas kernels, local(): pl.pallas_call(local_kernel, grid=(H,), in_specs=[slab(0, rows, DH)] * 3,...  10.2 us
    dot_general x1, matrix products, local(): jnp.einsum('td,dje->jte', normed, w_qkv.reshape(width, slabs, DH), prefer...  9.56 us
    all_to_all x1, starting transfers between devices, earlier_states(): lax.all_to_all(messages.reshape((rows_count * count,) + row_total.shape),...  7.72 us
    pallas_call x1, Pallas kernels, local(): pl.pallas_call(out_kernel, grid=(rows // tile,), in_specs=[pl.BlockSpec((...  7.59 us
    all_to_all x1, waiting for transfers between devices, earlier_states(): lax.all_to_all(messages.reshape((rows_count * count,) + row_total.shape),...  5.69 us
    all_to_all x1, starting transfers between devices, earlier_states(): mine = lax.all_to_all(quarters, 'sz', 0, 0).astype(jnp.float32)  5.69 us
    ppermute x1, starting transfers between devices, local(): lax.ppermute(projected[:, rows - (KW - 1):, :], seq_axes, [(i, i + 1) for...  3.91 us
  transfers between devices with their start and end apart: 3, of which 2 were waited for; matrix products, arithmetic and copies ran while one was open for 0% of the time, Pallas kernels for 23%

profile of v21, /device:TPU:0, one launch (start us, length us, event | category | flops | bytes accessed | tf_op | source)
XLA Modules:
  0.0 75.2 jit_solution(7911097542930792226)
XLA Ops:
  0.0 2.1 %fusion.3 = f32[1024]{0:T(1024)S(1)} fusion(bf16[1024,1024]{1,0:T(8,128)(2,1)} %param.6), kind=kLoop, calls=%fused_computation.6 | loop fusion | flops 3144704 | bytes 2101248 | tf_op jit(solution)/shard_map/reduce_sum | solution.py:137
  2.1 9.6 %convert_bitcast_fusion.refs_0_.refs_1_ = bf16[24,1024,128]{2,1,0:T(8,128)(2,1)S(1)} fusion(bf16[1024,1024]{1,0:T(8,128)(2,1)} %param.6, f32[1024]{0:T(1024)} %param.7, f32[1024]{0:T(1024)S(1)} %add_rsqrt_fusion, bf16[1024,3072]{1,0:T(8,128)(2,1)} %param.8), kind=kOutput, calls=%fused_computation.3 | convolution fusion | flops 6449790976 | bytes 14688256 | tf_op jit(solution)/shard_map/td,dje->jte/dot_general | solution.py:141
  11.7 0.0 copy-start
  11.7 2.6 %copy-done = bf16[24,1024,128]{2,1,0:T(8,128)(2,1)} copy-done((bf16[24,1024,128]{2,1,0:T(8,128)(2,1)}, bf16[24,1024,128]{2,1,0:T(8,128)(2,1)S(1)}, u32[]{:S(2)}) %copy-start) | copy-done | bytes 6291480
  14.3 3.9 %collective-permute-start = (bf16[24,3,128]{2,1,0:T(4,128)(2,1)S(1)}, bf16[24,3,128]{2,1,0:T(4,128)(2,1)S(1)}, u32[]{:S(2)}, u32[]{:S(2)}) collective-permute-start(bf16[24,3,128]{2,1,0:T(4,128)(2,1)S(1)} %slice.20), channel_id=1, source_target_pairs={{0,1},{1,2},{2,3},{3,4},{4,5},{5,6},{6,7},{7,8},{8,9},{9,10},{10,1... | collective-permute-start | bytes 55304 | tf_op jit(solution)/shard_map/ppermute | solution.py:147
  18.3 1.5 %collective-permute-done.refs_2_.refs_3_.refs_1_ = bf16[24,3,128]{2,1,0:T(4,128)(2,1)S(1)} collective-permute-done((bf16[24,3,128]{2,1,0:T(4,128)(2,1)S(1)}, bf16[24,3,128]{2,1,0:T(4,128)(2,1)S(1)}, u32[]{:S(2)}, u32[]{:S(2)}) %collective-permute-start) | collective-permute-done | bytes 18464 | tf_op jit(solution)/shard_map/ppermute | solution.py:147
  19.7 0.0 copy-start.1
  19.8 0.6 copy-done.1
  20.4 8.5 %shard_map.64 = (bf16[8,1024,128]{2,1,0:T(8,128)(2,1)}, bf16[8,1024,128]{2,1,0:T(8,128)(2,1)}, bf16[8,128,128]{2,1,0:T(8,128)(2,1)}) custom-call(bf16[24,1024,128]{2,1,0:T(8,128)(2,1)} %copy-done, bf16[24,1024,128]{2,1,0:T(8,128)(2,1)} %copy-done, bf16[24,3,128]{2,1,0:T(4,128)(2,1)} %copy-done.1, bf16[24,3,128]{2,1,0:T(4,128)(2,1)} %copy-done.1, ...), custom_call_target="tpu_custom_call" | custom-call | flops 562036736 | bytes 8388608 | tf_op jit(solution)/shard_map/pallas_call | solution.py:75
  28.8 5.7 %all-to-all-start = ((bf16[4,2,128,128]{3,2,1,0:T(8,128)(2,1)}), bf16[4,2,128,128]{3,2,1,0:T(8,128)(2,1)S(1)}, u32[]{:S(2)}, u32[]{:S(2)}) async-start(bf16[4,2,128,128]{3,2,1,0:T(8,128)(2,1)} %bitcast.31), calls=%async_computation | async-start | bytes 524288 | tf_op jit(solution)/shard_map/all_to_all | solution.py:27
  34.5 6.9 %shard_map.65.q_ref = bf16[8,1024,128]{2,1,0:T(8,128)(2,1)} custom-call(bf16[24,1024,128]{2,1,0:T(8,128)(2,1)} %copy-done, bf16[24,3,128]{2,1,0:T(4,128)(2,1)} %copy-done.1, f32[24,4,128]{2,1,0:T(4,128)} %bitcast.30), custom_call_target="tpu_custom_call" | custom-call | flops 281018368 | bytes 4194304 | tf_op jit(solution)/shard_map/pallas_call | solution.py:75
  41.4 0.0 all-to-all-done
  41.5 0.2 pad_maximum_fusion
  41.7 1.3 %add_convert_fusion = bf16[4,4,2,128,128]{4,3,2,1,0:T(8,128)(2,1)} fusion(f32[4,2,128,128]{3,2,1,0:T(8,128)S(1)} %get-tuple-element.18, f32[4]{0:T(128)S(1)} %compare_convert_fusion, f32[4,2,128,128]{3,2,1,0:T(8,128)S(1)} %get-tuple-element.19), kind=kLoop, calls=%fused_computation.11 | loop fusion | flops 1572864 | bytes 2097168 | tf_op jit(solution)/shard_map/convert_element_type | solution.py:39
  43.0 7.7 %all-to-all-start.1 = ((bf16[16,2,128,128]{3,2,1,0:T(8,128)(2,1)}), bf16[16,2,128,128]{3,2,1,0:T(8,128)(2,1)S(1)}, u32[]{:S(2)}, u32[]{:S(2)}) async-start(bf16[16,2,128,128]{3,2,1,0:T(8,128)(2,1)} %bitcast.7), calls=%async_computation.1 | async-start | bytes 2097152 | tf_op jit(solution)/shard_map/all_to_all | solution.py:40
  50.8 10.2 %shard_map.66.local_ref = f32[8,1024,128]{2,1,0:T(8,128)} custom-call(bf16[8,1024,128]{2,1,0:T(8,128)(2,1)} %shard_map.65.q_ref, bf16[8,1024,128]{2,1,0:T(8,128)(2,1)} %get-tuple-element.12.k_ref, bf16[8,1024,128]{2,1,0:T(8,128)(2,1)} %get-tuple-element.13.v_ref), custom_call_target="tpu_custom_call" | custom-call | flops 2952790016 | bytes 10485760 | tf_op jit(solution)/shard_map/pallas_call | solution.py:158
  61.0 5.7 %all-to-all-done.1 = bf16[16,2,128,128]{3,2,1,0:T(8,128)(2,1)S(1)} async-done(((bf16[16,2,128,128]{3,2,1,0:T(8,128)(2,1)}), bf16[16,2,128,128]{3,2,1,0:T(8,128)(2,1)S(1)}, u32[]{:S(2)}, u32[]{:S(2)}) %all-to-all-start.1) | async-done | bytes 1048608 | tf_op jit(solution)/shard_map/all_to_all | solution.py:40
  66.7 1.0 %convert_reduce_fusion = f32[4,2,128,128]{3,2,1,0:T(8,128)} fusion(bf16[4,4,2,128,128]{4,3,2,1,0:T(8,128)(2,1)S(1)} %bitcast.26), kind=kLoop, calls=%fused_computation.10 | loop fusion | flops 917504 | bytes 1572864 | tf_op jit(solution)/shard_map/reduce_sum | solution.py:47
  67.6 7.6 %shard_map.67 = bf16[1024,1024]{1,0:T(8,128)(2,1)} custom-call(bf16[8,1024,128]{2,1,0:T(8,128)(2,1)} %shard_map.65.q_ref, f32[8,1024,128]{2,1,0:T(8,128)} %shard_map.66.local_ref, f32[8,128,128]{2,1,0:T(8,128)} %bitcast.27, f32[8,1,128]{2,1,0:T(1,128)} %bitcast.32, bf16[1024,1024]{1,0:T(8,128)(2,1)} %w_ref.1), custom_call_target="tpu_custom_call" | custom-call | flops 2684354560 | bytes 10485760 | tf_op jit(solution)/shard_map/pallas_call | solution.py:172
  (8 shorter events, 0.1 us)
Async XLA Ops:
  11.7 2.7 %copy-start = (bf16[24,1024,128]{2,1,0:T(8,128)(2,1)}, bf16[24,1024,128]{2,1,0:T(8,128)(2,1)S(1)}, u32[]{:S(2)}) copy-start(bf16[24,1024,128]{2,1,0:T(8,128)(2,1)S(1)} %convert_bitcast_fusion.refs_0_.refs_1_) | copy-start | bytes 18874372
  14.3 5.4 %collective-permute-start = (bf16[24,3,128]{2,1,0:T(4,128)(2,1)S(1)}, bf16[24,3,128]{2,1,0:T(4,128)(2,1)S(1)}, u32[]{:S(2)}, u32[]{:S(2)}) collective-permute-start(bf16[24,3,128]{2,1,0:T(4,128)(2,1)S(1)} %slice.20), channel_id=1, source_target_pairs={{0,1},{1,2},{2,3},{3,4},{4,5},{5,6},{6,7},{7,8},{8,9},{9,10},{10,1... | collective-permute-start | bytes 55304 | tf_op jit(solution)/shard_map/ppermute | solution.py:147
  19.7 0.6 copy-start.1
  28.8 12.6 %all-to-all-start = ((bf16[4,2,128,128]{3,2,1,0:T(8,128)(2,1)}), bf16[4,2,128,128]{3,2,1,0:T(8,128)(2,1)S(1)}, u32[]{:S(2)}, u32[]{:S(2)}) async-start(bf16[4,2,128,128]{3,2,1,0:T(8,128)(2,1)} %bitcast.31), calls=%async_computation | async-start | bytes 524288 | tf_op jit(solution)/shard_map/all_to_all | solution.py:27
  43.0 23.6 %all-to-all-start.1 = ((bf16[16,2,128,128]{3,2,1,0:T(8,128)(2,1)}), bf16[16,2,128,128]{3,2,1,0:T(8,128)(2,1)S(1)}, u32[]{:S(2)}, u32[]{:S(2)}) async-start(bf16[16,2,128,128]{3,2,1,0:T(8,128)(2,1)} %bitcast.7), calls=%async_computation.1 | async-start | bytes 2097152 | tf_op jit(solution)/shard_map/all_to_all | solution.py:40

commit v22 on v15

--- a/solution.py
+++ b/solution.py
@@ -45,17 +45,22 @@
 
 
 def conv_kernel(pq, pk, pv, eq, ek, ev, tq, tk, tv, oq, ok, ov, state_ref, buf):
-    rows = pq.shape[0]
-    for proj, early, taps, out in ((pq, eq, tq, oq), (pk, ek, tk, ok), (pv, ev, tv, ov)):
-        buf[PAD - (KW - 1) : PAD, :] = early[...].astype(jnp.float32)
-        buf[PAD:, :] = proj[...].astype(jnp.float32)
-        summed = jnp.zeros((rows, DH), jnp.float32)
-        for offset in range(KW):
-            summed = summed + taps[offset : offset + 1, :] * buf[pl.ds(PAD - offset, rows), :]
-        out[...] = (summed * jax.nn.sigmoid(summed)).astype(out.dtype)
-    state_ref[...] = lax.dot_general(
-        ok[...], ov[...], (((0,), (0,)), ((), ())), preferred_element_type=jnp.float32
-    ).astype(state_ref.dtype)
+    rows = pq.shape[1]
+    for g in range(pq.shape[0]):
+        for proj, early, taps, out in ((pq, eq, tq, oq), (pk, ek, tk, ok), (pv, ev, tv, ov)):
+            buf[PAD - (KW - 1) : PAD, :] = early[g].astype(jnp.float32)
+            buf[PAD:, :] = proj[g].astype(jnp.float32)
+            summed = jnp.zeros((rows, DH), jnp.float32)
+            for offset in range(KW):
+                summed = summed + taps[g, offset : offset + 1, :] * buf[pl.ds(PAD - offset, rows), :]
+            out[g] = (summed * jax.nn.sigmoid(summed)).astype(out.dtype)
+        state_ref[g] = lax.dot_general(
+            ok[g], ov[g], (((0,), (0,)), ((), ())), preferred_element_type=jnp.float32
+        ).astype(state_ref.dtype)
+
+
+def group_slab(group, shift, rows, cols):
+    return pl.BlockSpec((group, rows, cols), lambda h: (h + shift // group, 0, 0))
 
 
 def local_kernel(q_ref, k_ref, v_ref, out_ref):
@@ -121,11 +126,11 @@
     mixed_shape = jax.ShapeDtypeStruct((H, rows, DH), jnp.bfloat16)
     query, key, value, state = pl.pallas_call(
         conv_kernel,
-        grid=(H,),
-        in_specs=[slab(0, rows, DH), slab(H, rows, DH), slab(2 * H, rows, DH)]
-        + [slab(0, KW - 1, DH), slab(H, KW - 1, DH), slab(2 * H, KW - 1, DH)]
-        + [slab(0, KW, DH), slab(H, KW, DH), slab(2 * H, KW, DH)],
-        out_specs=[slab(0, rows, DH)] * 3 + [slab(0, DH, DH)],
+        grid=(H // 2,),
+        in_specs=[group_slab(2, shift, rows, DH) for shift in (0, H, 2 * H)]
+        + [group_slab(2, shift, KW - 1, DH) for shift in (0, H, 2 * H)]
+        + [group_slab(2, shift, KW, DH) for shift in (0, H, 2 * H)],
+        out_specs=[group_slab(2, 0, rows, DH)] * 3 + [group_slab(2, 0, DH, DH)],
         out_shape=[mixed_shape] * 3 + [jax.ShapeDtypeStruct((H, DH, DH), jnp.bfloat16)],
         scratch_shapes=[pltpu.VMEM((rows + PAD, DH), jnp.float32)],
         cost_estimate=pl.CostEstimate(

time: 74.7 us -> 73.7 us (0.987)
  Pallas kernels: 28.4 us -> 27.5 us
    pallas_call x1, Pallas kernels: 10.6 us -> 9.75 us  [local(): pl.pallas_call(conv_kernel, grid=(H // 2,), in_specs=[group_slab(2, shift...]
where the time goes in v22:
time: 73.7 us; the launch traced here: 73.2 us
  Pallas kernels  27.5 us (37%)
  starting transfers between devices  15 us (20%)
  waiting for transfers between devices  13 us (18%)
  matrix products  9.56 us (13%)
  other arithmetic  4.62 us (6%)
  local copies, waits for them, and re-layouts  3.44 us (5%)
    pallas_call x1, Pallas kernels, local(): pl.pallas_call(local_kernel, grid=(H,), in_specs=[slab(0, rows, DH)] * 3,...  10.2 us
    pallas_call x1, Pallas kernels, local(): pl.pallas_call(conv_kernel, grid=(H // 2,), in_specs=[group_slab(2, shift...  9.75 us
    dot_general x1, matrix products, local(): jnp.einsum('td,dje->jte', normed, w_qkv.reshape(width, slabs, DH), prefer...  9.56 us
    pallas_call x1, Pallas kernels, local(): pl.pallas_call(out_kernel, grid=(rows // tile,), in_specs=[pl.BlockSpec((...  7.59 us
    all_to_all x1, waiting for transfers between devices, earlier_states(): mine = lax.all_to_all(quarters, 'sz', 0, 0).astype(jnp.float32)  6.51 us
    all_to_all x1, starting transfers between devices, earlier_states(): mine = lax.all_to_all(quarters, 'sz', 0, 0).astype(jnp.float32)  5.7 us
    all_to_all x1, starting transfers between devices, earlier_states(): lax.all_to_all(messages.astype(jnp.bfloat16).reshape((rows_count * count,...  5.36 us
    all_to_all x1, waiting for transfers between devices, earlier_states(): lax.all_to_all(messages.astype(jnp.bfloat16).reshape((rows_count * count,...  4.96 us
  transfers between devices with their start and end apart: 3, of which 3 were waited for; matrix products, arithmetic and copies ran while one was open for 0% of the time, Pallas kernels for 14%

profile of v22, /device:TPU:0, one launch (start us, length us, event | category | flops | bytes accessed | tf_op | source)
XLA Modules:
  0.0 73.2 jit_solution(11708789300239617399)
XLA Ops:
  0.0 2.1 %fusion.3 = f32[1024]{0:T(1024)S(1)} fusion(bf16[1024,1024]{1,0:T(8,128)(2,1)} %param.6), kind=kLoop, calls=%fused_computation.6 | loop fusion | flops 3144704 | bytes 2101248 | tf_op jit(solution)/shard_map/reduce_sum | solution.py:111
  2.1 9.6 %convert_bitcast_fusion.pq.pk.pv = bf16[24,1024,128]{2,1,0:T(8,128)(2,1)S(1)} fusion(bf16[1024,1024]{1,0:T(8,128)(2,1)} %param.6, f32[1024]{0:T(1024)} %param.7, f32[1024]{0:T(1024)S(1)} %add_rsqrt_fusion, bf16[1024,3072]{1,0:T(8,128)(2,1)} %param.8), kind=kOutput, calls=%fused_computation.3 | convolution fusion | flops 6449790976 | bytes 14688256 | tf_op jit(solution)/shard_map/td,dje->jte/dot_general | solution.py:115
  11.7 0.0 copy-start
  11.7 2.6 %copy-done = bf16[24,1024,128]{2,1,0:T(8,128)(2,1)} copy-done((bf16[24,1024,128]{2,1,0:T(8,128)(2,1)}, bf16[24,1024,128]{2,1,0:T(8,128)(2,1)S(1)}, u32[]{:S(2)}) %copy-start) | copy-done | bytes 6291480
  14.3 3.9 %collective-permute-start = (bf16[24,3,128]{2,1,0:T(4,128)(2,1)S(1)}, bf16[24,3,128]{2,1,0:T(4,128)(2,1)S(1)}, u32[]{:S(2)}, u32[]{:S(2)}) collective-permute-start(bf16[24,3,128]{2,1,0:T(4,128)(2,1)S(1)} %slice.20), channel_id=1, source_target_pairs={{0,1},{1,2},{2,3},{3,4},{4,5},{5,6},{6,7},{7,8},{8,9},{9,10},{10,1... | collective-permute-start | bytes 55304 | tf_op jit(solution)/shard_map/ppermute | solution.py:121
  18.3 1.5 %collective-permute-done.eq.ek.ev = bf16[24,3,128]{2,1,0:T(4,128)(2,1)S(1)} collective-permute-done((bf16[24,3,128]{2,1,0:T(4,128)(2,1)S(1)}, bf16[24,3,128]{2,1,0:T(4,128)(2,1)S(1)}, u32[]{:S(2)}, u32[]{:S(2)}) %collective-permute-start) | collective-permute-done | bytes 18464 | tf_op jit(solution)/shard_map/ppermute | solution.py:121
  19.7 0.0 copy-start.1
  19.8 0.6 copy-done.1
  20.4 9.7 %shard_map.64 = (bf16[8,1024,128]{2,1,0:T(8,128)(2,1)}, bf16[8,1024,128]{2,1,0:T(8,128)(2,1)}, bf16[8,1024,128]{2,1,0:T(8,128)(2,1)}, bf16[8,128,128]{2,1,0:T(8,128)(2,1)}) custom-call(bf16[24,1024,128]{2,1,0:T(8,128)(2,1)} %copy-done, bf16[24,1024,128]{2,1,0:T(8,128)(2,1)} %copy-done, bf16[24,1024,128]{2,1,0:T(8,128)(2,1)} %copy-done, ...), custom_call_target="tpu_custom_call" | custom-call | flops 306184192 | bytes 12582912 | tf_op jit(solution)/shard_map/pallas_call | solution.py:127
  30.1 5.7 %all-to-all-start = ((bf16[4,2,128,128]{3,2,1,0:T(8,128)(2,1)}), bf16[4,2,128,128]{3,2,1,0:T(8,128)(2,1)S(1)}, u32[]{:S(2)}, u32[]{:S(2)}) async-start(bf16[4,2,128,128]{3,2,1,0:T(8,128)(2,1)} %bitcast.38), calls=%async_computation | async-start | bytes 524288 | tf_op jit(solution)/shard_map/all_to_all | solution.py:25
  35.8 0.1 mul.65
  35.9 0.1 mul.66
  36.0 6.5 %all-to-all-done = bf16[4,2,128,128]{3,2,1,0:T(8,128)(2,1)S(1)} async-done(((bf16[4,2,128,128]{3,2,1,0:T(8,128)(2,1)}), bf16[4,2,128,128]{3,2,1,0:T(8,128)(2,1)S(1)}, u32[]{:S(2)}, u32[]{:S(2)}) %all-to-all-start) | async-done | bytes 262176 | tf_op jit(solution)/shard_map/all_to_all | solution.py:25
  42.6 0.2 pad_maximum_fusion
  42.7 1.3 %fusion.11 = bf16[16,2,128,128]{3,2,1,0:T(8,128)(2,1)} fusion(f32[4,2,128,128]{3,2,1,0:T(8,128)S(1)} %get-tuple-element.16, f32[16]{0:T(128)S(1)} %mul.66, f32[4,2,128,128]{3,2,1,0:T(8,128)S(1)} %get-tuple-element.17), kind=kLoop, calls=%fused_computation.13 | loop fusion | flops 1572864 | bytes 2097216 | tf_op jit(solution)/shard_map/convert_element_type | solution.py:38
  44.1 5.4 %all-to-all-start.1 = ((bf16[16,2,128,128]{3,2,1,0:T(8,128)(2,1)}), bf16[16,2,128,128]{3,2,1,0:T(8,128)(2,1)S(1)}, u32[]{:S(2)}, u32[]{:S(2)}) async-start(bf16[16,2,128,128]{3,2,1,0:T(8,128)(2,1)} %fusion.11), calls=%async_computation.1 | async-start | bytes 2097152 | tf_op jit(solution)/shard_map/all_to_all | solution.py:37
  49.4 10.2 %shard_map.65.local_ref = f32[8,1024,128]{2,1,0:T(8,128)} custom-call(bf16[8,1024,128]{2,1,0:T(8,128)(2,1)} %get-tuple-element.9.q_ref, bf16[8,1024,128]{2,1,0:T(8,128)(2,1)} %get-tuple-element.10.k_ref, bf16[8,1024,128]{2,1,0:T(8,128)(2,1)} %get-tuple-element.11.v_ref), custom_call_target="tpu_custom_call" | custom-call | flops 2952790016 | bytes 10485760 | tf_op jit(solution)/shard_map/pallas_call | solution.py:144
  59.6 5.0 %all-to-all-done.1 = bf16[16,2,128,128]{3,2,1,0:T(8,128)(2,1)S(1)} async-done(((bf16[16,2,128,128]{3,2,1,0:T(8,128)(2,1)}), bf16[16,2,128,128]{3,2,1,0:T(8,128)(2,1)S(1)}, u32[]{:S(2)}, u32[]{:S(2)}) %all-to-all-start.1) | async-done | bytes 1048608 | tf_op jit(solution)/shard_map/all_to_all | solution.py:37
  64.6 1.0 %convert_reduce_fusion = f32[4,2,128,128]{3,2,1,0:T(8,128)} fusion(bf16[4,4,2,128,128]{4,3,2,1,0:T(8,128)(2,1)S(1)} %bitcast.33), kind=kLoop, calls=%fused_computation.10 | loop fusion | flops 917504 | bytes 1572864 | tf_op jit(solution)/shard_map/reduce_sum | solution.py:44
  65.6 7.6 %shard_map.66 = bf16[1024,1024]{1,0:T(8,128)(2,1)} custom-call(bf16[8,1024,128]{2,1,0:T(8,128)(2,1)} %get-tuple-element.9.q_ref, f32[8,1024,128]{2,1,0:T(8,128)} %shard_map.65.local_ref, f32[8,128,128]{2,1,0:T(8,128)} %bitcast.34, f32[8,1,128]{2,1,0:T(1,128)} %bitcast.39, bf16[1024,1024]{1,0:T(8,128)(2,1)} %w_ref.1), custom_call_target="tpu_custom_call" | custom-call | flops 2684354560 | bytes 10485760 | tf_op jit(solution)/shard_map/pallas_call | solution.py:160
  (8 shorter events, 0.1 us)
Async XLA Ops:
  11.7 2.7 %copy-start = (bf16[24,1024,128]{2,1,0:T(8,128)(2,1)}, bf16[24,1024,128]{2,1,0:T(8,128)(2,1)S(1)}, u32[]{:S(2)}) copy-start(bf16[24,1024,128]{2,1,0:T(8,128)(2,1)S(1)} %convert_bitcast_fusion.pq.pk.pv) | copy-start | bytes 18874372
  14.3 5.4 %collective-permute-start = (bf16[24,3,128]{2,1,0:T(4,128)(2,1)S(1)}, bf16[24,3,128]{2,1,0:T(4,128)(2,1)S(1)}, u32[]{:S(2)}, u32[]{:S(2)}) collective-permute-start(bf16[24,3,128]{2,1,0:T(4,128)(2,1)S(1)} %slice.20), channel_id=1, source_target_pairs={{0,1},{1,2},{2,3},{3,4},{4,5},{5,6},{6,7},{7,8},{8,9},{9,10},{10,1... | collective-permute-start | bytes 55304 | tf_op jit(solution)/shard_map/ppermute | solution.py:121
  19.7 0.6 copy-start.1
  30.1 12.4 %all-to-all-start = ((bf16[4,2,128,128]{3,2,1,0:T(8,128)(2,1)}), bf16[4,2,128,128]{3,2,1,0:T(8,128)(2,1)S(1)}, u32[]{:S(2)}, u32[]{:S(2)}) async-start(bf16[4,2,128,128]{3,2,1,0:T(8,128)(2,1)} %bitcast.38), calls=%async_computation | async-start | bytes 524288 | tf_op jit(solution)/shard_map/all_to_all | solution.py:25
  44.1 20.5 %all-to-all-start.1 = ((bf16[16,2,128,128]{3,2,1,0:T(8,128)(2,1)}), bf16[16,2,128,128]{3,2,1,0:T(8,128)(2,1)S(1)}, u32[]{:S(2)}, u32[]{:S(2)}) async-start(bf16[16,2,128,128]{3,2,1,0:T(8,128)(2,1)} %fusion.11), calls=%async_computation.1 | async-start | bytes 2097152 | tf_op jit(solution)/shard_map/all_to_all | solution.py:37

commit v23 on v22

--- a/solution.py
+++ b/solution.py
@@ -126,11 +126,11 @@
     mixed_shape = jax.ShapeDtypeStruct((H, rows, DH), jnp.bfloat16)
     query, key, value, state = pl.pallas_call(
         conv_kernel,
-        grid=(H // 2,),
-        in_specs=[group_slab(2, shift, rows, DH) for shift in (0, H, 2 * H)]
-        + [group_slab(2, shift, KW - 1, DH) for shift in (0, H, 2 * H)]
-        + [group_slab(2, shift, KW, DH) for shift in (0, H, 2 * H)],
-        out_specs=[group_slab(2, 0, rows, DH)] * 3 + [group_slab(2, 0, DH, DH)],
+        grid=(H // 4,),
+        in_specs=[group_slab(4, shift, rows, DH) for shift in (0, H, 2 * H)]
+        + [group_slab(4, shift, KW - 1, DH) for shift in (0, H, 2 * H)]
+        + [group_slab(4, shift, KW, DH) for shift in (0, H, 2 * H)],
+        out_specs=[group_slab(4, 0, rows, DH)] * 3 + [group_slab(4, 0, DH, DH)],
         out_shape=[mixed_shape] * 3 + [jax.ShapeDtypeStruct((H, DH, DH), jnp.bfloat16)],
         scratch_shapes=[pltpu.VMEM((rows + PAD, DH), jnp.float32)],
         cost_estimate=pl.CostEstimate(

time: 73.7 us -> 74.2 us (level)
  no operation moved by 1% of the time
where the time goes in v23:
time: 74.2 us; the launch traced here: 73.7 us
  Pallas kernels  28.1 us (38%)
  starting transfers between devices  15 us (20%)
  waiting for transfers between devices  13 us (18%)
  matrix products  9.56 us (13%)
  other arithmetic  4.62 us (6%)
  local copies, waits for them, and re-layouts  3.44 us (5%)
    pallas_call x1, Pallas kernels, local(): pl.pallas_call(conv_kernel, grid=(H // 4,), in_specs=[group_slab(4, shift...  10.3 us
    pallas_call x1, Pallas kernels, local(): pl.pallas_call(local_kernel, grid=(H,), in_specs=[slab(0, rows, DH)] * 3,...  10.2 us
    dot_general x1, matrix products, local(): jnp.einsum('td,dje->jte', normed, w_qkv.reshape(width, slabs, DH), prefer...  9.56 us
    pallas_call x1, Pallas kernels, local(): pl.pallas_call(out_kernel, grid=(rows // tile,), in_specs=[pl.BlockSpec((...  7.59 us
    all_to_all x1, waiting for transfers between devices, earlier_states(): mine = lax.all_to_all(quarters, 'sz', 0, 0).astype(jnp.float32)  6.51 us
    all_to_all x1, starting transfers between devices, earlier_states(): mine = lax.all_to_all(quarters, 'sz', 0, 0).astype(jnp.float32)  5.7 us
    all_to_all x1, starting transfers between devices, earlier_states(): lax.all_to_all(messages.astype(jnp.bfloat16).reshape((rows_count * count,...  5.36 us
    all_to_all x1, waiting for transfers between devices, earlier_states(): lax.all_to_all(messages.astype(jnp.bfloat16).reshape((rows_count * count,...  4.97 us
  transfers between devices with their start and end apart: 3, of which 3 were waited for; matrix products, arithmetic and copies ran while one was open for 0% of the time, Pallas kernels for 14%

profile of v23, /device:TPU:0, one launch (start us, length us, event | category | flops | bytes accessed | tf_op | source)
XLA Modules:
  0.0 73.7 jit_solution(8373341308318332648)
XLA Ops:
  0.0 2.1 %fusion.3 = f32[1024]{0:T(1024)S(1)} fusion(bf16[1024,1024]{1,0:T(8,128)(2,1)} %param.6), kind=kLoop, calls=%fused_computation.6 | loop fusion | flops 3144704 | bytes 2101248 | tf_op jit(solution)/shard_map/reduce_sum | solution.py:111
  2.1 9.6 %convert_bitcast_fusion.pq.pk.pv = bf16[24,1024,128]{2,1,0:T(8,128)(2,1)S(1)} fusion(bf16[1024,1024]{1,0:T(8,128)(2,1)} %param.6, f32[1024]{0:T(1024)} %param.7, f32[1024]{0:T(1024)S(1)} %add_rsqrt_fusion, bf16[1024,3072]{1,0:T(8,128)(2,1)} %param.8), kind=kOutput, calls=%fused_computation.3 | convolution fusion | flops 6449790976 | bytes 14688256 | tf_op jit(solution)/shard_map/td,dje->jte/dot_general | solution.py:115
  11.7 0.0 copy-start
  11.7 2.6 %copy-done = bf16[24,1024,128]{2,1,0:T(8,128)(2,1)} copy-done((bf16[24,1024,128]{2,1,0:T(8,128)(2,1)}, bf16[24,1024,128]{2,1,0:T(8,128)(2,1)S(1)}, u32[]{:S(2)}) %copy-start) | copy-done | bytes 6291480
  14.3 3.9 %collective-permute-start = (bf16[24,3,128]{2,1,0:T(4,128)(2,1)S(1)}, bf16[24,3,128]{2,1,0:T(4,128)(2,1)S(1)}, u32[]{:S(2)}, u32[]{:S(2)}) collective-permute-start(bf16[24,3,128]{2,1,0:T(4,128)(2,1)S(1)} %slice.20), channel_id=1, source_target_pairs={{0,1},{1,2},{2,3},{3,4},{4,5},{5,6},{6,7},{7,8},{8,9},{9,10},{10,1... | collective-permute-start | bytes 55304 | tf_op jit(solution)/shard_map/ppermute | solution.py:121
  18.3 1.5 %collective-permute-done.eq.ek.ev = bf16[24,3,128]{2,1,0:T(4,128)(2,1)S(1)} collective-permute-done((bf16[24,3,128]{2,1,0:T(4,128)(2,1)S(1)}, bf16[24,3,128]{2,1,0:T(4,128)(2,1)S(1)}, u32[]{:S(2)}, u32[]{:S(2)}) %collective-permute-start) | collective-permute-done | bytes 18464 | tf_op jit(solution)/shard_map/ppermute | solution.py:121
  19.7 0.0 copy-start.1
  19.8 0.6 copy-done.1
  20.4 10.3 %shard_map.64 = (bf16[8,1024,128]{2,1,0:T(8,128)(2,1)}, bf16[8,1024,128]{2,1,0:T(8,128)(2,1)}, bf16[8,1024,128]{2,1,0:T(8,128)(2,1)}, bf16[8,128,128]{2,1,0:T(8,128)(2,1)}) custom-call(bf16[24,1024,128]{2,1,0:T(8,128)(2,1)} %copy-done, bf16[24,1024,128]{2,1,0:T(8,128)(2,1)} %copy-done, bf16[24,1024,128]{2,1,0:T(8,128)(2,1)} %copy-done, ...), custom_call_target="tpu_custom_call" | custom-call | flops 306184192 | bytes 12582912 | tf_op jit(solution)/shard_map/pallas_call | solution.py:127
  30.6 5.7 %all-to-all-start = ((bf16[4,2,128,128]{3,2,1,0:T(8,128)(2,1)}), bf16[4,2,128,128]{3,2,1,0:T(8,128)(2,1)S(1)}, u32[]{:S(2)}, u32[]{:S(2)}) async-start(bf16[4,2,128,128]{3,2,1,0:T(8,128)(2,1)} %bitcast.38), calls=%async_computation | async-start | bytes 524288 | tf_op jit(solution)/shard_map/all_to_all | solution.py:25
  36.3 0.1 mul.65
  36.4 0.1 mul.66
  36.5 6.5 %all-to-all-done = bf16[4,2,128,128]{3,2,1,0:T(8,128)(2,1)S(1)} async-done(((bf16[4,2,128,128]{3,2,1,0:T(8,128)(2,1)}), bf16[4,2,128,128]{3,2,1,0:T(8,128)(2,1)S(1)}, u32[]{:S(2)}, u32[]{:S(2)}) %all-to-all-start) | async-done | bytes 262176 | tf_op jit(solution)/shard_map/all_to_all | solution.py:25
  43.1 0.2 pad_maximum_fusion
  43.3 1.3 %fusion.11 = bf16[16,2,128,128]{3,2,1,0:T(8,128)(2,1)} fusion(f32[4,2,128,128]{3,2,1,0:T(8,128)S(1)} %get-tuple-element.16, f32[16]{0:T(128)S(1)} %mul.66, f32[4,2,128,128]{3,2,1,0:T(8,128)S(1)} %get-tuple-element.17), kind=kLoop, calls=%fused_computation.13 | loop fusion | flops 1572864 | bytes 2097216 | tf_op jit(solution)/shard_map/convert_element_type | solution.py:38
  44.6 5.4 %all-to-all-start.1 = ((bf16[16,2,128,128]{3,2,1,0:T(8,128)(2,1)}), bf16[16,2,128,128]{3,2,1,0:T(8,128)(2,1)S(1)}, u32[]{:S(2)}, u32[]{:S(2)}) async-start(bf16[16,2,128,128]{3,2,1,0:T(8,128)(2,1)} %fusion.11), calls=%async_computation.1 | async-start | bytes 2097152 | tf_op jit(solution)/shard_map/all_to_all | solution.py:37
  50.0 10.2 %shard_map.65.local_ref = f32[8,1024,128]{2,1,0:T(8,128)} custom-call(bf16[8,1024,128]{2,1,0:T(8,128)(2,1)} %get-tuple-element.9.q_ref, bf16[8,1024,128]{2,1,0:T(8,128)(2,1)} %get-tuple-element.10.k_ref, bf16[8,1024,128]{2,1,0:T(8,128)(2,1)} %get-tuple-element.11.v_ref), custom_call_target="tpu_custom_call" | custom-call | flops 2952790016 | bytes 10485760 | tf_op jit(solution)/shard_map/pallas_call | solution.py:144
  60.2 5.0 %all-to-all-done.1 = bf16[16,2,128,128]{3,2,1,0:T(8,128)(2,1)S(1)} async-done(((bf16[16,2,128,128]{3,2,1,0:T(8,128)(2,1)}), bf16[16,2,128,128]{3,2,1,0:T(8,128)(2,1)S(1)}, u32[]{:S(2)}, u32[]{:S(2)}) %all-to-all-start.1) | async-done | bytes 1048608 | tf_op jit(solution)/shard_map/all_to_all | solution.py:37
  65.1 1.0 %convert_reduce_fusion = f32[4,2,128,128]{3,2,1,0:T(8,128)} fusion(bf16[4,4,2,128,128]{4,3,2,1,0:T(8,128)(2,1)S(1)} %bitcast.33), kind=kLoop, calls=%fused_computation.10 | loop fusion | flops 917504 | bytes 1572864 | tf_op jit(solution)/shard_map/reduce_sum | solution.py:44
  66.1 7.6 %shard_map.66 = bf16[1024,1024]{1,0:T(8,128)(2,1)} custom-call(bf16[8,1024,128]{2,1,0:T(8,128)(2,1)} %get-tuple-element.9.q_ref, f32[8,1024,128]{2,1,0:T(8,128)} %shard_map.65.local_ref, f32[8,128,128]{2,1,0:T(8,128)} %bitcast.34, f32[8,1,128]{2,1,0:T(1,128)} %bitcast.39, bf16[1024,1024]{1,0:T(8,128)(2,1)} %w_ref.1), custom_call_target="tpu_custom_call" | custom-call | flops 2684354560 | bytes 10485760 | tf_op jit(solution)/shard_map/pallas_call | solution.py:160
  (8 shorter events, 0.1 us)
Async XLA Ops:
  11.7 2.7 %copy-start = (bf16[24,1024,128]{2,1,0:T(8,128)(2,1)}, bf16[24,1024,128]{2,1,0:T(8,128)(2,1)S(1)}, u32[]{:S(2)}) copy-start(bf16[24,1024,128]{2,1,0:T(8,128)(2,1)S(1)} %convert_bitcast_fusion.pq.pk.pv) | copy-start | bytes 18874372
  14.3 5.4 %collective-permute-start = (bf16[24,3,128]{2,1,0:T(4,128)(2,1)S(1)}, bf16[24,3,128]{2,1,0:T(4,128)(2,1)S(1)}, u32[]{:S(2)}, u32[]{:S(2)}) collective-permute-start(bf16[24,3,128]{2,1,0:T(4,128)(2,1)S(1)} %slice.20), channel_id=1, source_target_pairs={{0,1},{1,2},{2,3},{3,4},{4,5},{5,6},{6,7},{7,8},{8,9},{9,10},{10,1... | collective-permute-start | bytes 55304 | tf_op jit(solution)/shard_map/ppermute | solution.py:121
  19.7 0.6 copy-start.1
  30.6 12.4 %all-to-all-start = ((bf16[4,2,128,128]{3,2,1,0:T(8,128)(2,1)}), bf16[4,2,128,128]{3,2,1,0:T(8,128)(2,1)S(1)}, u32[]{:S(2)}, u32[]{:S(2)}) async-start(bf16[4,2,128,128]{3,2,1,0:T(8,128)(2,1)} %bitcast.38), calls=%async_computation | async-start | bytes 524288 | tf_op jit(solution)/shard_map/all_to_all | solution.py:25
  44.6 20.5 %all-to-all-start.1 = ((bf16[16,2,128,128]{3,2,1,0:T(8,128)(2,1)}), bf16[16,2,128,128]{3,2,1,0:T(8,128)(2,1)S(1)}, u32[]{:S(2)}, u32[]{:S(2)}) async-start(bf16[16,2,128,128]{3,2,1,0:T(8,128)(2,1)} %fusion.11), calls=%async_computation.1 | async-start | bytes 2097152 | tf_op jit(solution)/shard_map/all_to_all | solution.py:37

commit v24 on v22

--- a/solution.py
+++ b/solution.py
@@ -156,7 +156,7 @@
 
     prefix = earlier_states(state)
 
-    tile = min(512, rows)
+    tile = min(1024, rows)
     out = pl.pallas_call(
         out_kernel,
         grid=(rows // tile,),

time: 73.7 us -> 74.7 us (1.014)
  Pallas kernels: 27.5 us -> 28.6 us
    pallas_call x1, Pallas kernels: 7.59 us -> 8.62 us  [local(): pl.pallas_call(out_kernel, grid=(rows // tile,), in_specs=[pl.BlockSpec((...]
where the time goes in v24:
time: 74.7 us; the launch traced here: 74.2 us
  Pallas kernels  28.6 us (38%)
  starting transfers between devices  15 us (20%)
  waiting for transfers between devices  13 us (17%)
  matrix products  9.56 us (13%)
  other arithmetic  4.62 us (6%)
  local copies, waits for them, and re-layouts  3.44 us (5%)
    pallas_call x1, Pallas kernels, local(): pl.pallas_call(local_kernel, grid=(H,), in_specs=[slab(0, rows, DH)] * 3,...  10.2 us
    pallas_call x1, Pallas kernels, local(): pl.pallas_call(conv_kernel, grid=(H // 2,), in_specs=[group_slab(2, shift...  9.75 us
    dot_general x1, matrix products, local(): jnp.einsum('td,dje->jte', normed, w_qkv.reshape(width, slabs, DH), prefer...  9.56 us
    pallas_call x1, Pallas kernels, local(): pl.pallas_call(out_kernel, grid=(rows // tile,), in_specs=[pl.BlockSpec((...  8.62 us
    all_to_all x1, waiting for transfers between devices, earlier_states(): mine = lax.all_to_all(quarters, 'sz', 0, 0).astype(jnp.float32)  6.51 us
    all_to_all x1, starting transfers between devices, earlier_states(): mine = lax.all_to_all(quarters, 'sz', 0, 0).astype(jnp.float32)  5.7 us
    all_to_all x1, starting transfers between devices, earlier_states(): lax.all_to_all(messages.astype(jnp.bfloat16).reshape((rows_count * count,...  5.36 us
    all_to_all x1, waiting for transfers between devices, earlier_states(): lax.all_to_all(messages.astype(jnp.bfloat16).reshape((rows_count * count,...  4.96 us
  transfers between devices with their start and end apart: 3, of which 3 were waited for; matrix products, arithmetic and copies ran while one was open for 0% of the time, Pallas kernels for 14%

profile of v24, /device:TPU:0, one launch (start us, length us, event | category | flops | bytes accessed | tf_op | source)
XLA Modules:
  0.0 74.2 jit_solution(3369476108013721222)
XLA Ops:
  0.0 2.1 %fusion.3 = f32[1024]{0:T(1024)S(1)} fusion(bf16[1024,1024]{1,0:T(8,128)(2,1)} %param.6), kind=kLoop, calls=%fused_computation.6 | loop fusion | flops 3144704 | bytes 2101248 | tf_op jit(solution)/shard_map/reduce_sum | solution.py:111
  2.1 9.6 %convert_bitcast_fusion.pq.pk.pv = bf16[24,1024,128]{2,1,0:T(8,128)(2,1)S(1)} fusion(bf16[1024,1024]{1,0:T(8,128)(2,1)} %param.6, f32[1024]{0:T(1024)} %param.7, f32[1024]{0:T(1024)S(1)} %add_rsqrt_fusion, bf16[1024,3072]{1,0:T(8,128)(2,1)} %param.8), kind=kOutput, calls=%fused_computation.3 | convolution fusion | flops 6449790976 | bytes 14688256 | tf_op jit(solution)/shard_map/td,dje->jte/dot_general | solution.py:115
  11.7 0.0 copy-start
  11.7 2.6 %copy-done = bf16[24,1024,128]{2,1,0:T(8,128)(2,1)} copy-done((bf16[24,1024,128]{2,1,0:T(8,128)(2,1)}, bf16[24,1024,128]{2,1,0:T(8,128)(2,1)S(1)}, u32[]{:S(2)}) %copy-start) | copy-done | bytes 6291480
  14.3 3.9 %collective-permute-start = (bf16[24,3,128]{2,1,0:T(4,128)(2,1)S(1)}, bf16[24,3,128]{2,1,0:T(4,128)(2,1)S(1)}, u32[]{:S(2)}, u32[]{:S(2)}) collective-permute-start(bf16[24,3,128]{2,1,0:T(4,128)(2,1)S(1)} %slice.20), channel_id=1, source_target_pairs={{0,1},{1,2},{2,3},{3,4},{4,5},{5,6},{6,7},{7,8},{8,9},{9,10},{10,1... | collective-permute-start | bytes 55304 | tf_op jit(solution)/shard_map/ppermute | solution.py:121
  18.3 1.5 %collective-permute-done.eq.ek.ev = bf16[24,3,128]{2,1,0:T(4,128)(2,1)S(1)} collective-permute-done((bf16[24,3,128]{2,1,0:T(4,128)(2,1)S(1)}, bf16[24,3,128]{2,1,0:T(4,128)(2,1)S(1)}, u32[]{:S(2)}, u32[]{:S(2)}) %collective-permute-start) | collective-permute-done | bytes 18464 | tf_op jit(solution)/shard_map/ppermute | solution.py:121
  19.7 0.0 copy-start.1
  19.8 0.6 copy-done.1
  20.4 9.7 %shard_map.64 = (bf16[8,1024,128]{2,1,0:T(8,128)(2,1)}, bf16[8,1024,128]{2,1,0:T(8,128)(2,1)}, bf16[8,1024,128]{2,1,0:T(8,128)(2,1)}, bf16[8,128,128]{2,1,0:T(8,128)(2,1)}) custom-call(bf16[24,1024,128]{2,1,0:T(8,128)(2,1)} %copy-done, bf16[24,1024,128]{2,1,0:T(8,128)(2,1)} %copy-done, bf16[24,1024,128]{2,1,0:T(8,128)(2,1)} %copy-done, ...), custom_call_target="tpu_custom_call" | custom-call | flops 306184192 | bytes 12582912 | tf_op jit(solution)/shard_map/pallas_call | solution.py:127
  30.1 5.7 %all-to-all-start = ((bf16[4,2,128,128]{3,2,1,0:T(8,128)(2,1)}), bf16[4,2,128,128]{3,2,1,0:T(8,128)(2,1)S(1)}, u32[]{:S(2)}, u32[]{:S(2)}) async-start(bf16[4,2,128,128]{3,2,1,0:T(8,128)(2,1)} %bitcast.38), calls=%async_computation | async-start | bytes 524288 | tf_op jit(solution)/shard_map/all_to_all | solution.py:25
  35.8 0.1 mul.65
  35.9 0.1 mul.66
  36.0 6.5 %all-to-all-done = bf16[4,2,128,128]{3,2,1,0:T(8,128)(2,1)S(1)} async-done(((bf16[4,2,128,128]{3,2,1,0:T(8,128)(2,1)}), bf16[4,2,128,128]{3,2,1,0:T(8,128)(2,1)S(1)}, u32[]{:S(2)}, u32[]{:S(2)}) %all-to-all-start) | async-done | bytes 262176 | tf_op jit(solution)/shard_map/all_to_all | solution.py:25
  42.6 0.2 pad_maximum_fusion
  42.7 1.3 %fusion.11 = bf16[16,2,128,128]{3,2,1,0:T(8,128)(2,1)} fusion(f32[4,2,128,128]{3,2,1,0:T(8,128)S(1)} %get-tuple-element.16, f32[16]{0:T(128)S(1)} %mul.66, f32[4,2,128,128]{3,2,1,0:T(8,128)S(1)} %get-tuple-element.17), kind=kLoop, calls=%fused_computation.13 | loop fusion | flops 1572864 | bytes 2097216 | tf_op jit(solution)/shard_map/convert_element_type | solution.py:38
  44.1 5.4 %all-to-all-start.1 = ((bf16[16,2,128,128]{3,2,1,0:T(8,128)(2,1)}), bf16[16,2,128,128]{3,2,1,0:T(8,128)(2,1)S(1)}, u32[]{:S(2)}, u32[]{:S(2)}) async-start(bf16[16,2,128,128]{3,2,1,0:T(8,128)(2,1)} %fusion.11), calls=%async_computation.1 | async-start | bytes 2097152 | tf_op jit(solution)/shard_map/all_to_all | solution.py:37
  49.4 10.2 %shard_map.65.local_ref = f32[8,1024,128]{2,1,0:T(8,128)} custom-call(bf16[8,1024,128]{2,1,0:T(8,128)(2,1)} %get-tuple-element.9.q_ref, bf16[8,1024,128]{2,1,0:T(8,128)(2,1)} %get-tuple-element.10.k_ref, bf16[8,1024,128]{2,1,0:T(8,128)(2,1)} %get-tuple-element.11.v_ref), custom_call_target="tpu_custom_call" | custom-call | flops 2952790016 | bytes 10485760 | tf_op jit(solution)/shard_map/pallas_call | solution.py:144
  59.6 5.0 %all-to-all-done.1 = bf16[16,2,128,128]{3,2,1,0:T(8,128)(2,1)S(1)} async-done(((bf16[16,2,128,128]{3,2,1,0:T(8,128)(2,1)}), bf16[16,2,128,128]{3,2,1,0:T(8,128)(2,1)S(1)}, u32[]{:S(2)}, u32[]{:S(2)}) %all-to-all-start.1) | async-done | bytes 1048608 | tf_op jit(solution)/shard_map/all_to_all | solution.py:37
  64.6 1.0 %convert_reduce_fusion = f32[4,2,128,128]{3,2,1,0:T(8,128)} fusion(bf16[4,4,2,128,128]{4,3,2,1,0:T(8,128)(2,1)S(1)} %bitcast.33), kind=kLoop, calls=%fused_computation.10 | loop fusion | flops 917504 | bytes 1572864 | tf_op jit(solution)/shard_map/reduce_sum | solution.py:44
  65.6 8.6 %shard_map.66 = bf16[1024,1024]{1,0:T(8,128)(2,1)} custom-call(bf16[8,1024,128]{2,1,0:T(8,128)(2,1)} %get-tuple-element.9.q_ref, f32[8,1024,128]{2,1,0:T(8,128)} %shard_map.65.local_ref, f32[8,128,128]{2,1,0:T(8,128)} %bitcast.34, f32[8,1,128]{2,1,0:T(1,128)} %bitcast.39, bf16[1024,1024]{1,0:T(8,128)(2,1)} %w_ref.1), custom_call_target="tpu_custom_call" | custom-call | flops 2684354560 | bytes 10485760 | tf_op jit(solution)/shard_map/pallas_call | solution.py:160
  (8 shorter events, 0.1 us)
Async XLA Ops:
  11.7 2.7 %copy-start = (bf16[24,1024,128]{2,1,0:T(8,128)(2,1)}, bf16[24,1024,128]{2,1,0:T(8,128)(2,1)S(1)}, u32[]{:S(2)}) copy-start(bf16[24,1024,128]{2,1,0:T(8,128)(2,1)S(1)} %convert_bitcast_fusion.pq.pk.pv) | copy-start | bytes 18874372
  14.3 5.4 %collective-permute-start = (bf16[24,3,128]{2,1,0:T(4,128)(2,1)S(1)}, bf16[24,3,128]{2,1,0:T(4,128)(2,1)S(1)}, u32[]{:S(2)}, u32[]{:S(2)}) collective-permute-start(bf16[24,3,128]{2,1,0:T(4,128)(2,1)S(1)} %slice.20), channel_id=1, source_target_pairs={{0,1},{1,2},{2,3},{3,4},{4,5},{5,6},{6,7},{7,8},{8,9},{9,10},{10,1... | collective-permute-start | bytes 55304 | tf_op jit(solution)/shard_map/ppermute | solution.py:121
  19.7 0.6 copy-start.1
  30.1 12.4 %all-to-all-start = ((bf16[4,2,128,128]{3,2,1,0:T(8,128)(2,1)}), bf16[4,2,128,128]{3,2,1,0:T(8,128)(2,1)S(1)}, u32[]{:S(2)}, u32[]{:S(2)}) async-start(bf16[4,2,128,128]{3,2,1,0:T(8,128)(2,1)} %bitcast.38), calls=%async_computation | async-start | bytes 524288 | tf_op jit(solution)/shard_map/all_to_all | solution.py:25
  44.1 20.5 %all-to-all-start.1 = ((bf16[16,2,128,128]{3,2,1,0:T(8,128)(2,1)}), bf16[16,2,128,128]{3,2,1,0:T(8,128)(2,1)S(1)}, u32[]{:S(2)}, u32[]{:S(2)}) async-start(bf16[16,2,128,128]{3,2,1,0:T(8,128)(2,1)} %fusion.11), calls=%async_computation.1 | async-start | bytes 2097152 | tf_op jit(solution)/shard_map/all_to_all | solution.py:37
